TPU v7x, 768 devices: a whole 4x8x12 slice. The times are simulated.
768 devices in a mesh: pipe: 4 (over x), row: 24 (over z, core), col: 8 (over y).
Axes of the slice: x: 4, y: 8, z: 12, core: 2. Of those that a mesh axis runs over, the one named last changes fastest.
Arguments:
- grad_out: bfloat16 [4, 6144, 4608], P('pipe', 'row', 'col'), may hold values from -6 to 6
- out_weight: bfloat16 [4, 2048, 4608], P('pipe', 'col', 'row'), may hold values from -0.09375 to 0.09375
- query_act: bfloat16 [4, 6144, 2048], P('pipe', 'row', 'col'), may hold values from -6 to 6
- key_act: bfloat16 [4, 6144, 1024], P('pipe', 'row', 'col'), may hold values from -18 to 18
- value_act: bfloat16 [4, 6144, 1024], P('pipe', 'row', 'col'), may hold values from -6 to 6
- doc_ids: int32 [4, 6144], P('pipe'), may hold values from 0 to 7, never falling along the last dimension, each value on 1 to 1536 neighbouring positions
- doc_shared: int32 [4, 8], P('pipe'), may hold values 0 or 1
Outputs:
- grad_query: bfloat16 [4, 6144, 2048], P('pipe', 'row', 'col')
- grad_key: bfloat16 [4, 6144, 1024], P('pipe', 'row', 'col')
- grad_value: bfloat16 [4, 6144, 1024], P('pipe', 'row', 'col')
- grad_resid: bfloat16 [4, 6144, 4608], P('pipe', 'row', 'col')
Inputs may be any that keep to these rules, and one draw needn't show every extreme that they name: `doc_ids`: never falling along each section's tokens; each document has 1 to 1536 tokens, one exactly 1536.
All inputs are finite; a program needn't handle non-finite values. No bound on the sum of `doc_shared` on one device may be relied on, other than what follows from the above.
Results may differ from a plain program's by a relative error of at most 0.0058.
Values may be sent and summed in bfloat16 or wider, within the bound.
No kernel may reach another device: no remote copies, remote signals or barrier semaphores. Data moves between devices by JAX's collectives and lax.ppermute only.
A program may use at most 32 MiB of HBM per device.

v0:
```python
import jax
import jax.numpy as jnp
from jax import lax
from jax.sharding import PartitionSpec as P

HD = 128
WINDOW = 4096


logit_cap = 50.0
score_scale = 144.0 ** (-0.5)


def from_behind(block, axis, distance):
    devices = range(lax.axis_size(axis))
    route = [(i - distance, i) for i in devices if i - distance in devices]
    return lax.ppermute(block, axis, route)


def attend(query_act, key_near, value_near, d_attn, allowed):
    tok_rows = query_act.shape[0]
    span_rows = key_near.shape[0]
    key_width = key_near.shape[1]
    groups = key_width // HD
    query_heads = jnp.moveaxis(query_act.reshape(tok_rows, 2 * groups, HD), 1, 0)
    attn_heads = jnp.moveaxis(d_attn.reshape(tok_rows, 2 * groups, HD), 1, 0)
    key_heads = jnp.moveaxis(key_near.reshape(span_rows, groups, HD), 1, 0)
    value_heads = jnp.moveaxis(value_near.reshape(span_rows, groups, HD), 1, 0)

    def one_head(running, head_items):
        key_sums, value_sums = running
        head_index, query_h, attn_h = head_items
        group_index = head_index // 2
        key_g = lax.dynamic_index_in_dim(key_heads, group_index, 0, keepdims=False)
        value_g = lax.dynamic_index_in_dim(value_heads, group_index, 0, keepdims=False)
        raw_scores = (
            lax.dot_general(
                query_h, key_g, (((1,), (1,)), ((), ())), preferred_element_type=jnp.float32
            )
            * score_scale
        )
        capped = jnp.tanh(raw_scores / logit_cap)
        weights = jnp.where(allowed, jnp.exp(logit_cap * capped), 0.0)
        attn_probs = weights / jnp.sum(weights, axis=-1, keepdims=True)
        probs_low = attn_probs.astype(jnp.bfloat16)
        value_part = lax.dot_general(
            probs_low, attn_h, (((0,), (0,)), ((), ())), preferred_element_type=jnp.float32
        )
        grad_probs = lax.dot_general(
            attn_h, value_g, (((1,), (1,)), ((), ())), preferred_element_type=jnp.float32
        )
        row_delta = jnp.sum(attn_probs * grad_probs, axis=-1, keepdims=True)
        grad_raw = (
            attn_probs * (grad_probs - row_delta) * (1.0 - capped * capped) * score_scale
        ).astype(jnp.bfloat16)
        query_grad = jnp.dot(grad_raw, key_g, preferred_element_type=jnp.float32).astype(
            jnp.bfloat16
        )
        key_part = lax.dot_general(
            grad_raw, query_h, (((0,), (0,)), ((), ())), preferred_element_type=jnp.float32
        )
        key_sums = lax.dynamic_update_index_in_dim(
            key_sums,
            lax.dynamic_index_in_dim(key_sums, group_index, 0, keepdims=False) + key_part,
            group_index,
            0,
        )
        value_sums = lax.dynamic_update_index_in_dim(
            value_sums,
            lax.dynamic_index_in_dim(value_sums, group_index, 0, keepdims=False) + value_part,
            group_index,
            0,
        )
        return ((key_sums, value_sums), query_grad)

    zero_sums = jnp.zeros((groups, span_rows, HD), jnp.float32)
    head_numbers = jnp.arange(2 * groups, dtype=jnp.int32)
    (key_sums, value_sums), query_grads = lax.scan(
        one_head, (zero_sums, zero_sums), (head_numbers, query_heads, attn_heads)
    )
    query_grad = jnp.moveaxis(query_grads, 0, 1).reshape(tok_rows, 2 * groups * HD)
    key_sum = jnp.moveaxis(key_sums, 0, 1).reshape(span_rows, key_width)
    value_sum = jnp.moveaxis(value_sums, 0, 1).reshape(span_rows, key_width)
    return (query_grad, key_sum, value_sum)


def shared_lookup(key_doc, shared_flags):
    doc_numbers = jnp.arange(shared_flags.shape[0], dtype=jnp.int32)
    return jnp.sum(
        jnp.where(key_doc[:, None] == doc_numbers[None, :], shared_flags[None, :], 0), axis=1
    )


def per_device(grad_out, out_weight, query_act, key_act, value_act, doc_ids, doc_shared):
    grad_tile = grad_out[0]
    tok_rows = grad_tile.shape[0]
    grad_rows = lax.all_gather(grad_tile, "col", axis=1, tiled=True)
    d_attn = lax.dot_general(
        grad_rows,
        lax.all_gather(out_weight[0], "row", axis=1, tiled=True),
        (((1,), (1,)), ((), ())),
        preferred_element_type=jnp.float32,
    ).astype(jnp.bfloat16)
    reach_rows = min(lax.axis_size("row") - 1, WINDOW // tok_rows)
    span_rows = (reach_rows + 1) * tok_rows
    row_index = lax.axis_index("row")
    query_start = row_index * tok_rows
    doc_list = doc_ids[0]
    shared_flags = doc_shared[0]
    query_local = query_act[0]
    key_local = key_act[0]
    value_local = value_act[0]
    key_width = key_local.shape[1]
    key_all, value_all = (
        lax.all_gather(key_local, "row", axis=0, tiled=True),
        lax.all_gather(value_local, "row", axis=0, tiled=True),
    )
    lead_rows = jnp.zeros((reach_rows * tok_rows, key_width), key_all.dtype)
    key_near = lax.dynamic_slice_in_dim(
        jnp.concatenate([lead_rows, key_all], axis=0), query_start, span_rows, 0
    )
    value_near = lax.dynamic_slice_in_dim(
        jnp.concatenate([lead_rows, value_all], axis=0), query_start, span_rows, 0
    )
    key_start = query_start - reach_rows * tok_rows
    key_pos = key_start + jnp.arange(span_rows, dtype=jnp.int32)
    query_pos = query_start + jnp.arange(tok_rows, dtype=jnp.int32)
    query_doc = lax.dynamic_slice_in_dim(doc_list, query_start, tok_rows)
    padded_docs = jnp.concatenate([jnp.full((reach_rows * tok_rows,), -1, jnp.int32), doc_list])
    key_doc = lax.dynamic_slice_in_dim(padded_docs, query_start, span_rows)
    key_shared = shared_lookup(key_doc, shared_flags)
    allowed = (
        (key_pos[None, :] >= 0)
        & (key_pos[None, :] <= query_pos[:, None])
        & (query_pos[:, None] - key_pos[None, :] < WINDOW)
    )
    allowed = allowed & ((key_doc[None, :] == query_doc[:, None]) | (key_shared[None, :] == 1))
    query_grad, key_sum, value_sum = attend(query_local, key_near, value_near, d_attn, allowed)
    key_total = key_sum[reach_rows * tok_rows :]
    value_total = value_sum[reach_rows * tok_rows :]
    for distance in range(1, reach_rows + 1):
        low_row = (reach_rows - distance) * tok_rows
        back_key, back_value = from_behind(
            (key_sum[low_row : low_row + tok_rows], value_sum[low_row : low_row + tok_rows]),
            "row",
            -distance,
        )
        key_total = key_total + back_key
        value_total = value_total + back_value
    handed = from_behind(
        (query_grad, key_total.astype(jnp.bfloat16), value_total.astype(jnp.bfloat16), grad_tile),
        "pipe",
        -1,
    )
    return (handed[0][None], handed[1][None], handed[2][None], handed[3][None])


def solution(mesh):
    in_specs = (
        P("pipe", "row", "col"),
        P("pipe", "col", "row"),
        P("pipe", "row", "col"),
        P("pipe", "row", "col"),
        P("pipe", "row", "col"),
        P("pipe", None),
        P("pipe", None),
    )
    out_specs = (
        P("pipe", "row", "col"),
        P("pipe", "row", "col"),
        P("pipe", "row", "col"),
        P("pipe", "row", "col"),
    )
    return jax.shard_map(
        per_device, mesh=mesh, in_specs=in_specs, out_specs=out_specs, check_vma=False
    )
```

profile of v0, /device:TPU:91, one launch (start us, length us, event | category | flops | bytes accessed | tf_op | source)
XLA Modules:
  0.0 552.9 jit_solution(14749021295390775401)
XLA Ops:
  13.3 61.1 %all-gather.9.cloned.1.call-done = bf16[1,6144,128]{2,1,0:T(8,128)(2,1)} async-done(((bf16[1,256,128]{2,1,0:T(8,128)(2,1)}), bf16[1,6144,128]{2,1,0:T(8,128)(2,1)}) %all-gather.9.cloned.1.call-update) | async-done | bytes 1572880 | tf_op jit(solution)/shard_map/all_gather | solution.py:115
  74.4 1.3 fusion.35
  75.6 57.7 %all-gather.15.cloned.1.call-done = bf16[1,6144,128]{2,1,0:T(8,128)(2,1)} async-done(((bf16[1,256,128]{2,1,0:T(8,128)(2,1)}), bf16[1,6144,128]{2,1,0:T(8,128)(2,1)}) %all-gather.15.cloned.1.call-update) | async-done | bytes 1572880 | tf_op jit(solution)/shard_map/all_gather | solution.py:116
  133.4 2.3 fusion.36
  135.7 40.0 %all-gather.11.cloned.1.call-done = bf16[1,256,4608]{1,2,0:T(8,128)(2,1)} async-done(((bf16[1,256,576]{1,2,0:T(8,128)(2,1)}), bf16[1,256,4608]{1,2,0:T(8,128)(2,1)}) %all-gather.11.cloned.1.call-update) | async-done | bytes 2359312 | tf_op jit(solution)/shard_map/all_gather | solution.py:97
  175.7 65.3 %all-gather.13.cloned.1.call-done = bf16[1,256,4608]{1,2,0:T(8,128)(2,1)} async-done(((bf16[1,256,192]{1,2,0:T(8,128)(2,1)}), bf16[1,256,4608]{1,2,0:T(8,128)(2,1)}) %all-gather.13.cloned.1.call-update) | async-done | bytes 2359312 | tf_op jit(solution)/shard_map/all_gather | solution.py:100
  241.0 3.4 fusion.30
  245.3 1.5 broadcast_in_dim.77.clone
  246.9 38.4 %while.18 = (s32[]{:T(128)}, f32[1,4352,128]{2,1,0:T(8,128)S(1)}, f32[1,4352,128]{2,1,0:T(8,128)}, bf16[2,256,128]{2,1,0:T(8,128)(2,1)}, bf16[2,256,128]{1,2,0:T...) while((s32[]{:T(128)}, f32[1,4352,128]{2,1,0:T(8,128)S(1)}, ...), condition=%wide.region_4.5_spmd.clone, body=%wide.region_1.4_spmd.clone.sunk | while | flops 1488485888 | bytes 52247312 | solution.py:78
  246.9 3.3 fusion.88
  250.2 3.2 multiply_reduce_fusion.2
  253.4 3.8 multiply_convert_fusion.2
  257.2 1.4 fusion.89
  260.0 6.0 %fusion.90 = f32[1,4352,128]{2,1,0:T(8,128)} fusion(f32[1,4352,128]{2,1,0:T(8,128)} %get-tuple-element.384, bf16[2,256,128]{2,1,0:T(8,128)(2,1)S(1)} %copy-done.5, s32[]{:T(128)} %get-tuple-element.382, f32[256]{0:T(256)S(1)} %get-tuple-element.364, f32[256,4352]{1,0:T(8,128)S(1)} %get-tuple-element.363, pred[4352]{0:T(1024)(128)(4,1)S(1)} %get-tuple-element.410, ...), kind=kOutput, calls=%fused_computation.6.clone.1 | convolution fusion | flops 299139072 | bytes 9032708 | tf_op jit(solution)/shard_map/while/body/eval_jaxpr/dot_general | solution.py:46
  266.1 3.3 fusion.88
  269.4 3.2 multiply_reduce_fusion.2
  272.6 3.8 multiply_convert_fusion.2
  276.4 1.4 fusion.89
  279.2 6.0 %fusion.90 = f32[1,4352,128]{2,1,0:T(8,128)} fusion(f32[1,4352,128]{2,1,0:T(8,128)} %get-tuple-element.384, bf16[2,256,128]{2,1,0:T(8,128)(2,1)S(1)} %copy-done.5, s32[]{:T(128)} %get-tuple-element.382, f32[256]{0:T(256)S(1)} %get-tuple-element.364, f32[256,4352]{1,0:T(8,128)S(1)} %get-tuple-element.363, pred[4352]{0:T(1024)(128)(4,1)S(1)} %get-tuple-element.410, ...), kind=kOutput, calls=%fused_computation.6.clone.1 | convolution fusion | flops 299139072 | bytes 9032708 | tf_op jit(solution)/shard_map/while/body/eval_jaxpr/dot_general | solution.py:46
  285.3 1.7 slice_bitcast_fusion.15
  287.0 2.3 collective-permute-start.18
  289.4 4.0 collective-permute-start.19
  293.3 1.9 collective-permute-start.20
  295.3 1.3 collective-permute-start.21
  296.6 1.3 collective-permute-start.22
  297.9 1.3 collective-permute-start.23
  299.2 1.3 collective-permute-start.24
  300.5 3.4 collective-permute-done.20
  303.9 1.3 collective-permute-start.25
  305.2 3.9 collective-permute-done.21
  309.1 1.3 collective-permute-start.26
  310.3 5.1 collective-permute-done.22
  315.5 1.3 collective-permute-start.27
  316.8 4.8 collective-permute-done.23
  321.6 1.3 collective-permute-start.28
  322.9 18.9 %collective-permute-done.24 = f32[256,128]{1,0:T(8,128)S(1)} collective-permute-done((f32[256,128]{1,0:T(8,128)S(1)}, f32[256,128]{1,0:T(8,128)S(1)}, u32[]{:S(2)}, u32[]{:S(2)}) %collective-permute-start.24) | collective-permute-done | bytes 131104 | tf_op jit(solution)/shard_map/ppermute | solution.py:17
  343.2 3.1 collective-permute-done.25
  347.6 4.7 collective-permute-done.26
  353.6 6.7 %collective-permute-done.27 = f32[256,128]{1,0:T(8,128)S(1)} collective-permute-done((f32[256,128]{1,0:T(8,128)S(1)}, f32[256,128]{1,0:T(8,128)S(1)}, u32[]{:S(2)}, u32[]{:S(2)}) %collective-permute-start.27) | collective-permute-done | bytes 131104 | tf_op jit(solution)/shard_map/ppermute | solution.py:17
  361.6 32.7 %collective-permute-done.28 = f32[256,128]{1,0:T(8,128)S(1)} collective-permute-done((f32[256,128]{1,0:T(8,128)S(1)}, f32[256,128]{1,0:T(8,128)S(1)}, u32[]{:S(2)}, u32[]{:S(2)}) %collective-permute-start.28) | collective-permute-done | bytes 131104 | tf_op jit(solution)/shard_map/ppermute | solution.py:17
  395.6 1.7 collective-permute-done.29
  397.2 2.6 collective-permute-start.1
  399.8 1.3 collective-permute-start.10
  401.1 1.3 collective-permute-start.11
  402.5 1.3 collective-permute-start.12
  405.3 1.3 collective-permute-start.14
  406.6 15.1 %collective-permute-done.10 = f32[256,128]{1,0:T(8,128)S(1)} collective-permute-done((f32[256,128]{1,0:T(8,128)S(1)}, f32[256,128]{1,0:T(8,128)S(1)}, u32[]{:S(2)}, u32[]{:S(2)}) %collective-permute-start.10) | collective-permute-done | bytes 131104 | tf_op jit(solution)/shard_map/ppermute | solution.py:17
  423.0 6.8 %collective-permute-done.11 = f32[256,128]{1,0:T(8,128)S(1)} collective-permute-done((f32[256,128]{1,0:T(8,128)S(1)}, f32[256,128]{1,0:T(8,128)S(1)}, u32[]{:S(2)}, u32[]{:S(2)}) %collective-permute-start.11) | collective-permute-done | bytes 131104 | tf_op jit(solution)/shard_map/ppermute | solution.py:17
  431.1 1.9 collective-permute-start.2
  433.0 1.9 collective-permute-start.3
  435.0 1.3 collective-permute-start.4
  436.3 6.3 %collective-permute-done.15 = f32[256,128]{1,0:T(8,128)S(1)} collective-permute-done((f32[256,128]{1,0:T(8,128)S(1)}, f32[256,128]{1,0:T(8,128)S(1)}, u32[]{:S(2)}, u32[]{:S(2)}) %collective-permute-start.15) | collective-permute-done | bytes 131104 | tf_op jit(solution)/shard_map/ppermute | solution.py:17
  443.8 25.5 %collective-permute-done.16 = f32[256,128]{1,0:T(8,128)S(1)} collective-permute-done((f32[256,128]{1,0:T(8,128)S(1)}, f32[256,128]{1,0:T(8,128)S(1)}, u32[]{:S(2)}, u32[]{:S(2)}) %collective-permute-start.16) | collective-permute-done | bytes 131104 | tf_op jit(solution)/shard_map/ppermute | solution.py:17
  469.3 1.3 collective-permute-start.6
  470.6 1.3 collective-permute-start.7
  474.4 11.3 %collective-permute-done.4 = f32[256,128]{1,0:T(8,128)S(1)} collective-permute-done((f32[256,128]{1,0:T(8,128)S(1)}, f32[256,128]{1,0:T(8,128)S(1)}, u32[]{:S(2)}, u32[]{:S(2)}) %collective-permute-start.4) | collective-permute-done | bytes 131104 | tf_op jit(solution)/shard_map/ppermute | solution.py:17
  488.1 10.0 %collective-permute-done.5 = f32[256,128]{1,0:T(8,128)S(1)} collective-permute-done((f32[256,128]{1,0:T(8,128)S(1)}, f32[256,128]{1,0:T(8,128)S(1)}, u32[]{:S(2)}, u32[]{:S(2)}) %collective-permute-start.5) | collective-permute-done | bytes 131104 | tf_op jit(solution)/shard_map/ppermute | solution.py:17
  498.1 1.9 collective-permute-start.35
  500.0 1.9 collective-permute-start
  501.9 18.8 %collective-permute-done.7 = f32[256,128]{1,0:T(8,128)S(1)} collective-permute-done((f32[256,128]{1,0:T(8,128)S(1)}, f32[256,128]{1,0:T(8,128)S(1)}, u32[]{:S(2)}, u32[]{:S(2)}) %collective-permute-start.7) | collective-permute-done | bytes 131104 | tf_op jit(solution)/shard_map/ppermute | solution.py:17
  520.7 3.0 collective-permute-start.34
  523.7 14.9 %collective-permute-done.9 = f32[256,128]{1,0:T(8,128)S(1)} collective-permute-done((f32[256,128]{1,0:T(8,128)S(1)}, f32[256,128]{1,0:T(8,128)S(1)}, u32[]{:S(2)}, u32[]{:S(2)}) %collective-permute-start.9) | collective-permute-done | bytes 131104 | tf_op jit(solution)/shard_map/ppermute | solution.py:17
  538.7 1.9 collective-permute-start.17
  540.7 3.0 collective-permute-done.17
  (76 shorter events, 29.4 us)
Async XLA Ops:
  7.2 67.2 %all-gather.9.cloned.1.call-start = ((), (), s32[]{:S(2)}) async-start(), calls=%async_computation | async-start | bytes 1638400 | tf_op jit(solution)/shard_map/all_gather | solution.py:115
  7.9 125.5 %all-gather.15.cloned.1.call-start = ((), (), s32[]{:S(2)}) async-start(), calls=%async_computation.3 | async-start | bytes 1638400 | tf_op jit(solution)/shard_map/all_gather | solution.py:116
  8.6 167.1 %all-gather.11.cloned.1.call-start = ((), (), s32[]{:S(2)}) async-start(), calls=%async_computation.1 | async-start | bytes 2654208 | tf_op jit(solution)/shard_map/all_gather | solution.py:97
  9.4 231.6 %all-gather.13.cloned.1.call-start = ((), (), s32[]{:S(2)}) async-start(), calls=%async_computation.2 | async-start | bytes 2457600 | tf_op jit(solution)/shard_map/all_gather | solution.py:100
  246.9 3.3 copy-start
  246.9 3.3 copy-start.5
  257.2 1.4 copy-start.2
  259.4 0.7 copy-start.3
  266.1 3.3 copy-start
  266.1 3.3 copy-start.5
  276.4 1.4 copy-start.2
  278.6 0.7 copy-start.3
  287.0 149.2 %copy-start.4 = (bf16[2,256,128]{2,1,0:T(8,128)(2,1)S(1)}, bf16[2,256,128]{2,1,0:T(8,128)(2,1)}, u32[]{:S(2)}) copy-start(bf16[2,256,128]{2,1,0:T(8,128)(2,1)} %get-tuple-element.141) | copy-start | bytes 393220
  287.0 10.9 %collective-permute-start.18 = (f32[256,128]{1,0:T(8,128)S(1)}, f32[256,128]{1,0:T(8,128)S(1)}, u32[]{:S(2)}, u32[]{:S(2)}) collective-permute-start(f32[256,128]{1,0:T(8,128)S(1)} %get-tuple-element.240), channel_id=1, source_target_pairs={{8,0},{16,8},{24,16},{32,24},{40,32},{48,40},{56,48},{64,56},{72,6... | collective-permute-start | bytes 393224 | tf_op jit(solution)/shard_map/ppermute | solution.py:17
  289.4 9.8 %collective-permute-start.19 = (f32[256,128]{1,0:T(8,128)S(1)}, f32[256,128]{1,0:T(8,128)S(1)}, u32[]{:S(2)}, u32[]{:S(2)}) collective-permute-start(f32[256,128]{1,0:T(8,128)S(1)} %get-tuple-element.254), channel_id=1, source_target_pairs={{16,0},{24,8},{32,16},{40,24},{48,32},{56,40},{64,48},{72,56},{80,... | collective-permute-start | bytes 393224 | tf_op jit(solution)/shard_map/ppermute | solution.py:17
  293.3 10.6 %collective-permute-start.20 = (f32[256,128]{1,0:T(8,128)S(1)}, f32[256,128]{1,0:T(8,128)S(1)}, u32[]{:S(2)}, u32[]{:S(2)}) collective-permute-start(f32[256,128]{1,0:T(8,128)S(1)} %get-tuple-element.253), channel_id=1, source_target_pairs={{24,0},{32,8},{40,16},{48,24},{56,32},{64,40},{72,48},{80,56},{88,... | collective-permute-start | bytes 393224 | tf_op jit(solution)/shard_map/ppermute | solution.py:17
  295.3 13.8 %collective-permute-start.21 = (f32[256,128]{1,0:T(8,128)S(1)}, f32[256,128]{1,0:T(8,128)S(1)}, u32[]{:S(2)}, u32[]{:S(2)}) collective-permute-start(f32[256,128]{1,0:T(8,128)S(1)} %get-tuple-element.252), channel_id=1, source_target_pairs={{32,0},{40,8},{48,16},{56,24},{64,32},{72,40},{80,48},{88,56},{96,... | collective-permute-start | bytes 393224 | tf_op jit(solution)/shard_map/ppermute | solution.py:17
  296.6 18.9 %collective-permute-start.22 = (f32[256,128]{1,0:T(8,128)S(1)}, f32[256,128]{1,0:T(8,128)S(1)}, u32[]{:S(2)}, u32[]{:S(2)}) collective-permute-start(f32[256,128]{1,0:T(8,128)S(1)} %get-tuple-element.251), channel_id=1, source_target_pairs={{40,0},{48,8},{56,16},{64,24},{72,32},{80,40},{88,48},{96,56},{104... | collective-permute-start | bytes 393224 | tf_op jit(solution)/shard_map/ppermute | solution.py:17
  297.9 23.7 %collective-permute-start.23 = (f32[256,128]{1,0:T(8,128)S(1)}, f32[256,128]{1,0:T(8,128)S(1)}, u32[]{:S(2)}, u32[]{:S(2)}) collective-permute-start(f32[256,128]{1,0:T(8,128)S(1)} %get-tuple-element.250), channel_id=1, source_target_pairs={{48,0},{56,8},{64,16},{72,24},{80,32},{88,40},{96,48},{104,56},{11... | collective-permute-start | bytes 393224 | tf_op jit(solution)/shard_map/ppermute | solution.py:17
  299.2 42.6 %collective-permute-start.24 = (f32[256,128]{1,0:T(8,128)S(1)}, f32[256,128]{1,0:T(8,128)S(1)}, u32[]{:S(2)}, u32[]{:S(2)}) collective-permute-start(f32[256,128]{1,0:T(8,128)S(1)} %get-tuple-element.249), channel_id=1, source_target_pairs={{56,0},{64,8},{72,16},{80,24},{88,32},{96,40},{104,48},{112,56},{1... | collective-permute-start | bytes 393224 | tf_op jit(solution)/shard_map/ppermute | solution.py:17
  303.9 42.4 %collective-permute-start.25 = (f32[256,128]{1,0:T(8,128)S(1)}, f32[256,128]{1,0:T(8,128)S(1)}, u32[]{:S(2)}, u32[]{:S(2)}) collective-permute-start(f32[256,128]{1,0:T(8,128)S(1)} %get-tuple-element.248), channel_id=1, source_target_pairs={{64,0},{72,8},{80,16},{88,24},{96,32},{104,40},{112,48},{120,56},{... | collective-permute-start | bytes 393224 | tf_op jit(solution)/shard_map/ppermute | solution.py:17
  309.1 43.3 %collective-permute-start.26 = (f32[256,128]{1,0:T(8,128)S(1)}, f32[256,128]{1,0:T(8,128)S(1)}, u32[]{:S(2)}, u32[]{:S(2)}) collective-permute-start(f32[256,128]{1,0:T(8,128)S(1)} %get-tuple-element.247), channel_id=1, source_target_pairs={{72,0},{80,8},{88,16},{96,24},{104,32},{112,40},{120,48},{128,56},... | collective-permute-start | bytes 393224 | tf_op jit(solution)/shard_map/ppermute | solution.py:17
  315.5 44.8 %collective-permute-start.27 = (f32[256,128]{1,0:T(8,128)S(1)}, f32[256,128]{1,0:T(8,128)S(1)}, u32[]{:S(2)}, u32[]{:S(2)}) collective-permute-start(f32[256,128]{1,0:T(8,128)S(1)} %get-tuple-element.246), channel_id=1, source_target_pairs={{80,0},{88,8},{96,16},{104,24},{112,32},{120,40},{128,48},{136,56}... | collective-permute-start | bytes 393224 | tf_op jit(solution)/shard_map/ppermute | solution.py:17
  321.6 72.7 %collective-permute-start.28 = (f32[256,128]{1,0:T(8,128)S(1)}, f32[256,128]{1,0:T(8,128)S(1)}, u32[]{:S(2)}, u32[]{:S(2)}) collective-permute-start(f32[256,128]{1,0:T(8,128)S(1)} %get-tuple-element.245), channel_id=1, source_target_pairs={{88,0},{96,8},{104,16},{112,24},{120,32},{128,40},{136,48},{144,56... | collective-permute-start | bytes 393224 | tf_op jit(solution)/shard_map/ppermute | solution.py:17
  341.8 55.5 %collective-permute-start.29 = (f32[256,128]{1,0:T(8,128)S(1)}, f32[256,128]{1,0:T(8,128)S(1)}, u32[]{:S(2)}, u32[]{:S(2)}) collective-permute-start(f32[256,128]{1,0:T(8,128)S(1)} %get-tuple-element.244), channel_id=1, source_target_pairs={{96,0},{104,8},{112,16},{120,24},{128,32},{136,40},{144,48},{152,5... | collective-permute-start | bytes 393224 | tf_op jit(solution)/shard_map/ppermute | solution.py:17
  343.2 154.8 %copy-start.1 = (bf16[1,256,576]{1,2,0:T(8,128)(2,1)S(1)}, bf16[1,256,576]{1,2,0:T(8,128)(2,1)}, u32[]{:S(2)}) copy-start(bf16[1,256,576]{1,2,0:T(8,128)(2,1)} %param.9) | copy-start | bytes 884740
  346.3 53.5 %collective-permute-start.30 = (f32[256,128]{1,0:T(8,128)S(1)}, f32[256,128]{1,0:T(8,128)S(1)}, u32[]{:S(2)}, u32[]{:S(2)}) collective-permute-start(f32[256,128]{1,0:T(8,128)S(1)} %get-tuple-element.243), channel_id=1, source_target_pairs={{104,0},{112,8},{120,16},{128,24},{136,32},{144,40},{152,48},{160,... | collective-permute-start | bytes 393224 | tf_op jit(solution)/shard_map/ppermute | solution.py:17
  352.3 48.8 %collective-permute-start.31 = (f32[256,128]{1,0:T(8,128)S(1)}, f32[256,128]{1,0:T(8,128)S(1)}, u32[]{:S(2)}, u32[]{:S(2)}) collective-permute-start(f32[256,128]{1,0:T(8,128)S(1)} %get-tuple-element.242), channel_id=1, source_target_pairs={{112,0},{120,8},{128,16},{136,24},{144,32},{152,40},{160,48},{168,... | collective-permute-start | bytes 393224 | tf_op jit(solution)/shard_map/ppermute | solution.py:17
  360.3 42.2 %collective-permute-start.32 = (f32[256,128]{1,0:T(8,128)S(1)}, f32[256,128]{1,0:T(8,128)S(1)}, u32[]{:S(2)}, u32[]{:S(2)}) collective-permute-start(f32[256,128]{1,0:T(8,128)S(1)} %get-tuple-element.241), channel_id=1, source_target_pairs={{120,0},{128,8},{136,16},{144,24},{152,32},{160,40},{168,48},{176,... | collective-permute-start | bytes 393224 | tf_op jit(solution)/shard_map/ppermute | solution.py:17
  394.3 9.8 %collective-permute-start.33 = (f32[256,128]{1,0:T(8,128)S(1)}, f32[256,128]{1,0:T(8,128)S(1)}, u32[]{:S(2)}, u32[]{:S(2)}) collective-permute-start(f32[256,128]{1,0:T(8,128)S(1)} %get-tuple-element.255), channel_id=1, source_target_pairs={{128,0},{136,8},{144,16},{152,24},{160,32},{168,40},{176,48},{184,... | collective-permute-start | bytes 393224 | tf_op jit(solution)/shard_map/ppermute | solution.py:17
  397.2 8.1 %collective-permute-start.1 = (f32[256,128]{1,0:T(8,128)S(1)}, f32[256,128]{1,0:T(8,128)S(1)}, u32[]{:S(2)}, u32[]{:S(2)}) collective-permute-start(f32[256,128]{1,0:T(8,128)S(1)} %get-tuple-element.256), channel_id=1, source_target_pairs={{8,0},{16,8},{24,16},{32,24},{40,32},{48,40},{56,48},{64,56},{72,6... | collective-permute-start | bytes 393224 | tf_op jit(solution)/shard_map/ppermute | solution.py:17
  399.8 21.9 %collective-permute-start.10 = (f32[256,128]{1,0:T(8,128)S(1)}, f32[256,128]{1,0:T(8,128)S(1)}, u32[]{:S(2)}, u32[]{:S(2)}) collective-permute-start(f32[256,128]{1,0:T(8,128)S(1)} %get-tuple-element.262), channel_id=1, source_target_pairs={{80,0},{88,8},{96,16},{104,24},{112,32},{120,40},{128,48},{136,56}... | collective-permute-start | bytes 393224 | tf_op jit(solution)/shard_map/ppermute | solution.py:17
  401.1 28.6 %collective-permute-start.11 = (f32[256,128]{1,0:T(8,128)S(1)}, f32[256,128]{1,0:T(8,128)S(1)}, u32[]{:S(2)}, u32[]{:S(2)}) collective-permute-start(f32[256,128]{1,0:T(8,128)S(1)} %get-tuple-element.261), channel_id=1, source_target_pairs={{88,0},{96,8},{104,16},{112,24},{120,32},{128,40},{136,48},{144,56... | collective-permute-start | bytes 393224 | tf_op jit(solution)/shard_map/ppermute | solution.py:17
  402.5 28.6 %collective-permute-start.12 = (f32[256,128]{1,0:T(8,128)S(1)}, f32[256,128]{1,0:T(8,128)S(1)}, u32[]{:S(2)}, u32[]{:S(2)}) collective-permute-start(f32[256,128]{1,0:T(8,128)S(1)} %get-tuple-element.260), channel_id=1, source_target_pairs={{96,0},{104,8},{112,16},{120,24},{128,32},{136,40},{144,48},{152,5... | collective-permute-start | bytes 393224 | tf_op jit(solution)/shard_map/ppermute | solution.py:17
  404.0 29.0 %collective-permute-start.13 = (f32[256,128]{1,0:T(8,128)S(1)}, f32[256,128]{1,0:T(8,128)S(1)}, u32[]{:S(2)}, u32[]{:S(2)}) collective-permute-start(f32[256,128]{1,0:T(8,128)S(1)} %get-tuple-element.259), channel_id=1, source_target_pairs={{104,0},{112,8},{120,16},{128,24},{136,32},{144,40},{152,48},{160,... | collective-permute-start | bytes 393224 | tf_op jit(solution)/shard_map/ppermute | solution.py:17
  405.3 29.6 %collective-permute-start.14 = (f32[256,128]{1,0:T(8,128)S(1)}, f32[256,128]{1,0:T(8,128)S(1)}, u32[]{:S(2)}, u32[]{:S(2)}) collective-permute-start(f32[256,128]{1,0:T(8,128)S(1)} %get-tuple-element.258), channel_id=1, source_target_pairs={{112,0},{120,8},{128,16},{136,24},{144,32},{152,40},{160,48},{168,... | collective-permute-start | bytes 393224 | tf_op jit(solution)/shard_map/ppermute | solution.py:17
  421.7 20.8 %collective-permute-start.15 = (f32[256,128]{1,0:T(8,128)S(1)}, f32[256,128]{1,0:T(8,128)S(1)}, u32[]{:S(2)}, u32[]{:S(2)}) collective-permute-start(f32[256,128]{1,0:T(8,128)S(1)} %get-tuple-element.257), channel_id=1, source_target_pairs={{120,0},{128,8},{136,16},{144,24},{152,32},{160,40},{168,48},{176,... | collective-permute-start | bytes 393224 | tf_op jit(solution)/shard_map/ppermute | solution.py:17
  429.8 39.5 %collective-permute-start.16 = (f32[256,128]{1,0:T(8,128)S(1)}, f32[256,128]{1,0:T(8,128)S(1)}, u32[]{:S(2)}, u32[]{:S(2)}) collective-permute-start(f32[256,128]{1,0:T(8,128)S(1)} %get-tuple-element.271), channel_id=1, source_target_pairs={{128,0},{136,8},{144,16},{152,24},{160,32},{168,40},{176,48},{184,... | collective-permute-start | bytes 393224 | tf_op jit(solution)/shard_map/ppermute | solution.py:17
  431.1 39.5 %collective-permute-start.2 = (f32[256,128]{1,0:T(8,128)S(1)}, f32[256,128]{1,0:T(8,128)S(1)}, u32[]{:S(2)}, u32[]{:S(2)}) collective-permute-start(f32[256,128]{1,0:T(8,128)S(1)} %get-tuple-element.270), channel_id=1, source_target_pairs={{16,0},{24,8},{32,16},{40,24},{48,32},{56,40},{64,48},{72,56},{80,... | collective-permute-start | bytes 393224 | tf_op jit(solution)/shard_map/ppermute | solution.py:17
  433.0 40.1 %collective-permute-start.3 = (f32[256,128]{1,0:T(8,128)S(1)}, f32[256,128]{1,0:T(8,128)S(1)}, u32[]{:S(2)}, u32[]{:S(2)}) collective-permute-start(f32[256,128]{1,0:T(8,128)S(1)} %get-tuple-element.269), channel_id=1, source_target_pairs={{24,0},{32,8},{40,16},{48,24},{56,32},{64,40},{72,48},{80,56},{88,... | collective-permute-start | bytes 393224 | tf_op jit(solution)/shard_map/ppermute | solution.py:17
  435.0 50.8 %collective-permute-start.4 = (f32[256,128]{1,0:T(8,128)S(1)}, f32[256,128]{1,0:T(8,128)S(1)}, u32[]{:S(2)}, u32[]{:S(2)}) collective-permute-start(f32[256,128]{1,0:T(8,128)S(1)} %get-tuple-element.268), channel_id=1, source_target_pairs={{32,0},{40,8},{48,16},{56,24},{64,32},{72,40},{80,48},{88,56},{96,... | collective-permute-start | bytes 393224 | tf_op jit(solution)/shard_map/ppermute | solution.py:17
  442.6 55.5 %collective-permute-start.5 = (f32[256,128]{1,0:T(8,128)S(1)}, f32[256,128]{1,0:T(8,128)S(1)}, u32[]{:S(2)}, u32[]{:S(2)}) collective-permute-start(f32[256,128]{1,0:T(8,128)S(1)} %get-tuple-element.267), channel_id=1, source_target_pairs={{40,0},{48,8},{56,16},{64,24},{72,32},{80,40},{88,48},{96,56},{104... | collective-permute-start | bytes 393224 | tf_op jit(solution)/shard_map/ppermute | solution.py:17
  469.3 30.6 %collective-permute-start.6 = (f32[256,128]{1,0:T(8,128)S(1)}, f32[256,128]{1,0:T(8,128)S(1)}, u32[]{:S(2)}, u32[]{:S(2)}) collective-permute-start(f32[256,128]{1,0:T(8,128)S(1)} %get-tuple-element.266), channel_id=1, source_target_pairs={{48,0},{56,8},{64,16},{72,24},{80,32},{88,40},{96,48},{104,56},{11... | collective-permute-start | bytes 393224 | tf_op jit(solution)/shard_map/ppermute | solution.py:17
  470.6 50.1 %collective-permute-start.7 = (f32[256,128]{1,0:T(8,128)S(1)}, f32[256,128]{1,0:T(8,128)S(1)}, u32[]{:S(2)}, u32[]{:S(2)}) collective-permute-start(f32[256,128]{1,0:T(8,128)S(1)} %get-tuple-element.265), channel_id=1, source_target_pairs={{56,0},{64,8},{72,16},{80,24},{88,32},{96,40},{104,48},{112,56},{1... | collective-permute-start | bytes 393224 | tf_op jit(solution)/shard_map/ppermute | solution.py:17
  473.1 50.6 %collective-permute-start.8 = (f32[256,128]{1,0:T(8,128)S(1)}, f32[256,128]{1,0:T(8,128)S(1)}, u32[]{:S(2)}, u32[]{:S(2)}) collective-permute-start(f32[256,128]{1,0:T(8,128)S(1)} %get-tuple-element.264), channel_id=1, source_target_pairs={{64,0},{72,8},{80,16},{88,24},{96,32},{104,40},{112,48},{120,56},{... | collective-permute-start | bytes 393224 | tf_op jit(solution)/shard_map/ppermute | solution.py:17
  485.7 52.9 %collective-permute-start.9 = (f32[256,128]{1,0:T(8,128)S(1)}, f32[256,128]{1,0:T(8,128)S(1)}, u32[]{:S(2)}, u32[]{:S(2)}) collective-permute-start(f32[256,128]{1,0:T(8,128)S(1)} %get-tuple-element.263), channel_id=1, source_target_pairs={{72,0},{80,8},{88,16},{96,24},{104,32},{112,40},{120,48},{128,56},... | collective-permute-start | bytes 393224 | tf_op jit(solution)/shard_map/ppermute | solution.py:17
  498.1 42.6 %collective-permute-start.35 = (bf16[256,576]{0,1:T(8,128)(2,1)S(1)}, bf16[256,576]{0,1:T(8,128)(2,1)S(1)}, u32[]{:S(2)}, u32[]{:S(2)}) collective-permute-start(bf16[256,576]{0,1:T(8,128)(2,1)S(1)} %bitcast.240), channel_id=1, source_target_pairs={{192,0},{384,192},{576,384},{193,1},{385,193},{577,385},{194,2},{3... | collective-permute-start | bytes 884744 | tf_op jit(solution)/shard_map/ppermute | solution.py:17
  500.0 40.7 %collective-permute-start = (bf16[256,256]{1,0:T(8,128)(2,1)S(1)}, bf16[256,256]{1,0:T(8,128)(2,1)S(1)}, u32[]{:S(2)}, u32[]{:S(2)}) collective-permute-start(bf16[256,256]{1,0:T(8,128)(2,1)S(1)} %copy_bitcast_fusion), channel_id=1, source_target_pairs={{192,0},{384,192},{576,384},{193,1},{385,193},{577,385},{194,2},{3... | collective-permute-start | bytes 393224 | tf_op jit(solution)/shard_map/ppermute | solution.py:17
  520.7 20.0 %collective-permute-start.34 = (bf16[256,128]{1,0:T(8,128)(2,1)S(1)}, bf16[256,128]{1,0:T(8,128)(2,1)S(1)}, u32[]{:S(2)}, u32[]{:S(2)}) collective-permute-start(bf16[256,128]{1,0:T(8,128)(2,1)S(1)} %fusion.68), channel_id=1, source_target_pairs={{192,0},{384,192},{576,384},{193,1},{385,193},{577,385},{194,2},{3... | collective-permute-start | bytes 196616 | tf_op jit(solution)/shard_map/ppermute | solution.py:17
  538.7 5.0 collective-permute-start.17
Sparse Core Ops, SparseCore 0:
  10.4 63.8 all-gather.8
  76.8 56.5 all-gather.14
  135.8 39.9 all-gather.10
  178.0 62.9 all-gather.12
where the time goes:
time: 554 us; the launch traced here: 553 us
  waiting for transfers between devices  425 us (77%)
  starting transfers between devices  56.9 us (10%)
  matrix products  32.8 us (6%)
  between operations  14.3 us (3%)
  local copies, waits for them, and re-layouts  13.6 us (2%)
  other arithmetic  10.3 us (2%)
    ppermute x36, waiting for transfers between devices, from_behind(): return lax.ppermute(block, axis, route)  198 us
    all_gather x1, waiting for transfers between devices, per_device(): lax.all_gather(out_weight[0], 'row', axis=1, tiled=True)  65.3 us
    all_gather x1, waiting for transfers between devices, per_device(): lax.all_gather(key_local, 'row', axis=0, tiled=True)  61.1 us
    all_gather x1, waiting for transfers between devices, per_device(): lax.all_gather(value_local, 'row', axis=0, tiled=True)  57.7 us
    ppermute x36, starting transfers between devices, from_behind(): return lax.ppermute(block, axis, route)  56.8 us
    all_gather x1, waiting for transfers between devices, per_device(): grad_rows = lax.all_gather(grad_tile, 'col', axis=1, tiled=True)  40 us
    dot_general x2, matrix products, one_head(): lax.dot_general(probs_low, attn_h, (((0,), (0,)), ((), ())), preferred_el...  12.1 us
  transfers between devices with their start and end apart: 40, of which 25 were waited for; matrix products, arithmetic and copies ran while one was open for 1% of the time, Pallas kernels for 0%

commit v1 on v0

--- a/solution.py
+++ b/solution.py
@@ -111,17 +111,15 @@
     key_local = key_act[0]
     value_local = value_act[0]
     key_width = key_local.shape[1]
-    key_all, value_all = (
-        lax.all_gather(key_local, "row", axis=0, tiled=True),
-        lax.all_gather(value_local, "row", axis=0, tiled=True),
-    )
-    lead_rows = jnp.zeros((reach_rows * tok_rows, key_width), key_all.dtype)
-    key_near = lax.dynamic_slice_in_dim(
-        jnp.concatenate([lead_rows, key_all], axis=0), query_start, span_rows, 0
-    )
-    value_near = lax.dynamic_slice_in_dim(
-        jnp.concatenate([lead_rows, value_all], axis=0), query_start, span_rows, 0
-    )
+    pair_local = jnp.concatenate([key_local, value_local], axis=1)
+    near_blocks = [pair_local]
+    moving = pair_local
+    for _ in range(reach_rows):
+        moving = from_behind(moving, "row", 1)
+        near_blocks.append(moving)
+    pair_near = jnp.concatenate(near_blocks[::-1], axis=0)
+    key_near = pair_near[:, :key_width]
+    value_near = pair_near[:, key_width:]
     key_start = query_start - reach_rows * tok_rows
     key_pos = key_start + jnp.arange(span_rows, dtype=jnp.int32)
     query_pos = query_start + jnp.arange(tok_rows, dtype=jnp.int32)
@@ -136,17 +134,12 @@
     )
     allowed = allowed & ((key_doc[None, :] == query_doc[:, None]) | (key_shared[None, :] == 1))
     query_grad, key_sum, value_sum = attend(query_local, key_near, value_near, d_attn, allowed)
-    key_total = key_sum[reach_rows * tok_rows :]
-    value_total = value_sum[reach_rows * tok_rows :]
-    for distance in range(1, reach_rows + 1):
-        low_row = (reach_rows - distance) * tok_rows
-        back_key, back_value = from_behind(
-            (key_sum[low_row : low_row + tok_rows], value_sum[low_row : low_row + tok_rows]),
-            "row",
-            -distance,
-        )
-        key_total = key_total + back_key
-        value_total = value_total + back_value
+    pair_sum = jnp.concatenate([key_sum, value_sum], axis=1)
+    running = pair_sum[:tok_rows]
+    for step in range(1, reach_rows + 1):
+        running = from_behind(running, "row", -1) + pair_sum[step * tok_rows : (step + 1) * tok_rows]
+    key_total = running[:, :key_width]
+    value_total = running[:, key_width:]
     handed = from_behind(
         (query_grad, key_total.astype(jnp.bfloat16), value_total.astype(jnp.bfloat16), grad_tile),
         "pipe",

time: 554 us -> 356 us (0.64)
  the two profiles are of different devices: /device:TPU:91 before, /device:TPU:196 now
where the time goes in v1:
time: 356 us; the launch traced here: 349 us
  starting transfers between devices  146 us (41%)
  waiting for transfers between devices  120 us (34%)
  matrix products  32.7 us (9%)
  other arithmetic  26.1 us (7%)
  between operations  14.7 us (4%)
  local copies, waits for them, and re-layouts  9.51 us (3%)
    ppermute x36, starting transfers between devices, from_behind(): return lax.ppermute(block, axis, route)  146 us
    ppermute x36, waiting for transfers between devices, from_behind(): return lax.ppermute(block, axis, route)  114 us
    add x15, other arithmetic, per_device(): from_behind(running, 'row', -1)  14.2 us
    dot_general x2, matrix products, one_head(): lax.dot_general(probs_low, attn_h, (((0,), (0,)), ((), ())), preferred_el...  12 us
    convert_element_type x2, other arithmetic, one_head(): grad_raw = (attn_probs * (grad_probs - row_delta) * (1.0 - capped * cappe...  7.56 us
  transfers between devices with their start and end apart: 38, of which 33 were waited for; matrix products, arithmetic and copies ran while one was open for 2% of the time, Pallas kernels for 0%

profile of v1, /device:TPU:196, one launch (start us, length us, event | category | flops | bytes accessed | tf_op | source)
XLA Modules:
  0.0 349.5 jit_solution(13077278164150199501)
XLA Ops:
  8.8 1.9 collective-permute-start
  10.8 4.4 %collective-permute-done = bf16[256,256]{1,0:T(8,128)(2,1)S(1)} collective-permute-done((bf16[256,256]{1,0:T(8,128)(2,1)S(1)}, bf16[256,256]{1,0:T(8,128)(2,1)S(1)}, u32[]{:S(2)}, u32[]{:S(2)}) %collective-permute-start) | collective-permute-done | bytes 131104 | tf_op jit(solution)/shard_map/ppermute | solution.py:17
  15.1 3.1 collective-permute-start.1
  18.3 3.1 collective-permute-done.1
  21.4 4.4 %collective-permute-start.2 = (bf16[256,256]{1,0:T(8,128)(2,1)S(1)}, bf16[256,256]{1,0:T(8,128)(2,1)S(1)}, u32[]{:S(2)}, u32[]{:S(2)}) collective-permute-start(bf16[256,256]{1,0:T(8,128)(2,1)S(1)} %collective-permute-done.1), channel_id=1, source_target_pairs={{0,8},{8,16},{16,24},{24,32},{32,40},{40,48},{48,56},{56,64},{64,7... | collective-permute-start | bytes 393224 | tf_op jit(solution)/shard_map/ppermute | solution.py:17
  27.7 5.6 %collective-permute-start.3 = (bf16[256,256]{1,0:T(8,128)(2,1)S(1)}, bf16[256,256]{1,0:T(8,128)(2,1)S(1)}, u32[]{:S(2)}, u32[]{:S(2)}) collective-permute-start(bf16[256,256]{1,0:T(8,128)(2,1)S(1)} %collective-permute-done.2), channel_id=1, source_target_pairs={{0,8},{8,16},{16,24},{24,32},{32,40},{40,48},{48,56},{56,64},{64,7... | collective-permute-start | bytes 393224 | tf_op jit(solution)/shard_map/ppermute | solution.py:17
  34.2 6.5 %collective-permute-start.4 = (bf16[256,256]{1,0:T(8,128)(2,1)S(1)}, bf16[256,256]{1,0:T(8,128)(2,1)S(1)}, u32[]{:S(2)}, u32[]{:S(2)}) collective-permute-start(bf16[256,256]{1,0:T(8,128)(2,1)S(1)} %collective-permute-done.3), channel_id=1, source_target_pairs={{0,8},{8,16},{16,24},{24,32},{32,40},{40,48},{48,56},{56,64},{64,7... | collective-permute-start | bytes 393224 | tf_op jit(solution)/shard_map/ppermute | solution.py:17
  41.7 6.5 %collective-permute-start.5 = (bf16[256,256]{1,0:T(8,128)(2,1)S(1)}, bf16[256,256]{1,0:T(8,128)(2,1)S(1)}, u32[]{:S(2)}, u32[]{:S(2)}) collective-permute-start(bf16[256,256]{1,0:T(8,128)(2,1)S(1)} %collective-permute-done.4), channel_id=1, source_target_pairs={{0,8},{8,16},{16,24},{24,32},{32,40},{40,48},{48,56},{56,64},{64,7... | collective-permute-start | bytes 393224 | tf_op jit(solution)/shard_map/ppermute | solution.py:17
  49.2 6.5 %collective-permute-start.6 = (bf16[256,256]{1,0:T(8,128)(2,1)S(1)}, bf16[256,256]{1,0:T(8,128)(2,1)S(1)}, u32[]{:S(2)}, u32[]{:S(2)}) collective-permute-start(bf16[256,256]{1,0:T(8,128)(2,1)S(1)} %collective-permute-done.5), channel_id=1, source_target_pairs={{0,8},{8,16},{16,24},{24,32},{32,40},{40,48},{48,56},{56,64},{64,7... | collective-permute-start | bytes 393224 | tf_op jit(solution)/shard_map/ppermute | solution.py:17
  56.7 6.5 %collective-permute-start.7 = (bf16[256,256]{1,0:T(8,128)(2,1)S(1)}, bf16[256,256]{1,0:T(8,128)(2,1)S(1)}, u32[]{:S(2)}, u32[]{:S(2)}) collective-permute-start(bf16[256,256]{1,0:T(8,128)(2,1)S(1)} %collective-permute-done.6), channel_id=1, source_target_pairs={{0,8},{8,16},{16,24},{24,32},{32,40},{40,48},{48,56},{56,64},{64,7... | collective-permute-start | bytes 393224 | tf_op jit(solution)/shard_map/ppermute | solution.py:17
  64.2 6.5 %collective-permute-start.8 = (bf16[256,256]{1,0:T(8,128)(2,1)S(1)}, bf16[256,256]{1,0:T(8,128)(2,1)S(1)}, u32[]{:S(2)}, u32[]{:S(2)}) collective-permute-start(bf16[256,256]{1,0:T(8,128)(2,1)S(1)} %collective-permute-done.7), channel_id=1, source_target_pairs={{0,8},{8,16},{16,24},{24,32},{32,40},{40,48},{48,56},{56,64},{64,7... | collective-permute-start | bytes 393224 | tf_op jit(solution)/shard_map/ppermute | solution.py:17
  71.7 6.5 %collective-permute-start.9 = (bf16[256,256]{1,0:T(8,128)(2,1)S(1)}, bf16[256,256]{1,0:T(8,128)(2,1)S(1)}, u32[]{:S(2)}, u32[]{:S(2)}) collective-permute-start(bf16[256,256]{1,0:T(8,128)(2,1)S(1)} %collective-permute-done.8), channel_id=1, source_target_pairs={{0,8},{8,16},{16,24},{24,32},{32,40},{40,48},{48,56},{56,64},{64,7... | collective-permute-start | bytes 393224 | tf_op jit(solution)/shard_map/ppermute | solution.py:17
  79.1 6.5 %collective-permute-start.10 = (bf16[256,256]{1,0:T(8,128)(2,1)S(1)}, bf16[256,256]{1,0:T(8,128)(2,1)S(1)}, u32[]{:S(2)}, u32[]{:S(2)}) collective-permute-start(bf16[256,256]{1,0:T(8,128)(2,1)S(1)} %collective-permute-done.9), channel_id=1, source_target_pairs={{0,8},{8,16},{16,24},{24,32},{32,40},{40,48},{48,56},{56,64},{64,7... | collective-permute-start | bytes 393224 | tf_op jit(solution)/shard_map/ppermute | solution.py:17
  86.6 6.5 %collective-permute-start.11 = (bf16[256,256]{1,0:T(8,128)(2,1)S(1)}, bf16[256,256]{1,0:T(8,128)(2,1)S(1)}, u32[]{:S(2)}, u32[]{:S(2)}) collective-permute-start(bf16[256,256]{1,0:T(8,128)(2,1)S(1)} %collective-permute-done.10), channel_id=1, source_target_pairs={{0,8},{8,16},{16,24},{24,32},{32,40},{40,48},{48,56},{56,64},{64,7... | collective-permute-start | bytes 393224 | tf_op jit(solution)/shard_map/ppermute | solution.py:17
  94.1 7.6 %collective-permute-start.12 = (bf16[256,256]{1,0:T(8,128)(2,1)S(1)}, bf16[256,256]{1,0:T(8,128)(2,1)S(1)}, u32[]{:S(2)}, u32[]{:S(2)}) collective-permute-start(bf16[256,256]{1,0:T(8,128)(2,1)S(1)} %collective-permute-done.11), channel_id=1, source_target_pairs={{0,8},{8,16},{16,24},{24,32},{32,40},{40,48},{48,56},{56,64},{64,7... | collective-permute-start | bytes 393224 | tf_op jit(solution)/shard_map/ppermute | solution.py:17
  102.7 7.5 %collective-permute-start.13 = (bf16[256,256]{1,0:T(8,128)(2,1)S(1)}, bf16[256,256]{1,0:T(8,128)(2,1)S(1)}, u32[]{:S(2)}, u32[]{:S(2)}) collective-permute-start(bf16[256,256]{1,0:T(8,128)(2,1)S(1)} %collective-permute-done.12), channel_id=1, source_target_pairs={{0,8},{8,16},{16,24},{24,32},{32,40},{40,48},{48,56},{56,64},{64,7... | collective-permute-start | bytes 393224 | tf_op jit(solution)/shard_map/ppermute | solution.py:17
  111.8 6.0 %collective-permute-start.14 = (bf16[256,256]{1,0:T(8,128)(2,1)S(1)}, bf16[256,256]{1,0:T(8,128)(2,1)S(1)}, u32[]{:S(2)}, u32[]{:S(2)}) collective-permute-start(bf16[256,256]{1,0:T(8,128)(2,1)S(1)} %collective-permute-done.13), channel_id=1, source_target_pairs={{0,8},{8,16},{16,24},{24,32},{32,40},{40,48},{48,56},{56,64},{64,7... | collective-permute-start | bytes 393224 | tf_op jit(solution)/shard_map/ppermute | solution.py:17
  118.8 6.9 %collective-permute-start.15 = (bf16[256,256]{1,0:T(8,128)(2,1)S(1)}, bf16[256,256]{1,0:T(8,128)(2,1)S(1)}, u32[]{:S(2)}, u32[]{:S(2)}) collective-permute-start(bf16[256,256]{1,0:T(8,128)(2,1)S(1)} %collective-permute-done.14), channel_id=1, source_target_pairs={{0,8},{8,16},{16,24},{24,32},{32,40},{40,48},{48,56},{56,64},{64,7... | collective-permute-start | bytes 393224 | tf_op jit(solution)/shard_map/ppermute | solution.py:17
  129.0 5.2 %all-gather.7.cloned.1.call-done = bf16[1,256,4608]{1,2,0:T(8,128)(2,1)} async-done(((bf16[1,256,192]{1,2,0:T(8,128)(2,1)}), bf16[1,256,4608]{1,2,0:T(8,128)(2,1)}) %all-gather.7.cloned.1.call-update) | async-done | bytes 2359312 | tf_op jit(solution)/shard_map/all_gather | solution.py:100
  134.2 3.4 fusion.30
  140.1 38.3 %while.18 = (s32[]{:T(128)}, f32[1,4352,128]{2,1,0:T(8,128)S(1)}, f32[1,4352,128]{2,1,0:T(8,128)}, bf16[2,256,128]{2,1,0:T(8,128)(2,1)}, bf16[2,256,128]{1,2,0:T...) while((s32[]{:T(128)}, f32[1,4352,128]{2,1,0:T(8,128)S(1)}, ...), condition=%wide.region_4.5_spmd.clone, body=%wide.region_1.4_spmd.clone.sunk | while | flops 1488485888 | bytes 52247312 | solution.py:78
  140.1 3.3 fusion.88
  143.4 3.2 multiply_reduce_fusion.2
  146.6 3.8 %multiply_convert_fusion.2 = bf16[256,4352]{1,0:T(8,128)(2,1)S(1)} fusion(f32[256,4352]{1,0:T(8,128)S(1)} %get-tuple-element.335, f32[256,4352]{1,0:T(8,128)S(1)} %get-tuple-element.337, f32[256]{0:T(256)S(1)} %get-tuple-element.338, f32[256]{0:T(256)S(1)} %get-tuple-element.336, pred[4352]{0:T(1024)(128)(4,1)S(1)} %get-tuple-element.382, ...), kind=kLoop, calls=%fused_computation.8.clone.1 | loop fusion | flops 20054016 | bytes 11188736 | tf_op jit(solution)/shard_map/while/body/eval_jaxpr/convert_element_type | solution.py:55
  153.2 6.0 %fusion.90 = f32[1,4352,128]{2,1,0:T(8,128)} fusion(f32[1,4352,128]{2,1,0:T(8,128)} %get-tuple-element.356, bf16[2,256,128]{2,1,0:T(8,128)(2,1)S(1)} %copy-done.7, s32[]{:T(128)} %get-tuple-element.354, f32[256]{0:T(256)S(1)} %get-tuple-element.336, f32[256,4352]{1,0:T(8,128)S(1)} %get-tuple-element.335, pred[4352]{0:T(1024)(128)(4,1)S(1)} %get-tuple-element.382, ...), kind=kOutput, calls=%fused_computation.6.clone.1 | convolution fusion | flops 299139072 | bytes 9032708 | tf_op jit(solution)/shard_map/while/body/eval_jaxpr/dot_general | solution.py:46
  159.3 3.3 fusion.88
  162.6 3.2 multiply_reduce_fusion.2
  165.8 3.8 %multiply_convert_fusion.2 = bf16[256,4352]{1,0:T(8,128)(2,1)S(1)} fusion(f32[256,4352]{1,0:T(8,128)S(1)} %get-tuple-element.335, f32[256,4352]{1,0:T(8,128)S(1)} %get-tuple-element.337, f32[256]{0:T(256)S(1)} %get-tuple-element.338, f32[256]{0:T(256)S(1)} %get-tuple-element.336, pred[4352]{0:T(1024)(128)(4,1)S(1)} %get-tuple-element.382, ...), kind=kLoop, calls=%fused_computation.8.clone.1 | loop fusion | flops 20054016 | bytes 11188736 | tf_op jit(solution)/shard_map/while/body/eval_jaxpr/convert_element_type | solution.py:55
  172.4 6.0 %fusion.90 = f32[1,4352,128]{2,1,0:T(8,128)} fusion(f32[1,4352,128]{2,1,0:T(8,128)} %get-tuple-element.356, bf16[2,256,128]{2,1,0:T(8,128)(2,1)S(1)} %copy-done.7, s32[]{:T(128)} %get-tuple-element.354, f32[256]{0:T(256)S(1)} %get-tuple-element.336, f32[256,4352]{1,0:T(8,128)S(1)} %get-tuple-element.335, pred[4352]{0:T(1024)(128)(4,1)S(1)} %get-tuple-element.382, ...), kind=kOutput, calls=%fused_computation.6.clone.1 | convolution fusion | flops 299139072 | bytes 9032708 | tf_op jit(solution)/shard_map/while/body/eval_jaxpr/dot_general | solution.py:46
  179.3 3.3 collective-permute-start.17
  182.6 3.9 %collective-permute-done.17 = f32[256,256]{1,0:T(8,128)S(1)} collective-permute-done((f32[256,256]{1,0:T(8,128)S(1)}, f32[256,256]{1,0:T(8,128)S(1)}, u32[]{:S(2)}, u32[]{:S(2)}) %collective-permute-start.17) | collective-permute-done | bytes 262176 | tf_op jit(solution)/shard_map/ppermute | solution.py:17
  187.5 3.8 %collective-permute-start.18 = (f32[256,256]{1,0:T(8,128)S(1)}, f32[256,256]{1,0:T(8,128)S(1)}, u32[]{:S(2)}, u32[]{:S(2)}) collective-permute-start(f32[256,256]{1,0:T(8,128)S(1)} %fusion.64), channel_id=1, source_target_pairs={{8,0},{16,8},{24,16},{32,24},{40,32},{48,40},{56,48},{64,56},{72,6... | collective-permute-start | bytes 786440 | tf_op jit(solution)/shard_map/ppermute | solution.py:17
  191.3 3.9 %collective-permute-done.18 = f32[256,256]{1,0:T(8,128)S(1)} collective-permute-done((f32[256,256]{1,0:T(8,128)S(1)}, f32[256,256]{1,0:T(8,128)S(1)}, u32[]{:S(2)}, u32[]{:S(2)}) %collective-permute-start.18) | collective-permute-done | bytes 262176 | tf_op jit(solution)/shard_map/ppermute | solution.py:17
  196.1 3.8 %collective-permute-start.19 = (f32[256,256]{1,0:T(8,128)S(1)}, f32[256,256]{1,0:T(8,128)S(1)}, u32[]{:S(2)}, u32[]{:S(2)}) collective-permute-start(f32[256,256]{1,0:T(8,128)S(1)} %fusion.63), channel_id=1, source_target_pairs={{8,0},{16,8},{24,16},{32,24},{40,32},{48,40},{56,48},{64,56},{72,6... | collective-permute-start | bytes 786440 | tf_op jit(solution)/shard_map/ppermute | solution.py:17
  199.9 3.9 %collective-permute-done.19 = f32[256,256]{1,0:T(8,128)S(1)} collective-permute-done((f32[256,256]{1,0:T(8,128)S(1)}, f32[256,256]{1,0:T(8,128)S(1)}, u32[]{:S(2)}, u32[]{:S(2)}) %collective-permute-start.19) | collective-permute-done | bytes 262176 | tf_op jit(solution)/shard_map/ppermute | solution.py:17
  204.7 3.8 %collective-permute-start.20 = (f32[256,256]{1,0:T(8,128)S(1)}, f32[256,256]{1,0:T(8,128)S(1)}, u32[]{:S(2)}, u32[]{:S(2)}) collective-permute-start(f32[256,256]{1,0:T(8,128)S(1)} %fusion.62), channel_id=1, source_target_pairs={{8,0},{16,8},{24,16},{32,24},{40,32},{48,40},{56,48},{64,56},{72,6... | collective-permute-start | bytes 786440 | tf_op jit(solution)/shard_map/ppermute | solution.py:17
  208.6 3.9 %collective-permute-done.20 = f32[256,256]{1,0:T(8,128)S(1)} collective-permute-done((f32[256,256]{1,0:T(8,128)S(1)}, f32[256,256]{1,0:T(8,128)S(1)}, u32[]{:S(2)}, u32[]{:S(2)}) %collective-permute-start.20) | collective-permute-done | bytes 262176 | tf_op jit(solution)/shard_map/ppermute | solution.py:17
  213.4 3.8 %collective-permute-start.21 = (f32[256,256]{1,0:T(8,128)S(1)}, f32[256,256]{1,0:T(8,128)S(1)}, u32[]{:S(2)}, u32[]{:S(2)}) collective-permute-start(f32[256,256]{1,0:T(8,128)S(1)} %fusion.61), channel_id=1, source_target_pairs={{8,0},{16,8},{24,16},{32,24},{40,32},{48,40},{56,48},{64,56},{72,6... | collective-permute-start | bytes 786440 | tf_op jit(solution)/shard_map/ppermute | solution.py:17
  217.2 4.7 %collective-permute-done.21 = f32[256,256]{1,0:T(8,128)S(1)} collective-permute-done((f32[256,256]{1,0:T(8,128)S(1)}, f32[256,256]{1,0:T(8,128)S(1)}, u32[]{:S(2)}, u32[]{:S(2)}) %collective-permute-start.21) | collective-permute-done | bytes 262176 | tf_op jit(solution)/shard_map/ppermute | solution.py:17
  222.8 3.0 collective-permute-start.22
  225.8 5.9 %collective-permute-done.22 = f32[256,256]{1,0:T(8,128)S(1)} collective-permute-done((f32[256,256]{1,0:T(8,128)S(1)}, f32[256,256]{1,0:T(8,128)S(1)}, u32[]{:S(2)}, u32[]{:S(2)}) %collective-permute-start.22) | collective-permute-done | bytes 262176 | tf_op jit(solution)/shard_map/ppermute | solution.py:17
  232.7 1.9 collective-permute-start.23
  234.6 7.0 %collective-permute-done.23 = f32[256,256]{1,0:T(8,128)S(1)} collective-permute-done((f32[256,256]{1,0:T(8,128)S(1)}, f32[256,256]{1,0:T(8,128)S(1)}, u32[]{:S(2)}, u32[]{:S(2)}) %collective-permute-start.23) | collective-permute-done | bytes 262176 | tf_op jit(solution)/shard_map/ppermute | solution.py:17
  242.5 1.9 collective-permute-start.24
  244.5 7.0 %collective-permute-done.24 = f32[256,256]{1,0:T(8,128)S(1)} collective-permute-done((f32[256,256]{1,0:T(8,128)S(1)}, f32[256,256]{1,0:T(8,128)S(1)}, u32[]{:S(2)}, u32[]{:S(2)}) %collective-permute-start.24) | collective-permute-done | bytes 262176 | tf_op jit(solution)/shard_map/ppermute | solution.py:17
  252.4 1.9 collective-permute-start.25
  254.3 7.0 %collective-permute-done.25 = f32[256,256]{1,0:T(8,128)S(1)} collective-permute-done((f32[256,256]{1,0:T(8,128)S(1)}, f32[256,256]{1,0:T(8,128)S(1)}, u32[]{:S(2)}, u32[]{:S(2)}) %collective-permute-start.25) | collective-permute-done | bytes 262176 | tf_op jit(solution)/shard_map/ppermute | solution.py:17
  262.2 1.9 collective-permute-start.26
  264.2 7.0 %collective-permute-done.26 = f32[256,256]{1,0:T(8,128)S(1)} collective-permute-done((f32[256,256]{1,0:T(8,128)S(1)}, f32[256,256]{1,0:T(8,128)S(1)}, u32[]{:S(2)}, u32[]{:S(2)}) %collective-permute-start.26) | collective-permute-done | bytes 262176 | tf_op jit(solution)/shard_map/ppermute | solution.py:17
  272.1 1.9 collective-permute-start.27
  274.0 7.0 %collective-permute-done.27 = f32[256,256]{1,0:T(8,128)S(1)} collective-permute-done((f32[256,256]{1,0:T(8,128)S(1)}, f32[256,256]{1,0:T(8,128)S(1)}, u32[]{:S(2)}, u32[]{:S(2)}) %collective-permute-start.27) | collective-permute-done | bytes 262176 | tf_op jit(solution)/shard_map/ppermute | solution.py:17
  281.9 1.9 collective-permute-start.28
  283.9 7.0 %collective-permute-done.28 = f32[256,256]{1,0:T(8,128)S(1)} collective-permute-done((f32[256,256]{1,0:T(8,128)S(1)}, f32[256,256]{1,0:T(8,128)S(1)}, u32[]{:S(2)}, u32[]{:S(2)}) %collective-permute-start.28) | collective-permute-done | bytes 262176 | tf_op jit(solution)/shard_map/ppermute | solution.py:17
  291.8 1.9 collective-permute-start.29
  293.7 7.0 %collective-permute-done.29 = f32[256,256]{1,0:T(8,128)S(1)} collective-permute-done((f32[256,256]{1,0:T(8,128)S(1)}, f32[256,256]{1,0:T(8,128)S(1)}, u32[]{:S(2)}, u32[]{:S(2)}) %collective-permute-start.29) | collective-permute-done | bytes 262176 | tf_op jit(solution)/shard_map/ppermute | solution.py:17
  301.6 1.9 collective-permute-start.30
  303.6 7.0 %collective-permute-done.30 = f32[256,256]{1,0:T(8,128)S(1)} collective-permute-done((f32[256,256]{1,0:T(8,128)S(1)}, f32[256,256]{1,0:T(8,128)S(1)}, u32[]{:S(2)}, u32[]{:S(2)}) %collective-permute-start.30) | collective-permute-done | bytes 262176 | tf_op jit(solution)/shard_map/ppermute | solution.py:17
  311.5 2.1 collective-permute-start.31
  313.6 7.0 %collective-permute-done.31 = f32[256,256]{1,0:T(8,128)S(1)} collective-permute-done((f32[256,256]{1,0:T(8,128)S(1)}, f32[256,256]{1,0:T(8,128)S(1)}, u32[]{:S(2)}, u32[]{:S(2)}) %collective-permute-start.31) | collective-permute-done | bytes 262176 | tf_op jit(solution)/shard_map/ppermute | solution.py:17
  323.4 2.5 collective-permute-start.35
  325.9 2.4 collective-permute-start.16
  328.4 2.0 collective-permute-done.32
  331.4 2.5 collective-permute-start.33
  333.8 2.4 collective-permute-start.34
  (105 shorter events, 51.3 us)
Async XLA Ops:
  7.2 121.8 %all-gather.5.cloned.1.call-start = ((), (), s32[]{:S(2)}) async-start(), calls=%async_computation | async-start | bytes 2654208 | tf_op jit(solution)/shard_map/all_gather | solution.py:97
  7.9 126.3 %all-gather.7.cloned.1.call-start = ((), (), s32[]{:S(2)}) async-start(), calls=%async_computation.1 | async-start | bytes 2457600 | tf_op jit(solution)/shard_map/all_gather | solution.py:100
  8.8 6.3 %collective-permute-start = (bf16[256,256]{1,0:T(8,128)(2,1)S(1)}, bf16[256,256]{1,0:T(8,128)(2,1)S(1)}, u32[]{:S(2)}, u32[]{:S(2)}) collective-permute-start(bf16[256,256]{1,0:T(8,128)(2,1)S(1)} %pad_maximum_fusion.1), channel_id=1, source_target_pairs={{0,8},{8,16},{16,24},{24,32},{32,40},{40,48},{48,56},{56,64},{64,7... | collective-permute-start | bytes 393224 | tf_op jit(solution)/shard_map/ppermute | solution.py:17
  15.1 6.3 %collective-permute-start.1 = (bf16[256,256]{1,0:T(8,128)(2,1)S(1)}, bf16[256,256]{1,0:T(8,128)(2,1)S(1)}, u32[]{:S(2)}, u32[]{:S(2)}) collective-permute-start(bf16[256,256]{1,0:T(8,128)(2,1)S(1)} %collective-permute-done), channel_id=1, source_target_pairs={{0,8},{8,16},{16,24},{24,32},{32,40},{40,48},{48,56},{56,64},{64,7... | collective-permute-start | bytes 393224 | tf_op jit(solution)/shard_map/ppermute | solution.py:17
  21.4 6.3 %collective-permute-start.2 = (bf16[256,256]{1,0:T(8,128)(2,1)S(1)}, bf16[256,256]{1,0:T(8,128)(2,1)S(1)}, u32[]{:S(2)}, u32[]{:S(2)}) collective-permute-start(bf16[256,256]{1,0:T(8,128)(2,1)S(1)} %collective-permute-done.1), channel_id=1, source_target_pairs={{0,8},{8,16},{16,24},{24,32},{32,40},{40,48},{48,56},{56,64},{64,7... | collective-permute-start | bytes 393224 | tf_op jit(solution)/shard_map/ppermute | solution.py:17
  27.7 6.5 %collective-permute-start.3 = (bf16[256,256]{1,0:T(8,128)(2,1)S(1)}, bf16[256,256]{1,0:T(8,128)(2,1)S(1)}, u32[]{:S(2)}, u32[]{:S(2)}) collective-permute-start(bf16[256,256]{1,0:T(8,128)(2,1)S(1)} %collective-permute-done.2), channel_id=1, source_target_pairs={{0,8},{8,16},{16,24},{24,32},{32,40},{40,48},{48,56},{56,64},{64,7... | collective-permute-start | bytes 393224 | tf_op jit(solution)/shard_map/ppermute | solution.py:17
  34.2 7.5 %collective-permute-start.4 = (bf16[256,256]{1,0:T(8,128)(2,1)S(1)}, bf16[256,256]{1,0:T(8,128)(2,1)S(1)}, u32[]{:S(2)}, u32[]{:S(2)}) collective-permute-start(bf16[256,256]{1,0:T(8,128)(2,1)S(1)} %collective-permute-done.3), channel_id=1, source_target_pairs={{0,8},{8,16},{16,24},{24,32},{32,40},{40,48},{48,56},{56,64},{64,7... | collective-permute-start | bytes 393224 | tf_op jit(solution)/shard_map/ppermute | solution.py:17
  41.7 7.5 %collective-permute-start.5 = (bf16[256,256]{1,0:T(8,128)(2,1)S(1)}, bf16[256,256]{1,0:T(8,128)(2,1)S(1)}, u32[]{:S(2)}, u32[]{:S(2)}) collective-permute-start(bf16[256,256]{1,0:T(8,128)(2,1)S(1)} %collective-permute-done.4), channel_id=1, source_target_pairs={{0,8},{8,16},{16,24},{24,32},{32,40},{40,48},{48,56},{56,64},{64,7... | collective-permute-start | bytes 393224 | tf_op jit(solution)/shard_map/ppermute | solution.py:17
  49.2 7.5 %collective-permute-start.6 = (bf16[256,256]{1,0:T(8,128)(2,1)S(1)}, bf16[256,256]{1,0:T(8,128)(2,1)S(1)}, u32[]{:S(2)}, u32[]{:S(2)}) collective-permute-start(bf16[256,256]{1,0:T(8,128)(2,1)S(1)} %collective-permute-done.5), channel_id=1, source_target_pairs={{0,8},{8,16},{16,24},{24,32},{32,40},{40,48},{48,56},{56,64},{64,7... | collective-permute-start | bytes 393224 | tf_op jit(solution)/shard_map/ppermute | solution.py:17
  56.7 7.5 %collective-permute-start.7 = (bf16[256,256]{1,0:T(8,128)(2,1)S(1)}, bf16[256,256]{1,0:T(8,128)(2,1)S(1)}, u32[]{:S(2)}, u32[]{:S(2)}) collective-permute-start(bf16[256,256]{1,0:T(8,128)(2,1)S(1)} %collective-permute-done.6), channel_id=1, source_target_pairs={{0,8},{8,16},{16,24},{24,32},{32,40},{40,48},{48,56},{56,64},{64,7... | collective-permute-start | bytes 393224 | tf_op jit(solution)/shard_map/ppermute | solution.py:17
  64.2 7.5 %collective-permute-start.8 = (bf16[256,256]{1,0:T(8,128)(2,1)S(1)}, bf16[256,256]{1,0:T(8,128)(2,1)S(1)}, u32[]{:S(2)}, u32[]{:S(2)}) collective-permute-start(bf16[256,256]{1,0:T(8,128)(2,1)S(1)} %collective-permute-done.7), channel_id=1, source_target_pairs={{0,8},{8,16},{16,24},{24,32},{32,40},{40,48},{48,56},{56,64},{64,7... | collective-permute-start | bytes 393224 | tf_op jit(solution)/shard_map/ppermute | solution.py:17
  71.7 7.5 %collective-permute-start.9 = (bf16[256,256]{1,0:T(8,128)(2,1)S(1)}, bf16[256,256]{1,0:T(8,128)(2,1)S(1)}, u32[]{:S(2)}, u32[]{:S(2)}) collective-permute-start(bf16[256,256]{1,0:T(8,128)(2,1)S(1)} %collective-permute-done.8), channel_id=1, source_target_pairs={{0,8},{8,16},{16,24},{24,32},{32,40},{40,48},{48,56},{56,64},{64,7... | collective-permute-start | bytes 393224 | tf_op jit(solution)/shard_map/ppermute | solution.py:17
  79.1 7.5 %collective-permute-start.10 = (bf16[256,256]{1,0:T(8,128)(2,1)S(1)}, bf16[256,256]{1,0:T(8,128)(2,1)S(1)}, u32[]{:S(2)}, u32[]{:S(2)}) collective-permute-start(bf16[256,256]{1,0:T(8,128)(2,1)S(1)} %collective-permute-done.9), channel_id=1, source_target_pairs={{0,8},{8,16},{16,24},{24,32},{32,40},{40,48},{48,56},{56,64},{64,7... | collective-permute-start | bytes 393224 | tf_op jit(solution)/shard_map/ppermute | solution.py:17
  86.6 7.5 %collective-permute-start.11 = (bf16[256,256]{1,0:T(8,128)(2,1)S(1)}, bf16[256,256]{1,0:T(8,128)(2,1)S(1)}, u32[]{:S(2)}, u32[]{:S(2)}) collective-permute-start(bf16[256,256]{1,0:T(8,128)(2,1)S(1)} %collective-permute-done.10), channel_id=1, source_target_pairs={{0,8},{8,16},{16,24},{24,32},{32,40},{40,48},{48,56},{56,64},{64,7... | collective-permute-start | bytes 393224 | tf_op jit(solution)/shard_map/ppermute | solution.py:17
  94.1 8.6 %collective-permute-start.12 = (bf16[256,256]{1,0:T(8,128)(2,1)S(1)}, bf16[256,256]{1,0:T(8,128)(2,1)S(1)}, u32[]{:S(2)}, u32[]{:S(2)}) collective-permute-start(bf16[256,256]{1,0:T(8,128)(2,1)S(1)} %collective-permute-done.11), channel_id=1, source_target_pairs={{0,8},{8,16},{16,24},{24,32},{32,40},{40,48},{48,56},{56,64},{64,7... | collective-permute-start | bytes 393224 | tf_op jit(solution)/shard_map/ppermute | solution.py:17
  102.7 9.1 %collective-permute-start.13 = (bf16[256,256]{1,0:T(8,128)(2,1)S(1)}, bf16[256,256]{1,0:T(8,128)(2,1)S(1)}, u32[]{:S(2)}, u32[]{:S(2)}) collective-permute-start(bf16[256,256]{1,0:T(8,128)(2,1)S(1)} %collective-permute-done.12), channel_id=1, source_target_pairs={{0,8},{8,16},{16,24},{24,32},{32,40},{40,48},{48,56},{56,64},{64,7... | collective-permute-start | bytes 393224 | tf_op jit(solution)/shard_map/ppermute | solution.py:17
  111.8 7.1 %collective-permute-start.14 = (bf16[256,256]{1,0:T(8,128)(2,1)S(1)}, bf16[256,256]{1,0:T(8,128)(2,1)S(1)}, u32[]{:S(2)}, u32[]{:S(2)}) collective-permute-start(bf16[256,256]{1,0:T(8,128)(2,1)S(1)} %collective-permute-done.13), channel_id=1, source_target_pairs={{0,8},{8,16},{16,24},{24,32},{32,40},{40,48},{48,56},{56,64},{64,7... | collective-permute-start | bytes 393224 | tf_op jit(solution)/shard_map/ppermute | solution.py:17
  118.8 8.6 %collective-permute-start.15 = (bf16[256,256]{1,0:T(8,128)(2,1)S(1)}, bf16[256,256]{1,0:T(8,128)(2,1)S(1)}, u32[]{:S(2)}, u32[]{:S(2)}) collective-permute-start(bf16[256,256]{1,0:T(8,128)(2,1)S(1)} %collective-permute-done.14), channel_id=1, source_target_pairs={{0,8},{8,16},{16,24},{24,32},{32,40},{40,48},{48,56},{56,64},{64,7... | collective-permute-start | bytes 393224 | tf_op jit(solution)/shard_map/ppermute | solution.py:17
  126.4 1.4 copy-start.2
  126.4 1.4 copy-start.3
  140.1 3.3 copy-start
  140.1 3.3 copy-start.7
  150.4 1.4 copy-start.4
  152.6 0.7 copy-start.5
  159.2 3.3 copy-start
  159.3 3.3 copy-start.7
  169.5 1.4 copy-start.4
  171.7 0.7 copy-start.5
  179.3 7.2 %collective-permute-start.17 = (f32[256,256]{1,0:T(8,128)S(1)}, f32[256,256]{1,0:T(8,128)S(1)}, u32[]{:S(2)}, u32[]{:S(2)}) collective-permute-start(f32[256,256]{1,0:T(8,128)S(1)} %fusion.36), channel_id=1, source_target_pairs={{8,0},{16,8},{24,16},{32,24},{40,32},{48,40},{56,48},{64,56},{72,6... | collective-permute-start | bytes 786440 | tf_op jit(solution)/shard_map/ppermute | solution.py:17
  187.5 7.7 %collective-permute-start.18 = (f32[256,256]{1,0:T(8,128)S(1)}, f32[256,256]{1,0:T(8,128)S(1)}, u32[]{:S(2)}, u32[]{:S(2)}) collective-permute-start(f32[256,256]{1,0:T(8,128)S(1)} %fusion.64), channel_id=1, source_target_pairs={{8,0},{16,8},{24,16},{32,24},{40,32},{48,40},{56,48},{64,56},{72,6... | collective-permute-start | bytes 786440 | tf_op jit(solution)/shard_map/ppermute | solution.py:17
  196.1 7.7 %collective-permute-start.19 = (f32[256,256]{1,0:T(8,128)S(1)}, f32[256,256]{1,0:T(8,128)S(1)}, u32[]{:S(2)}, u32[]{:S(2)}) collective-permute-start(f32[256,256]{1,0:T(8,128)S(1)} %fusion.63), channel_id=1, source_target_pairs={{8,0},{16,8},{24,16},{32,24},{40,32},{48,40},{56,48},{64,56},{72,6... | collective-permute-start | bytes 786440 | tf_op jit(solution)/shard_map/ppermute | solution.py:17
  204.7 7.7 %collective-permute-start.20 = (f32[256,256]{1,0:T(8,128)S(1)}, f32[256,256]{1,0:T(8,128)S(1)}, u32[]{:S(2)}, u32[]{:S(2)}) collective-permute-start(f32[256,256]{1,0:T(8,128)S(1)} %fusion.62), channel_id=1, source_target_pairs={{8,0},{16,8},{24,16},{32,24},{40,32},{48,40},{56,48},{64,56},{72,6... | collective-permute-start | bytes 786440 | tf_op jit(solution)/shard_map/ppermute | solution.py:17
  213.4 8.5 %collective-permute-start.21 = (f32[256,256]{1,0:T(8,128)S(1)}, f32[256,256]{1,0:T(8,128)S(1)}, u32[]{:S(2)}, u32[]{:S(2)}) collective-permute-start(f32[256,256]{1,0:T(8,128)S(1)} %fusion.61), channel_id=1, source_target_pairs={{8,0},{16,8},{24,16},{32,24},{40,32},{48,40},{56,48},{64,56},{72,6... | collective-permute-start | bytes 786440 | tf_op jit(solution)/shard_map/ppermute | solution.py:17
  222.8 8.9 %collective-permute-start.22 = (f32[256,256]{1,0:T(8,128)S(1)}, f32[256,256]{1,0:T(8,128)S(1)}, u32[]{:S(2)}, u32[]{:S(2)}) collective-permute-start(f32[256,256]{1,0:T(8,128)S(1)} %fusion.60), channel_id=1, source_target_pairs={{8,0},{16,8},{24,16},{32,24},{40,32},{48,40},{56,48},{64,56},{72,6... | collective-permute-start | bytes 786440 | tf_op jit(solution)/shard_map/ppermute | solution.py:17
  232.7 8.9 %collective-permute-start.23 = (f32[256,256]{1,0:T(8,128)S(1)}, f32[256,256]{1,0:T(8,128)S(1)}, u32[]{:S(2)}, u32[]{:S(2)}) collective-permute-start(f32[256,256]{1,0:T(8,128)S(1)} %fusion.59), channel_id=1, source_target_pairs={{8,0},{16,8},{24,16},{32,24},{40,32},{48,40},{56,48},{64,56},{72,6... | collective-permute-start | bytes 786440 | tf_op jit(solution)/shard_map/ppermute | solution.py:17
  242.5 8.9 %collective-permute-start.24 = (f32[256,256]{1,0:T(8,128)S(1)}, f32[256,256]{1,0:T(8,128)S(1)}, u32[]{:S(2)}, u32[]{:S(2)}) collective-permute-start(f32[256,256]{1,0:T(8,128)S(1)} %fusion.58), channel_id=1, source_target_pairs={{8,0},{16,8},{24,16},{32,24},{40,32},{48,40},{56,48},{64,56},{72,6... | collective-permute-start | bytes 786440 | tf_op jit(solution)/shard_map/ppermute | solution.py:17
  252.4 8.9 %collective-permute-start.25 = (f32[256,256]{1,0:T(8,128)S(1)}, f32[256,256]{1,0:T(8,128)S(1)}, u32[]{:S(2)}, u32[]{:S(2)}) collective-permute-start(f32[256,256]{1,0:T(8,128)S(1)} %fusion.57), channel_id=1, source_target_pairs={{8,0},{16,8},{24,16},{32,24},{40,32},{48,40},{56,48},{64,56},{72,6... | collective-permute-start | bytes 786440 | tf_op jit(solution)/shard_map/ppermute | solution.py:17
  262.2 8.9 %collective-permute-start.26 = (f32[256,256]{1,0:T(8,128)S(1)}, f32[256,256]{1,0:T(8,128)S(1)}, u32[]{:S(2)}, u32[]{:S(2)}) collective-permute-start(f32[256,256]{1,0:T(8,128)S(1)} %fusion.56), channel_id=1, source_target_pairs={{8,0},{16,8},{24,16},{32,24},{40,32},{48,40},{56,48},{64,56},{72,6... | collective-permute-start | bytes 786440 | tf_op jit(solution)/shard_map/ppermute | solution.py:17
  272.1 8.9 %collective-permute-start.27 = (f32[256,256]{1,0:T(8,128)S(1)}, f32[256,256]{1,0:T(8,128)S(1)}, u32[]{:S(2)}, u32[]{:S(2)}) collective-permute-start(f32[256,256]{1,0:T(8,128)S(1)} %fusion.55), channel_id=1, source_target_pairs={{8,0},{16,8},{24,16},{32,24},{40,32},{48,40},{56,48},{64,56},{72,6... | collective-permute-start | bytes 786440 | tf_op jit(solution)/shard_map/ppermute | solution.py:17
  281.9 8.9 %collective-permute-start.28 = (f32[256,256]{1,0:T(8,128)S(1)}, f32[256,256]{1,0:T(8,128)S(1)}, u32[]{:S(2)}, u32[]{:S(2)}) collective-permute-start(f32[256,256]{1,0:T(8,128)S(1)} %fusion.54), channel_id=1, source_target_pairs={{8,0},{16,8},{24,16},{32,24},{40,32},{48,40},{56,48},{64,56},{72,6... | collective-permute-start | bytes 786440 | tf_op jit(solution)/shard_map/ppermute | solution.py:17
  291.8 8.9 %collective-permute-start.29 = (f32[256,256]{1,0:T(8,128)S(1)}, f32[256,256]{1,0:T(8,128)S(1)}, u32[]{:S(2)}, u32[]{:S(2)}) collective-permute-start(f32[256,256]{1,0:T(8,128)S(1)} %fusion.53), channel_id=1, source_target_pairs={{8,0},{16,8},{24,16},{32,24},{40,32},{48,40},{56,48},{64,56},{72,6... | collective-permute-start | bytes 786440 | tf_op jit(solution)/shard_map/ppermute | solution.py:17
  301.6 8.9 %collective-permute-start.30 = (f32[256,256]{1,0:T(8,128)S(1)}, f32[256,256]{1,0:T(8,128)S(1)}, u32[]{:S(2)}, u32[]{:S(2)}) collective-permute-start(f32[256,256]{1,0:T(8,128)S(1)} %fusion.52), channel_id=1, source_target_pairs={{8,0},{16,8},{24,16},{32,24},{40,32},{48,40},{56,48},{64,56},{72,6... | collective-permute-start | bytes 786440 | tf_op jit(solution)/shard_map/ppermute | solution.py:17
  311.5 11.9 %copy-start.1 = (bf16[1,256,576]{1,2,0:T(8,128)(2,1)S(1)}, bf16[1,256,576]{1,2,0:T(8,128)(2,1)}, u32[]{:S(2)}) copy-start(bf16[1,256,576]{1,2,0:T(8,128)(2,1)} %param.9) | copy-start | bytes 884740
  311.5 14.4 %copy-start.6 = (bf16[2,256,128]{2,1,0:T(8,128)(2,1)S(1)}, bf16[2,256,128]{2,1,0:T(8,128)(2,1)}, u32[]{:S(2)}) copy-start(bf16[2,256,128]{2,1,0:T(8,128)(2,1)} %get-tuple-element.141) | copy-start | bytes 393220
  311.5 9.0 %collective-permute-start.31 = (f32[256,256]{1,0:T(8,128)S(1)}, f32[256,256]{1,0:T(8,128)S(1)}, u32[]{:S(2)}, u32[]{:S(2)}) collective-permute-start(f32[256,256]{1,0:T(8,128)S(1)} %fusion.51), channel_id=1, source_target_pairs={{8,0},{16,8},{24,16},{32,24},{40,32},{48,40},{56,48},{64,56},{72,6... | collective-permute-start | bytes 786440 | tf_op jit(solution)/shard_map/ppermute | solution.py:17
  321.5 8.9 %collective-permute-start.32 = (f32[256,256]{1,0:T(8,128)S(1)}, f32[256,256]{1,0:T(8,128)S(1)}, u32[]{:S(2)}, u32[]{:S(2)}) collective-permute-start(f32[256,256]{1,0:T(8,128)S(1)} %fusion.65), channel_id=1, source_target_pairs={{8,0},{16,8},{24,16},{32,24},{40,32},{48,40},{56,48},{64,56},{72,6... | collective-permute-start | bytes 786440 | tf_op jit(solution)/shard_map/ppermute | solution.py:17
  323.4 12.9 %collective-permute-start.35 = (bf16[256,576]{0,1:T(8,128)(2,1)S(1)}, bf16[256,576]{0,1:T(8,128)(2,1)S(1)}, u32[]{:S(2)}, u32[]{:S(2)}) collective-permute-start(bf16[256,576]{0,1:T(8,128)(2,1)S(1)} %bitcast.125), channel_id=1, source_target_pairs={{192,0},{384,192},{576,384},{193,1},{385,193},{577,385},{194,2},{3... | collective-permute-start | bytes 884744 | tf_op jit(solution)/shard_map/ppermute | solution.py:17
  325.9 10.4 %collective-permute-start.16 = (bf16[256,256]{1,0:T(8,128)(2,1)S(1)}, bf16[256,256]{1,0:T(8,128)(2,1)S(1)}, u32[]{:S(2)}, u32[]{:S(2)}) collective-permute-start(bf16[256,256]{1,0:T(8,128)(2,1)S(1)} %copy_bitcast_fusion), channel_id=1, source_target_pairs={{192,0},{384,192},{576,384},{193,1},{385,193},{577,385},{194,2},{3... | collective-permute-start | bytes 393224 | tf_op jit(solution)/shard_map/ppermute | solution.py:17
  331.4 6.9 %collective-permute-start.33 = (bf16[256,128]{1,0:T(8,128)(2,1)S(1)}, bf16[256,128]{1,0:T(8,128)(2,1)S(1)}, u32[]{:S(2)}, u32[]{:S(2)}) collective-permute-start(bf16[256,128]{1,0:T(8,128)(2,1)S(1)} %get-tuple-element.243), channel_id=1, source_target_pairs={{192,0},{384,192},{576,384},{193,1},{385,193},{577,385},{194,2},{3... | collective-permute-start | bytes 196616 | tf_op jit(solution)/shard_map/ppermute | solution.py:17
  333.8 6.2 %collective-permute-start.34 = (bf16[256,128]{1,0:T(8,128)(2,1)S(1)}, bf16[256,128]{1,0:T(8,128)(2,1)S(1)}, u32[]{:S(2)}, u32[]{:S(2)}) collective-permute-start(bf16[256,128]{1,0:T(8,128)(2,1)S(1)} %get-tuple-element.242), channel_id=1, source_target_pairs={{192,0},{384,192},{576,384},{193,1},{385,193},{577,385},{194,2},{3... | collective-permute-start | bytes 196616 | tf_op jit(solution)/shard_map/ppermute | solution.py:17
Sparse Core Ops, SparseCore 0:
  10.3 50.6 all-gather.4
  70.8 63.3 all-gather.6

commit v2 on v1

--- a/solution.py
+++ b/solution.py
@@ -135,9 +135,23 @@
     allowed = allowed & ((key_doc[None, :] == query_doc[:, None]) | (key_shared[None, :] == 1))
     query_grad, key_sum, value_sum = attend(query_local, key_near, value_near, d_attn, allowed)
     pair_sum = jnp.concatenate([key_sum, value_sum], axis=1)
-    running = pair_sum[:tok_rows]
-    for step in range(1, reach_rows + 1):
-        running = from_behind(running, "row", -1) + pair_sum[step * tok_rows : (step + 1) * tok_rows]
+    pair_sum = pair_sum.reshape(reach_rows + 1, tok_rows, 2 * key_width)
+    even_part = pair_sum[0::2]
+    odd_part = pair_sum[1::2]
+    partner = lax.ppermute(
+        odd_part, "row", [(i, i ^ 1) for i in range(lax.axis_size("row"))]
+    )
+    core_bit = row_index % 2
+    zero_block = jnp.zeros_like(odd_part[:1])
+    partner_aligned = jnp.where(
+        core_bit == 0,
+        jnp.concatenate([zero_block, partner], axis=0),
+        jnp.concatenate([partner, zero_block], axis=0),
+    )
+    chip_sum = even_part + partner_aligned
+    running = chip_sum[0]
+    for step in range(1, reach_rows // 2 + 1):
+        running = from_behind(running, "row", -2) + chip_sum[step]
     key_total = running[:, :key_width]
     value_total = running[:, key_width:]
     handed = from_behind(

time: 356 us -> 292 us (0.82)
  the two profiles are of different devices: /device:TPU:196 before, /device:TPU:194 now
where the time goes in v2:
time: 292 us; the launch traced here: 291 us
  starting transfers between devices  123 us (42%)
  waiting for transfers between devices  92.7 us (32%)
  matrix products  33.9 us (12%)
  between operations  14.6 us (5%)
  other arithmetic  14.3 us (5%)
  local copies, waits for them, and re-layouts  12.7 us (4%)
    ppermute x28, starting transfers between devices, from_behind(): return lax.ppermute(block, axis, route)  121 us
    ppermute x28, waiting for transfers between devices, from_behind(): return lax.ppermute(block, axis, route)  82.6 us
    dot_general x2, matrix products, one_head(): lax.dot_general(probs_low, attn_h, (((0,), (0,)), ((), ())), preferred_el...  12 us
    convert_element_type x2, other arithmetic, one_head(): grad_raw = (attn_probs * (grad_probs - row_delta) * (1.0 - capped * cappe...  7.59 us
    dot_general x2, matrix products, one_head(): lax.dot_general(query_h, key_g, (((1,), (1,)), ((), ())), preferred_eleme...  6.66 us
    dot_general x2, matrix products, one_head(): lax.dot_general(attn_h, value_g, (((1,), (1,)), ((), ())), preferred_elem...  6.26 us
    unnamed x29, local copies, waits for them, and re-layouts  5.91 us
  transfers between devices with their start and end apart: 31, of which 26 were waited for; matrix products, arithmetic and copies ran while one was open for 2% of the time, Pallas kernels for 0%

profile of v2, /device:TPU:194, one launch (start us, length us, event | category | flops | bytes accessed | tf_op | source)
XLA Modules:
  0.0 291.2 jit_solution(18024653312345397496)
XLA Ops:
  8.8 1.9 collective-permute-start
  10.8 4.4 %collective-permute-done = bf16[256,256]{1,0:T(8,128)(2,1)S(1)} collective-permute-done((bf16[256,256]{1,0:T(8,128)(2,1)S(1)}, bf16[256,256]{1,0:T(8,128)(2,1)S(1)}, u32[]{:S(2)}, u32[]{:S(2)}) %collective-permute-start) | collective-permute-done | bytes 131104 | tf_op jit(solution)/shard_map/ppermute | solution.py:17
  15.1 3.1 %collective-permute-start.1 = (bf16[256,256]{1,0:T(8,128)(2,1)S(1)}, bf16[256,256]{1,0:T(8,128)(2,1)S(1)}, u32[]{:S(2)}, u32[]{:S(2)}) collective-permute-start(bf16[256,256]{1,0:T(8,128)(2,1)S(1)} %collective-permute-done), channel_id=1, source_target_pairs={{0,8},{8,16},{16,24},{24,32},{32,40},{40,48},{48,56},{56,64},{64,7... | collective-permute-start | bytes 393224 | tf_op jit(solution)/shard_map/ppermute | solution.py:17
  18.3 3.1 %collective-permute-done.1 = bf16[256,256]{1,0:T(8,128)(2,1)S(1)} collective-permute-done((bf16[256,256]{1,0:T(8,128)(2,1)S(1)}, bf16[256,256]{1,0:T(8,128)(2,1)S(1)}, u32[]{:S(2)}, u32[]{:S(2)}) %collective-permute-start.1) | collective-permute-done | bytes 131104 | tf_op jit(solution)/shard_map/ppermute | solution.py:17
  21.4 4.4 %collective-permute-start.2 = (bf16[256,256]{1,0:T(8,128)(2,1)S(1)}, bf16[256,256]{1,0:T(8,128)(2,1)S(1)}, u32[]{:S(2)}, u32[]{:S(2)}) collective-permute-start(bf16[256,256]{1,0:T(8,128)(2,1)S(1)} %collective-permute-done.1), channel_id=1, source_target_pairs={{0,8},{8,16},{16,24},{24,32},{32,40},{40,48},{48,56},{56,64},{64,7... | collective-permute-start | bytes 393224 | tf_op jit(solution)/shard_map/ppermute | solution.py:17
  25.8 1.9 collective-permute-done.2
  27.7 5.6 %collective-permute-start.3 = (bf16[256,256]{1,0:T(8,128)(2,1)S(1)}, bf16[256,256]{1,0:T(8,128)(2,1)S(1)}, u32[]{:S(2)}, u32[]{:S(2)}) collective-permute-start(bf16[256,256]{1,0:T(8,128)(2,1)S(1)} %collective-permute-done.2), channel_id=1, source_target_pairs={{0,8},{8,16},{16,24},{24,32},{32,40},{40,48},{48,56},{56,64},{64,7... | collective-permute-start | bytes 393224 | tf_op jit(solution)/shard_map/ppermute | solution.py:17
  34.2 6.5 %collective-permute-start.4 = (bf16[256,256]{1,0:T(8,128)(2,1)S(1)}, bf16[256,256]{1,0:T(8,128)(2,1)S(1)}, u32[]{:S(2)}, u32[]{:S(2)}) collective-permute-start(bf16[256,256]{1,0:T(8,128)(2,1)S(1)} %collective-permute-done.3), channel_id=1, source_target_pairs={{0,8},{8,16},{16,24},{24,32},{32,40},{40,48},{48,56},{56,64},{64,7... | collective-permute-start | bytes 393224 | tf_op jit(solution)/shard_map/ppermute | solution.py:17
  41.7 6.5 %collective-permute-start.5 = (bf16[256,256]{1,0:T(8,128)(2,1)S(1)}, bf16[256,256]{1,0:T(8,128)(2,1)S(1)}, u32[]{:S(2)}, u32[]{:S(2)}) collective-permute-start(bf16[256,256]{1,0:T(8,128)(2,1)S(1)} %collective-permute-done.4), channel_id=1, source_target_pairs={{0,8},{8,16},{16,24},{24,32},{32,40},{40,48},{48,56},{56,64},{64,7... | collective-permute-start | bytes 393224 | tf_op jit(solution)/shard_map/ppermute | solution.py:17
  49.2 6.5 %collective-permute-start.6 = (bf16[256,256]{1,0:T(8,128)(2,1)S(1)}, bf16[256,256]{1,0:T(8,128)(2,1)S(1)}, u32[]{:S(2)}, u32[]{:S(2)}) collective-permute-start(bf16[256,256]{1,0:T(8,128)(2,1)S(1)} %collective-permute-done.5), channel_id=1, source_target_pairs={{0,8},{8,16},{16,24},{24,32},{32,40},{40,48},{48,56},{56,64},{64,7... | collective-permute-start | bytes 393224 | tf_op jit(solution)/shard_map/ppermute | solution.py:17
  56.7 6.5 %collective-permute-start.7 = (bf16[256,256]{1,0:T(8,128)(2,1)S(1)}, bf16[256,256]{1,0:T(8,128)(2,1)S(1)}, u32[]{:S(2)}, u32[]{:S(2)}) collective-permute-start(bf16[256,256]{1,0:T(8,128)(2,1)S(1)} %collective-permute-done.6), channel_id=1, source_target_pairs={{0,8},{8,16},{16,24},{24,32},{32,40},{40,48},{48,56},{56,64},{64,7... | collective-permute-start | bytes 393224 | tf_op jit(solution)/shard_map/ppermute | solution.py:17
  64.2 6.5 %collective-permute-start.8 = (bf16[256,256]{1,0:T(8,128)(2,1)S(1)}, bf16[256,256]{1,0:T(8,128)(2,1)S(1)}, u32[]{:S(2)}, u32[]{:S(2)}) collective-permute-start(bf16[256,256]{1,0:T(8,128)(2,1)S(1)} %collective-permute-done.7), channel_id=1, source_target_pairs={{0,8},{8,16},{16,24},{24,32},{32,40},{40,48},{48,56},{56,64},{64,7... | collective-permute-start | bytes 393224 | tf_op jit(solution)/shard_map/ppermute | solution.py:17
  71.7 6.5 %collective-permute-start.9 = (bf16[256,256]{1,0:T(8,128)(2,1)S(1)}, bf16[256,256]{1,0:T(8,128)(2,1)S(1)}, u32[]{:S(2)}, u32[]{:S(2)}) collective-permute-start(bf16[256,256]{1,0:T(8,128)(2,1)S(1)} %collective-permute-done.8), channel_id=1, source_target_pairs={{0,8},{8,16},{16,24},{24,32},{32,40},{40,48},{48,56},{56,64},{64,7... | collective-permute-start | bytes 393224 | tf_op jit(solution)/shard_map/ppermute | solution.py:17
  79.1 6.5 %collective-permute-start.10 = (bf16[256,256]{1,0:T(8,128)(2,1)S(1)}, bf16[256,256]{1,0:T(8,128)(2,1)S(1)}, u32[]{:S(2)}, u32[]{:S(2)}) collective-permute-start(bf16[256,256]{1,0:T(8,128)(2,1)S(1)} %collective-permute-done.9), channel_id=1, source_target_pairs={{0,8},{8,16},{16,24},{24,32},{32,40},{40,48},{48,56},{56,64},{64,7... | collective-permute-start | bytes 393224 | tf_op jit(solution)/shard_map/ppermute | solution.py:17
  86.6 6.5 %collective-permute-start.11 = (bf16[256,256]{1,0:T(8,128)(2,1)S(1)}, bf16[256,256]{1,0:T(8,128)(2,1)S(1)}, u32[]{:S(2)}, u32[]{:S(2)}) collective-permute-start(bf16[256,256]{1,0:T(8,128)(2,1)S(1)} %collective-permute-done.10), channel_id=1, source_target_pairs={{0,8},{8,16},{16,24},{24,32},{32,40},{40,48},{48,56},{56,64},{64,7... | collective-permute-start | bytes 393224 | tf_op jit(solution)/shard_map/ppermute | solution.py:17
  94.1 7.6 %collective-permute-start.12 = (bf16[256,256]{1,0:T(8,128)(2,1)S(1)}, bf16[256,256]{1,0:T(8,128)(2,1)S(1)}, u32[]{:S(2)}, u32[]{:S(2)}) collective-permute-start(bf16[256,256]{1,0:T(8,128)(2,1)S(1)} %collective-permute-done.11), channel_id=1, source_target_pairs={{0,8},{8,16},{16,24},{24,32},{32,40},{40,48},{48,56},{56,64},{64,7... | collective-permute-start | bytes 393224 | tf_op jit(solution)/shard_map/ppermute | solution.py:17
  102.7 7.5 %collective-permute-start.13 = (bf16[256,256]{1,0:T(8,128)(2,1)S(1)}, bf16[256,256]{1,0:T(8,128)(2,1)S(1)}, u32[]{:S(2)}, u32[]{:S(2)}) collective-permute-start(bf16[256,256]{1,0:T(8,128)(2,1)S(1)} %collective-permute-done.12), channel_id=1, source_target_pairs={{0,8},{8,16},{16,24},{24,32},{32,40},{40,48},{48,56},{56,64},{64,7... | collective-permute-start | bytes 393224 | tf_op jit(solution)/shard_map/ppermute | solution.py:17
  111.8 6.1 %collective-permute-start.14 = (bf16[256,256]{1,0:T(8,128)(2,1)S(1)}, bf16[256,256]{1,0:T(8,128)(2,1)S(1)}, u32[]{:S(2)}, u32[]{:S(2)}) collective-permute-start(bf16[256,256]{1,0:T(8,128)(2,1)S(1)} %collective-permute-done.13), channel_id=1, source_target_pairs={{0,8},{8,16},{16,24},{24,32},{32,40},{40,48},{48,56},{56,64},{64,7... | collective-permute-start | bytes 393224 | tf_op jit(solution)/shard_map/ppermute | solution.py:17
  118.9 6.9 %collective-permute-start.15 = (bf16[256,256]{1,0:T(8,128)(2,1)S(1)}, bf16[256,256]{1,0:T(8,128)(2,1)S(1)}, u32[]{:S(2)}, u32[]{:S(2)}) collective-permute-start(bf16[256,256]{1,0:T(8,128)(2,1)S(1)} %collective-permute-done.14), channel_id=1, source_target_pairs={{0,8},{8,16},{16,24},{24,32},{32,40},{40,48},{48,56},{56,64},{64,7... | collective-permute-start | bytes 393224 | tf_op jit(solution)/shard_map/ppermute | solution.py:17
  127.8 1.2 slice_bitcast_fusion
  129.0 5.3 %all-gather.7.cloned.1.call-done = bf16[1,256,4608]{1,2,0:T(8,128)(2,1)} async-done(((bf16[1,256,192]{1,2,0:T(8,128)(2,1)}), bf16[1,256,4608]{1,2,0:T(8,128)(2,1)}) %all-gather.7.cloned.1.call-update) | async-done | bytes 2359312 | tf_op jit(solution)/shard_map/all_gather | solution.py:100
  134.3 3.4 %fusion.30 = bf16[256,256]{0,1:T(8,128)(2,1)S(1)} fusion(bf16[1,256,4608]{1,2,0:T(8,128)(2,1)} %all-gather.7.cloned.1.call-done, bf16[1,256,4608]{1,2,0:T(8,128)(2,1)} %all-gather.5.cloned.1.call-done), kind=kOutput, calls=%fused_computation.40 | convolution fusion | flops 604045312 | bytes 4849664 | tf_op jit(solution)/shard_map/dot_general | solution.py:98
  138.6 1.5 broadcast_in_dim.77.clone
  140.1 38.1 %while.18 = (s32[]{:T(128)}, f32[1,4352,128]{2,1,0:T(8,128)S(1)}, f32[1,4352,128]{2,1,0:T(8,128)}, bf16[2,256,128]{2,1,0:T(8,128)(2,1)}, bf16[2,256,128]{1,2,0:T...) while((s32[]{:T(128)}, f32[1,4352,128]{2,1,0:T(8,128)S(1)}, ...), condition=%wide.region_4.5_spmd.clone, body=%wide.region_1.4_spmd.clone.sunk | while | flops 1488485888 | bytes 51199188 | solution.py:78
  140.1 3.3 %fusion.64 = (f32[256]{0:T(256)S(1)}, f32[256,4352]{1,0:T(8,128)S(1)}) fusion(pred[4352]{0:T(1024)(128)(4,1)S(1)} %get-tuple-element.382, s32[256]{0:T(256)S(1)} %get-tuple-element.380, s32[4352]{0:T(1024)S(1)} %get-tuple-element.381, s32[256]{0:T(256)S(1)} %get-tuple-element.379, s32[4352]{0:T(1024)S(1)} %get-tuple-element.378, ...), kind=kOutput, calls=%fused_computation.34.clone.1 | convolution fusion | flops 298581760 | bytes 5690372 | tf_op jit(solution)/shard_map/while/body/eval_jaxpr/dot_general | solution.py:37
  143.5 3.1 %multiply_reduce_fusion.2 = (f32[256]{0:T(256)S(1)}, f32[256,4352]{1,0:T(8,128)S(1)}) fusion(f32[256]{0:T(256)S(1)} %get-tuple-element.336, f32[256,4352]{1,0:T(8,128)S(1)} %get-tuple-element.335, pred[4352]{0:T(1024)(128)(4,1)S(1)} %get-tuple-element.382, s32[256]{0:T(256)S(1)} %get-tuple-element.380, s32[4352]{0:T(1024)S(1)} %get-tuple-element.381, ...), kind=kOutput, calls=%fused_computation.9.clone.1 | convolution fusion | flops 299695872 | bytes 10147844 | tf_op jit(solution)/shard_map/while/body/eval_jaxpr/dot_general | solution.py:49
  146.6 3.8 %multiply_convert_fusion.2 = bf16[256,4352]{1,0:T(8,128)(2,1)S(1)} fusion(f32[256,4352]{1,0:T(8,128)S(1)} %get-tuple-element.335, f32[256,4352]{1,0:T(8,128)S(1)} %get-tuple-element.337, f32[256]{0:T(256)S(1)} %get-tuple-element.338, f32[256]{0:T(256)S(1)} %get-tuple-element.336, pred[4352]{0:T(1024)(128)(4,1)S(1)} %get-tuple-element.382, ...), kind=kLoop, calls=%fused_computation.8.clone.1 | loop fusion | flops 20054016 | bytes 11188736 | tf_op jit(solution)/shard_map/while/body/eval_jaxpr/convert_element_type | solution.py:55
  150.4 1.4 fusion.65
  151.8 1.4 fusion.67
  153.1 6.0 %fusion.66 = f32[1,4352,128]{2,1,0:T(8,128)} fusion(f32[1,4352,128]{2,1,0:T(8,128)} %get-tuple-element.356, bf16[2,256,128]{2,1,0:T(8,128)(2,1)S(1)} %copy-done.5, s32[]{:T(128)} %get-tuple-element.354, f32[256]{0:T(256)S(1)} %get-tuple-element.336, f32[256,4352]{1,0:T(8,128)S(1)} %get-tuple-element.335, pred[4352]{0:T(1024)(128)(4,1)S(1)} %get-tuple-element.382, ...), kind=kOutput, calls=%fused_computation.6.clone.1 | convolution fusion | flops 299139072 | bytes 9032708 | tf_op jit(solution)/shard_map/while/body/eval_jaxpr/dot_general | solution.py:46
  159.2 3.3 %fusion.64 = (f32[256]{0:T(256)S(1)}, f32[256,4352]{1,0:T(8,128)S(1)}) fusion(pred[4352]{0:T(1024)(128)(4,1)S(1)} %get-tuple-element.382, s32[256]{0:T(256)S(1)} %get-tuple-element.380, s32[4352]{0:T(1024)S(1)} %get-tuple-element.381, s32[256]{0:T(256)S(1)} %get-tuple-element.379, s32[4352]{0:T(1024)S(1)} %get-tuple-element.378, ...), kind=kOutput, calls=%fused_computation.34.clone.1 | convolution fusion | flops 298581760 | bytes 5690372 | tf_op jit(solution)/shard_map/while/body/eval_jaxpr/dot_general | solution.py:37
  162.5 3.1 %multiply_reduce_fusion.2 = (f32[256]{0:T(256)S(1)}, f32[256,4352]{1,0:T(8,128)S(1)}) fusion(f32[256]{0:T(256)S(1)} %get-tuple-element.336, f32[256,4352]{1,0:T(8,128)S(1)} %get-tuple-element.335, pred[4352]{0:T(1024)(128)(4,1)S(1)} %get-tuple-element.382, s32[256]{0:T(256)S(1)} %get-tuple-element.380, s32[4352]{0:T(1024)S(1)} %get-tuple-element.381, ...), kind=kOutput, calls=%fused_computation.9.clone.1 | convolution fusion | flops 299695872 | bytes 10147844 | tf_op jit(solution)/shard_map/while/body/eval_jaxpr/dot_general | solution.py:49
  165.6 3.8 %multiply_convert_fusion.2 = bf16[256,4352]{1,0:T(8,128)(2,1)S(1)} fusion(f32[256,4352]{1,0:T(8,128)S(1)} %get-tuple-element.335, f32[256,4352]{1,0:T(8,128)S(1)} %get-tuple-element.337, f32[256]{0:T(256)S(1)} %get-tuple-element.338, f32[256]{0:T(256)S(1)} %get-tuple-element.336, pred[4352]{0:T(1024)(128)(4,1)S(1)} %get-tuple-element.382, ...), kind=kLoop, calls=%fused_computation.8.clone.1 | loop fusion | flops 20054016 | bytes 11188736 | tf_op jit(solution)/shard_map/while/body/eval_jaxpr/convert_element_type | solution.py:55
  169.5 1.4 fusion.65
  170.8 1.4 fusion.67
  172.2 6.0 %fusion.66 = f32[1,4352,128]{2,1,0:T(8,128)} fusion(f32[1,4352,128]{2,1,0:T(8,128)} %get-tuple-element.356, bf16[2,256,128]{2,1,0:T(8,128)(2,1)S(1)} %copy-done.5, s32[]{:T(128)} %get-tuple-element.354, f32[256]{0:T(256)S(1)} %get-tuple-element.336, f32[256,4352]{1,0:T(8,128)S(1)} %get-tuple-element.335, pred[4352]{0:T(1024)(128)(4,1)S(1)} %get-tuple-element.382, ...), kind=kOutput, calls=%fused_computation.6.clone.1 | convolution fusion | flops 299139072 | bytes 9032708 | tf_op jit(solution)/shard_map/while/body/eval_jaxpr/dot_general | solution.py:46
  178.2 1.9 pad_maximum_fusion
  180.2 2.1 copy-done
  182.2 1.5 slice.50
  183.7 2.1 collective-permute-start.17
  185.9 4.1 %collective-permute-done.17 = f32[8,256,256]{2,1,0:T(8,128)S(1)} collective-permute-done((f32[8,256,256]{2,1,0:T(8,128)}, f32[8,256,256]{2,1,0:T(8,128)S(1)}, u32[]{:S(2)}, u32[]{:S(2)}) %collective-permute-start.17) | collective-permute-done | bytes 2097184 | tf_op jit(solution)/shard_map/ppermute | solution.py:141
  190.0 2.0 select_add_fusion
  192.0 3.3 %collective-permute-start.18 = (f32[256,256]{1,0:T(8,128)S(1)}, f32[256,256]{1,0:T(8,128)S(1)}, u32[]{:S(2)}, u32[]{:S(2)}) collective-permute-start(f32[256,256]{1,0:T(8,128)S(1)} %slice_bitcast_fusion.10), channel_id=1, source_target_pairs={{16,0},{24,8},{32,16},{40,24},{48,32},{56,40},{64,48},{72,56},{80,... | collective-permute-start | bytes 786440 | tf_op jit(solution)/shard_map/ppermute | solution.py:17
  195.2 8.3 %collective-permute-done.18 = f32[256,256]{1,0:T(8,128)S(1)} collective-permute-done((f32[256,256]{1,0:T(8,128)S(1)}, f32[256,256]{1,0:T(8,128)S(1)}, u32[]{:S(2)}, u32[]{:S(2)}) %collective-permute-start.18) | collective-permute-done | bytes 262176 | tf_op jit(solution)/shard_map/ppermute | solution.py:17
  203.6 2.2 collective-permute-start.19
  205.8 8.6 %collective-permute-done.19 = f32[256,256]{1,0:T(8,128)S(1)} collective-permute-done((f32[256,256]{1,0:T(8,128)S(1)}, f32[256,256]{1,0:T(8,128)S(1)}, u32[]{:S(2)}, u32[]{:S(2)}) %collective-permute-start.19) | collective-permute-done | bytes 262176 | tf_op jit(solution)/shard_map/ppermute | solution.py:17
  214.4 1.9 collective-permute-start.20
  216.3 7.9 %collective-permute-done.20 = f32[256,256]{1,0:T(8,128)S(1)} collective-permute-done((f32[256,256]{1,0:T(8,128)S(1)}, f32[256,256]{1,0:T(8,128)S(1)}, u32[]{:S(2)}, u32[]{:S(2)}) %collective-permute-start.20) | collective-permute-done | bytes 262176 | tf_op jit(solution)/shard_map/ppermute | solution.py:17
  224.3 1.9 collective-permute-start.21
  226.2 7.5 %collective-permute-done.21 = f32[256,256]{1,0:T(8,128)S(1)} collective-permute-done((f32[256,256]{1,0:T(8,128)S(1)}, f32[256,256]{1,0:T(8,128)S(1)}, u32[]{:S(2)}, u32[]{:S(2)}) %collective-permute-start.21) | collective-permute-done | bytes 262176 | tf_op jit(solution)/shard_map/ppermute | solution.py:17
  233.8 1.9 collective-permute-start.22
  235.7 7.5 %collective-permute-done.22 = f32[256,256]{1,0:T(8,128)S(1)} collective-permute-done((f32[256,256]{1,0:T(8,128)S(1)}, f32[256,256]{1,0:T(8,128)S(1)}, u32[]{:S(2)}, u32[]{:S(2)}) %collective-permute-start.22) | collective-permute-done | bytes 262176 | tf_op jit(solution)/shard_map/ppermute | solution.py:17
  243.3 1.9 collective-permute-start.23
  245.3 7.6 %collective-permute-done.23 = f32[256,256]{1,0:T(8,128)S(1)} collective-permute-done((f32[256,256]{1,0:T(8,128)S(1)}, f32[256,256]{1,0:T(8,128)S(1)}, u32[]{:S(2)}, u32[]{:S(2)}) %collective-permute-start.23) | collective-permute-done | bytes 262176 | tf_op jit(solution)/shard_map/ppermute | solution.py:17
  252.9 1.9 collective-permute-start.24
  254.8 8.7 %collective-permute-done.24 = f32[256,256]{1,0:T(8,128)S(1)} collective-permute-done((f32[256,256]{1,0:T(8,128)S(1)}, f32[256,256]{1,0:T(8,128)S(1)}, u32[]{:S(2)}, u32[]{:S(2)}) %collective-permute-start.24) | collective-permute-done | bytes 262176 | tf_op jit(solution)/shard_map/ppermute | solution.py:17
  263.6 1.9 collective-permute-start.25
  265.5 2.4 collective-permute-start.28
  268.9 1.9 collective-permute-start.16
  270.8 2.2 collective-permute-done.25
  273.1 2.4 collective-permute-start.26
  275.6 1.9 collective-permute-start.27
  277.5 1.8 collective-permute-done.26
  279.3 2.5 collective-permute-done.27
  (78 shorter events, 20.6 us)
Async XLA Ops:
  7.2 121.8 %all-gather.5.cloned.1.call-start = ((), (), s32[]{:S(2)}) async-start(), calls=%async_computation | async-start | bytes 2654208 | tf_op jit(solution)/shard_map/all_gather | solution.py:97
  7.9 126.4 %all-gather.7.cloned.1.call-start = ((), (), s32[]{:S(2)}) async-start(), calls=%async_computation.1 | async-start | bytes 2457600 | tf_op jit(solution)/shard_map/all_gather | solution.py:100
  8.8 6.3 %collective-permute-start = (bf16[256,256]{1,0:T(8,128)(2,1)S(1)}, bf16[256,256]{1,0:T(8,128)(2,1)S(1)}, u32[]{:S(2)}, u32[]{:S(2)}) collective-permute-start(bf16[256,256]{1,0:T(8,128)(2,1)S(1)} %pad_maximum_fusion.1), channel_id=1, source_target_pairs={{0,8},{8,16},{16,24},{24,32},{32,40},{40,48},{48,56},{56,64},{64,7... | collective-permute-start | bytes 393224 | tf_op jit(solution)/shard_map/ppermute | solution.py:17
  15.1 6.3 %collective-permute-start.1 = (bf16[256,256]{1,0:T(8,128)(2,1)S(1)}, bf16[256,256]{1,0:T(8,128)(2,1)S(1)}, u32[]{:S(2)}, u32[]{:S(2)}) collective-permute-start(bf16[256,256]{1,0:T(8,128)(2,1)S(1)} %collective-permute-done), channel_id=1, source_target_pairs={{0,8},{8,16},{16,24},{24,32},{32,40},{40,48},{48,56},{56,64},{64,7... | collective-permute-start | bytes 393224 | tf_op jit(solution)/shard_map/ppermute | solution.py:17
  21.4 6.3 %collective-permute-start.2 = (bf16[256,256]{1,0:T(8,128)(2,1)S(1)}, bf16[256,256]{1,0:T(8,128)(2,1)S(1)}, u32[]{:S(2)}, u32[]{:S(2)}) collective-permute-start(bf16[256,256]{1,0:T(8,128)(2,1)S(1)} %collective-permute-done.1), channel_id=1, source_target_pairs={{0,8},{8,16},{16,24},{24,32},{32,40},{40,48},{48,56},{56,64},{64,7... | collective-permute-start | bytes 393224 | tf_op jit(solution)/shard_map/ppermute | solution.py:17
  27.7 6.5 %collective-permute-start.3 = (bf16[256,256]{1,0:T(8,128)(2,1)S(1)}, bf16[256,256]{1,0:T(8,128)(2,1)S(1)}, u32[]{:S(2)}, u32[]{:S(2)}) collective-permute-start(bf16[256,256]{1,0:T(8,128)(2,1)S(1)} %collective-permute-done.2), channel_id=1, source_target_pairs={{0,8},{8,16},{16,24},{24,32},{32,40},{40,48},{48,56},{56,64},{64,7... | collective-permute-start | bytes 393224 | tf_op jit(solution)/shard_map/ppermute | solution.py:17
  34.2 7.5 %collective-permute-start.4 = (bf16[256,256]{1,0:T(8,128)(2,1)S(1)}, bf16[256,256]{1,0:T(8,128)(2,1)S(1)}, u32[]{:S(2)}, u32[]{:S(2)}) collective-permute-start(bf16[256,256]{1,0:T(8,128)(2,1)S(1)} %collective-permute-done.3), channel_id=1, source_target_pairs={{0,8},{8,16},{16,24},{24,32},{32,40},{40,48},{48,56},{56,64},{64,7... | collective-permute-start | bytes 393224 | tf_op jit(solution)/shard_map/ppermute | solution.py:17
  41.7 7.5 %collective-permute-start.5 = (bf16[256,256]{1,0:T(8,128)(2,1)S(1)}, bf16[256,256]{1,0:T(8,128)(2,1)S(1)}, u32[]{:S(2)}, u32[]{:S(2)}) collective-permute-start(bf16[256,256]{1,0:T(8,128)(2,1)S(1)} %collective-permute-done.4), channel_id=1, source_target_pairs={{0,8},{8,16},{16,24},{24,32},{32,40},{40,48},{48,56},{56,64},{64,7... | collective-permute-start | bytes 393224 | tf_op jit(solution)/shard_map/ppermute | solution.py:17
  49.2 7.5 %collective-permute-start.6 = (bf16[256,256]{1,0:T(8,128)(2,1)S(1)}, bf16[256,256]{1,0:T(8,128)(2,1)S(1)}, u32[]{:S(2)}, u32[]{:S(2)}) collective-permute-start(bf16[256,256]{1,0:T(8,128)(2,1)S(1)} %collective-permute-done.5), channel_id=1, source_target_pairs={{0,8},{8,16},{16,24},{24,32},{32,40},{40,48},{48,56},{56,64},{64,7... | collective-permute-start | bytes 393224 | tf_op jit(solution)/shard_map/ppermute | solution.py:17
  56.7 7.5 %collective-permute-start.7 = (bf16[256,256]{1,0:T(8,128)(2,1)S(1)}, bf16[256,256]{1,0:T(8,128)(2,1)S(1)}, u32[]{:S(2)}, u32[]{:S(2)}) collective-permute-start(bf16[256,256]{1,0:T(8,128)(2,1)S(1)} %collective-permute-done.6), channel_id=1, source_target_pairs={{0,8},{8,16},{16,24},{24,32},{32,40},{40,48},{48,56},{56,64},{64,7... | collective-permute-start | bytes 393224 | tf_op jit(solution)/shard_map/ppermute | solution.py:17
  64.2 7.5 %collective-permute-start.8 = (bf16[256,256]{1,0:T(8,128)(2,1)S(1)}, bf16[256,256]{1,0:T(8,128)(2,1)S(1)}, u32[]{:S(2)}, u32[]{:S(2)}) collective-permute-start(bf16[256,256]{1,0:T(8,128)(2,1)S(1)} %collective-permute-done.7), channel_id=1, source_target_pairs={{0,8},{8,16},{16,24},{24,32},{32,40},{40,48},{48,56},{56,64},{64,7... | collective-permute-start | bytes 393224 | tf_op jit(solution)/shard_map/ppermute | solution.py:17
  71.7 7.5 %collective-permute-start.9 = (bf16[256,256]{1,0:T(8,128)(2,1)S(1)}, bf16[256,256]{1,0:T(8,128)(2,1)S(1)}, u32[]{:S(2)}, u32[]{:S(2)}) collective-permute-start(bf16[256,256]{1,0:T(8,128)(2,1)S(1)} %collective-permute-done.8), channel_id=1, source_target_pairs={{0,8},{8,16},{16,24},{24,32},{32,40},{40,48},{48,56},{56,64},{64,7... | collective-permute-start | bytes 393224 | tf_op jit(solution)/shard_map/ppermute | solution.py:17
  79.1 7.5 %collective-permute-start.10 = (bf16[256,256]{1,0:T(8,128)(2,1)S(1)}, bf16[256,256]{1,0:T(8,128)(2,1)S(1)}, u32[]{:S(2)}, u32[]{:S(2)}) collective-permute-start(bf16[256,256]{1,0:T(8,128)(2,1)S(1)} %collective-permute-done.9), channel_id=1, source_target_pairs={{0,8},{8,16},{16,24},{24,32},{32,40},{40,48},{48,56},{56,64},{64,7... | collective-permute-start | bytes 393224 | tf_op jit(solution)/shard_map/ppermute | solution.py:17
  86.6 7.5 %collective-permute-start.11 = (bf16[256,256]{1,0:T(8,128)(2,1)S(1)}, bf16[256,256]{1,0:T(8,128)(2,1)S(1)}, u32[]{:S(2)}, u32[]{:S(2)}) collective-permute-start(bf16[256,256]{1,0:T(8,128)(2,1)S(1)} %collective-permute-done.10), channel_id=1, source_target_pairs={{0,8},{8,16},{16,24},{24,32},{32,40},{40,48},{48,56},{56,64},{64,7... | collective-permute-start | bytes 393224 | tf_op jit(solution)/shard_map/ppermute | solution.py:17
  94.1 8.5 %collective-permute-start.12 = (bf16[256,256]{1,0:T(8,128)(2,1)S(1)}, bf16[256,256]{1,0:T(8,128)(2,1)S(1)}, u32[]{:S(2)}, u32[]{:S(2)}) collective-permute-start(bf16[256,256]{1,0:T(8,128)(2,1)S(1)} %collective-permute-done.11), channel_id=1, source_target_pairs={{0,8},{8,16},{16,24},{24,32},{32,40},{40,48},{48,56},{56,64},{64,7... | collective-permute-start | bytes 393224 | tf_op jit(solution)/shard_map/ppermute | solution.py:17
  102.7 9.1 %collective-permute-start.13 = (bf16[256,256]{1,0:T(8,128)(2,1)S(1)}, bf16[256,256]{1,0:T(8,128)(2,1)S(1)}, u32[]{:S(2)}, u32[]{:S(2)}) collective-permute-start(bf16[256,256]{1,0:T(8,128)(2,1)S(1)} %collective-permute-done.12), channel_id=1, source_target_pairs={{0,8},{8,16},{16,24},{24,32},{32,40},{40,48},{48,56},{56,64},{64,7... | collective-permute-start | bytes 393224 | tf_op jit(solution)/shard_map/ppermute | solution.py:17
  111.8 7.1 %collective-permute-start.14 = (bf16[256,256]{1,0:T(8,128)(2,1)S(1)}, bf16[256,256]{1,0:T(8,128)(2,1)S(1)}, u32[]{:S(2)}, u32[]{:S(2)}) collective-permute-start(bf16[256,256]{1,0:T(8,128)(2,1)S(1)} %collective-permute-done.13), channel_id=1, source_target_pairs={{0,8},{8,16},{16,24},{24,32},{32,40},{40,48},{48,56},{56,64},{64,7... | collective-permute-start | bytes 393224 | tf_op jit(solution)/shard_map/ppermute | solution.py:17
  118.9 8.6 %collective-permute-start.15 = (bf16[256,256]{1,0:T(8,128)(2,1)S(1)}, bf16[256,256]{1,0:T(8,128)(2,1)S(1)}, u32[]{:S(2)}, u32[]{:S(2)}) collective-permute-start(bf16[256,256]{1,0:T(8,128)(2,1)S(1)} %collective-permute-done.14), channel_id=1, source_target_pairs={{0,8},{8,16},{16,24},{24,32},{32,40},{40,48},{48,56},{56,64},{64,7... | collective-permute-start | bytes 393224 | tf_op jit(solution)/shard_map/ppermute | solution.py:17
  126.4 1.4 copy-start.3
  126.4 1.4 copy-start.4
  140.1 3.3 %copy-start.1 = (bf16[1,4352,128]{2,1,0:T(8,128)(2,1)S(1)}, bf16[1,4352,128]{2,1,0:T(8,128)(2,1)}, u32[]{:S(2)}) copy-start(bf16[1,4352,128]{2,1,0:T(8,128)(2,1)} %get-tuple-element.376) | copy-start | bytes 3342340 | tf_op jit(solution)/shard_map/while
  140.1 3.3 %copy-start.5 = (bf16[2,256,128]{2,1,0:T(8,128)(2,1)S(1)}, bf16[2,256,128]{2,1,0:T(8,128)(2,1)}, u32[]{:S(2)}) copy-start(bf16[2,256,128]{2,1,0:T(8,128)(2,1)} %get-tuple-element.375) | copy-start | bytes 393220 | tf_op jit(solution)/shard_map/while
  159.2 3.3 %copy-start.1 = (bf16[1,4352,128]{2,1,0:T(8,128)(2,1)S(1)}, bf16[1,4352,128]{2,1,0:T(8,128)(2,1)}, u32[]{:S(2)}) copy-start(bf16[1,4352,128]{2,1,0:T(8,128)(2,1)} %get-tuple-element.376) | copy-start | bytes 3342340 | tf_op jit(solution)/shard_map/while
  159.2 3.3 %copy-start.5 = (bf16[2,256,128]{2,1,0:T(8,128)(2,1)S(1)}, bf16[2,256,128]{2,1,0:T(8,128)(2,1)}, u32[]{:S(2)}) copy-start(bf16[2,256,128]{2,1,0:T(8,128)(2,1)} %get-tuple-element.375) | copy-start | bytes 393220 | tf_op jit(solution)/shard_map/while
  180.2 2.1 copy-start
  183.7 6.3 %collective-permute-start.17 = (f32[8,256,256]{2,1,0:T(8,128)}, f32[8,256,256]{2,1,0:T(8,128)S(1)}, u32[]{:S(2)}, u32[]{:S(2)}) collective-permute-start(f32[8,256,256]{2,1,0:T(8,128)} %slice.50), channel_id=1, source_target_pairs={{0,8},{8,0},{16,24},{24,16},{32,40},{40,32},{48,56},{56,48},{64,72... | collective-permute-start | bytes 6291464 | tf_op jit(solution)/shard_map/ppermute | solution.py:141
  192.0 11.5 %collective-permute-start.18 = (f32[256,256]{1,0:T(8,128)S(1)}, f32[256,256]{1,0:T(8,128)S(1)}, u32[]{:S(2)}, u32[]{:S(2)}) collective-permute-start(f32[256,256]{1,0:T(8,128)S(1)} %slice_bitcast_fusion.10), channel_id=1, source_target_pairs={{16,0},{24,8},{32,16},{40,24},{48,32},{56,40},{64,48},{72,56},{80,... | collective-permute-start | bytes 786440 | tf_op jit(solution)/shard_map/ppermute | solution.py:17
  203.5 62.0 %copy-start.2 = (bf16[1,256,576]{1,2,0:T(8,128)(2,1)S(1)}, bf16[1,256,576]{1,2,0:T(8,128)(2,1)}, u32[]{:S(2)}) copy-start(bf16[1,256,576]{1,2,0:T(8,128)(2,1)} %param.9) | copy-start | bytes 884740
  203.6 10.8 %collective-permute-start.19 = (f32[256,256]{1,0:T(8,128)S(1)}, f32[256,256]{1,0:T(8,128)S(1)}, u32[]{:S(2)}, u32[]{:S(2)}) collective-permute-start(f32[256,256]{1,0:T(8,128)S(1)} %fusion.43), channel_id=1, source_target_pairs={{16,0},{24,8},{32,16},{40,24},{48,32},{56,40},{64,48},{72,56},{80,... | collective-permute-start | bytes 786440 | tf_op jit(solution)/shard_map/ppermute | solution.py:17
  214.4 9.8 %collective-permute-start.20 = (f32[256,256]{1,0:T(8,128)S(1)}, f32[256,256]{1,0:T(8,128)S(1)}, u32[]{:S(2)}, u32[]{:S(2)}) collective-permute-start(f32[256,256]{1,0:T(8,128)S(1)} %fusion.42), channel_id=1, source_target_pairs={{16,0},{24,8},{32,16},{40,24},{48,32},{56,40},{64,48},{72,56},{80,... | collective-permute-start | bytes 786440 | tf_op jit(solution)/shard_map/ppermute | solution.py:17
  224.3 9.5 %collective-permute-start.21 = (f32[256,256]{1,0:T(8,128)S(1)}, f32[256,256]{1,0:T(8,128)S(1)}, u32[]{:S(2)}, u32[]{:S(2)}) collective-permute-start(f32[256,256]{1,0:T(8,128)S(1)} %fusion.41), channel_id=1, source_target_pairs={{16,0},{24,8},{32,16},{40,24},{48,32},{56,40},{64,48},{72,56},{80,... | collective-permute-start | bytes 786440 | tf_op jit(solution)/shard_map/ppermute | solution.py:17
  233.8 9.5 %collective-permute-start.22 = (f32[256,256]{1,0:T(8,128)S(1)}, f32[256,256]{1,0:T(8,128)S(1)}, u32[]{:S(2)}, u32[]{:S(2)}) collective-permute-start(f32[256,256]{1,0:T(8,128)S(1)} %fusion.40), channel_id=1, source_target_pairs={{16,0},{24,8},{32,16},{40,24},{48,32},{56,40},{64,48},{72,56},{80,... | collective-permute-start | bytes 786440 | tf_op jit(solution)/shard_map/ppermute | solution.py:17
  243.3 9.5 %collective-permute-start.23 = (f32[256,256]{1,0:T(8,128)S(1)}, f32[256,256]{1,0:T(8,128)S(1)}, u32[]{:S(2)}, u32[]{:S(2)}) collective-permute-start(f32[256,256]{1,0:T(8,128)S(1)} %fusion.39), channel_id=1, source_target_pairs={{16,0},{24,8},{32,16},{40,24},{48,32},{56,40},{64,48},{72,56},{80,... | collective-permute-start | bytes 786440 | tf_op jit(solution)/shard_map/ppermute | solution.py:17
  252.9 10.7 %collective-permute-start.24 = (f32[256,256]{1,0:T(8,128)S(1)}, f32[256,256]{1,0:T(8,128)S(1)}, u32[]{:S(2)}, u32[]{:S(2)}) collective-permute-start(f32[256,256]{1,0:T(8,128)S(1)} %fusion.38), channel_id=1, source_target_pairs={{16,0},{24,8},{32,16},{40,24},{48,32},{56,40},{64,48},{72,56},{80,... | collective-permute-start | bytes 786440 | tf_op jit(solution)/shard_map/ppermute | solution.py:17
  263.6 9.5 %collective-permute-start.25 = (f32[256,256]{1,0:T(8,128)S(1)}, f32[256,256]{1,0:T(8,128)S(1)}, u32[]{:S(2)}, u32[]{:S(2)}) collective-permute-start(f32[256,256]{1,0:T(8,128)S(1)} %fusion.37), channel_id=1, source_target_pairs={{16,0},{24,8},{32,16},{40,24},{48,32},{56,40},{64,48},{72,56},{80,... | collective-permute-start | bytes 786440 | tf_op jit(solution)/shard_map/ppermute | solution.py:17
  265.5 12.0 %collective-permute-start.28 = (bf16[256,576]{0,1:T(8,128)(2,1)S(1)}, bf16[256,576]{0,1:T(8,128)(2,1)S(1)}, u32[]{:S(2)}, u32[]{:S(2)}) collective-permute-start(bf16[256,576]{0,1:T(8,128)(2,1)S(1)} %bitcast.145), channel_id=1, source_target_pairs={{192,0},{384,192},{576,384},{193,1},{385,193},{577,385},{194,2},{3... | collective-permute-start | bytes 884744 | tf_op jit(solution)/shard_map/ppermute | solution.py:17
  268.9 8.6 %collective-permute-start.16 = (bf16[256,256]{1,0:T(8,128)(2,1)S(1)}, bf16[256,256]{1,0:T(8,128)(2,1)S(1)}, u32[]{:S(2)}, u32[]{:S(2)}) collective-permute-start(bf16[256,256]{1,0:T(8,128)(2,1)S(1)} %copy_bitcast_fusion), channel_id=1, source_target_pairs={{192,0},{384,192},{576,384},{193,1},{385,193},{577,385},{194,2},{3... | collective-permute-start | bytes 393224 | tf_op jit(solution)/shard_map/ppermute | solution.py:17
  273.1 6.2 %collective-permute-start.26 = (bf16[256,128]{1,0:T(8,128)(2,1)S(1)}, bf16[256,128]{1,0:T(8,128)(2,1)S(1)}, u32[]{:S(2)}, u32[]{:S(2)}) collective-permute-start(bf16[256,128]{1,0:T(8,128)(2,1)S(1)} %get-tuple-element.243), channel_id=1, source_target_pairs={{192,0},{384,192},{576,384},{193,1},{385,193},{577,385},{194,2},{3... | collective-permute-start | bytes 196616 | tf_op jit(solution)/shard_map/ppermute | solution.py:17
  275.6 6.2 %collective-permute-start.27 = (bf16[256,128]{1,0:T(8,128)(2,1)S(1)}, bf16[256,128]{1,0:T(8,128)(2,1)S(1)}, u32[]{:S(2)}, u32[]{:S(2)}) collective-permute-start(bf16[256,128]{1,0:T(8,128)(2,1)S(1)} %get-tuple-element.242), channel_id=1, source_target_pairs={{192,0},{384,192},{576,384},{193,1},{385,193},{577,385},{194,2},{3... | collective-permute-start | bytes 196616 | tf_op jit(solution)/shard_map/ppermute | solution.py:17
Sparse Core Ops, SparseCore 0:
  10.3 50.6 all-gather.4
  70.8 63.3 all-gather.6

commit v3 on v2

--- a/solution.py
+++ b/solution.py
@@ -15,6 +15,28 @@
     devices = range(lax.axis_size(axis))
     route = [(i - distance, i) for i in devices if i - distance in devices]
     return lax.ppermute(block, axis, route)
+
+
+def cyclic_shift(block, axis, distance):
+    size = lax.axis_size(axis)
+    return lax.ppermute(block, axis, [(i, (i + distance) % size) for i in range(size)])
+
+
+def ring_gather(block, axis):
+    size = lax.axis_size(axis)
+    ahead = [block]
+    behind = []
+    forward = block
+    backward = block
+    for _ in range(size // 2):
+        forward = cyclic_shift(forward, axis, 1)
+        behind.append(forward)
+    for _ in range((size - 1) // 2):
+        backward = cyclic_shift(backward, axis, -1)
+        ahead.append(backward)
+    relative = jnp.stack(ahead + behind[::-1], axis=0)
+    rolled = jnp.roll(relative, lax.axis_index(axis), axis=0)
+    return jnp.moveaxis(rolled, 0, 1).reshape(block.shape[0], size * block.shape[1])
 
 
 def attend(query_act, key_near, value_near, d_attn, allowed):
@@ -94,7 +116,7 @@
 def per_device(grad_out, out_weight, query_act, key_act, value_act, doc_ids, doc_shared):
     grad_tile = grad_out[0]
     tok_rows = grad_tile.shape[0]
-    grad_rows = lax.all_gather(grad_tile, "col", axis=1, tiled=True)
+    grad_rows = ring_gather(grad_tile, "col")
     d_attn = lax.dot_general(
         grad_rows,
         lax.all_gather(out_weight[0], "row", axis=1, tiled=True),
@@ -112,12 +134,22 @@
     value_local = value_act[0]
     key_width = key_local.shape[1]
     pair_local = jnp.concatenate([key_local, value_local], axis=1)
-    near_blocks = [pair_local]
-    moving = pair_local
-    for _ in range(reach_rows):
-        moving = from_behind(moving, "row", 1)
+    core_bit = row_index % 2
+    pair_partner = lax.ppermute(
+        pair_local, "row", [(i, i ^ 1) for i in range(lax.axis_size("row"))]
+    )
+    moving = jnp.where(
+        core_bit == 0,
+        jnp.concatenate([pair_local, pair_partner], axis=0),
+        jnp.concatenate([pair_partner, pair_local], axis=0),
+    )
+    near_blocks = [moving]
+    for _ in range(reach_rows // 2):
+        moving = from_behind(moving, "row", 2)
         near_blocks.append(moving)
-    pair_near = jnp.concatenate(near_blocks[::-1], axis=0)
+    pair_near = lax.dynamic_slice_in_dim(
+        jnp.concatenate(near_blocks[::-1], axis=0), core_bit * tok_rows, span_rows, 0
+    )
     key_near = pair_near[:, :key_width]
     value_near = pair_near[:, key_width:]
     key_start = query_start - reach_rows * tok_rows
@@ -141,7 +173,6 @@
     partner = lax.ppermute(
         odd_part, "row", [(i, i ^ 1) for i in range(lax.axis_size("row"))]
     )
-    core_bit = row_index % 2
     zero_block = jnp.zeros_like(odd_part[:1])
     partner_aligned = jnp.where(
         core_bit == 0,

time: 292 us -> 262 us (0.90)
  the two profiles are of different devices: /device:TPU:194 before, /device:TPU:196 now
where the time goes in v3:
time: 262 us; the launch traced here: 261 us
  starting transfers between devices  89.9 us (34%)
  waiting for transfers between devices  83.8 us (32%)
  matrix products  32.7 us (12%)
  local copies, waits for them, and re-layouts  25.8 us (10%)
  between operations  14.6 us (6%)
  other arithmetic  13.6 us (5%)
    ppermute x20, waiting for transfers between devices, from_behind(): return lax.ppermute(block, axis, route)  79.1 us
    ppermute x20, starting transfers between devices, from_behind(): return lax.ppermute(block, axis, route)  63.6 us
    ppermute x7, starting transfers between devices, cyclic_shift(): lax.ppermute(block, axis, [(i, (i + distance) % size) for i in range(size)])  22.4 us
    unnamed x52, local copies, waits for them, and re-layouts  16.5 us
    dot_general x2, matrix products, one_head(): lax.dot_general(probs_low, attn_h, (((0,), (0,)), ((), ())), preferred_el...  12 us
    convert_element_type x2, other arithmetic, one_head(): grad_raw = (attn_probs * (grad_probs - row_delta) * (1.0 - capped * cappe...  7.61 us
    dot_general x2, matrix products, one_head(): lax.dot_general(query_h, key_g, (((1,), (1,)), ((), ())), preferred_eleme...  6.69 us
    dot_general x2, matrix products, one_head(): lax.dot_general(attn_h, value_g, (((1,), (1,)), ((), ())), preferred_elem...  6.26 us
  transfers between devices with their start and end apart: 30, of which 18 were waited for; matrix products, arithmetic and copies ran while one was open for 8% of the time, Pallas kernels for 0%

profile of v3, /device:TPU:196, one launch (start us, length us, event | category | flops | bytes accessed | tf_op | source)
XLA Modules:
  0.0 260.7 jit_solution(5026266157149644361)
XLA Ops:
  8.1 1.9 collective-permute-start
  10.0 5.4 %collective-permute-start.9 = (bf16[256,576]{0,1:T(8,128)(2,1)}, bf16[256,576]{0,1:T(8,128)(2,1)S(1)}, u32[]{:S(2)}, u32[]{:S(2)}) collective-permute-start(bf16[256,576]{0,1:T(8,128)(2,1)} %bitcast.166), channel_id=1, source_target_pairs={{0,7},{1,0},{2,1},{3,2},{4,3},{5,4},{6,5},{7,6},{8,15},{9,8},{10,9... | collective-permute-start | bytes 884744 | tf_op jit(solution)/shard_map/ppermute | solution.py:22
  15.4 1.9 collective-permute-start.12
  18.2 1.0 maximum_select_fusion
  19.2 5.5 %collective-permute-start.1 = (bf16[512,256]{1,0:T(8,128)(2,1)S(1)}, bf16[512,256]{1,0:T(8,128)(2,1)S(1)}, u32[]{:S(2)}, u32[]{:S(2)}) collective-permute-start(bf16[512,256]{1,0:T(8,128)(2,1)S(1)} %maximum_select_fusion), channel_id=1, source_target_pairs={{0,16},{8,24},{16,32},{24,40},{32,48},{40,56},{48,64},{56,72},{64,... | collective-permute-start | bytes 786440 | tf_op jit(solution)/shard_map/ppermute | solution.py:17
  25.5 1.7 constant_dynamic-update-slice_fusion.10
  27.9 1.9 collective-permute-start.13
  30.7 5.6 %collective-permute-start.2 = (bf16[512,256]{1,0:T(8,128)(2,1)S(1)}, bf16[512,256]{1,0:T(8,128)(2,1)S(1)}, u32[]{:S(2)}, u32[]{:S(2)}) collective-permute-start(bf16[512,256]{1,0:T(8,128)(2,1)S(1)} %collective-permute-done.1), channel_id=1, source_target_pairs={{0,16},{8,24},{16,32},{24,40},{32,48},{40,56},{48,64},{56,72},{64,... | collective-permute-start | bytes 786440 | tf_op jit(solution)/shard_map/ppermute | solution.py:17
  36.3 4.9 %collective-permute-start.10 = (bf16[256,576]{0,1:T(8,128)(2,1)S(1)}, bf16[256,576]{0,1:T(8,128)(2,1)S(1)}, u32[]{:S(2)}, u32[]{:S(2)}) collective-permute-start(bf16[256,576]{0,1:T(8,128)(2,1)S(1)} %collective-permute-done.9), channel_id=1, source_target_pairs={{0,7},{1,0},{2,1},{3,2},{4,3},{5,4},{6,5},{7,6},{8,15},{9,8},{10,9... | collective-permute-start | bytes 884744 | tf_op jit(solution)/shard_map/ppermute | solution.py:22
  41.2 1.9 collective-permute-start.14
  43.7 5.6 %collective-permute-start.3 = (bf16[512,256]{1,0:T(8,128)(2,1)S(1)}, bf16[512,256]{1,0:T(8,128)(2,1)S(1)}, u32[]{:S(2)}, u32[]{:S(2)}) collective-permute-start(bf16[512,256]{1,0:T(8,128)(2,1)S(1)} %collective-permute-done.2), channel_id=1, source_target_pairs={{0,16},{8,24},{16,32},{24,40},{32,48},{40,56},{48,64},{56,72},{64,... | collective-permute-start | bytes 786440 | tf_op jit(solution)/shard_map/ppermute | solution.py:17
  50.0 1.7 copy.17
  51.7 4.5 %collective-permute-start.11 = (bf16[256,576]{0,1:T(8,128)(2,1)S(1)}, bf16[256,576]{0,1:T(8,128)(2,1)S(1)}, u32[]{:S(2)}, u32[]{:S(2)}) collective-permute-start(bf16[256,576]{0,1:T(8,128)(2,1)S(1)} %collective-permute-done.10), channel_id=1, source_target_pairs={{0,7},{1,0},{2,1},{3,2},{4,3},{5,4},{6,5},{7,6},{8,15},{9,8},{10,9... | collective-permute-start | bytes 884744 | tf_op jit(solution)/shard_map/ppermute | solution.py:22
  57.0 1.9 collective-permute-start.15
  58.9 2.5 collective-permute-start.4
  62.8 6.3 %collective-permute-done.4 = bf16[512,256]{1,0:T(8,128)(2,1)S(1)} collective-permute-done((bf16[512,256]{1,0:T(8,128)(2,1)S(1)}, bf16[512,256]{1,0:T(8,128)(2,1)S(1)}, u32[]{:S(2)}, u32[]{:S(2)}) %collective-permute-start.4) | collective-permute-done | bytes 262176 | tf_op jit(solution)/shard_map/ppermute | solution.py:17
  69.2 3.7 %collective-permute-start.5 = (bf16[512,256]{1,0:T(8,128)(2,1)S(1)}, bf16[512,256]{1,0:T(8,128)(2,1)S(1)}, u32[]{:S(2)}, u32[]{:S(2)}) collective-permute-start(bf16[512,256]{1,0:T(8,128)(2,1)S(1)} %collective-permute-done.4), channel_id=1, source_target_pairs={{0,16},{8,24},{16,32},{24,40},{32,48},{40,56},{48,64},{56,72},{64,... | collective-permute-start | bytes 786440 | tf_op jit(solution)/shard_map/ppermute | solution.py:17
  78.1 4.7 %collective-permute-start.6 = (bf16[512,256]{1,0:T(8,128)(2,1)S(1)}, bf16[512,256]{1,0:T(8,128)(2,1)S(1)}, u32[]{:S(2)}, u32[]{:S(2)}) collective-permute-start(bf16[512,256]{1,0:T(8,128)(2,1)S(1)} %collective-permute-done.5), channel_id=1, source_target_pairs={{0,16},{8,24},{16,32},{24,40},{32,48},{40,56},{48,64},{56,72},{64,... | collective-permute-start | bytes 786440 | tf_op jit(solution)/shard_map/ppermute | solution.py:17
  84.2 2.4 collective-permute-done.6
  86.6 5.6 %collective-permute-start.7 = (bf16[512,256]{1,0:T(8,128)(2,1)S(1)}, bf16[512,256]{1,0:T(8,128)(2,1)S(1)}, u32[]{:S(2)}, u32[]{:S(2)}) collective-permute-start(bf16[512,256]{1,0:T(8,128)(2,1)S(1)} %collective-permute-done.6), channel_id=1, source_target_pairs={{0,16},{8,24},{16,32},{24,40},{32,48},{40,56},{48,64},{56,72},{64,... | collective-permute-start | bytes 786440 | tf_op jit(solution)/shard_map/ppermute | solution.py:17
  93.7 2.5 collective-permute-done.7
  96.2 5.6 %collective-permute-start.8 = (bf16[512,256]{1,0:T(8,128)(2,1)S(1)}, bf16[512,256]{1,0:T(8,128)(2,1)S(1)}, u32[]{:S(2)}, u32[]{:S(2)}) collective-permute-start(bf16[512,256]{1,0:T(8,128)(2,1)S(1)} %collective-permute-done.7), channel_id=1, source_target_pairs={{0,16},{8,24},{16,32},{24,40},{32,48},{40,56},{48,64},{56,72},{64,... | collective-permute-start | bytes 786440 | tf_op jit(solution)/shard_map/ppermute | solution.py:17
  102.5 1.8 constant_dynamic-slice_fusion
  104.4 1.3 collective-permute-done.8
  105.9 1.2 dynamic-slice_bitcast_fusion
  107.1 3.4 %fusion.29 = bf16[256,256]{0,1:T(8,128)(2,1)} fusion(bf16[256,4608]{0,1:T(8,128)(2,1)S(1)} %bitcast.164, bf16[1,256,4608]{1,2,0:T(8,128)(2,1)} %all-gather.3.cloned.1.call-done), kind=kOutput, calls=%fused_computation.39 | convolution fusion | flops 604045312 | bytes 4849664 | tf_op jit(solution)/shard_map/dot_general | solution.py:120
  110.5 1.7 copy.18
  112.3 1.5 broadcast_in_dim.77.clone
  113.9 38.3 %while.18 = (s32[]{:T(128)}, f32[1,4352,128]{2,1,0:T(8,128)S(1)}, f32[1,4352,128]{2,1,0:T(8,128)}, bf16[2,256,128]{2,1,0:T(8,128)(2,1)}, bf16[2,256,128]{1,2,0:T...) while((s32[]{:T(128)}, f32[1,4352,128]{2,1,0:T(8,128)S(1)}, ...), condition=%wide.region_4.5_spmd.clone, body=%wide.region_1.4_spmd.clone.sunk | while | flops 1488485888 | bytes 52247312 | solution.py:100
  113.9 3.3 %fusion.62 = (f32[256]{0:T(256)S(1)}, f32[256,4352]{1,0:T(8,128)S(1)}) fusion(pred[4352]{0:T(1024)(128)(4,1)S(1)} %get-tuple-element.382, s32[256]{0:T(256)S(1)} %get-tuple-element.380, s32[4352]{0:T(1024)S(1)} %get-tuple-element.381, s32[256]{0:T(256)S(1)} %get-tuple-element.379, s32[4352]{0:T(1024)S(1)} %get-tuple-element.378, ...), kind=kOutput, calls=%fused_computation.34.clone.1 | convolution fusion | flops 298581760 | bytes 5690372 | tf_op jit(solution)/shard_map/while/body/eval_jaxpr/dot_general | solution.py:59
  117.2 3.1 %multiply_reduce_fusion.2 = (f32[256]{0:T(256)S(1)}, f32[256,4352]{1,0:T(8,128)S(1)}) fusion(f32[256]{0:T(256)S(1)} %get-tuple-element.336, f32[256,4352]{1,0:T(8,128)S(1)} %get-tuple-element.335, pred[4352]{0:T(1024)(128)(4,1)S(1)} %get-tuple-element.382, s32[256]{0:T(256)S(1)} %get-tuple-element.380, s32[4352]{0:T(1024)S(1)} %get-tuple-element.381, ...), kind=kOutput, calls=%fused_computation.9.clone.1 | convolution fusion | flops 299695872 | bytes 10147844 | tf_op jit(solution)/shard_map/while/body/eval_jaxpr/dot_general | solution.py:71
  120.3 3.8 %multiply_convert_fusion.2 = bf16[256,4352]{1,0:T(8,128)(2,1)S(1)} fusion(f32[256,4352]{1,0:T(8,128)S(1)} %get-tuple-element.335, f32[256,4352]{1,0:T(8,128)S(1)} %get-tuple-element.337, f32[256]{0:T(256)S(1)} %get-tuple-element.338, f32[256]{0:T(256)S(1)} %get-tuple-element.336, pred[4352]{0:T(1024)(128)(4,1)S(1)} %get-tuple-element.382, ...), kind=kLoop, calls=%fused_computation.8.clone.1 | loop fusion | flops 20054016 | bytes 11188736 | tf_op jit(solution)/shard_map/while/body/eval_jaxpr/convert_element_type | solution.py:77
  124.2 1.4 fusion.63
  127.0 6.0 %fusion.64 = f32[1,4352,128]{2,1,0:T(8,128)} fusion(f32[1,4352,128]{2,1,0:T(8,128)} %get-tuple-element.356, bf16[2,256,128]{2,1,0:T(8,128)(2,1)S(1)} %copy-done.15, s32[]{:T(128)} %get-tuple-element.354, f32[256]{0:T(256)S(1)} %get-tuple-element.336, f32[256,4352]{1,0:T(8,128)S(1)} %get-tuple-element.335, ...), kind=kOutput, calls=%fused_computation.6.clone.1 | convolution fusion | flops 299139072 | bytes 9032708 | tf_op jit(solution)/shard_map/while/body/eval_jaxpr/dot_general | solution.py:68
  133.0 3.3 %fusion.62 = (f32[256]{0:T(256)S(1)}, f32[256,4352]{1,0:T(8,128)S(1)}) fusion(pred[4352]{0:T(1024)(128)(4,1)S(1)} %get-tuple-element.382, s32[256]{0:T(256)S(1)} %get-tuple-element.380, s32[4352]{0:T(1024)S(1)} %get-tuple-element.381, s32[256]{0:T(256)S(1)} %get-tuple-element.379, s32[4352]{0:T(1024)S(1)} %get-tuple-element.378, ...), kind=kOutput, calls=%fused_computation.34.clone.1 | convolution fusion | flops 298581760 | bytes 5690372 | tf_op jit(solution)/shard_map/while/body/eval_jaxpr/dot_general | solution.py:59
  136.4 3.1 %multiply_reduce_fusion.2 = (f32[256]{0:T(256)S(1)}, f32[256,4352]{1,0:T(8,128)S(1)}) fusion(f32[256]{0:T(256)S(1)} %get-tuple-element.336, f32[256,4352]{1,0:T(8,128)S(1)} %get-tuple-element.335, pred[4352]{0:T(1024)(128)(4,1)S(1)} %get-tuple-element.382, s32[256]{0:T(256)S(1)} %get-tuple-element.380, s32[4352]{0:T(1024)S(1)} %get-tuple-element.381, ...), kind=kOutput, calls=%fused_computation.9.clone.1 | convolution fusion | flops 299695872 | bytes 10147844 | tf_op jit(solution)/shard_map/while/body/eval_jaxpr/dot_general | solution.py:71
  139.5 3.8 %multiply_convert_fusion.2 = bf16[256,4352]{1,0:T(8,128)(2,1)S(1)} fusion(f32[256,4352]{1,0:T(8,128)S(1)} %get-tuple-element.335, f32[256,4352]{1,0:T(8,128)S(1)} %get-tuple-element.337, f32[256]{0:T(256)S(1)} %get-tuple-element.338, f32[256]{0:T(256)S(1)} %get-tuple-element.336, pred[4352]{0:T(1024)(128)(4,1)S(1)} %get-tuple-element.382, ...), kind=kLoop, calls=%fused_computation.8.clone.1 | loop fusion | flops 20054016 | bytes 11188736 | tf_op jit(solution)/shard_map/while/body/eval_jaxpr/convert_element_type | solution.py:77
  143.3 1.4 fusion.63
  146.2 6.0 %fusion.64 = f32[1,4352,128]{2,1,0:T(8,128)} fusion(f32[1,4352,128]{2,1,0:T(8,128)} %get-tuple-element.356, bf16[2,256,128]{2,1,0:T(8,128)(2,1)S(1)} %copy-done.15, s32[]{:T(128)} %get-tuple-element.354, f32[256]{0:T(256)S(1)} %get-tuple-element.336, f32[256,4352]{1,0:T(8,128)S(1)} %get-tuple-element.335, ...), kind=kOutput, calls=%fused_computation.6.clone.1 | convolution fusion | flops 299139072 | bytes 9032708 | tf_op jit(solution)/shard_map/while/body/eval_jaxpr/dot_general | solution.py:68
  152.2 1.9 pad_maximum_fusion
  154.2 1.9 collective-permute-start.17
  156.2 4.1 %collective-permute-done.17 = f32[8,256,256]{2,1,0:T(8,128)S(1)} collective-permute-done((f32[8,256,256]{2,1,0:T(8,128)S(1)}, f32[8,256,256]{2,1,0:T(8,128)S(1)}, u32[]{:S(2)}, u32[]{:S(2)}) %collective-permute-start.17) | collective-permute-done | bytes 2097184 | tf_op jit(solution)/shard_map/ppermute | solution.py:173
  160.6 1.9 collective-permute-start.18
  162.5 10.3 %collective-permute-done.18 = f32[256,256]{1,0:T(8,128)S(1)} collective-permute-done((f32[256,256]{1,0:T(8,128)S(1)}, f32[256,256]{1,0:T(8,128)S(1)}, u32[]{:S(2)}, u32[]{:S(2)}) %collective-permute-start.18) | collective-permute-done | bytes 262176 | tf_op jit(solution)/shard_map/ppermute | solution.py:17
  172.9 2.1 collective-permute-start.19
  174.9 8.9 %collective-permute-done.19 = f32[256,256]{1,0:T(8,128)S(1)} collective-permute-done((f32[256,256]{1,0:T(8,128)S(1)}, f32[256,256]{1,0:T(8,128)S(1)}, u32[]{:S(2)}, u32[]{:S(2)}) %collective-permute-start.19) | collective-permute-done | bytes 262176 | tf_op jit(solution)/shard_map/ppermute | solution.py:17
  183.9 1.9 collective-permute-start.20
  185.8 8.1 %collective-permute-done.20 = f32[256,256]{1,0:T(8,128)S(1)} collective-permute-done((f32[256,256]{1,0:T(8,128)S(1)}, f32[256,256]{1,0:T(8,128)S(1)}, u32[]{:S(2)}, u32[]{:S(2)}) %collective-permute-start.20) | collective-permute-done | bytes 262176 | tf_op jit(solution)/shard_map/ppermute | solution.py:17
  194.0 1.9 collective-permute-start.21
  195.9 7.5 %collective-permute-done.21 = f32[256,256]{1,0:T(8,128)S(1)} collective-permute-done((f32[256,256]{1,0:T(8,128)S(1)}, f32[256,256]{1,0:T(8,128)S(1)}, u32[]{:S(2)}, u32[]{:S(2)}) %collective-permute-start.21) | collective-permute-done | bytes 262176 | tf_op jit(solution)/shard_map/ppermute | solution.py:17
  203.5 1.9 collective-permute-start.22
  205.4 7.5 %collective-permute-done.22 = f32[256,256]{1,0:T(8,128)S(1)} collective-permute-done((f32[256,256]{1,0:T(8,128)S(1)}, f32[256,256]{1,0:T(8,128)S(1)}, u32[]{:S(2)}, u32[]{:S(2)}) %collective-permute-start.22) | collective-permute-done | bytes 262176 | tf_op jit(solution)/shard_map/ppermute | solution.py:17
  213.0 1.9 collective-permute-start.23
  214.9 7.5 %collective-permute-done.23 = f32[256,256]{1,0:T(8,128)S(1)} collective-permute-done((f32[256,256]{1,0:T(8,128)S(1)}, f32[256,256]{1,0:T(8,128)S(1)}, u32[]{:S(2)}, u32[]{:S(2)}) %collective-permute-start.23) | collective-permute-done | bytes 262176 | tf_op jit(solution)/shard_map/ppermute | solution.py:17
  222.5 1.9 collective-permute-start.24
  224.5 8.6 %collective-permute-done.24 = f32[256,256]{1,0:T(8,128)S(1)} collective-permute-done((f32[256,256]{1,0:T(8,128)S(1)}, f32[256,256]{1,0:T(8,128)S(1)}, u32[]{:S(2)}, u32[]{:S(2)}) %collective-permute-start.24) | collective-permute-done | bytes 262176 | tf_op jit(solution)/shard_map/ppermute | solution.py:17
  233.0 1.9 collective-permute-start.25
  235.0 2.4 collective-permute-start.28
  237.5 2.3 collective-permute-start.16
  239.8 2.8 %collective-permute-done.25 = f32[256,256]{1,0:T(8,128)S(1)} collective-permute-done((f32[256,256]{1,0:T(8,128)S(1)}, f32[256,256]{1,0:T(8,128)S(1)}, u32[]{:S(2)}, u32[]{:S(2)}) %collective-permute-start.25) | collective-permute-done | bytes 262176 | tf_op jit(solution)/shard_map/ppermute | solution.py:17
  242.6 2.4 collective-permute-start.26
  245.0 2.3 collective-permute-start.27
  247.4 1.4 collective-permute-done.26
  248.7 2.4 collective-permute-done.27
  (109 shorter events, 23.1 us)
Async XLA Ops:
  7.2 99.9 %all-gather.3.cloned.1.call-start = ((), (), s32[]{:S(2)}) async-start(), calls=%async_computation | async-start | bytes 2457600 | tf_op jit(solution)/shard_map/all_gather | solution.py:122
  8.1 10.1 %collective-permute-start = (bf16[256,256]{1,0:T(8,128)(2,1)S(1)}, bf16[256,256]{1,0:T(8,128)(2,1)S(1)}, u32[]{:S(2)}, u32[]{:S(2)}) collective-permute-start(bf16[256,256]{1,0:T(8,128)(2,1)S(1)} %pad_maximum_fusion.1), channel_id=1, source_target_pairs={{0,8},{8,0},{16,24},{24,16},{32,40},{40,32},{48,56},{56,48},{64,72... | collective-permute-start | bytes 393224 | tf_op jit(solution)/shard_map/ppermute | solution.py:138
  10.0 26.3 %collective-permute-start.9 = (bf16[256,576]{0,1:T(8,128)(2,1)}, bf16[256,576]{0,1:T(8,128)(2,1)S(1)}, u32[]{:S(2)}, u32[]{:S(2)}) collective-permute-start(bf16[256,576]{0,1:T(8,128)(2,1)} %bitcast.166), channel_id=1, source_target_pairs={{0,7},{1,0},{2,1},{3,2},{4,3},{5,4},{6,5},{7,6},{8,15},{9,8},{10,9... | collective-permute-start | bytes 884744 | tf_op jit(solution)/shard_map/ppermute | solution.py:22
  15.4 12.4 %collective-permute-start.12 = (bf16[256,576]{0,1:T(8,128)(2,1)}, bf16[256,576]{0,1:T(8,128)(2,1)S(1)}, u32[]{:S(2)}, u32[]{:S(2)}) collective-permute-start(bf16[256,576]{0,1:T(8,128)(2,1)} %bitcast.167), channel_id=1, source_target_pairs={{0,1},{1,2},{2,3},{3,4},{4,5},{5,6},{6,7},{7,0},{8,9},{9,10},{10,1... | collective-permute-start | bytes 884744 | tf_op jit(solution)/shard_map/ppermute | solution.py:22
  19.2 8.6 %copy-start.4 = (bf16[512,256]{1,0:T(8,128)(2,1)}, bf16[512,256]{1,0:T(8,128)(2,1)S(1)}, u32[]{:S(2)}) copy-start(bf16[512,256]{1,0:T(8,128)(2,1)S(1)} %maximum_select_fusion) | copy-start | bytes 786436
  19.2 11.4 %collective-permute-start.1 = (bf16[512,256]{1,0:T(8,128)(2,1)S(1)}, bf16[512,256]{1,0:T(8,128)(2,1)S(1)}, u32[]{:S(2)}, u32[]{:S(2)}) collective-permute-start(bf16[512,256]{1,0:T(8,128)(2,1)S(1)} %maximum_select_fusion), channel_id=1, source_target_pairs={{0,16},{8,24},{16,32},{24,40},{32,48},{40,56},{48,64},{56,72},{64,... | collective-permute-start | bytes 786440 | tf_op jit(solution)/shard_map/ppermute | solution.py:17
  27.2 48.6 %copy-start.1 = (bf16[1,256,576]{1,2,0:T(8,128)(2,1)S(1)}, bf16[1,256,576]{1,2,0:T(8,128)(2,1)}, u32[]{:S(2)}) copy-start(bf16[1,256,576]{1,2,0:T(8,128)(2,1)} %param.9) | copy-start | bytes 884740
  27.9 13.3 %collective-permute-start.13 = (bf16[256,576]{0,1:T(8,128)(2,1)S(1)}, bf16[256,576]{0,1:T(8,128)(2,1)S(1)}, u32[]{:S(2)}, u32[]{:S(2)}) collective-permute-start(bf16[256,576]{0,1:T(8,128)(2,1)S(1)} %collective-permute-done.12), channel_id=1, source_target_pairs={{0,1},{1,2},{2,3},{3,4},{4,5},{5,6},{6,7},{7,0},{8,9},{9,10},{10,1... | collective-permute-start | bytes 884744 | tf_op jit(solution)/shard_map/ppermute | solution.py:22
  30.7 45.9 %copy-start.6 = (bf16[512,256]{1,0:T(8,128)(2,1)}, bf16[512,256]{1,0:T(8,128)(2,1)S(1)}, u32[]{:S(2)}) copy-start(bf16[512,256]{1,0:T(8,128)(2,1)S(1)} %collective-permute-done.1) | copy-start | bytes 786436
  30.7 13.0 %collective-permute-start.2 = (bf16[512,256]{1,0:T(8,128)(2,1)S(1)}, bf16[512,256]{1,0:T(8,128)(2,1)S(1)}, u32[]{:S(2)}, u32[]{:S(2)}) collective-permute-start(bf16[512,256]{1,0:T(8,128)(2,1)S(1)} %collective-permute-done.1), channel_id=1, source_target_pairs={{0,16},{8,24},{16,32},{24,40},{32,48},{40,56},{48,64},{56,72},{64,... | collective-permute-start | bytes 786440 | tf_op jit(solution)/shard_map/ppermute | solution.py:17
  36.3 15.4 %collective-permute-start.10 = (bf16[256,576]{0,1:T(8,128)(2,1)S(1)}, bf16[256,576]{0,1:T(8,128)(2,1)S(1)}, u32[]{:S(2)}, u32[]{:S(2)}) collective-permute-start(bf16[256,576]{0,1:T(8,128)(2,1)S(1)} %collective-permute-done.9), channel_id=1, source_target_pairs={{0,7},{1,0},{2,1},{3,2},{4,3},{5,4},{6,5},{7,6},{8,15},{9,8},{10,9... | collective-permute-start | bytes 884744 | tf_op jit(solution)/shard_map/ppermute | solution.py:22
  41.2 15.8 %collective-permute-start.14 = (bf16[256,576]{0,1:T(8,128)(2,1)S(1)}, bf16[256,576]{0,1:T(8,128)(2,1)S(1)}, u32[]{:S(2)}, u32[]{:S(2)}) collective-permute-start(bf16[256,576]{0,1:T(8,128)(2,1)S(1)} %collective-permute-done.13), channel_id=1, source_target_pairs={{0,1},{1,2},{2,3},{3,4},{4,5},{5,6},{6,7},{7,0},{8,9},{9,10},{10,1... | collective-permute-start | bytes 884744 | tf_op jit(solution)/shard_map/ppermute | solution.py:22
  43.7 32.9 %copy-start.8 = (bf16[512,256]{1,0:T(8,128)(2,1)}, bf16[512,256]{1,0:T(8,128)(2,1)S(1)}, u32[]{:S(2)}) copy-start(bf16[512,256]{1,0:T(8,128)(2,1)S(1)} %collective-permute-done.2) | copy-start | bytes 786436
  43.7 15.2 %collective-permute-start.3 = (bf16[512,256]{1,0:T(8,128)(2,1)S(1)}, bf16[512,256]{1,0:T(8,128)(2,1)S(1)}, u32[]{:S(2)}, u32[]{:S(2)}) collective-permute-start(bf16[512,256]{1,0:T(8,128)(2,1)S(1)} %collective-permute-done.2), channel_id=1, source_target_pairs={{0,16},{8,24},{16,32},{24,40},{32,48},{40,56},{48,64},{56,72},{64,... | collective-permute-start | bytes 786440 | tf_op jit(solution)/shard_map/ppermute | solution.py:17
  51.7 10.4 %collective-permute-start.11 = (bf16[256,576]{0,1:T(8,128)(2,1)S(1)}, bf16[256,576]{0,1:T(8,128)(2,1)S(1)}, u32[]{:S(2)}, u32[]{:S(2)}) collective-permute-start(bf16[256,576]{0,1:T(8,128)(2,1)S(1)} %collective-permute-done.10), channel_id=1, source_target_pairs={{0,7},{1,0},{2,1},{3,2},{4,3},{5,4},{6,5},{7,6},{8,15},{9,8},{10,9... | collective-permute-start | bytes 884744 | tf_op jit(solution)/shard_map/ppermute | solution.py:22
  57.0 15.9 %collective-permute-start.15 = (bf16[256,576]{0,1:T(8,128)(2,1)S(1)}, bf16[256,576]{0,1:T(8,128)(2,1)S(1)}, u32[]{:S(2)}, u32[]{:S(2)}) collective-permute-start(bf16[256,576]{0,1:T(8,128)(2,1)S(1)} %collective-permute-done.14), channel_id=1, source_target_pairs={{0,1},{1,2},{2,3},{3,4},{4,5},{5,6},{6,7},{7,0},{8,9},{9,10},{10,1... | collective-permute-start | bytes 884744 | tf_op jit(solution)/shard_map/ppermute | solution.py:22
  58.9 18.5 %copy-start.10 = (bf16[512,256]{1,0:T(8,128)(2,1)}, bf16[512,256]{1,0:T(8,128)(2,1)S(1)}, u32[]{:S(2)}) copy-start(bf16[512,256]{1,0:T(8,128)(2,1)S(1)} %collective-permute-done.3) | copy-start | bytes 786436
  58.9 10.3 %collective-permute-start.4 = (bf16[512,256]{1,0:T(8,128)(2,1)S(1)}, bf16[512,256]{1,0:T(8,128)(2,1)S(1)}, u32[]{:S(2)}, u32[]{:S(2)}) collective-permute-start(bf16[512,256]{1,0:T(8,128)(2,1)S(1)} %collective-permute-done.3), channel_id=1, source_target_pairs={{0,16},{8,24},{16,32},{24,40},{32,48},{40,56},{48,64},{56,72},{64,... | collective-permute-start | bytes 786440 | tf_op jit(solution)/shard_map/ppermute | solution.py:17
  69.2 8.9 %collective-permute-start.5 = (bf16[512,256]{1,0:T(8,128)(2,1)S(1)}, bf16[512,256]{1,0:T(8,128)(2,1)S(1)}, u32[]{:S(2)}, u32[]{:S(2)}) collective-permute-start(bf16[512,256]{1,0:T(8,128)(2,1)S(1)} %collective-permute-done.4), channel_id=1, source_target_pairs={{0,16},{8,24},{16,32},{24,40},{32,48},{40,56},{48,64},{56,72},{64,... | collective-permute-start | bytes 786440 | tf_op jit(solution)/shard_map/ppermute | solution.py:17
  78.1 8.6 %collective-permute-start.6 = (bf16[512,256]{1,0:T(8,128)(2,1)S(1)}, bf16[512,256]{1,0:T(8,128)(2,1)S(1)}, u32[]{:S(2)}, u32[]{:S(2)}) collective-permute-start(bf16[512,256]{1,0:T(8,128)(2,1)S(1)} %collective-permute-done.5), channel_id=1, source_target_pairs={{0,16},{8,24},{16,32},{24,40},{32,48},{40,56},{48,64},{56,72},{64,... | collective-permute-start | bytes 786440 | tf_op jit(solution)/shard_map/ppermute | solution.py:17
  86.6 9.6 %collective-permute-start.7 = (bf16[512,256]{1,0:T(8,128)(2,1)S(1)}, bf16[512,256]{1,0:T(8,128)(2,1)S(1)}, u32[]{:S(2)}, u32[]{:S(2)}) collective-permute-start(bf16[512,256]{1,0:T(8,128)(2,1)S(1)} %collective-permute-done.6), channel_id=1, source_target_pairs={{0,16},{8,24},{16,32},{24,40},{32,48},{40,56},{48,64},{56,72},{64,... | collective-permute-start | bytes 786440 | tf_op jit(solution)/shard_map/ppermute | solution.py:17
  96.2 9.5 %collective-permute-start.8 = (bf16[512,256]{1,0:T(8,128)(2,1)S(1)}, bf16[512,256]{1,0:T(8,128)(2,1)S(1)}, u32[]{:S(2)}, u32[]{:S(2)}) collective-permute-start(bf16[512,256]{1,0:T(8,128)(2,1)S(1)} %collective-permute-done.7), channel_id=1, source_target_pairs={{0,16},{8,24},{16,32},{24,40},{32,48},{40,56},{48,64},{56,72},{64,... | collective-permute-start | bytes 786440 | tf_op jit(solution)/shard_map/ppermute | solution.py:17
  104.3 1.4 copy-start.11
  104.3 1.5 copy-start.9
  104.3 1.5 copy-start.7
  104.4 1.5 copy-start.5
  110.5 3.4 %copy-start = (bf16[1,256,256]{1,2,0:T(8,128)(2,1)S(1)}, bf16[1,256,256]{1,2,0:T(8,128)(2,1)}, u32[]{:S(2)}) copy-start(bf16[1,256,256]{1,2,0:T(8,128)(2,1)} %copy.17) | copy-start | bytes 393220
  113.9 3.3 %copy-start.3 = (bf16[1,4352,128]{2,1,0:T(8,128)(2,1)S(1)}, bf16[1,4352,128]{2,1,0:T(8,128)(2,1)}, u32[]{:S(2)}) copy-start(bf16[1,4352,128]{2,1,0:T(8,128)(2,1)} %get-tuple-element.376) | copy-start | bytes 3342340 | tf_op jit(solution)/shard_map/while
  113.9 3.4 %copy-start.15 = (bf16[2,256,128]{2,1,0:T(8,128)(2,1)S(1)}, bf16[2,256,128]{2,1,0:T(8,128)(2,1)}, u32[]{:S(2)}) copy-start(bf16[2,256,128]{2,1,0:T(8,128)(2,1)} %get-tuple-element.375) | copy-start | bytes 393220 | tf_op jit(solution)/shard_map/while
  124.2 1.4 copy-start.12
  126.3 0.7 copy-start.13
  133.0 3.4 %copy-start.3 = (bf16[1,4352,128]{2,1,0:T(8,128)(2,1)S(1)}, bf16[1,4352,128]{2,1,0:T(8,128)(2,1)}, u32[]{:S(2)}) copy-start(bf16[1,4352,128]{2,1,0:T(8,128)(2,1)} %get-tuple-element.376) | copy-start | bytes 3342340 | tf_op jit(solution)/shard_map/while
  133.0 3.4 %copy-start.15 = (bf16[2,256,128]{2,1,0:T(8,128)(2,1)S(1)}, bf16[2,256,128]{2,1,0:T(8,128)(2,1)}, u32[]{:S(2)}) copy-start(bf16[2,256,128]{2,1,0:T(8,128)(2,1)} %get-tuple-element.375) | copy-start | bytes 393220 | tf_op jit(solution)/shard_map/while
  143.3 1.4 copy-start.12
  145.5 0.7 copy-start.13
  154.2 6.1 %collective-permute-start.17 = (f32[8,256,256]{2,1,0:T(8,128)S(1)}, f32[8,256,256]{2,1,0:T(8,128)S(1)}, u32[]{:S(2)}, u32[]{:S(2)}) collective-permute-start(f32[8,256,256]{2,1,0:T(8,128)S(1)} %slice.50), channel_id=1, source_target_pairs={{0,8},{8,0},{16,24},{24,16},{32,40},{40,32},{48,56},{56,48},{64,72... | collective-permute-start | bytes 6291464 | tf_op jit(solution)/shard_map/ppermute | solution.py:173
  160.6 12.2 %collective-permute-start.18 = (f32[256,256]{1,0:T(8,128)S(1)}, f32[256,256]{1,0:T(8,128)S(1)}, u32[]{:S(2)}, u32[]{:S(2)}) collective-permute-start(f32[256,256]{1,0:T(8,128)S(1)} %slice_bitcast_fusion.8), channel_id=1, source_target_pairs={{16,0},{24,8},{32,16},{40,24},{48,32},{56,40},{64,48},{72,56},{80,... | collective-permute-start | bytes 786440 | tf_op jit(solution)/shard_map/ppermute | solution.py:17
  172.8 62.1 %copy-start.2 = (bf16[1,256,576]{1,2,0:T(8,128)(2,1)S(1)}, bf16[1,256,576]{1,2,0:T(8,128)(2,1)}, u32[]{:S(2)}) copy-start(bf16[1,256,576]{1,2,0:T(8,128)(2,1)} %param.9) | copy-start | bytes 884740
  172.9 64.6 %copy-start.14 = (bf16[2,256,128]{2,1,0:T(8,128)(2,1)S(1)}, bf16[2,256,128]{2,1,0:T(8,128)(2,1)}, u32[]{:S(2)}) copy-start(bf16[2,256,128]{2,1,0:T(8,128)(2,1)} %get-tuple-element.141) | copy-start | bytes 393220
  172.9 11.0 %collective-permute-start.19 = (f32[256,256]{1,0:T(8,128)S(1)}, f32[256,256]{1,0:T(8,128)S(1)}, u32[]{:S(2)}, u32[]{:S(2)}) collective-permute-start(f32[256,256]{1,0:T(8,128)S(1)} %fusion.40), channel_id=1, source_target_pairs={{16,0},{24,8},{32,16},{40,24},{48,32},{56,40},{64,48},{72,56},{80,... | collective-permute-start | bytes 786440 | tf_op jit(solution)/shard_map/ppermute | solution.py:17
  183.9 10.0 %collective-permute-start.20 = (f32[256,256]{1,0:T(8,128)S(1)}, f32[256,256]{1,0:T(8,128)S(1)}, u32[]{:S(2)}, u32[]{:S(2)}) collective-permute-start(f32[256,256]{1,0:T(8,128)S(1)} %fusion.39), channel_id=1, source_target_pairs={{16,0},{24,8},{32,16},{40,24},{48,32},{56,40},{64,48},{72,56},{80,... | collective-permute-start | bytes 786440 | tf_op jit(solution)/shard_map/ppermute | solution.py:17
  194.0 9.5 %collective-permute-start.21 = (f32[256,256]{1,0:T(8,128)S(1)}, f32[256,256]{1,0:T(8,128)S(1)}, u32[]{:S(2)}, u32[]{:S(2)}) collective-permute-start(f32[256,256]{1,0:T(8,128)S(1)} %fusion.38), channel_id=1, source_target_pairs={{16,0},{24,8},{32,16},{40,24},{48,32},{56,40},{64,48},{72,56},{80,... | collective-permute-start | bytes 786440 | tf_op jit(solution)/shard_map/ppermute | solution.py:17
  203.5 9.5 %collective-permute-start.22 = (f32[256,256]{1,0:T(8,128)S(1)}, f32[256,256]{1,0:T(8,128)S(1)}, u32[]{:S(2)}, u32[]{:S(2)}) collective-permute-start(f32[256,256]{1,0:T(8,128)S(1)} %fusion.37), channel_id=1, source_target_pairs={{16,0},{24,8},{32,16},{40,24},{48,32},{56,40},{64,48},{72,56},{80,... | collective-permute-start | bytes 786440 | tf_op jit(solution)/shard_map/ppermute | solution.py:17
  213.0 9.5 %collective-permute-start.23 = (f32[256,256]{1,0:T(8,128)S(1)}, f32[256,256]{1,0:T(8,128)S(1)}, u32[]{:S(2)}, u32[]{:S(2)}) collective-permute-start(f32[256,256]{1,0:T(8,128)S(1)} %fusion.36), channel_id=1, source_target_pairs={{16,0},{24,8},{32,16},{40,24},{48,32},{56,40},{64,48},{72,56},{80,... | collective-permute-start | bytes 786440 | tf_op jit(solution)/shard_map/ppermute | solution.py:17
  222.5 10.5 %collective-permute-start.24 = (f32[256,256]{1,0:T(8,128)S(1)}, f32[256,256]{1,0:T(8,128)S(1)}, u32[]{:S(2)}, u32[]{:S(2)}) collective-permute-start(f32[256,256]{1,0:T(8,128)S(1)} %fusion.35), channel_id=1, source_target_pairs={{16,0},{24,8},{32,16},{40,24},{48,32},{56,40},{64,48},{72,56},{80,... | collective-permute-start | bytes 786440 | tf_op jit(solution)/shard_map/ppermute | solution.py:17
  233.0 9.5 %collective-permute-start.25 = (f32[256,256]{1,0:T(8,128)S(1)}, f32[256,256]{1,0:T(8,128)S(1)}, u32[]{:S(2)}, u32[]{:S(2)}) collective-permute-start(f32[256,256]{1,0:T(8,128)S(1)} %fusion.34), channel_id=1, source_target_pairs={{16,0},{24,8},{32,16},{40,24},{48,32},{56,40},{64,48},{72,56},{80,... | collective-permute-start | bytes 786440 | tf_op jit(solution)/shard_map/ppermute | solution.py:17
  235.0 12.4 %collective-permute-start.28 = (bf16[256,576]{0,1:T(8,128)(2,1)S(1)}, bf16[256,576]{0,1:T(8,128)(2,1)S(1)}, u32[]{:S(2)}, u32[]{:S(2)}) collective-permute-start(bf16[256,576]{0,1:T(8,128)(2,1)S(1)} %bitcast.168), channel_id=1, source_target_pairs={{192,0},{384,192},{576,384},{193,1},{385,193},{577,385},{194,2},{3... | collective-permute-start | bytes 884744 | tf_op jit(solution)/shard_map/ppermute | solution.py:17
  237.5 9.9 %collective-permute-start.16 = (bf16[256,256]{1,0:T(8,128)(2,1)S(1)}, bf16[256,256]{1,0:T(8,128)(2,1)S(1)}, u32[]{:S(2)}, u32[]{:S(2)}) collective-permute-start(bf16[256,256]{1,0:T(8,128)(2,1)S(1)} %copy_bitcast_fusion), channel_id=1, source_target_pairs={{192,0},{384,192},{576,384},{193,1},{385,193},{577,385},{194,2},{3... | collective-permute-start | bytes 393224 | tf_op jit(solution)/shard_map/ppermute | solution.py:17
  242.6 6.2 %collective-permute-start.26 = (bf16[256,128]{1,0:T(8,128)(2,1)S(1)}, bf16[256,128]{1,0:T(8,128)(2,1)S(1)}, u32[]{:S(2)}, u32[]{:S(2)}) collective-permute-start(bf16[256,128]{1,0:T(8,128)(2,1)S(1)} %get-tuple-element.243), channel_id=1, source_target_pairs={{192,0},{384,192},{576,384},{193,1},{385,193},{577,385},{194,2},{3... | collective-permute-start | bytes 196616 | tf_op jit(solution)/shard_map/ppermute | solution.py:17
  245.0 6.2 %collective-permute-start.27 = (bf16[256,128]{1,0:T(8,128)(2,1)S(1)}, bf16[256,128]{1,0:T(8,128)(2,1)S(1)}, u32[]{:S(2)}, u32[]{:S(2)}) collective-permute-start(bf16[256,128]{1,0:T(8,128)(2,1)S(1)} %get-tuple-element.242), channel_id=1, source_target_pairs={{192,0},{384,192},{576,384},{193,1},{385,193},{577,385},{194,2},{3... | collective-permute-start | bytes 196616 | tf_op jit(solution)/shard_map/ppermute | solution.py:17
Sparse Core Ops, SparseCore 0:
  17.5 61.6 all-gather.2

commit v4 on v3

--- a/solution.py
+++ b/solution.py
@@ -135,20 +135,22 @@
     key_width = key_local.shape[1]
     pair_local = jnp.concatenate([key_local, value_local], axis=1)
     core_bit = row_index % 2
-    pair_partner = lax.ppermute(
-        pair_local, "row", [(i, i ^ 1) for i in range(lax.axis_size("row"))]
-    )
-    moving = jnp.where(
-        core_bit == 0,
-        jnp.concatenate([pair_local, pair_partner], axis=0),
-        jnp.concatenate([pair_partner, pair_local], axis=0),
-    )
-    near_blocks = [moving]
+    moving = pair_local
+    same_core = []
     for _ in range(reach_rows // 2):
         moving = from_behind(moving, "row", 2)
-        near_blocks.append(moving)
+        same_core.append(moving)
+    same_core = jnp.stack([pair_local] + same_core, axis=0)
+    other_core = lax.ppermute(
+        same_core, "row", [(i, i ^ 1) for i in range(lax.axis_size("row"))]
+    )
+    pairs = jnp.where(
+        core_bit == 0,
+        jnp.stack([same_core, other_core], axis=1),
+        jnp.stack([other_core, same_core], axis=1),
+    )
     pair_near = lax.dynamic_slice_in_dim(
-        jnp.concatenate(near_blocks[::-1], axis=0), core_bit * tok_rows, span_rows, 0
+        pairs[::-1].reshape(-1, pair_local.shape[1]), core_bit * tok_rows, span_rows, 0
     )
     key_near = pair_near[:, :key_width]
     value_near = pair_near[:, key_width:]

time: 262 us -> 258 us (0.985)
  local copies, waits for them, and re-layouts: 25.8 us -> 18.5 us
    unnamed x52 -> x45, local copies, waits for them, and re-layouts: 16.5 us -> 6.57 us
    rev x0 -> x2, local copies, waits for them, and re-layouts: none -> 3.42 us  [per_device(): pairs[::-1].reshape(-1, pair_local.shape[1])]
  transfers between devices with their start and end apart: 30 -> 30, of which waited for: 18 -> 17; matrix products, arithmetic and copies ran while one was open for 8% -> 6% of each run, Pallas kernels for 0% -> 0%
where the time goes in v4:
time: 258 us; the launch traced here: 256 us
  starting transfers between devices  89.7 us (35%)
  waiting for transfers between devices  84.3 us (33%)
  matrix products  33.8 us (13%)
  local copies, waits for them, and re-layouts  18.5 us (7%)
  other arithmetic  15 us (6%)
  between operations  14.7 us (6%)
    ppermute x20, waiting for transfers between devices, from_behind(): return lax.ppermute(block, axis, route)  79.5 us
    ppermute x20, starting transfers between devices, from_behind(): return lax.ppermute(block, axis, route)  61.7 us
    ppermute x7, starting transfers between devices, cyclic_shift(): lax.ppermute(block, axis, [(i, (i + distance) % size) for i in range(size)])  24 us
    dot_general x2, matrix products, one_head(): lax.dot_general(probs_low, attn_h, (((0,), (0,)), ((), ())), preferred_el...  12 us
    convert_element_type x2, other arithmetic, one_head(): grad_raw = (attn_probs * (grad_probs - row_delta) * (1.0 - capped * cappe...  7.59 us
    dot_general x2, matrix products, one_head(): lax.dot_general(query_h, key_g, (((1,), (1,)), ((), ())), preferred_eleme...  6.66 us
    unnamed x45, local copies, waits for them, and re-layouts  6.57 us
    dot_general x2, matrix products, one_head(): lax.dot_general(attn_h, value_g, (((1,), (1,)), ((), ())), preferred_elem...  6.27 us
  transfers between devices with their start and end apart: 30, of which 17 were waited for; matrix products, arithmetic and copies ran while one was open for 6% of the time, Pallas kernels for 0%

profile of v4, /device:TPU:196, one launch (start us, length us, event | category | flops | bytes accessed | tf_op | source)
XLA Modules:
  0.0 256.4 jit_solution(7768631057809589949)
XLA Ops:
  7.2 5.4 %collective-permute-start.9 = (bf16[256,576]{0,1:T(8,128)(2,1)}, bf16[256,576]{0,1:T(8,128)(2,1)S(1)}, u32[]{:S(2)}, u32[]{:S(2)}) collective-permute-start(bf16[256,576]{0,1:T(8,128)(2,1)} %bitcast.190), channel_id=1, source_target_pairs={{0,7},{1,0},{2,1},{3,2},{4,3},{5,4},{6,5},{7,6},{8,15},{9,8},{10,9... | collective-permute-start | bytes 884744 | tf_op jit(solution)/shard_map/ppermute | solution.py:22
  12.6 1.9 collective-permute-start.12
  15.4 5.5 %collective-permute-start = (bf16[256,256]{1,0:T(8,128)(2,1)S(1)}, bf16[256,256]{1,0:T(8,128)(2,1)S(1)}, u32[]{:S(2)}, u32[]{:S(2)}) collective-permute-start(bf16[256,256]{1,0:T(8,128)(2,1)S(1)} %pad_maximum_fusion.1), channel_id=1, source_target_pairs={{0,16},{8,24},{16,32},{24,40},{32,48},{40,56},{48,64},{56,72},{64,... | collective-permute-start | bytes 393224 | tf_op jit(solution)/shard_map/ppermute | solution.py:17
  25.8 1.7 copy.19
  28.5 4.3 %collective-permute-start.1 = (bf16[256,256]{1,0:T(8,128)(2,1)S(1)}, bf16[256,256]{1,0:T(8,128)(2,1)S(1)}, u32[]{:S(2)}, u32[]{:S(2)}) collective-permute-start(bf16[256,256]{1,0:T(8,128)(2,1)S(1)} %collective-permute-done), channel_id=1, source_target_pairs={{0,16},{8,24},{16,32},{24,40},{32,48},{40,56},{48,64},{56,72},{64,... | collective-permute-start | bytes 393224 | tf_op jit(solution)/shard_map/ppermute | solution.py:17
  32.8 3.7 %collective-permute-done.1 = bf16[256,256]{1,0:T(8,128)(2,1)S(1)} collective-permute-done((bf16[256,256]{1,0:T(8,128)(2,1)S(1)}, bf16[256,256]{1,0:T(8,128)(2,1)S(1)}, u32[]{:S(2)}, u32[]{:S(2)}) %collective-permute-start.1) | collective-permute-done | bytes 131104 | tf_op jit(solution)/shard_map/ppermute | solution.py:17
  36.5 5.6 %collective-permute-start.2 = (bf16[256,256]{1,0:T(8,128)(2,1)S(1)}, bf16[256,256]{1,0:T(8,128)(2,1)S(1)}, u32[]{:S(2)}, u32[]{:S(2)}) collective-permute-start(bf16[256,256]{1,0:T(8,128)(2,1)S(1)} %collective-permute-done.1), channel_id=1, source_target_pairs={{0,16},{8,24},{16,32},{24,40},{32,48},{40,56},{48,64},{56,72},{64,... | collective-permute-start | bytes 393224 | tf_op jit(solution)/shard_map/ppermute | solution.py:17
  42.1 5.1 %collective-permute-start.10 = (bf16[256,576]{0,1:T(8,128)(2,1)S(1)}, bf16[256,576]{0,1:T(8,128)(2,1)S(1)}, u32[]{:S(2)}, u32[]{:S(2)}) collective-permute-start(bf16[256,576]{0,1:T(8,128)(2,1)S(1)} %collective-permute-done.9), channel_id=1, source_target_pairs={{0,7},{1,0},{2,1},{3,2},{4,3},{5,4},{6,5},{7,6},{8,15},{9,8},{10,9... | collective-permute-start | bytes 884744 | tf_op jit(solution)/shard_map/ppermute | solution.py:22
  47.2 1.9 collective-permute-start.13
  49.2 3.0 %collective-permute-start.3 = (bf16[256,256]{1,0:T(8,128)(2,1)S(1)}, bf16[256,256]{1,0:T(8,128)(2,1)S(1)}, u32[]{:S(2)}, u32[]{:S(2)}) collective-permute-start(bf16[256,256]{1,0:T(8,128)(2,1)S(1)} %collective-permute-done.2), channel_id=1, source_target_pairs={{0,16},{8,24},{16,32},{24,40},{32,48},{40,56},{48,64},{56,72},{64,... | collective-permute-start | bytes 393224 | tf_op jit(solution)/shard_map/ppermute | solution.py:17
  52.2 4.4 %collective-permute-done.3 = bf16[256,256]{1,0:T(8,128)(2,1)S(1)} collective-permute-done((bf16[256,256]{1,0:T(8,128)(2,1)S(1)}, bf16[256,256]{1,0:T(8,128)(2,1)S(1)}, u32[]{:S(2)}, u32[]{:S(2)}) %collective-permute-start.3) | collective-permute-done | bytes 131104 | tf_op jit(solution)/shard_map/ppermute | solution.py:17
  56.6 4.4 %collective-permute-start.4 = (bf16[256,256]{1,0:T(8,128)(2,1)S(1)}, bf16[256,256]{1,0:T(8,128)(2,1)S(1)}, u32[]{:S(2)}, u32[]{:S(2)}) collective-permute-start(bf16[256,256]{1,0:T(8,128)(2,1)S(1)} %collective-permute-done.3), channel_id=1, source_target_pairs={{0,16},{8,24},{16,32},{24,40},{32,48},{40,56},{48,64},{56,72},{64,... | collective-permute-start | bytes 393224 | tf_op jit(solution)/shard_map/ppermute | solution.py:17
  61.0 5.8 %collective-permute-start.11 = (bf16[256,576]{0,1:T(8,128)(2,1)S(1)}, bf16[256,576]{0,1:T(8,128)(2,1)S(1)}, u32[]{:S(2)}, u32[]{:S(2)}) collective-permute-start(bf16[256,576]{0,1:T(8,128)(2,1)S(1)} %collective-permute-done.10), channel_id=1, source_target_pairs={{0,7},{1,0},{2,1},{3,2},{4,3},{5,4},{6,5},{7,6},{8,15},{9,8},{10,9... | collective-permute-start | bytes 884744 | tf_op jit(solution)/shard_map/ppermute | solution.py:22
  66.8 1.9 collective-permute-start.14
  68.8 2.8 %collective-permute-start.5 = (bf16[256,256]{1,0:T(8,128)(2,1)S(1)}, bf16[256,256]{1,0:T(8,128)(2,1)S(1)}, u32[]{:S(2)}, u32[]{:S(2)}) collective-permute-start(bf16[256,256]{1,0:T(8,128)(2,1)S(1)} %collective-permute-done.4), channel_id=1, source_target_pairs={{0,16},{8,24},{16,32},{24,40},{32,48},{40,56},{48,64},{56,72},{64,... | collective-permute-start | bytes 393224 | tf_op jit(solution)/shard_map/ppermute | solution.py:17
  71.7 4.0 %collective-permute-done.5 = bf16[256,256]{1,0:T(8,128)(2,1)S(1)} collective-permute-done((bf16[256,256]{1,0:T(8,128)(2,1)S(1)}, bf16[256,256]{1,0:T(8,128)(2,1)S(1)}, u32[]{:S(2)}, u32[]{:S(2)}) %collective-permute-start.5) | collective-permute-done | bytes 131104 | tf_op jit(solution)/shard_map/ppermute | solution.py:17
  75.7 5.2 %collective-permute-start.6 = (bf16[256,256]{1,0:T(8,128)(2,1)S(1)}, bf16[256,256]{1,0:T(8,128)(2,1)S(1)}, u32[]{:S(2)}, u32[]{:S(2)}) collective-permute-start(bf16[256,256]{1,0:T(8,128)(2,1)S(1)} %collective-permute-done.5), channel_id=1, source_target_pairs={{0,16},{8,24},{16,32},{24,40},{32,48},{40,56},{48,64},{56,72},{64,... | collective-permute-start | bytes 393224 | tf_op jit(solution)/shard_map/ppermute | solution.py:17
  81.0 1.9 collective-permute-start.15
  83.9 5.6 %collective-permute-start.7 = (bf16[256,256]{1,0:T(8,128)(2,1)S(1)}, bf16[256,256]{1,0:T(8,128)(2,1)S(1)}, u32[]{:S(2)}, u32[]{:S(2)}) collective-permute-start(bf16[256,256]{1,0:T(8,128)(2,1)S(1)} %collective-permute-done.6), channel_id=1, source_target_pairs={{0,16},{8,24},{16,32},{24,40},{32,48},{40,56},{48,64},{56,72},{64,... | collective-permute-start | bytes 393224 | tf_op jit(solution)/shard_map/ppermute | solution.py:17
  89.6 2.5 collective-permute-done.7
  92.1 1.9 collective-permute-start.8
  94.4 1.6 constant_dynamic-slice_fusion
  97.2 1.6 rev.3
  98.8 1.8 copy.20
  102.7 3.4 %fusion.29 = bf16[256,256]{0,1:T(8,128)(2,1)} fusion(bf16[256,4608]{0,1:T(8,128)(2,1)S(1)} %bitcast.186, bf16[1,256,4608]{1,2,0:T(8,128)(2,1)} %all-gather.3.cloned.1.call-done), kind=kOutput, calls=%fused_computation.40 | convolution fusion | flops 604045312 | bytes 4849664 | tf_op jit(solution)/shard_map/dot_general | solution.py:120
  106.1 1.7 copy.21
  107.9 1.5 broadcast_in_dim.77.clone
  109.4 38.3 %while.18 = (s32[]{:T(128)}, f32[1,4352,128]{2,1,0:T(8,128)S(1)}, f32[1,4352,128]{2,1,0:T(8,128)}, bf16[2,256,128]{2,1,0:T(8,128)(2,1)}, bf16[2,256,128]{1,2,0:T...) while((s32[]{:T(128)}, f32[1,4352,128]{2,1,0:T(8,128)S(1)}, ...), condition=%wide.region_4.5_spmd.clone, body=%wide.region_1.4_spmd.clone.sunk | while | flops 1488485888 | bytes 51199188 | solution.py:100
  109.7 3.3 %fusion.62 = (f32[256]{0:T(256)S(1)}, f32[256,4352]{1,0:T(8,128)S(1)}) fusion(pred[4352]{0:T(1024)(128)(4,1)S(1)} %get-tuple-element.382, s32[256]{0:T(256)S(1)} %get-tuple-element.380, s32[4352]{0:T(1024)S(1)} %get-tuple-element.381, s32[256]{0:T(256)S(1)} %get-tuple-element.379, s32[4352]{0:T(1024)S(1)} %get-tuple-element.378, ...), kind=kOutput, calls=%fused_computation.34.clone.1 | convolution fusion | flops 298581760 | bytes 5690372 | tf_op jit(solution)/shard_map/while/body/eval_jaxpr/dot_general | solution.py:59
  113.0 3.1 %multiply_reduce_fusion.2 = (f32[256]{0:T(256)S(1)}, f32[256,4352]{1,0:T(8,128)S(1)}) fusion(f32[256]{0:T(256)S(1)} %get-tuple-element.336, f32[256,4352]{1,0:T(8,128)S(1)} %get-tuple-element.335, pred[4352]{0:T(1024)(128)(4,1)S(1)} %get-tuple-element.382, s32[256]{0:T(256)S(1)} %get-tuple-element.380, s32[4352]{0:T(1024)S(1)} %get-tuple-element.381, ...), kind=kOutput, calls=%fused_computation.9.clone.1 | convolution fusion | flops 299695872 | bytes 10147844 | tf_op jit(solution)/shard_map/while/body/eval_jaxpr/dot_general | solution.py:71
  116.1 3.8 %multiply_convert_fusion.2 = bf16[256,4352]{1,0:T(8,128)(2,1)S(1)} fusion(f32[256,4352]{1,0:T(8,128)S(1)} %get-tuple-element.335, f32[256,4352]{1,0:T(8,128)S(1)} %get-tuple-element.337, f32[256]{0:T(256)S(1)} %get-tuple-element.338, f32[256]{0:T(256)S(1)} %get-tuple-element.336, pred[4352]{0:T(1024)(128)(4,1)S(1)} %get-tuple-element.382, ...), kind=kLoop, calls=%fused_computation.8.clone.1 | loop fusion | flops 20054016 | bytes 11188736 | tf_op jit(solution)/shard_map/while/body/eval_jaxpr/convert_element_type | solution.py:77
  119.9 1.4 fusion.63
  121.3 1.4 fusion.65
  122.7 6.0 %fusion.64 = f32[1,4352,128]{2,1,0:T(8,128)} fusion(f32[1,4352,128]{2,1,0:T(8,128)} %get-tuple-element.356, bf16[2,256,128]{2,1,0:T(8,128)(2,1)S(1)} %copy-done.8, s32[]{:T(128)} %get-tuple-element.354, f32[256]{0:T(256)S(1)} %get-tuple-element.336, f32[256,4352]{1,0:T(8,128)S(1)} %get-tuple-element.335, pred[4352]{0:T(1024)(128)(4,1)S(1)} %get-tuple-element.382, ...), kind=kOutput, calls=%fused_computation.6.clone.1 | convolution fusion | flops 299139072 | bytes 9032708 | tf_op jit(solution)/shard_map/while/body/eval_jaxpr/dot_general | solution.py:68
  128.7 3.3 %fusion.62 = (f32[256]{0:T(256)S(1)}, f32[256,4352]{1,0:T(8,128)S(1)}) fusion(pred[4352]{0:T(1024)(128)(4,1)S(1)} %get-tuple-element.382, s32[256]{0:T(256)S(1)} %get-tuple-element.380, s32[4352]{0:T(1024)S(1)} %get-tuple-element.381, s32[256]{0:T(256)S(1)} %get-tuple-element.379, s32[4352]{0:T(1024)S(1)} %get-tuple-element.378, ...), kind=kOutput, calls=%fused_computation.34.clone.1 | convolution fusion | flops 298581760 | bytes 5690372 | tf_op jit(solution)/shard_map/while/body/eval_jaxpr/dot_general | solution.py:59
  132.1 3.1 %multiply_reduce_fusion.2 = (f32[256]{0:T(256)S(1)}, f32[256,4352]{1,0:T(8,128)S(1)}) fusion(f32[256]{0:T(256)S(1)} %get-tuple-element.336, f32[256,4352]{1,0:T(8,128)S(1)} %get-tuple-element.335, pred[4352]{0:T(1024)(128)(4,1)S(1)} %get-tuple-element.382, s32[256]{0:T(256)S(1)} %get-tuple-element.380, s32[4352]{0:T(1024)S(1)} %get-tuple-element.381, ...), kind=kOutput, calls=%fused_computation.9.clone.1 | convolution fusion | flops 299695872 | bytes 10147844 | tf_op jit(solution)/shard_map/while/body/eval_jaxpr/dot_general | solution.py:71
  135.2 3.8 %multiply_convert_fusion.2 = bf16[256,4352]{1,0:T(8,128)(2,1)S(1)} fusion(f32[256,4352]{1,0:T(8,128)S(1)} %get-tuple-element.335, f32[256,4352]{1,0:T(8,128)S(1)} %get-tuple-element.337, f32[256]{0:T(256)S(1)} %get-tuple-element.338, f32[256]{0:T(256)S(1)} %get-tuple-element.336, pred[4352]{0:T(1024)(128)(4,1)S(1)} %get-tuple-element.382, ...), kind=kLoop, calls=%fused_computation.8.clone.1 | loop fusion | flops 20054016 | bytes 11188736 | tf_op jit(solution)/shard_map/while/body/eval_jaxpr/convert_element_type | solution.py:77
  139.0 1.4 fusion.63
  140.4 1.4 fusion.65
  141.8 6.0 %fusion.64 = f32[1,4352,128]{2,1,0:T(8,128)} fusion(f32[1,4352,128]{2,1,0:T(8,128)} %get-tuple-element.356, bf16[2,256,128]{2,1,0:T(8,128)(2,1)S(1)} %copy-done.8, s32[]{:T(128)} %get-tuple-element.354, f32[256]{0:T(256)S(1)} %get-tuple-element.336, f32[256,4352]{1,0:T(8,128)S(1)} %get-tuple-element.335, pred[4352]{0:T(1024)(128)(4,1)S(1)} %get-tuple-element.382, ...), kind=kOutput, calls=%fused_computation.6.clone.1 | convolution fusion | flops 299139072 | bytes 9032708 | tf_op jit(solution)/shard_map/while/body/eval_jaxpr/dot_general | solution.py:68
  147.8 1.9 pad_maximum_fusion
  149.8 2.0 collective-permute-start.17
  151.9 4.0 %collective-permute-done.17 = f32[8,256,256]{2,1,0:T(8,128)S(1)} collective-permute-done((f32[8,256,256]{2,1,0:T(8,128)S(1)}, f32[8,256,256]{2,1,0:T(8,128)S(1)}, u32[]{:S(2)}, u32[]{:S(2)}) %collective-permute-start.17) | collective-permute-done | bytes 2097184 | tf_op jit(solution)/shard_map/ppermute | solution.py:175
  156.2 1.9 collective-permute-start.18
  158.1 10.2 %collective-permute-done.18 = f32[256,256]{1,0:T(8,128)S(1)} collective-permute-done((f32[256,256]{1,0:T(8,128)S(1)}, f32[256,256]{1,0:T(8,128)S(1)}, u32[]{:S(2)}, u32[]{:S(2)}) %collective-permute-start.18) | collective-permute-done | bytes 262176 | tf_op jit(solution)/shard_map/ppermute | solution.py:17
  168.4 2.1 collective-permute-start.19
  170.5 8.9 %collective-permute-done.19 = f32[256,256]{1,0:T(8,128)S(1)} collective-permute-done((f32[256,256]{1,0:T(8,128)S(1)}, f32[256,256]{1,0:T(8,128)S(1)}, u32[]{:S(2)}, u32[]{:S(2)}) %collective-permute-start.19) | collective-permute-done | bytes 262176 | tf_op jit(solution)/shard_map/ppermute | solution.py:17
  179.5 1.9 collective-permute-start.20
  181.4 8.1 %collective-permute-done.20 = f32[256,256]{1,0:T(8,128)S(1)} collective-permute-done((f32[256,256]{1,0:T(8,128)S(1)}, f32[256,256]{1,0:T(8,128)S(1)}, u32[]{:S(2)}, u32[]{:S(2)}) %collective-permute-start.20) | collective-permute-done | bytes 262176 | tf_op jit(solution)/shard_map/ppermute | solution.py:17
  189.5 1.9 collective-permute-start.21
  191.5 7.5 %collective-permute-done.21 = f32[256,256]{1,0:T(8,128)S(1)} collective-permute-done((f32[256,256]{1,0:T(8,128)S(1)}, f32[256,256]{1,0:T(8,128)S(1)}, u32[]{:S(2)}, u32[]{:S(2)}) %collective-permute-start.21) | collective-permute-done | bytes 262176 | tf_op jit(solution)/shard_map/ppermute | solution.py:17
  199.1 1.9 collective-permute-start.22
  201.0 7.5 %collective-permute-done.22 = f32[256,256]{1,0:T(8,128)S(1)} collective-permute-done((f32[256,256]{1,0:T(8,128)S(1)}, f32[256,256]{1,0:T(8,128)S(1)}, u32[]{:S(2)}, u32[]{:S(2)}) %collective-permute-start.22) | collective-permute-done | bytes 262176 | tf_op jit(solution)/shard_map/ppermute | solution.py:17
  208.6 1.9 collective-permute-start.23
  210.5 7.5 %collective-permute-done.23 = f32[256,256]{1,0:T(8,128)S(1)} collective-permute-done((f32[256,256]{1,0:T(8,128)S(1)}, f32[256,256]{1,0:T(8,128)S(1)}, u32[]{:S(2)}, u32[]{:S(2)}) %collective-permute-start.23) | collective-permute-done | bytes 262176 | tf_op jit(solution)/shard_map/ppermute | solution.py:17
  218.1 1.9 collective-permute-start.24
  220.0 8.6 %collective-permute-done.24 = f32[256,256]{1,0:T(8,128)S(1)} collective-permute-done((f32[256,256]{1,0:T(8,128)S(1)}, f32[256,256]{1,0:T(8,128)S(1)}, u32[]{:S(2)}, u32[]{:S(2)}) %collective-permute-start.24) | collective-permute-done | bytes 262176 | tf_op jit(solution)/shard_map/ppermute | solution.py:17
  228.6 1.9 collective-permute-start.25
  230.6 2.6 %collective-permute-start.28 = (bf16[256,576]{0,1:T(8,128)(2,1)S(1)}, bf16[256,576]{0,1:T(8,128)(2,1)S(1)}, u32[]{:S(2)}, u32[]{:S(2)}) collective-permute-start(bf16[256,576]{0,1:T(8,128)(2,1)S(1)} %bitcast.192), channel_id=1, source_target_pairs={{192,0},{384,192},{576,384},{193,1},{385,193},{577,385},{194,2},{3... | collective-permute-start | bytes 884744 | tf_op jit(solution)/shard_map/ppermute | solution.py:17
  234.1 2.4 collective-permute-start.16
  236.4 1.7 collective-permute-done.25
  238.2 2.6 %collective-permute-start.26 = (bf16[256,128]{1,0:T(8,128)(2,1)S(1)}, bf16[256,128]{1,0:T(8,128)(2,1)S(1)}, u32[]{:S(2)}, u32[]{:S(2)}) collective-permute-start(bf16[256,128]{1,0:T(8,128)(2,1)S(1)} %get-tuple-element.243), channel_id=1, source_target_pairs={{192,0},{384,192},{576,384},{193,1},{385,193},{577,385},{194,2},{3... | collective-permute-start | bytes 196616 | tf_op jit(solution)/shard_map/ppermute | solution.py:17
  240.7 2.4 collective-permute-start.27
  244.3 2.6 %collective-permute-done.27 = bf16[256,128]{1,0:T(8,128)(2,1)S(1)} collective-permute-done((bf16[256,128]{1,0:T(8,128)(2,1)S(1)}, bf16[256,128]{1,0:T(8,128)(2,1)S(1)}, u32[]{:S(2)}, u32[]{:S(2)}) %collective-permute-start.27) | collective-permute-done | bytes 65568 | tf_op jit(solution)/shard_map/ppermute | solution.py:17
  (97 shorter events, 17.2 us)
Async XLA Ops:
  7.2 94.6 %all-gather.3.cloned.1.call-start = ((), (), s32[]{:S(2)}) async-start(), calls=%async_computation | async-start | bytes 2457600 | tf_op jit(solution)/shard_map/all_gather | solution.py:122
  7.2 34.9 %collective-permute-start.9 = (bf16[256,576]{0,1:T(8,128)(2,1)}, bf16[256,576]{0,1:T(8,128)(2,1)S(1)}, u32[]{:S(2)}, u32[]{:S(2)}) collective-permute-start(bf16[256,576]{0,1:T(8,128)(2,1)} %bitcast.190), channel_id=1, source_target_pairs={{0,7},{1,0},{2,1},{3,2},{4,3},{5,4},{6,5},{7,6},{8,15},{9,8},{10,9... | collective-permute-start | bytes 884744 | tf_op jit(solution)/shard_map/ppermute | solution.py:22
  12.6 34.6 %collective-permute-start.12 = (bf16[256,576]{0,1:T(8,128)(2,1)}, bf16[256,576]{0,1:T(8,128)(2,1)S(1)}, u32[]{:S(2)}, u32[]{:S(2)}) collective-permute-start(bf16[256,576]{0,1:T(8,128)(2,1)} %bitcast.191), channel_id=1, source_target_pairs={{0,1},{1,2},{2,3},{3,4},{4,5},{5,6},{6,7},{7,0},{8,9},{9,10},{10,1... | collective-permute-start | bytes 884744 | tf_op jit(solution)/shard_map/ppermute | solution.py:22
  15.4 13.0 %collective-permute-start = (bf16[256,256]{1,0:T(8,128)(2,1)S(1)}, bf16[256,256]{1,0:T(8,128)(2,1)S(1)}, u32[]{:S(2)}, u32[]{:S(2)}) collective-permute-start(bf16[256,256]{1,0:T(8,128)(2,1)S(1)} %pad_maximum_fusion.1), channel_id=1, source_target_pairs={{0,16},{8,24},{16,32},{24,40},{32,48},{40,56},{48,64},{56,72},{64,... | collective-permute-start | bytes 393224 | tf_op jit(solution)/shard_map/ppermute | solution.py:17
  23.8 23.4 %copy-start.5 = (s32[4352]{0:T(1024)}, s32[4352]{0:T(1024)S(1)}, u32[]{:S(2)}) copy-start(s32[4352]{0:T(1024)S(1)} %get-tuple-element.351) | copy-start | bytes 52228
  28.5 8.0 %collective-permute-start.1 = (bf16[256,256]{1,0:T(8,128)(2,1)S(1)}, bf16[256,256]{1,0:T(8,128)(2,1)S(1)}, u32[]{:S(2)}, u32[]{:S(2)}) collective-permute-start(bf16[256,256]{1,0:T(8,128)(2,1)S(1)} %collective-permute-done), channel_id=1, source_target_pairs={{0,16},{8,24},{16,32},{24,40},{32,48},{40,56},{48,64},{56,72},{64,... | collective-permute-start | bytes 393224 | tf_op jit(solution)/shard_map/ppermute | solution.py:17
  36.5 12.7 %collective-permute-start.2 = (bf16[256,256]{1,0:T(8,128)(2,1)S(1)}, bf16[256,256]{1,0:T(8,128)(2,1)S(1)}, u32[]{:S(2)}, u32[]{:S(2)}) collective-permute-start(bf16[256,256]{1,0:T(8,128)(2,1)S(1)} %collective-permute-done.1), channel_id=1, source_target_pairs={{0,16},{8,24},{16,32},{24,40},{32,48},{40,56},{48,64},{56,72},{64,... | collective-permute-start | bytes 393224 | tf_op jit(solution)/shard_map/ppermute | solution.py:17
  42.1 18.9 %collective-permute-start.10 = (bf16[256,576]{0,1:T(8,128)(2,1)S(1)}, bf16[256,576]{0,1:T(8,128)(2,1)S(1)}, u32[]{:S(2)}, u32[]{:S(2)}) collective-permute-start(bf16[256,576]{0,1:T(8,128)(2,1)S(1)} %collective-permute-done.9), channel_id=1, source_target_pairs={{0,7},{1,0},{2,1},{3,2},{4,3},{5,4},{6,5},{7,6},{8,15},{9,8},{10,9... | collective-permute-start | bytes 884744 | tf_op jit(solution)/shard_map/ppermute | solution.py:22
  47.2 19.6 %collective-permute-start.13 = (bf16[256,576]{0,1:T(8,128)(2,1)S(1)}, bf16[256,576]{0,1:T(8,128)(2,1)S(1)}, u32[]{:S(2)}, u32[]{:S(2)}) collective-permute-start(bf16[256,576]{0,1:T(8,128)(2,1)S(1)} %collective-permute-done.12), channel_id=1, source_target_pairs={{0,1},{1,2},{2,3},{3,4},{4,5},{5,6},{6,7},{7,0},{8,9},{9,10},{10,1... | collective-permute-start | bytes 884744 | tf_op jit(solution)/shard_map/ppermute | solution.py:22
  49.2 7.4 %collective-permute-start.3 = (bf16[256,256]{1,0:T(8,128)(2,1)S(1)}, bf16[256,256]{1,0:T(8,128)(2,1)S(1)}, u32[]{:S(2)}, u32[]{:S(2)}) collective-permute-start(bf16[256,256]{1,0:T(8,128)(2,1)S(1)} %collective-permute-done.2), channel_id=1, source_target_pairs={{0,16},{8,24},{16,32},{24,40},{32,48},{40,56},{48,64},{56,72},{64,... | collective-permute-start | bytes 393224 | tf_op jit(solution)/shard_map/ppermute | solution.py:17
  56.6 12.2 %collective-permute-start.4 = (bf16[256,256]{1,0:T(8,128)(2,1)S(1)}, bf16[256,256]{1,0:T(8,128)(2,1)S(1)}, u32[]{:S(2)}, u32[]{:S(2)}) collective-permute-start(bf16[256,256]{1,0:T(8,128)(2,1)S(1)} %collective-permute-done.3), channel_id=1, source_target_pairs={{0,16},{8,24},{16,32},{24,40},{32,48},{40,56},{48,64},{56,72},{64,... | collective-permute-start | bytes 393224 | tf_op jit(solution)/shard_map/ppermute | solution.py:17
  61.0 33.1 %copy-start.2 = (bf16[1,256,576]{1,2,0:T(8,128)(2,1)S(1)}, bf16[1,256,576]{1,2,0:T(8,128)(2,1)}, u32[]{:S(2)}) copy-start(bf16[1,256,576]{1,2,0:T(8,128)(2,1)} %param.9) | copy-start | bytes 884740
  61.0 21.9 %collective-permute-start.11 = (bf16[256,576]{0,1:T(8,128)(2,1)S(1)}, bf16[256,576]{0,1:T(8,128)(2,1)S(1)}, u32[]{:S(2)}, u32[]{:S(2)}) collective-permute-start(bf16[256,576]{0,1:T(8,128)(2,1)S(1)} %collective-permute-done.10), channel_id=1, source_target_pairs={{0,7},{1,0},{2,1},{3,2},{4,3},{5,4},{6,5},{7,6},{8,15},{9,8},{10,9... | collective-permute-start | bytes 884744 | tf_op jit(solution)/shard_map/ppermute | solution.py:22
  66.8 14.1 %collective-permute-start.14 = (bf16[256,576]{0,1:T(8,128)(2,1)S(1)}, bf16[256,576]{0,1:T(8,128)(2,1)S(1)}, u32[]{:S(2)}, u32[]{:S(2)}) collective-permute-start(bf16[256,576]{0,1:T(8,128)(2,1)S(1)} %collective-permute-done.13), channel_id=1, source_target_pairs={{0,1},{1,2},{2,3},{3,4},{4,5},{5,6},{6,7},{7,0},{8,9},{9,10},{10,1... | collective-permute-start | bytes 884744 | tf_op jit(solution)/shard_map/ppermute | solution.py:22
  68.8 6.9 %collective-permute-start.5 = (bf16[256,256]{1,0:T(8,128)(2,1)S(1)}, bf16[256,256]{1,0:T(8,128)(2,1)S(1)}, u32[]{:S(2)}, u32[]{:S(2)}) collective-permute-start(bf16[256,256]{1,0:T(8,128)(2,1)S(1)} %collective-permute-done.4), channel_id=1, source_target_pairs={{0,16},{8,24},{16,32},{24,40},{32,48},{40,56},{48,64},{56,72},{64,... | collective-permute-start | bytes 393224 | tf_op jit(solution)/shard_map/ppermute | solution.py:17
  75.7 8.3 %collective-permute-start.6 = (bf16[256,256]{1,0:T(8,128)(2,1)S(1)}, bf16[256,256]{1,0:T(8,128)(2,1)S(1)}, u32[]{:S(2)}, u32[]{:S(2)}) collective-permute-start(bf16[256,256]{1,0:T(8,128)(2,1)S(1)} %collective-permute-done.5), channel_id=1, source_target_pairs={{0,16},{8,24},{16,32},{24,40},{32,48},{40,56},{48,64},{56,72},{64,... | collective-permute-start | bytes 393224 | tf_op jit(solution)/shard_map/ppermute | solution.py:17
  81.0 13.0 %collective-permute-start.15 = (bf16[256,576]{0,1:T(8,128)(2,1)S(1)}, bf16[256,576]{0,1:T(8,128)(2,1)S(1)}, u32[]{:S(2)}, u32[]{:S(2)}) collective-permute-start(bf16[256,576]{0,1:T(8,128)(2,1)S(1)} %collective-permute-done.14), channel_id=1, source_target_pairs={{0,1},{1,2},{2,3},{3,4},{4,5},{5,6},{6,7},{7,0},{8,9},{9,10},{10,1... | collective-permute-start | bytes 884744 | tf_op jit(solution)/shard_map/ppermute | solution.py:22
  83.9 8.1 %collective-permute-start.7 = (bf16[256,256]{1,0:T(8,128)(2,1)S(1)}, bf16[256,256]{1,0:T(8,128)(2,1)S(1)}, u32[]{:S(2)}, u32[]{:S(2)}) collective-permute-start(bf16[256,256]{1,0:T(8,128)(2,1)S(1)} %collective-permute-done.6), channel_id=1, source_target_pairs={{0,16},{8,24},{16,32},{24,40},{32,48},{40,56},{48,64},{56,72},{64,... | collective-permute-start | bytes 393224 | tf_op jit(solution)/shard_map/ppermute | solution.py:17
  92.1 4.7 %collective-permute-start.8 = (bf16[9,256,256]{2,1,0:T(8,128)(2,1)S(1)}, bf16[9,256,256]{2,1,0:T(8,128)(2,1)S(1)}, u32[]{:S(2)}, u32[]{:S(2)}) collective-permute-start(bf16[9,256,256]{2,1,0:T(8,128)(2,1)S(1)} %bitcast_dynamic-update-slice_fusion.14), channel_id=1, source_target_pairs={{0,8},{8,0},{16,24},{24,16},{32,40},{40,32},{48,56},{56,48},{64,72... | collective-permute-start | bytes 3538952 | tf_op jit(solution)/shard_map/ppermute | solution.py:144
  100.6 2.1 copy-start
  106.0 3.4 %copy-start.1 = (bf16[1,256,256]{1,2,0:T(8,128)(2,1)S(1)}, bf16[1,256,256]{1,2,0:T(8,128)(2,1)}, u32[]{:S(2)}) copy-start(bf16[1,256,256]{1,2,0:T(8,128)(2,1)} %copy.19) | copy-start | bytes 393220
  106.0 3.4 %copy-start.6 = (s32[4352]{0:T(1024)S(1)}, s32[4352]{0:T(1024)}, u32[]{:S(2)}) copy-start(s32[4352]{0:T(1024)} %copy-done.5) | copy-start | bytes 52228
  106.0 3.4 %copy-start.7 = (s32[4352]{0:T(1024)S(1)}, s32[4352]{0:T(1024)}, u32[]{:S(2)}) copy-start(s32[4352]{0:T(1024)} %get-tuple-element.348) | copy-start | bytes 52228
  106.0 3.4 %copy-start.9 = (s32[1,256]{1,0:T(1,128)S(1)}, s32[1,256]{1,0:T(1,128)}, u32[]{:S(2)}) copy-start(s32[1,256]{1,0:T(1,128)} %constant_dynamic-slice_fusion.1) | copy-start | bytes 3076
  106.1 3.4 %copy-start.10 = (s32[256]{0:T(256)S(1)}, s32[256]{0:T(256)}, u32[]{:S(2)}) copy-start(s32[256]{0:T(256)} %iota_add_fusion.1) | copy-start | bytes 3076
  109.6 3.4 %copy-start.4 = (bf16[1,4352,128]{2,1,0:T(8,128)(2,1)S(1)}, bf16[1,4352,128]{2,1,0:T(8,128)(2,1)}, u32[]{:S(2)}) copy-start(bf16[1,4352,128]{2,1,0:T(8,128)(2,1)} %get-tuple-element.376) | copy-start | bytes 3342340 | tf_op jit(solution)/shard_map/while
  109.6 3.4 %copy-start.8 = (bf16[2,256,128]{2,1,0:T(8,128)(2,1)S(1)}, bf16[2,256,128]{2,1,0:T(8,128)(2,1)}, u32[]{:S(2)}) copy-start(bf16[2,256,128]{2,1,0:T(8,128)(2,1)} %get-tuple-element.375) | copy-start | bytes 393220 | tf_op jit(solution)/shard_map/while
  128.7 3.3 %copy-start.4 = (bf16[1,4352,128]{2,1,0:T(8,128)(2,1)S(1)}, bf16[1,4352,128]{2,1,0:T(8,128)(2,1)}, u32[]{:S(2)}) copy-start(bf16[1,4352,128]{2,1,0:T(8,128)(2,1)} %get-tuple-element.376) | copy-start | bytes 3342340 | tf_op jit(solution)/shard_map/while
  128.7 3.3 %copy-start.8 = (bf16[2,256,128]{2,1,0:T(8,128)(2,1)S(1)}, bf16[2,256,128]{2,1,0:T(8,128)(2,1)}, u32[]{:S(2)}) copy-start(bf16[2,256,128]{2,1,0:T(8,128)(2,1)} %get-tuple-element.375) | copy-start | bytes 393220 | tf_op jit(solution)/shard_map/while
  149.8 6.1 %collective-permute-start.17 = (f32[8,256,256]{2,1,0:T(8,128)S(1)}, f32[8,256,256]{2,1,0:T(8,128)S(1)}, u32[]{:S(2)}, u32[]{:S(2)}) collective-permute-start(f32[8,256,256]{2,1,0:T(8,128)S(1)} %slice.50), channel_id=1, source_target_pairs={{0,8},{8,0},{16,24},{24,16},{32,40},{40,32},{48,56},{56,48},{64,72... | collective-permute-start | bytes 6291464 | tf_op jit(solution)/shard_map/ppermute | solution.py:175
  156.2 12.2 %collective-permute-start.18 = (f32[256,256]{1,0:T(8,128)S(1)}, f32[256,256]{1,0:T(8,128)S(1)}, u32[]{:S(2)}, u32[]{:S(2)}) collective-permute-start(f32[256,256]{1,0:T(8,128)S(1)} %slice_bitcast_fusion.8), channel_id=1, source_target_pairs={{16,0},{24,8},{32,16},{40,24},{48,32},{56,40},{64,48},{72,56},{80,... | collective-permute-start | bytes 786440 | tf_op jit(solution)/shard_map/ppermute | solution.py:17
  168.4 62.1 %copy-start.3 = (bf16[1,256,576]{1,2,0:T(8,128)(2,1)S(1)}, bf16[1,256,576]{1,2,0:T(8,128)(2,1)}, u32[]{:S(2)}) copy-start(bf16[1,256,576]{1,2,0:T(8,128)(2,1)} %param.9) | copy-start | bytes 884740
  168.4 11.0 %collective-permute-start.19 = (f32[256,256]{1,0:T(8,128)S(1)}, f32[256,256]{1,0:T(8,128)S(1)}, u32[]{:S(2)}, u32[]{:S(2)}) collective-permute-start(f32[256,256]{1,0:T(8,128)S(1)} %fusion.40), channel_id=1, source_target_pairs={{16,0},{24,8},{32,16},{40,24},{48,32},{56,40},{64,48},{72,56},{80,... | collective-permute-start | bytes 786440 | tf_op jit(solution)/shard_map/ppermute | solution.py:17
  179.5 10.0 %collective-permute-start.20 = (f32[256,256]{1,0:T(8,128)S(1)}, f32[256,256]{1,0:T(8,128)S(1)}, u32[]{:S(2)}, u32[]{:S(2)}) collective-permute-start(f32[256,256]{1,0:T(8,128)S(1)} %fusion.39), channel_id=1, source_target_pairs={{16,0},{24,8},{32,16},{40,24},{48,32},{56,40},{64,48},{72,56},{80,... | collective-permute-start | bytes 786440 | tf_op jit(solution)/shard_map/ppermute | solution.py:17
  189.5 9.5 %collective-permute-start.21 = (f32[256,256]{1,0:T(8,128)S(1)}, f32[256,256]{1,0:T(8,128)S(1)}, u32[]{:S(2)}, u32[]{:S(2)}) collective-permute-start(f32[256,256]{1,0:T(8,128)S(1)} %fusion.38), channel_id=1, source_target_pairs={{16,0},{24,8},{32,16},{40,24},{48,32},{56,40},{64,48},{72,56},{80,... | collective-permute-start | bytes 786440 | tf_op jit(solution)/shard_map/ppermute | solution.py:17
  199.1 9.5 %collective-permute-start.22 = (f32[256,256]{1,0:T(8,128)S(1)}, f32[256,256]{1,0:T(8,128)S(1)}, u32[]{:S(2)}, u32[]{:S(2)}) collective-permute-start(f32[256,256]{1,0:T(8,128)S(1)} %fusion.37), channel_id=1, source_target_pairs={{16,0},{24,8},{32,16},{40,24},{48,32},{56,40},{64,48},{72,56},{80,... | collective-permute-start | bytes 786440 | tf_op jit(solution)/shard_map/ppermute | solution.py:17
  208.6 9.5 %collective-permute-start.23 = (f32[256,256]{1,0:T(8,128)S(1)}, f32[256,256]{1,0:T(8,128)S(1)}, u32[]{:S(2)}, u32[]{:S(2)}) collective-permute-start(f32[256,256]{1,0:T(8,128)S(1)} %fusion.36), channel_id=1, source_target_pairs={{16,0},{24,8},{32,16},{40,24},{48,32},{56,40},{64,48},{72,56},{80,... | collective-permute-start | bytes 786440 | tf_op jit(solution)/shard_map/ppermute | solution.py:17
  218.1 10.5 %collective-permute-start.24 = (f32[256,256]{1,0:T(8,128)S(1)}, f32[256,256]{1,0:T(8,128)S(1)}, u32[]{:S(2)}, u32[]{:S(2)}) collective-permute-start(f32[256,256]{1,0:T(8,128)S(1)} %fusion.35), channel_id=1, source_target_pairs={{16,0},{24,8},{32,16},{40,24},{48,32},{56,40},{64,48},{72,56},{80,... | collective-permute-start | bytes 786440 | tf_op jit(solution)/shard_map/ppermute | solution.py:17
  228.6 9.5 %collective-permute-start.25 = (f32[256,256]{1,0:T(8,128)S(1)}, f32[256,256]{1,0:T(8,128)S(1)}, u32[]{:S(2)}, u32[]{:S(2)}) collective-permute-start(f32[256,256]{1,0:T(8,128)S(1)} %fusion.34), channel_id=1, source_target_pairs={{16,0},{24,8},{32,16},{40,24},{48,32},{56,40},{64,48},{72,56},{80,... | collective-permute-start | bytes 786440 | tf_op jit(solution)/shard_map/ppermute | solution.py:17
  230.6 12.5 %collective-permute-start.28 = (bf16[256,576]{0,1:T(8,128)(2,1)S(1)}, bf16[256,576]{0,1:T(8,128)(2,1)S(1)}, u32[]{:S(2)}, u32[]{:S(2)}) collective-permute-start(bf16[256,576]{0,1:T(8,128)(2,1)S(1)} %bitcast.192), channel_id=1, source_target_pairs={{192,0},{384,192},{576,384},{193,1},{385,193},{577,385},{194,2},{3... | collective-permute-start | bytes 884744 | tf_op jit(solution)/shard_map/ppermute | solution.py:17
  234.1 9.0 %collective-permute-start.16 = (bf16[256,256]{1,0:T(8,128)(2,1)S(1)}, bf16[256,256]{1,0:T(8,128)(2,1)S(1)}, u32[]{:S(2)}, u32[]{:S(2)}) collective-permute-start(bf16[256,256]{1,0:T(8,128)(2,1)S(1)} %copy_bitcast_fusion), channel_id=1, source_target_pairs={{192,0},{384,192},{576,384},{193,1},{385,193},{577,385},{194,2},{3... | collective-permute-start | bytes 393224 | tf_op jit(solution)/shard_map/ppermute | solution.py:17
  238.2 6.2 %collective-permute-start.26 = (bf16[256,128]{1,0:T(8,128)(2,1)S(1)}, bf16[256,128]{1,0:T(8,128)(2,1)S(1)}, u32[]{:S(2)}, u32[]{:S(2)}) collective-permute-start(bf16[256,128]{1,0:T(8,128)(2,1)S(1)} %get-tuple-element.243), channel_id=1, source_target_pairs={{192,0},{384,192},{576,384},{193,1},{385,193},{577,385},{194,2},{3... | collective-permute-start | bytes 196616 | tf_op jit(solution)/shard_map/ppermute | solution.py:17
  240.7 6.2 %collective-permute-start.27 = (bf16[256,128]{1,0:T(8,128)(2,1)S(1)}, bf16[256,128]{1,0:T(8,128)(2,1)S(1)}, u32[]{:S(2)}, u32[]{:S(2)}) collective-permute-start(bf16[256,128]{1,0:T(8,128)(2,1)S(1)} %get-tuple-element.242), channel_id=1, source_target_pairs={{192,0},{384,192},{576,384},{193,1},{385,193},{577,385},{194,2},{3... | collective-permute-start | bytes 196616 | tf_op jit(solution)/shard_map/ppermute | solution.py:17
Sparse Core Ops, SparseCore 0:
  14.7 60.9 all-gather.2

commit v5 on v4

--- a/solution.py
+++ b/solution.py
@@ -44,66 +44,39 @@
     span_rows = key_near.shape[0]
     key_width = key_near.shape[1]
     groups = key_width // HD
-    query_heads = jnp.moveaxis(query_act.reshape(tok_rows, 2 * groups, HD), 1, 0)
-    attn_heads = jnp.moveaxis(d_attn.reshape(tok_rows, 2 * groups, HD), 1, 0)
-    key_heads = jnp.moveaxis(key_near.reshape(span_rows, groups, HD), 1, 0)
-    value_heads = jnp.moveaxis(value_near.reshape(span_rows, groups, HD), 1, 0)
-
-    def one_head(running, head_items):
-        key_sums, value_sums = running
-        head_index, query_h, attn_h = head_items
-        group_index = head_index // 2
-        key_g = lax.dynamic_index_in_dim(key_heads, group_index, 0, keepdims=False)
-        value_g = lax.dynamic_index_in_dim(value_heads, group_index, 0, keepdims=False)
-        raw_scores = (
-            lax.dot_general(
-                query_h, key_g, (((1,), (1,)), ((), ())), preferred_element_type=jnp.float32
-            )
-            * score_scale
-        )
-        capped = jnp.tanh(raw_scores / logit_cap)
-        weights = jnp.where(allowed, jnp.exp(logit_cap * capped), 0.0)
-        attn_probs = weights / jnp.sum(weights, axis=-1, keepdims=True)
-        probs_low = attn_probs.astype(jnp.bfloat16)
-        value_part = lax.dot_general(
-            probs_low, attn_h, (((0,), (0,)), ((), ())), preferred_element_type=jnp.float32
-        )
-        grad_probs = lax.dot_general(
-            attn_h, value_g, (((1,), (1,)), ((), ())), preferred_element_type=jnp.float32
-        )
-        row_delta = jnp.sum(attn_probs * grad_probs, axis=-1, keepdims=True)
-        grad_raw = (
-            attn_probs * (grad_probs - row_delta) * (1.0 - capped * capped) * score_scale
-        ).astype(jnp.bfloat16)
-        query_grad = jnp.dot(grad_raw, key_g, preferred_element_type=jnp.float32).astype(
-            jnp.bfloat16
-        )
-        key_part = lax.dot_general(
-            grad_raw, query_h, (((0,), (0,)), ((), ())), preferred_element_type=jnp.float32
-        )
-        key_sums = lax.dynamic_update_index_in_dim(
-            key_sums,
-            lax.dynamic_index_in_dim(key_sums, group_index, 0, keepdims=False) + key_part,
-            group_index,
-            0,
-        )
-        value_sums = lax.dynamic_update_index_in_dim(
-            value_sums,
-            lax.dynamic_index_in_dim(value_sums, group_index, 0, keepdims=False) + value_part,
-            group_index,
-            0,
-        )
-        return ((key_sums, value_sums), query_grad)
-
-    zero_sums = jnp.zeros((groups, span_rows, HD), jnp.float32)
-    head_numbers = jnp.arange(2 * groups, dtype=jnp.int32)
-    (key_sums, value_sums), query_grads = lax.scan(
-        one_head, (zero_sums, zero_sums), (head_numbers, query_heads, attn_heads)
+    query_g = query_act.reshape(tok_rows, groups, 2, HD)
+    attn_g = d_attn.reshape(tok_rows, groups, 2, HD)
+    key_g = key_near.reshape(span_rows, groups, HD)
+    value_g = value_near.reshape(span_rows, groups, HD)
+    raw_scores = (
+        jnp.einsum("qgrd,kgd->grqk", query_g, key_g, preferred_element_type=jnp.float32)
+        * score_scale
     )
-    query_grad = jnp.moveaxis(query_grads, 0, 1).reshape(tok_rows, 2 * groups * HD)
-    key_sum = jnp.moveaxis(key_sums, 0, 1).reshape(span_rows, key_width)
-    value_sum = jnp.moveaxis(value_sums, 0, 1).reshape(span_rows, key_width)
-    return (query_grad, key_sum, value_sum)
+    capped = jnp.tanh(raw_scores / logit_cap)
+    weights = jnp.where(allowed[None, None], jnp.exp(logit_cap * capped), 0.0)
+    attn_probs = weights / jnp.sum(weights, axis=-1, keepdims=True)
+    probs_low = attn_probs.astype(jnp.bfloat16)
+    value_sum = jnp.einsum(
+        "grqk,qgrd->kgd", probs_low, attn_g, preferred_element_type=jnp.float32
+    )
+    grad_probs = jnp.einsum(
+        "qgrd,kgd->grqk", attn_g, value_g, preferred_element_type=jnp.float32
+    )
+    row_delta = jnp.sum(attn_probs * grad_probs, axis=-1, keepdims=True)
+    grad_raw = (
+        attn_probs * (grad_probs - row_delta) * (1.0 - capped * capped) * score_scale
+    ).astype(jnp.bfloat16)
+    query_grad = jnp.einsum(
+        "grqk,kgd->qgrd", grad_raw, key_g, preferred_element_type=jnp.float32
+    ).astype(jnp.bfloat16)
+    key_sum = jnp.einsum(
+        "grqk,qgrd->kgd", grad_raw, query_g, preferred_element_type=jnp.float32
+    )
+    return (
+        query_grad.reshape(tok_rows, key_width * 2),
+        key_sum.reshape(span_rows, key_width),
+        value_sum.reshape(span_rows, key_width),
+    )
 
 
 def shared_lookup(key_doc, shared_flags):
@@ -116,6 +89,7 @@
 def per_device(grad_out, out_weight, query_act, key_act, value_act, doc_ids, doc_shared):
     grad_tile = grad_out[0]
     tok_rows = grad_tile.shape[0]
+    grad_handed = from_behind(grad_tile, "pipe", -1)
     grad_rows = ring_gather(grad_tile, "col")
     d_attn = lax.dot_general(
         grad_rows,
@@ -168,6 +142,7 @@
     )
     allowed = allowed & ((key_doc[None, :] == query_doc[:, None]) | (key_shared[None, :] == 1))
     query_grad, key_sum, value_sum = attend(query_local, key_near, value_near, d_attn, allowed)
+    query_handed = from_behind(query_grad, "pipe", -1)
     pair_sum = jnp.concatenate([key_sum, value_sum], axis=1)
     pair_sum = pair_sum.reshape(reach_rows + 1, tok_rows, 2 * key_width)
     even_part = pair_sum[0::2]
@@ -187,12 +162,10 @@
         running = from_behind(running, "row", -2) + chip_sum[step]
     key_total = running[:, :key_width]
     value_total = running[:, key_width:]
-    handed = from_behind(
-        (query_grad, key_total.astype(jnp.bfloat16), value_total.astype(jnp.bfloat16), grad_tile),
-        "pipe",
-        -1,
+    key_handed, value_handed = from_behind(
+        (key_total.astype(jnp.bfloat16), value_total.astype(jnp.bfloat16)), "pipe", -1
     )
-    return (handed[0][None], handed[1][None], handed[2][None], handed[3][None])
+    return (query_handed[None], key_handed[None], value_handed[None], grad_handed[None])
 
 
 def solution(mesh):

time: 258 us -> 247 us (0.957)
  the two profiles are of different devices: /device:TPU:196 before, /device:TPU:218 now
where the time goes in v5:
time: 247 us; the launch traced here: 245 us
  starting transfers between devices  85.8 us (35%)
  waiting for transfers between devices  82.5 us (33%)
  matrix products  24.8 us (10%)
  other arithmetic  19.6 us (8%)
  local copies, waits for them, and re-layouts  17.7 us (7%)
  between operations  14.8 us (6%)
    ppermute x20, waiting for transfers between devices, from_behind(): return lax.ppermute(block, axis, route)  77.8 us
    ppermute x20, starting transfers between devices, from_behind(): return lax.ppermute(block, axis, route)  58.4 us
    ppermute x7, starting transfers between devices, cyclic_shift(): lax.ppermute(block, axis, [(i, (i + distance) % size) for i in range(size)])  23.1 us
    convert_element_type x1, other arithmetic, attend(): grad_raw = (attn_probs * (grad_probs - row_delta) * (1.0 - capped * cappe...  8.11 us
    dot_general x1, matrix products, attend(): jnp.einsum('grqk,qgrd->kgd', probs_low, attn_g, preferred_element_type=jn...  7.71 us
    dot_general x1, matrix products, attend(): jnp.einsum('qgrd,kgd->grqk', attn_g, value_g, preferred_element_type=jnp....  4.96 us
    dot_general x1, matrix products, attend(): jnp.einsum('qgrd,kgd->grqk', query_g, key_g, preferred_element_type=jnp.f...  4.94 us
  transfers between devices with their start and end apart: 30, of which 17 were waited for; matrix products, arithmetic and copies ran while one was open for 11% of the time, Pallas kernels for 0%

profile of v5, /device:TPU:218, one launch (start us, length us, event | category | flops | bytes accessed | tf_op | source)
XLA Modules:
  0.0 245.2 jit_solution(89932961508521258)
XLA Ops:
  7.2 2.4 collective-permute-start.9
  9.6 4.7 %collective-permute-start.12 = (bf16[256,576]{0,1:T(8,128)(2,1)}, bf16[256,576]{0,1:T(8,128)(2,1)S(1)}, u32[]{:S(2)}, u32[]{:S(2)}) collective-permute-start(bf16[256,576]{0,1:T(8,128)(2,1)} %bitcast.185), channel_id=1, source_target_pairs={{0,1},{1,2},{2,3},{3,4},{4,5},{5,6},{6,7},{7,0},{8,9},{9,10},{10,1... | collective-permute-start | bytes 884744 | tf_op jit(solution)/shard_map/ppermute | solution.py:22
  14.3 0.9 pad_maximum_fusion.1
  15.2 5.6 %collective-permute-start = (bf16[256,256]{1,0:T(8,128)(2,1)S(1)}, bf16[256,256]{1,0:T(8,128)(2,1)S(1)}, u32[]{:S(2)}, u32[]{:S(2)}) collective-permute-start(bf16[256,256]{1,0:T(8,128)(2,1)S(1)} %pad_maximum_fusion.1), channel_id=1, source_target_pairs={{0,16},{8,24},{16,32},{24,40},{32,48},{40,56},{48,64},{56,72},{64,... | collective-permute-start | bytes 393224 | tf_op jit(solution)/shard_map/ppermute | solution.py:17
  23.1 4.0 %fusion.11 = pred[256,4352]{0,1:T(8,128)(4,1)S(1)} fusion(s32[256]{0:T(256)S(1)} %bitcast.197, s32[256]{0:T(256)S(1)} %iota_add_fusion.1, s32[4352]{0:T(1024)S(1)} %get-tuple-element.22, s32[4352]{0:T(1024)S(1)} %get-tuple-element.23, pred[4352]{0:T(1024)(128)(4,1)S(1)} %broadcast_compare_fusion, pred[4352]{0:T(1024)(128)(4,1)S(1)} %broadcast_compare_fusion.1), kind=kLoop, calls=%fused_computation.19 | loop fusion | flops 8912896 | bytes 1159680 | tf_op jit(solution)/shard_map/and | solution.py:143
  27.2 0.9 bitcast_dynamic-update-slice_fusion.22
  28.1 1.6 reshape.212
  29.7 1.0 constant_dynamic-update-slice_fusion.1
  30.7 4.3 %collective-permute-start.1 = (bf16[256,256]{1,0:T(8,128)(2,1)S(1)}, bf16[256,256]{1,0:T(8,128)(2,1)S(1)}, u32[]{:S(2)}, u32[]{:S(2)}) collective-permute-start(bf16[256,256]{1,0:T(8,128)(2,1)S(1)} %collective-permute-done), channel_id=1, source_target_pairs={{0,16},{8,24},{16,32},{24,40},{32,48},{40,56},{48,64},{56,72},{64,... | collective-permute-start | bytes 393224 | tf_op jit(solution)/shard_map/ppermute | solution.py:17
  35.0 2.5 %collective-permute-done.1 = bf16[256,256]{1,0:T(8,128)(2,1)S(1)} collective-permute-done((bf16[256,256]{1,0:T(8,128)(2,1)S(1)}, bf16[256,256]{1,0:T(8,128)(2,1)S(1)}, u32[]{:S(2)}, u32[]{:S(2)}) %collective-permute-start.1) | collective-permute-done | bytes 131104 | tf_op jit(solution)/shard_map/ppermute | solution.py:17
  37.5 5.5 %collective-permute-start.2 = (bf16[256,256]{1,0:T(8,128)(2,1)S(1)}, bf16[256,256]{1,0:T(8,128)(2,1)S(1)}, u32[]{:S(2)}, u32[]{:S(2)}) collective-permute-start(bf16[256,256]{1,0:T(8,128)(2,1)S(1)} %collective-permute-done.1), channel_id=1, source_target_pairs={{0,16},{8,24},{16,32},{24,40},{32,48},{40,56},{48,64},{56,72},{64,... | collective-permute-start | bytes 393224 | tf_op jit(solution)/shard_map/ppermute | solution.py:17
  43.1 1.9 collective-permute-start.10
  45.0 5.1 %collective-permute-start.13 = (bf16[256,576]{0,1:T(8,128)(2,1)S(1)}, bf16[256,576]{0,1:T(8,128)(2,1)S(1)}, u32[]{:S(2)}, u32[]{:S(2)}) collective-permute-start(bf16[256,576]{0,1:T(8,128)(2,1)S(1)} %collective-permute-done.12), channel_id=1, source_target_pairs={{0,1},{1,2},{2,3},{3,4},{4,5},{5,6},{6,7},{7,0},{8,9},{9,10},{10,1... | collective-permute-start | bytes 884744 | tf_op jit(solution)/shard_map/ppermute | solution.py:22
  50.2 3.1 %collective-permute-start.3 = (bf16[256,256]{1,0:T(8,128)(2,1)S(1)}, bf16[256,256]{1,0:T(8,128)(2,1)S(1)}, u32[]{:S(2)}, u32[]{:S(2)}) collective-permute-start(bf16[256,256]{1,0:T(8,128)(2,1)S(1)} %collective-permute-done.2), channel_id=1, source_target_pairs={{0,16},{8,24},{16,32},{24,40},{32,48},{40,56},{48,64},{56,72},{64,... | collective-permute-start | bytes 393224 | tf_op jit(solution)/shard_map/ppermute | solution.py:17
  53.3 4.5 %collective-permute-done.3 = bf16[256,256]{1,0:T(8,128)(2,1)S(1)} collective-permute-done((bf16[256,256]{1,0:T(8,128)(2,1)S(1)}, bf16[256,256]{1,0:T(8,128)(2,1)S(1)}, u32[]{:S(2)}, u32[]{:S(2)}) %collective-permute-start.3) | collective-permute-done | bytes 131104 | tf_op jit(solution)/shard_map/ppermute | solution.py:17
  57.8 4.4 %collective-permute-start.4 = (bf16[256,256]{1,0:T(8,128)(2,1)S(1)}, bf16[256,256]{1,0:T(8,128)(2,1)S(1)}, u32[]{:S(2)}, u32[]{:S(2)}) collective-permute-start(bf16[256,256]{1,0:T(8,128)(2,1)S(1)} %collective-permute-done.3), channel_id=1, source_target_pairs={{0,16},{8,24},{16,32},{24,40},{32,48},{40,56},{48,64},{56,72},{64,... | collective-permute-start | bytes 393224 | tf_op jit(solution)/shard_map/ppermute | solution.py:17
  62.3 1.9 collective-permute-start.11
  64.2 5.1 %collective-permute-start.14 = (bf16[256,576]{0,1:T(8,128)(2,1)S(1)}, bf16[256,576]{0,1:T(8,128)(2,1)S(1)}, u32[]{:S(2)}, u32[]{:S(2)}) collective-permute-start(bf16[256,576]{0,1:T(8,128)(2,1)S(1)} %collective-permute-done.13), channel_id=1, source_target_pairs={{0,1},{1,2},{2,3},{3,4},{4,5},{5,6},{6,7},{7,0},{8,9},{9,10},{10,1... | collective-permute-start | bytes 884744 | tf_op jit(solution)/shard_map/ppermute | solution.py:22
  69.4 2.8 %collective-permute-start.5 = (bf16[256,256]{1,0:T(8,128)(2,1)S(1)}, bf16[256,256]{1,0:T(8,128)(2,1)S(1)}, u32[]{:S(2)}, u32[]{:S(2)}) collective-permute-start(bf16[256,256]{1,0:T(8,128)(2,1)S(1)} %collective-permute-done.4), channel_id=1, source_target_pairs={{0,16},{8,24},{16,32},{24,40},{32,48},{40,56},{48,64},{56,72},{64,... | collective-permute-start | bytes 393224 | tf_op jit(solution)/shard_map/ppermute | solution.py:17
  72.2 4.6 %collective-permute-done.5 = bf16[256,256]{1,0:T(8,128)(2,1)S(1)} collective-permute-done((bf16[256,256]{1,0:T(8,128)(2,1)S(1)}, bf16[256,256]{1,0:T(8,128)(2,1)S(1)}, u32[]{:S(2)}, u32[]{:S(2)}) %collective-permute-start.5) | collective-permute-done | bytes 131104 | tf_op jit(solution)/shard_map/ppermute | solution.py:17
  76.9 3.7 %collective-permute-start.6 = (bf16[256,256]{1,0:T(8,128)(2,1)S(1)}, bf16[256,256]{1,0:T(8,128)(2,1)S(1)}, u32[]{:S(2)}, u32[]{:S(2)}) collective-permute-start(bf16[256,256]{1,0:T(8,128)(2,1)S(1)} %collective-permute-done.5), channel_id=1, source_target_pairs={{0,16},{8,24},{16,32},{24,40},{32,48},{40,56},{48,64},{56,72},{64,... | collective-permute-start | bytes 393224 | tf_op jit(solution)/shard_map/ppermute | solution.py:17
  80.6 1.9 collective-permute-start.15
  82.5 2.2 collective-permute-done.6
  84.7 4.0 %collective-permute-start.7 = (bf16[256,256]{1,0:T(8,128)(2,1)S(1)}, bf16[256,256]{1,0:T(8,128)(2,1)S(1)}, u32[]{:S(2)}, u32[]{:S(2)}) collective-permute-start(bf16[256,256]{1,0:T(8,128)(2,1)S(1)} %collective-permute-done.6), channel_id=1, source_target_pairs={{0,16},{8,24},{16,32},{24,40},{32,48},{40,56},{48,64},{56,72},{64,... | collective-permute-start | bytes 393224 | tf_op jit(solution)/shard_map/ppermute | solution.py:17
  88.7 2.9 %collective-permute-done.7 = bf16[256,256]{1,0:T(8,128)(2,1)S(1)} collective-permute-done((bf16[256,256]{1,0:T(8,128)(2,1)S(1)}, bf16[256,256]{1,0:T(8,128)(2,1)S(1)}, u32[]{:S(2)}, u32[]{:S(2)}) %collective-permute-start.7) | collective-permute-done | bytes 131104 | tf_op jit(solution)/shard_map/ppermute | solution.py:17
  91.6 2.1 collective-permute-start.8
  94.1 1.7 constant_dynamic-slice_fusion
  96.3 2.1 maximum_select_fusion
  98.4 1.6 rev.3
  100.0 1.9 copy.35
  101.9 4.9 %fusion.5 = (f32[2,256]{1,0:T(2,128)S(1)}, f32[4352,256,2]{1,0,2:T(8,128)}) fusion(pred[256,4352]{0,1:T(8,128)(4,1)S(1)} %fusion.11, bf16[256,2,128]{2,1,0:T(2,128)(2,1)S(1)} %copy-done.4, bf16[4608,256]{1,0:T(8,128)(2,1)S(1)} %bitcast.177, s32[]{:T(128)S(6)} %select_n.55), kind=kOutput, calls=%fused_computation.10 | convolution fusion | flops 579337728 | bytes 11274244 | tf_op jit(solution)/shard_map/qgrd,kgd->grqk/dot_general | solution.py:52
  106.8 3.6 %fusion.15 = bf16[256,256]{0,1:T(8,128)(2,1)S(1)} fusion(bf16[256,4608]{0,1:T(8,128)(2,1)} %bitcast.180, bf16[1,256,4608]{1,2,0:T(8,128)(2,1)} %all-gather.3.cloned.1.call-done), kind=kOutput, calls=%fused_computation.25 | convolution fusion | flops 604045312 | bytes 4849664 | tf_op jit(solution)/shard_map/dot_general | solution.py:94
  110.4 7.7 %convolution_bitcast_fusion = f32[4352,1,128]{0,2,1:T(8,128)} fusion(bf16[256,2,128]{0,2,1:T(8,128)(2,1)S(1)} %bitcast.199, f32[4352,256,2]{1,0,2:T(8,128)} %get-tuple-element.19, f32[2,256]{1,0:T(2,128)S(1)} %get-tuple-element.18, pred[256,4352]{0,1:T(8,128)(4,1)S(1)} %fusion.11), kind=kOutput, calls=%fused_computation.11 | convolution fusion | flops 579338240 | bytes 12388352 | tf_op jit(solution)/shard_map/grqk,qgrd->kgd/dot_general | solution.py:59
  118.1 5.0 %fusion.2 = (f32[2,256]{1,0:T(2,128)S(1)}, f32[4352,256,2]{1,0,2:T(8,128)}) fusion(f32[2,256]{1,0:T(2,128)S(1)} %get-tuple-element.18, f32[4352,256,2]{1,0,2:T(8,128)S(1)} %bitcast.175, pred[256,4352]{0,1:T(8,128)(4,1)S(1)} %fusion.11, bf16[256,2,128]{0,2,1:T(8,128)(2,1)S(1)} %bitcast.200, bf16[4608,256]{1,0:T(8,128)(2,1)S(1)} %bitcast.178, ...), kind=kOutput, calls=%fused_computation.6 | convolution fusion | flops 581565952 | bytes 20189192 | tf_op jit(solution)/shard_map/qgrd,kgd->grqk/dot_general | solution.py:62
  123.1 3.0 %copy.43 = f32[4352,1,128]{2,0,1:T(8,128)} copy(f32[4352,1,128]{0,2,1:T(8,128)} %convolution_bitcast_fusion) | data formatting | bytes 4456448 | tf_op jit(solution)/shard_map/grqk,qgrd->kgd/transpose | solution.py:59
  126.1 2.0 copy.44
  128.1 8.1 %fusion.1 = bf16[1,2,256,4352]{2,3,1,0:T(8,128)(2,1)S(1)} fusion(f32[4352,256,2]{1,0,2:T(8,128)} %get-tuple-element.21, f32[4352,256,2]{1,0,2:T(8,128)} %get-tuple-element.19, f32[2,256]{1,0:T(2,128)S(1)} %get-tuple-element.20, f32[2,256]{1,0:T(2,128)S(1)} %get-tuple-element.18, pred[256,4352]{0,1:T(8,128)(4,1)S(1)} %fusion.11), kind=kLoop, calls=%fused_computation.2 | loop fusion | flops 22282240 | bytes 23400448 | tf_op jit(solution)/shard_map/convert_element_type | solution.py:68
  136.3 1.6 convolution_bitcast_fusion.1
  138.5 2.2 collective-permute-start.17
  140.7 4.0 %collective-permute-done.17 = f32[8,256,256]{1,2,0:T(8,128)S(1)} collective-permute-done((f32[8,256,256]{1,2,0:T(8,128)S(1)}, f32[8,256,256]{1,2,0:T(8,128)S(1)}, u32[]{:S(2)}, u32[]{:S(2)}) %collective-permute-start.17) | collective-permute-done | bytes 2097184 | tf_op jit(solution)/shard_map/ppermute | solution.py:150
  145.1 2.3 collective-permute-start.18
  147.5 9.5 %collective-permute-done.18 = f32[256,256]{0,1:T(8,128)S(1)} collective-permute-done((f32[256,256]{0,1:T(8,128)S(1)}, f32[256,256]{0,1:T(8,128)S(1)}, u32[]{:S(2)}, u32[]{:S(2)}) %collective-permute-start.18) | collective-permute-done | bytes 262176 | tf_op jit(solution)/shard_map/ppermute | solution.py:17
  157.0 1.9 collective-permute-start.19
  158.9 9.0 %collective-permute-done.19 = f32[256,256]{0,1:T(8,128)S(1)} collective-permute-done((f32[256,256]{0,1:T(8,128)S(1)}, f32[256,256]{0,1:T(8,128)S(1)}, u32[]{:S(2)}, u32[]{:S(2)}) %collective-permute-start.19) | collective-permute-done | bytes 262176 | tf_op jit(solution)/shard_map/ppermute | solution.py:17
  167.9 1.9 collective-permute-start.20
  169.8 8.1 %collective-permute-done.20 = f32[256,256]{0,1:T(8,128)S(1)} collective-permute-done((f32[256,256]{0,1:T(8,128)S(1)}, f32[256,256]{0,1:T(8,128)S(1)}, u32[]{:S(2)}, u32[]{:S(2)}) %collective-permute-start.20) | collective-permute-done | bytes 262176 | tf_op jit(solution)/shard_map/ppermute | solution.py:17
  178.0 1.9 collective-permute-start.21
  179.9 7.5 %collective-permute-done.21 = f32[256,256]{0,1:T(8,128)S(1)} collective-permute-done((f32[256,256]{0,1:T(8,128)S(1)}, f32[256,256]{0,1:T(8,128)S(1)}, u32[]{:S(2)}, u32[]{:S(2)}) %collective-permute-start.21) | collective-permute-done | bytes 262176 | tf_op jit(solution)/shard_map/ppermute | solution.py:17
  187.5 1.9 collective-permute-start.22
  189.4 7.5 %collective-permute-done.22 = f32[256,256]{0,1:T(8,128)S(1)} collective-permute-done((f32[256,256]{0,1:T(8,128)S(1)}, f32[256,256]{0,1:T(8,128)S(1)}, u32[]{:S(2)}, u32[]{:S(2)}) %collective-permute-start.22) | collective-permute-done | bytes 262176 | tf_op jit(solution)/shard_map/ppermute | solution.py:17
  197.0 1.9 collective-permute-start.23
  198.9 7.5 %collective-permute-done.23 = f32[256,256]{0,1:T(8,128)S(1)} collective-permute-done((f32[256,256]{0,1:T(8,128)S(1)}, f32[256,256]{0,1:T(8,128)S(1)}, u32[]{:S(2)}, u32[]{:S(2)}) %collective-permute-start.23) | collective-permute-done | bytes 262176 | tf_op jit(solution)/shard_map/ppermute | solution.py:17
  206.5 1.9 collective-permute-start.24
  208.5 2.4 collective-permute-start.28
  210.9 6.1 %collective-permute-done.24 = f32[256,256]{0,1:T(8,128)S(1)} collective-permute-done((f32[256,256]{0,1:T(8,128)S(1)}, f32[256,256]{0,1:T(8,128)S(1)}, u32[]{:S(2)}, u32[]{:S(2)}) %collective-permute-start.24) | collective-permute-done | bytes 262176 | tf_op jit(solution)/shard_map/ppermute | solution.py:17
  217.0 1.9 collective-permute-start.25
  219.0 2.1 fusion.18
  221.8 2.5 collective-permute-start.16
  224.2 2.4 collective-permute-done.25
  226.6 1.0 fusion.23
  227.6 2.5 %collective-permute-start.26 = (bf16[256,128]{0,1:T(8,128)(2,1)S(1)}, bf16[256,128]{0,1:T(8,128)(2,1)S(1)}, u32[]{:S(2)}, u32[]{:S(2)}) collective-permute-start(bf16[256,128]{0,1:T(8,128)(2,1)S(1)} %get-tuple-element.17), channel_id=1, source_target_pairs={{192,0},{384,192},{576,384},{193,1},{385,193},{577,385},{194,2},{3... | collective-permute-start | bytes 196616 | tf_op jit(solution)/shard_map/ppermute | solution.py:17
  230.1 1.9 collective-permute-start.27
  232.0 1.7 collective-permute-done.26
  234.5 1.7 collective-permute-done.27
  (81 shorter events, 8.3 us)
Async XLA Ops:
  7.2 99.6 %all-gather.3.cloned.1.call-start = ((), (), s32[]{:S(2)}) async-start(), calls=%async_computation | async-start | bytes 2457600 | tf_op jit(solution)/shard_map/all_gather | solution.py:96
  7.2 35.8 %collective-permute-start.9 = (bf16[256,576]{0,1:T(8,128)(2,1)}, bf16[256,576]{0,1:T(8,128)(2,1)S(1)}, u32[]{:S(2)}, u32[]{:S(2)}) collective-permute-start(bf16[256,576]{0,1:T(8,128)(2,1)} %bitcast.184), channel_id=1, source_target_pairs={{0,7},{1,0},{2,1},{3,2},{4,3},{5,4},{6,5},{7,6},{8,15},{9,8},{10,9... | collective-permute-start | bytes 884744 | tf_op jit(solution)/shard_map/ppermute | solution.py:22
  9.6 35.4 %collective-permute-start.12 = (bf16[256,576]{0,1:T(8,128)(2,1)}, bf16[256,576]{0,1:T(8,128)(2,1)S(1)}, u32[]{:S(2)}, u32[]{:S(2)}) collective-permute-start(bf16[256,576]{0,1:T(8,128)(2,1)} %bitcast.185), channel_id=1, source_target_pairs={{0,1},{1,2},{2,3},{3,4},{4,5},{5,6},{6,7},{7,0},{8,9},{9,10},{10,1... | collective-permute-start | bytes 884744 | tf_op jit(solution)/shard_map/ppermute | solution.py:22
  15.2 78.7 %copy-start.2 = (bf16[1,256,576]{1,2,0:T(8,128)(2,1)S(1)}, bf16[1,256,576]{1,2,0:T(8,128)(2,1)}, u32[]{:S(2)}) copy-start(bf16[1,256,576]{1,2,0:T(8,128)(2,1)} %param.7) | copy-start | bytes 884740
  15.2 15.5 %collective-permute-start = (bf16[256,256]{1,0:T(8,128)(2,1)S(1)}, bf16[256,256]{1,0:T(8,128)(2,1)S(1)}, u32[]{:S(2)}, u32[]{:S(2)}) collective-permute-start(bf16[256,256]{1,0:T(8,128)(2,1)S(1)} %pad_maximum_fusion.1), channel_id=1, source_target_pairs={{0,16},{8,24},{16,32},{24,40},{32,48},{40,56},{48,64},{56,72},{64,... | collective-permute-start | bytes 393224 | tf_op jit(solution)/shard_map/ppermute | solution.py:17
  30.7 6.9 %collective-permute-start.1 = (bf16[256,256]{1,0:T(8,128)(2,1)S(1)}, bf16[256,256]{1,0:T(8,128)(2,1)S(1)}, u32[]{:S(2)}, u32[]{:S(2)}) collective-permute-start(bf16[256,256]{1,0:T(8,128)(2,1)S(1)} %collective-permute-done), channel_id=1, source_target_pairs={{0,16},{8,24},{16,32},{24,40},{32,48},{40,56},{48,64},{56,72},{64,... | collective-permute-start | bytes 393224 | tf_op jit(solution)/shard_map/ppermute | solution.py:17
  37.5 12.6 %collective-permute-start.2 = (bf16[256,256]{1,0:T(8,128)(2,1)S(1)}, bf16[256,256]{1,0:T(8,128)(2,1)S(1)}, u32[]{:S(2)}, u32[]{:S(2)}) collective-permute-start(bf16[256,256]{1,0:T(8,128)(2,1)S(1)} %collective-permute-done.1), channel_id=1, source_target_pairs={{0,16},{8,24},{16,32},{24,40},{32,48},{40,56},{48,64},{56,72},{64,... | collective-permute-start | bytes 393224 | tf_op jit(solution)/shard_map/ppermute | solution.py:17
  43.1 19.2 %collective-permute-start.10 = (bf16[256,576]{0,1:T(8,128)(2,1)S(1)}, bf16[256,576]{0,1:T(8,128)(2,1)S(1)}, u32[]{:S(2)}, u32[]{:S(2)}) collective-permute-start(bf16[256,576]{0,1:T(8,128)(2,1)S(1)} %collective-permute-done.9), channel_id=1, source_target_pairs={{0,7},{1,0},{2,1},{3,2},{4,3},{5,4},{6,5},{7,6},{8,15},{9,8},{10,9... | collective-permute-start | bytes 884744 | tf_op jit(solution)/shard_map/ppermute | solution.py:22
  45.0 19.2 %collective-permute-start.13 = (bf16[256,576]{0,1:T(8,128)(2,1)S(1)}, bf16[256,576]{0,1:T(8,128)(2,1)S(1)}, u32[]{:S(2)}, u32[]{:S(2)}) collective-permute-start(bf16[256,576]{0,1:T(8,128)(2,1)S(1)} %collective-permute-done.12), channel_id=1, source_target_pairs={{0,1},{1,2},{2,3},{3,4},{4,5},{5,6},{6,7},{7,0},{8,9},{9,10},{10,1... | collective-permute-start | bytes 884744 | tf_op jit(solution)/shard_map/ppermute | solution.py:22
  50.2 7.6 %collective-permute-start.3 = (bf16[256,256]{1,0:T(8,128)(2,1)S(1)}, bf16[256,256]{1,0:T(8,128)(2,1)S(1)}, u32[]{:S(2)}, u32[]{:S(2)}) collective-permute-start(bf16[256,256]{1,0:T(8,128)(2,1)S(1)} %collective-permute-done.2), channel_id=1, source_target_pairs={{0,16},{8,24},{16,32},{24,40},{32,48},{40,56},{48,64},{56,72},{64,... | collective-permute-start | bytes 393224 | tf_op jit(solution)/shard_map/ppermute | solution.py:17
  57.8 11.6 %collective-permute-start.4 = (bf16[256,256]{1,0:T(8,128)(2,1)S(1)}, bf16[256,256]{1,0:T(8,128)(2,1)S(1)}, u32[]{:S(2)}, u32[]{:S(2)}) collective-permute-start(bf16[256,256]{1,0:T(8,128)(2,1)S(1)} %collective-permute-done.3), channel_id=1, source_target_pairs={{0,16},{8,24},{16,32},{24,40},{32,48},{40,56},{48,64},{56,72},{64,... | collective-permute-start | bytes 393224 | tf_op jit(solution)/shard_map/ppermute | solution.py:17
  62.3 20.2 %collective-permute-start.11 = (bf16[256,576]{0,1:T(8,128)(2,1)S(1)}, bf16[256,576]{0,1:T(8,128)(2,1)S(1)}, u32[]{:S(2)}, u32[]{:S(2)}) collective-permute-start(bf16[256,576]{0,1:T(8,128)(2,1)S(1)} %collective-permute-done.10), channel_id=1, source_target_pairs={{0,7},{1,0},{2,1},{3,2},{4,3},{5,4},{6,5},{7,6},{8,15},{9,8},{10,9... | collective-permute-start | bytes 884744 | tf_op jit(solution)/shard_map/ppermute | solution.py:22
  64.2 16.4 %collective-permute-start.14 = (bf16[256,576]{0,1:T(8,128)(2,1)S(1)}, bf16[256,576]{0,1:T(8,128)(2,1)S(1)}, u32[]{:S(2)}, u32[]{:S(2)}) collective-permute-start(bf16[256,576]{0,1:T(8,128)(2,1)S(1)} %collective-permute-done.13), channel_id=1, source_target_pairs={{0,1},{1,2},{2,3},{3,4},{4,5},{5,6},{6,7},{7,0},{8,9},{9,10},{10,1... | collective-permute-start | bytes 884744 | tf_op jit(solution)/shard_map/ppermute | solution.py:22
  69.4 7.5 %collective-permute-start.5 = (bf16[256,256]{1,0:T(8,128)(2,1)S(1)}, bf16[256,256]{1,0:T(8,128)(2,1)S(1)}, u32[]{:S(2)}, u32[]{:S(2)}) collective-permute-start(bf16[256,256]{1,0:T(8,128)(2,1)S(1)} %collective-permute-done.4), channel_id=1, source_target_pairs={{0,16},{8,24},{16,32},{24,40},{32,48},{40,56},{48,64},{56,72},{64,... | collective-permute-start | bytes 393224 | tf_op jit(solution)/shard_map/ppermute | solution.py:17
  76.9 7.8 %collective-permute-start.6 = (bf16[256,256]{1,0:T(8,128)(2,1)S(1)}, bf16[256,256]{1,0:T(8,128)(2,1)S(1)}, u32[]{:S(2)}, u32[]{:S(2)}) collective-permute-start(bf16[256,256]{1,0:T(8,128)(2,1)S(1)} %collective-permute-done.5), channel_id=1, source_target_pairs={{0,16},{8,24},{16,32},{24,40},{32,48},{40,56},{48,64},{56,72},{64,... | collective-permute-start | bytes 393224 | tf_op jit(solution)/shard_map/ppermute | solution.py:17
  80.6 13.1 %collective-permute-start.15 = (bf16[256,576]{0,1:T(8,128)(2,1)S(1)}, bf16[256,576]{0,1:T(8,128)(2,1)S(1)}, u32[]{:S(2)}, u32[]{:S(2)}) collective-permute-start(bf16[256,576]{0,1:T(8,128)(2,1)S(1)} %collective-permute-done.14), channel_id=1, source_target_pairs={{0,1},{1,2},{2,3},{3,4},{4,5},{5,6},{6,7},{7,0},{8,9},{9,10},{10,1... | collective-permute-start | bytes 884744 | tf_op jit(solution)/shard_map/ppermute | solution.py:22
  84.7 6.8 %collective-permute-start.7 = (bf16[256,256]{1,0:T(8,128)(2,1)S(1)}, bf16[256,256]{1,0:T(8,128)(2,1)S(1)}, u32[]{:S(2)}, u32[]{:S(2)}) collective-permute-start(bf16[256,256]{1,0:T(8,128)(2,1)S(1)} %collective-permute-done.6), channel_id=1, source_target_pairs={{0,16},{8,24},{16,32},{24,40},{32,48},{40,56},{48,64},{56,72},{64,... | collective-permute-start | bytes 393224 | tf_op jit(solution)/shard_map/ppermute | solution.py:17
  91.6 4.2 %copy-start.1 = (bf16[9,256,256]{2,1,0:T(8,128)(2,1)}, bf16[9,256,256]{2,1,0:T(8,128)(2,1)S(1)}, u32[]{:S(2)}) copy-start(bf16[9,256,256]{2,1,0:T(8,128)(2,1)S(1)} %bitcast_dynamic-update-slice_fusion.14) | copy-start | bytes 3538948
  91.6 4.7 %collective-permute-start.8 = (bf16[9,256,256]{2,1,0:T(8,128)(2,1)S(1)}, bf16[9,256,256]{2,1,0:T(8,128)(2,1)S(1)}, u32[]{:S(2)}, u32[]{:S(2)}) collective-permute-start(bf16[9,256,256]{2,1,0:T(8,128)(2,1)S(1)} %bitcast_dynamic-update-slice_fusion.14), channel_id=1, source_target_pairs={{0,8},{8,0},{16,24},{24,16},{32,40},{40,32},{48,56},{56,48},{64,72... | collective-permute-start | bytes 3538952 | tf_op jit(solution)/shard_map/ppermute | solution.py:118
  100.0 1.9 copy-start.4
  101.8 16.3 %copy-start = (bf16[9,2,256,256]{3,2,1,0:T(8,128)(2,1)}, bf16[9,2,256,256]{3,2,1,0:T(8,128)(2,1)S(1)}, u32[]{:S(2)}) copy-start(bf16[9,2,256,256]{3,2,1,0:T(8,128)(2,1)S(1)} %copy.35) | copy-start | bytes 7077892
  106.8 11.3 %slice-start = ((s8[8912896]{0:T(1024)(128)(4,1)}), s8[4194304]{0:T(1024)(128)(4,1)S(1)}, s32[]{:S(2)}) async-start(s8[8912896]{0:T(1024)(128)(4,1)} %bitcast.174), calls=%async_computation.1 | async-start | bytes 8388608
  110.4 7.7 %slice-start.1 = ((s8[8912896]{0:T(1024)(128)(4,1)}), s8[4194304]{0:T(1024)(128)(4,1)S(1)}, s32[]{:S(2)}) async-start(s8[8912896]{0:T(1024)(128)(4,1)} %bitcast.174), calls=%async_computation.2 | async-start | bytes 8388608
  110.4 7.7 %slice-start.2 = ((s8[8912896]{0:T(1024)(128)(4,1)}), s8[524288]{0:T(1024)(128)(4,1)S(1)}, s32[]{:S(2)}) async-start(s8[8912896]{0:T(1024)(128)(4,1)} %bitcast.174), calls=%async_computation.3 | async-start | bytes 1048576
  128.1 8.1 %copy-start.5 = (bf16[256,2,128]{2,1,0:T(2,128)(2,1)S(1)}, bf16[256,2,128]{2,1,0:T(2,128)(2,1)}, u32[]{:S(2)}) copy-start(bf16[256,2,128]{2,1,0:T(2,128)(2,1)} %reshape.212) | copy-start | bytes 393220
  138.5 69.9 %copy-start.3 = (bf16[1,256,576]{1,2,0:T(8,128)(2,1)S(1)}, bf16[1,256,576]{1,2,0:T(8,128)(2,1)}, u32[]{:S(2)}) copy-start(bf16[1,256,576]{1,2,0:T(8,128)(2,1)} %param.7) | copy-start | bytes 884740
  138.5 6.2 %collective-permute-start.17 = (f32[8,256,256]{1,2,0:T(8,128)S(1)}, f32[8,256,256]{1,2,0:T(8,128)S(1)}, u32[]{:S(2)}, u32[]{:S(2)}) collective-permute-start(f32[8,256,256]{1,2,0:T(8,128)S(1)} %slice.50), channel_id=1, source_target_pairs={{0,8},{8,0},{16,24},{24,16},{32,40},{40,32},{48,56},{56,48},{64,72... | collective-permute-start | bytes 6291464 | tf_op jit(solution)/shard_map/ppermute | solution.py:150
  145.1 11.8 %collective-permute-start.18 = (f32[256,256]{0,1:T(8,128)S(1)}, f32[256,256]{0,1:T(8,128)S(1)}, u32[]{:S(2)}, u32[]{:S(2)}) collective-permute-start(f32[256,256]{0,1:T(8,128)S(1)} %slice_bitcast_fusion.8), channel_id=1, source_target_pairs={{16,0},{24,8},{32,16},{40,24},{48,32},{56,40},{64,48},{72,56},{80,... | collective-permute-start | bytes 786440 | tf_op jit(solution)/shard_map/ppermute | solution.py:17
  157.0 10.9 %collective-permute-start.19 = (f32[256,256]{0,1:T(8,128)S(1)}, f32[256,256]{0,1:T(8,128)S(1)}, u32[]{:S(2)}, u32[]{:S(2)}) collective-permute-start(f32[256,256]{0,1:T(8,128)S(1)} %fusion.30), channel_id=1, source_target_pairs={{16,0},{24,8},{32,16},{40,24},{48,32},{56,40},{64,48},{72,56},{80,... | collective-permute-start | bytes 786440 | tf_op jit(solution)/shard_map/ppermute | solution.py:17
  167.9 10.0 %collective-permute-start.20 = (f32[256,256]{0,1:T(8,128)S(1)}, f32[256,256]{0,1:T(8,128)S(1)}, u32[]{:S(2)}, u32[]{:S(2)}) collective-permute-start(f32[256,256]{0,1:T(8,128)S(1)} %fusion.29), channel_id=1, source_target_pairs={{16,0},{24,8},{32,16},{40,24},{48,32},{56,40},{64,48},{72,56},{80,... | collective-permute-start | bytes 786440 | tf_op jit(solution)/shard_map/ppermute | solution.py:17
  178.0 9.5 %collective-permute-start.21 = (f32[256,256]{0,1:T(8,128)S(1)}, f32[256,256]{0,1:T(8,128)S(1)}, u32[]{:S(2)}, u32[]{:S(2)}) collective-permute-start(f32[256,256]{0,1:T(8,128)S(1)} %fusion.28), channel_id=1, source_target_pairs={{16,0},{24,8},{32,16},{40,24},{48,32},{56,40},{64,48},{72,56},{80,... | collective-permute-start | bytes 786440 | tf_op jit(solution)/shard_map/ppermute | solution.py:17
  187.5 9.5 %collective-permute-start.22 = (f32[256,256]{0,1:T(8,128)S(1)}, f32[256,256]{0,1:T(8,128)S(1)}, u32[]{:S(2)}, u32[]{:S(2)}) collective-permute-start(f32[256,256]{0,1:T(8,128)S(1)} %fusion.27), channel_id=1, source_target_pairs={{16,0},{24,8},{32,16},{40,24},{48,32},{56,40},{64,48},{72,56},{80,... | collective-permute-start | bytes 786440 | tf_op jit(solution)/shard_map/ppermute | solution.py:17
  197.0 9.5 %collective-permute-start.23 = (f32[256,256]{0,1:T(8,128)S(1)}, f32[256,256]{0,1:T(8,128)S(1)}, u32[]{:S(2)}, u32[]{:S(2)}) collective-permute-start(f32[256,256]{0,1:T(8,128)S(1)} %fusion.26), channel_id=1, source_target_pairs={{16,0},{24,8},{32,16},{40,24},{48,32},{56,40},{64,48},{72,56},{80,... | collective-permute-start | bytes 786440 | tf_op jit(solution)/shard_map/ppermute | solution.py:17
  206.5 10.5 %collective-permute-start.24 = (f32[256,256]{0,1:T(8,128)S(1)}, f32[256,256]{0,1:T(8,128)S(1)}, u32[]{:S(2)}, u32[]{:S(2)}) collective-permute-start(f32[256,256]{0,1:T(8,128)S(1)} %fusion.25), channel_id=1, source_target_pairs={{16,0},{24,8},{32,16},{40,24},{48,32},{56,40},{64,48},{72,56},{80,... | collective-permute-start | bytes 786440 | tf_op jit(solution)/shard_map/ppermute | solution.py:17
  208.5 23.6 %collective-permute-start.28 = (bf16[256,576]{0,1:T(8,128)(2,1)S(1)}, bf16[256,576]{0,1:T(8,128)(2,1)S(1)}, u32[]{:S(2)}, u32[]{:S(2)}) collective-permute-start(bf16[256,576]{0,1:T(8,128)(2,1)S(1)} %bitcast.186), channel_id=1, source_target_pairs={{192,0},{384,192},{576,384},{193,1},{385,193},{577,385},{194,2},{3... | collective-permute-start | bytes 884744 | tf_op jit(solution)/shard_map/ppermute | solution.py:17
  217.0 9.6 %collective-permute-start.25 = (f32[256,256]{0,1:T(8,128)S(1)}, f32[256,256]{0,1:T(8,128)}, u32[]{:S(2)}, u32[]{:S(2)}) collective-permute-start(f32[256,256]{0,1:T(8,128)S(1)} %fusion.24), channel_id=1, source_target_pairs={{16,0},{24,8},{32,16},{40,24},{48,32},{56,40},{64,48},{72,56},{80,... | collective-permute-start | bytes 786440 | tf_op jit(solution)/shard_map/ppermute | solution.py:17
  221.8 10.2 %collective-permute-start.16 = (bf16[256,256]{1,0:T(8,128)(2,1)}, bf16[256,256]{1,0:T(8,128)(2,1)S(1)}, u32[]{:S(2)}, u32[]{:S(2)}) collective-permute-start(bf16[256,256]{1,0:T(8,128)(2,1)} %copy.40), channel_id=1, source_target_pairs={{192,0},{384,192},{576,384},{193,1},{385,193},{577,385},{194,2},{3... | collective-permute-start | bytes 393224 | tf_op jit(solution)/shard_map/ppermute | solution.py:17
  227.6 6.2 %collective-permute-start.26 = (bf16[256,128]{0,1:T(8,128)(2,1)S(1)}, bf16[256,128]{0,1:T(8,128)(2,1)S(1)}, u32[]{:S(2)}, u32[]{:S(2)}) collective-permute-start(bf16[256,128]{0,1:T(8,128)(2,1)S(1)} %get-tuple-element.17), channel_id=1, source_target_pairs={{192,0},{384,192},{576,384},{193,1},{385,193},{577,385},{194,2},{3... | collective-permute-start | bytes 196616 | tf_op jit(solution)/shard_map/ppermute | solution.py:17
  230.1 6.2 %collective-permute-start.27 = (bf16[256,128]{0,1:T(8,128)(2,1)S(1)}, bf16[256,128]{0,1:T(8,128)(2,1)S(1)}, u32[]{:S(2)}, u32[]{:S(2)}) collective-permute-start(bf16[256,128]{0,1:T(8,128)(2,1)S(1)} %get-tuple-element.16), channel_id=1, source_target_pairs={{192,0},{384,192},{576,384},{193,1},{385,193},{577,385},{194,2},{3... | collective-permute-start | bytes 196616 | tf_op jit(solution)/shard_map/ppermute | solution.py:17
Sparse Core Ops, SparseCore 0:
  21.0 59.1 all-gather.2

commit v6 on v5

--- a/solution.py
+++ b/solution.py
@@ -97,9 +97,14 @@
         (((1,), (1,)), ((), ())),
         preferred_element_type=jnp.float32,
     ).astype(jnp.bfloat16)
-    reach_rows = min(lax.axis_size("row") - 1, WINDOW // tok_rows)
-    span_rows = (reach_rows + 1) * tok_rows
+    row_count = lax.axis_size("row")
+    pipe_count = lax.axis_size("pipe")
+    reach_rows = min(row_count - 1, WINDOW // tok_rows)
+    hops = reach_rows // 2
     row_index = lax.axis_index("row")
+    core_bit = row_index % 2
+    partner_index = row_index + 1 - 2 * core_bit
+    swap_pairs = [(i, i ^ 1) for i in range(row_count)]
     query_start = row_index * tok_rows
     doc_list = doc_ids[0]
     shared_flags = doc_shared[0]
@@ -108,32 +113,22 @@
     value_local = value_act[0]
     key_width = key_local.shape[1]
     pair_local = jnp.concatenate([key_local, value_local], axis=1)
-    core_bit = row_index % 2
     moving = pair_local
-    same_core = []
-    for _ in range(reach_rows // 2):
+    same_blocks = [pair_local]
+    for _ in range(hops):
         moving = from_behind(moving, "row", 2)
-        same_core.append(moving)
-    same_core = jnp.stack([pair_local] + same_core, axis=0)
-    other_core = lax.ppermute(
-        same_core, "row", [(i, i ^ 1) for i in range(lax.axis_size("row"))]
-    )
-    pairs = jnp.where(
-        core_bit == 0,
-        jnp.stack([same_core, other_core], axis=1),
-        jnp.stack([other_core, same_core], axis=1),
-    )
-    pair_near = lax.dynamic_slice_in_dim(
-        pairs[::-1].reshape(-1, pair_local.shape[1]), core_bit * tok_rows, span_rows, 0
-    )
-    key_near = pair_near[:, :key_width]
-    value_near = pair_near[:, key_width:]
-    key_start = query_start - reach_rows * tok_rows
-    key_pos = key_start + jnp.arange(span_rows, dtype=jnp.int32)
+        same_blocks.append(moving)
+    same_stack = jnp.stack(same_blocks, axis=0)
+    other_stack = lax.ppermute(same_stack, "row", swap_pairs)
+    pair_near = jnp.concatenate([same_stack, other_stack], axis=0).reshape(-1, 2 * key_width)
+    back_steps = 2 * jnp.arange(hops + 1, dtype=jnp.int32)
+    block_ids = jnp.concatenate([row_index - back_steps, partner_index - back_steps])
+    key_pos = (block_ids[:, None] * tok_rows + jnp.arange(tok_rows, dtype=jnp.int32)[None, :]).reshape(-1)
     query_pos = query_start + jnp.arange(tok_rows, dtype=jnp.int32)
     query_doc = lax.dynamic_slice_in_dim(doc_list, query_start, tok_rows)
-    padded_docs = jnp.concatenate([jnp.full((reach_rows * tok_rows,), -1, jnp.int32), doc_list])
-    key_doc = lax.dynamic_slice_in_dim(padded_docs, query_start, span_rows)
+    lead = reach_rows * tok_rows
+    padded_docs = jnp.concatenate([jnp.full((lead,), -1, jnp.int32), doc_list])
+    key_doc = jnp.take(padded_docs, jnp.clip(key_pos + lead, 0, padded_docs.shape[0] - 1))
     key_shared = shared_lookup(key_doc, shared_flags)
     allowed = (
         (key_pos[None, :] >= 0)
@@ -141,30 +136,26 @@
         & (query_pos[:, None] - key_pos[None, :] < WINDOW)
     )
     allowed = allowed & ((key_doc[None, :] == query_doc[:, None]) | (key_shared[None, :] == 1))
-    query_grad, key_sum, value_sum = attend(query_local, key_near, value_near, d_attn, allowed)
+    query_grad, key_sum, value_sum = attend(
+        query_local, pair_near[:, :key_width], pair_near[:, key_width:], d_attn, allowed
+    )
     query_handed = from_behind(query_grad, "pipe", -1)
-    pair_sum = jnp.concatenate([key_sum, value_sum], axis=1)
-    pair_sum = pair_sum.reshape(reach_rows + 1, tok_rows, 2 * key_width)
-    even_part = pair_sum[0::2]
-    odd_part = pair_sum[1::2]
-    partner = lax.ppermute(
-        odd_part, "row", [(i, i ^ 1) for i in range(lax.axis_size("row"))]
+    pair_sum = jnp.concatenate([key_sum, value_sum], axis=1).reshape(
+        2, hops + 1, tok_rows, 2 * key_width
     )
-    zero_block = jnp.zeros_like(odd_part[:1])
-    partner_aligned = jnp.where(
-        core_bit == 0,
-        jnp.concatenate([zero_block, partner], axis=0),
-        jnp.concatenate([partner, zero_block], axis=0),
-    )
-    chip_sum = even_part + partner_aligned
-    running = chip_sum[0]
-    for step in range(1, reach_rows // 2 + 1):
-        running = from_behind(running, "row", -2) + chip_sum[step]
-    key_total = running[:, :key_width]
-    value_total = running[:, key_width:]
-    key_handed, value_handed = from_behind(
-        (key_total.astype(jnp.bfloat16), value_total.astype(jnp.bfloat16)), "pipe", -1
-    )
+    chip_sum = pair_sum[0] + lax.ppermute(pair_sum[1], "row", swap_pairs)
+    own_handed = from_behind(chip_sum[0], "pipe", -1)
+    running = chip_sum[hops]
+    for step in range(1, hops):
+        running = from_behind(running, "row", -2) + chip_sum[hops - step]
+    last_pairs = [
+        (p * row_count + r, (p - 1) * row_count + r - 2)
+        for p in range(1, pipe_count)
+        for r in range(2, row_count)
+    ]
+    total = lax.ppermute(running, ("pipe", "row"), last_pairs) + own_handed
+    key_handed = total[:, :key_width].astype(jnp.bfloat16)
+    value_handed = total[:, key_width:].astype(jnp.bfloat16)
     return (query_handed[None], key_handed[None], value_handed[None], grad_handed[None])
 
 

time: 247 us -> 256 us (1.036)
  the two profiles are of different devices: /device:TPU:218 before, /device:TPU:196 now
where the time goes in v6:
time: 256 us; the launch traced here: 255 us
  starting transfers between devices  82.2 us (32%)
  waiting for transfers between devices  77.1 us (30%)
  local copies, waits for them, and re-layouts  42.2 us (16%)
  matrix products  22.9 us (9%)
  other arithmetic  15.3 us (6%)
  between operations  14.8 us (6%)
    ppermute x18, waiting for transfers between devices, from_behind(): return lax.ppermute(block, axis, route)  72.1 us
    ppermute x18, starting transfers between devices, from_behind(): return lax.ppermute(block, axis, route)  53.1 us
    gather x1, local copies, waits for them, and re-layouts, per_device(): jnp.take(padded_docs, jnp.clip(key_pos + lead, 0, padded_docs.shape[0] - 1))  24.1 us
    ppermute x7, starting transfers between devices, cyclic_shift(): lax.ppermute(block, axis, [(i, (i + distance) % size) for i in range(size)])  23 us
    unnamed x53, local copies, waits for them, and re-layouts  9.05 us
    dot_general x1, matrix products, attend(): jnp.einsum('qgrd,kgd->grqk', query_g, key_g, preferred_element_type=jnp.f...  6.56 us
    dot_general x1, matrix products, attend(): jnp.einsum('qgrd,kgd->grqk', attn_g, value_g, preferred_element_type=jnp....  6.28 us
  transfers between devices with their start and end apart: 29, of which 15 were waited for; matrix products, arithmetic and copies ran while one was open for 20% of the time, Pallas kernels for 0%

profile of v6, /device:TPU:196, one launch (start us, length us, event | category | flops | bytes accessed | tf_op | source)
XLA Modules:
  0.0 254.6 jit_solution(3940521166936008801)
XLA Ops:
  7.2 5.4 %collective-permute-start.9 = (bf16[256,576]{0,1:T(8,128)(2,1)}, bf16[256,576]{0,1:T(8,128)(2,1)S(1)}, u32[]{:S(2)}, u32[]{:S(2)}) collective-permute-start(bf16[256,576]{0,1:T(8,128)(2,1)} %bitcast.194), channel_id=1, source_target_pairs={{0,7},{1,0},{2,1},{3,2},{4,3},{5,4},{6,5},{7,6},{8,15},{9,8},{10,9... | collective-permute-start | bytes 884744 | tf_op jit(solution)/shard_map/ppermute | solution.py:22
  12.6 1.9 collective-permute-start.12
  14.5 0.9 pad_maximum_fusion.1
  15.4 5.5 %collective-permute-start = (bf16[256,256]{1,0:T(8,128)(2,1)S(1)}, bf16[256,256]{1,0:T(8,128)(2,1)S(1)}, u32[]{:S(2)}, u32[]{:S(2)}) collective-permute-start(bf16[256,256]{1,0:T(8,128)(2,1)S(1)} %pad_maximum_fusion.1), channel_id=1, source_target_pairs={{0,16},{8,24},{16,32},{24,40},{32,48},{40,56},{48,64},{56,72},{64,... | collective-permute-start | bytes 393224 | tf_op jit(solution)/shard_map/ppermute | solution.py:17
  22.0 0.7 concatenate.28
  22.8 24.1 %gather_fusion = s32[4608]{0:T(1024)S(1)} fusion(s32[10240]{0:T(1024)S(1)} %concatenate.28, s32[5120]{0:T(1024)S(1)} %pad_clamp_fusion), kind=kCustom, calls=%fused_computation | custom fusion | bytes 55296 | tf_op jit(solution)/shard_map/jit(_take)/gather | solution.py:131
  47.0 4.6 %fusion.10 = pred[256,4608]{0,1:T(8,128)(4,1)S(1)} fusion(s32[256]{0:T(256)S(1)} %bitcast.207, s32[256]{0:T(256)S(1)} %iota_add_fusion.1, s32[4608]{0:T(1024)S(1)} %and_select_fusion, s32[4608]{0:T(1024)S(1)} %add.160, pred[4608]{0:T(1024)(128)(4,1)S(1)} %broadcast_compare_fusion, pred[4608]{0:T(1024)(128)(4,1)S(1)} %broadcast_compare_fusion.1), kind=kLoop, calls=%fused_computation.21 | loop fusion | flops 9437184 | bytes 1227776 | tf_op jit(solution)/shard_map/and | solution.py:138
  52.4 0.8 copy.47
  53.2 4.3 %collective-permute-start.1 = (bf16[256,256]{1,0:T(8,128)(2,1)S(1)}, bf16[256,256]{1,0:T(8,128)(2,1)S(1)}, u32[]{:S(2)}, u32[]{:S(2)}) collective-permute-start(bf16[256,256]{1,0:T(8,128)(2,1)S(1)} %collective-permute-done), channel_id=1, source_target_pairs={{0,16},{8,24},{16,32},{24,40},{32,48},{40,56},{48,64},{56,72},{64,... | collective-permute-start | bytes 393224 | tf_op jit(solution)/shard_map/ppermute | solution.py:17
  57.5 0.7 bitcast_dynamic-update-slice_fusion.29
  58.2 2.8 %collective-permute-done.1 = bf16[256,256]{1,0:T(8,128)(2,1)S(1)} collective-permute-done((bf16[256,256]{1,0:T(8,128)(2,1)S(1)}, bf16[256,256]{1,0:T(8,128)(2,1)S(1)}, u32[]{:S(2)}, u32[]{:S(2)}) %collective-permute-start.1) | collective-permute-done | bytes 131104 | tf_op jit(solution)/shard_map/ppermute | solution.py:17
  61.0 5.6 %collective-permute-start.2 = (bf16[256,256]{1,0:T(8,128)(2,1)S(1)}, bf16[256,256]{1,0:T(8,128)(2,1)S(1)}, u32[]{:S(2)}, u32[]{:S(2)}) collective-permute-start(bf16[256,256]{1,0:T(8,128)(2,1)S(1)} %collective-permute-done.1), channel_id=1, source_target_pairs={{0,16},{8,24},{16,32},{24,40},{32,48},{40,56},{48,64},{56,72},{64,... | collective-permute-start | bytes 393224 | tf_op jit(solution)/shard_map/ppermute | solution.py:17
  67.4 4.8 %collective-permute-start.10 = (bf16[256,576]{0,1:T(8,128)(2,1)S(1)}, bf16[256,576]{0,1:T(8,128)(2,1)S(1)}, u32[]{:S(2)}, u32[]{:S(2)}) collective-permute-start(bf16[256,576]{0,1:T(8,128)(2,1)S(1)} %collective-permute-done.9), channel_id=1, source_target_pairs={{0,7},{1,0},{2,1},{3,2},{4,3},{5,4},{6,5},{7,6},{8,15},{9,8},{10,9... | collective-permute-start | bytes 884744 | tf_op jit(solution)/shard_map/ppermute | solution.py:22
  72.2 1.9 collective-permute-start.13
  74.1 3.1 %collective-permute-start.3 = (bf16[256,256]{1,0:T(8,128)(2,1)S(1)}, bf16[256,256]{1,0:T(8,128)(2,1)S(1)}, u32[]{:S(2)}, u32[]{:S(2)}) collective-permute-start(bf16[256,256]{1,0:T(8,128)(2,1)S(1)} %collective-permute-done.2), channel_id=1, source_target_pairs={{0,16},{8,24},{16,32},{24,40},{32,48},{40,56},{48,64},{56,72},{64,... | collective-permute-start | bytes 393224 | tf_op jit(solution)/shard_map/ppermute | solution.py:17
  77.3 0.7 bitcast_dynamic-update-slice_fusion.25
  78.0 3.0 %collective-permute-done.3 = bf16[256,256]{1,0:T(8,128)(2,1)S(1)} collective-permute-done((bf16[256,256]{1,0:T(8,128)(2,1)S(1)}, bf16[256,256]{1,0:T(8,128)(2,1)S(1)}, u32[]{:S(2)}, u32[]{:S(2)}) %collective-permute-start.3) | collective-permute-done | bytes 131104 | tf_op jit(solution)/shard_map/ppermute | solution.py:17
  81.0 4.3 %collective-permute-start.4 = (bf16[256,256]{1,0:T(8,128)(2,1)S(1)}, bf16[256,256]{1,0:T(8,128)(2,1)S(1)}, u32[]{:S(2)}, u32[]{:S(2)}) collective-permute-start(bf16[256,256]{1,0:T(8,128)(2,1)S(1)} %collective-permute-done.3), channel_id=1, source_target_pairs={{0,16},{8,24},{16,32},{24,40},{32,48},{40,56},{48,64},{56,72},{64,... | collective-permute-start | bytes 393224 | tf_op jit(solution)/shard_map/ppermute | solution.py:17
  86.1 5.1 %collective-permute-start.11 = (bf16[256,576]{0,1:T(8,128)(2,1)S(1)}, bf16[256,576]{0,1:T(8,128)(2,1)S(1)}, u32[]{:S(2)}, u32[]{:S(2)}) collective-permute-start(bf16[256,576]{0,1:T(8,128)(2,1)S(1)} %collective-permute-done.10), channel_id=1, source_target_pairs={{0,7},{1,0},{2,1},{3,2},{4,3},{5,4},{6,5},{7,6},{8,15},{9,8},{10,9... | collective-permute-start | bytes 884744 | tf_op jit(solution)/shard_map/ppermute | solution.py:22
  91.2 1.9 collective-permute-start.14
  93.2 2.3 collective-permute-start.5
  96.3 3.8 %collective-permute-done.5 = bf16[256,256]{1,0:T(8,128)(2,1)S(1)} collective-permute-done((bf16[256,256]{1,0:T(8,128)(2,1)S(1)}, bf16[256,256]{1,0:T(8,128)(2,1)S(1)}, u32[]{:S(2)}, u32[]{:S(2)}) %collective-permute-start.5) | collective-permute-done | bytes 131104 | tf_op jit(solution)/shard_map/ppermute | solution.py:17
  100.1 3.5 %collective-permute-start.6 = (bf16[256,256]{1,0:T(8,128)(2,1)S(1)}, bf16[256,256]{1,0:T(8,128)(2,1)S(1)}, u32[]{:S(2)}, u32[]{:S(2)}) collective-permute-start(bf16[256,256]{1,0:T(8,128)(2,1)S(1)} %collective-permute-done.5), channel_id=1, source_target_pairs={{0,16},{8,24},{16,32},{24,40},{32,48},{40,56},{48,64},{56,72},{64,... | collective-permute-start | bytes 393224 | tf_op jit(solution)/shard_map/ppermute | solution.py:17
  104.3 1.9 collective-permute-start.15
  106.3 1.8 collective-permute-done.6
  108.1 3.7 %collective-permute-start.7 = (bf16[256,256]{1,0:T(8,128)(2,1)S(1)}, bf16[256,256]{1,0:T(8,128)(2,1)S(1)}, u32[]{:S(2)}, u32[]{:S(2)}) collective-permute-start(bf16[256,256]{1,0:T(8,128)(2,1)S(1)} %collective-permute-done.6), channel_id=1, source_target_pairs={{0,16},{8,24},{16,32},{24,40},{32,48},{40,56},{48,64},{56,72},{64,... | collective-permute-start | bytes 393224 | tf_op jit(solution)/shard_map/ppermute | solution.py:17
  112.5 2.4 collective-permute-done.7
  115.0 0.7 bitcast_dynamic-update-slice_fusion.15
  115.7 2.1 collective-permute-start.8
  118.3 2.3 collective-permute-done.8
  120.6 1.1 constant_dynamic-update-slice_fusion
  121.8 6.6 %fusion.5 = (f32[2,256]{1,0:T(2,128)S(1)}, f32[4608,256,2]{1,0,2:T(8,128)}) fusion(pred[256,4608]{0,1:T(8,128)(4,1)S(1)} %fusion.10, bf16[256,2,128]{0,2,1:T(8,128)(2,1)S(1)} %bitcast.197, bf16[4608,256]{1,0:T(8,128)(2,1)} %bitcast.11), kind=kOutput, calls=%fused_computation.11 | convolution fusion | flops 613416448 | bytes 11929600 | tf_op jit(solution)/shard_map/qgrd,kgd->grqk/dot_general | solution.py:52
  128.3 2.8 %fusion.16 = bf16[256,256]{0,1:T(8,128)(2,1)S(1)} fusion(bf16[256,4608]{0,1:T(8,128)(2,1)S(1)} %bitcast.191, bf16[1,256,4608]{1,2,0:T(8,128)(2,1)} %all-gather.3.cloned.1.call-done), kind=kOutput, calls=%fused_computation.29 | convolution fusion | flops 604045312 | bytes 4849664 | tf_op jit(solution)/shard_map/dot_general | solution.py:94
  131.2 6.3 %fusion.2 = (f32[2,256]{1,0:T(2,128)S(1)}, f32[4608,256,2]{1,0,2:T(8,128)S(1)}) fusion(f32[2,256]{1,0:T(2,128)S(1)} %get-tuple-element.30, f32[4608,256,2]{1,0,2:T(8,128)} %get-tuple-element.31, pred[256,4608]{0,1:T(8,128)(4,1)S(1)} %fusion.10, bf16[256,2,128]{0,2,1:T(8,128)(2,1)S(1)} %bitcast.209, bf16[4608,256]{1,0:T(8,128)(2,1)} %bitcast.11), kind=kOutput, calls=%fused_computation.7 | convolution fusion | flops 618135040 | bytes 21368832 | tf_op jit(solution)/shard_map/qgrd,kgd->grqk/dot_general | solution.py:62
  137.5 3.5 %convolution_bitcast_fusion = f32[4608,128]{0,1:T(8,128)S(1)} fusion(bf16[256,2,128]{0,2,1:T(8,128)(2,1)S(1)} %bitcast.210, f32[4608,256,2]{1,0,2:T(8,128)S(1)} %bitcast.189, f32[2,256]{1,0:T(2,128)S(1)} %get-tuple-element.30, pred[256,4608]{0,1:T(8,128)(4,1)S(1)} %fusion.10), kind=kOutput, calls=%fused_computation.12 | convolution fusion | flops 615776256 | bytes 13109248 | tf_op jit(solution)/shard_map/grqk,qgrd->kgd/dot_general | solution.py:59
  141.0 4.6 %fusion.6 = bf16[2,256,4608]{1,2,0:T(8,128)(2,1)S(1)} fusion(f32[4608,256,2]{1,0,2:T(8,128)S(1)} %bitcast.189, f32[4608,256,2]{1,0,2:T(8,128)S(1)} %get-tuple-element.33, f32[2,256]{1,0:T(2,128)S(1)} %get-tuple-element.32, f32[2,256]{1,0:T(2,128)S(1)} %get-tuple-element.30, pred[256,4608]{0,1:T(8,128)(4,1)S(1)} %fusion.10), kind=kLoop, calls=%fused_computation.14 | loop fusion | flops 25952256 | bytes 24776704 | tf_op jit(solution)/shard_map/reshape.23
  145.7 2.2 copy-done
  147.8 1.6 convolution_bitcast_fusion.1
  149.5 1.7 pad_maximum_fusion
  151.2 2.0 copy.40
  153.2 2.0 collective-permute-start.17
  155.2 2.0 copy.39
  157.3 2.7 %collective-permute-done.17 = f32[9,256,256]{2,1,0:T(8,128)} collective-permute-done((f32[9,256,256]{2,1,0:T(8,128)}, f32[9,256,256]{2,1,0:T(8,128)}, u32[]{:S(2)}, u32[]{:S(2)}) %collective-permute-start.17) | collective-permute-done | bytes 2359328 | tf_op jit(solution)/shard_map/ppermute | solution.py:146
  159.9 2.1 add.174
  162.1 2.1 collective-permute-start.18
  164.2 9.6 %collective-permute-done.18 = f32[256,256]{1,0:T(8,128)S(1)} collective-permute-done((f32[256,256]{1,0:T(8,128)S(1)}, f32[256,256]{1,0:T(8,128)S(1)}, u32[]{:S(2)}, u32[]{:S(2)}) %collective-permute-start.18) | collective-permute-done | bytes 262176 | tf_op jit(solution)/shard_map/ppermute | solution.py:17
  173.8 1.9 collective-permute-start.19
  175.8 8.7 %collective-permute-done.19 = f32[256,256]{1,0:T(8,128)S(1)} collective-permute-done((f32[256,256]{1,0:T(8,128)S(1)}, f32[256,256]{1,0:T(8,128)S(1)}, u32[]{:S(2)}, u32[]{:S(2)}) %collective-permute-start.19) | collective-permute-done | bytes 262176 | tf_op jit(solution)/shard_map/ppermute | solution.py:17
  184.5 1.9 collective-permute-start.20
  186.5 7.9 %collective-permute-done.20 = f32[256,256]{1,0:T(8,128)S(1)} collective-permute-done((f32[256,256]{1,0:T(8,128)S(1)}, f32[256,256]{1,0:T(8,128)S(1)}, u32[]{:S(2)}, u32[]{:S(2)}) %collective-permute-start.20) | collective-permute-done | bytes 262176 | tf_op jit(solution)/shard_map/ppermute | solution.py:17
  194.4 1.9 collective-permute-start.21
  196.3 7.5 %collective-permute-done.21 = f32[256,256]{1,0:T(8,128)S(1)} collective-permute-done((f32[256,256]{1,0:T(8,128)S(1)}, f32[256,256]{1,0:T(8,128)S(1)}, u32[]{:S(2)}, u32[]{:S(2)}) %collective-permute-start.21) | collective-permute-done | bytes 262176 | tf_op jit(solution)/shard_map/ppermute | solution.py:17
  203.9 1.9 collective-permute-start.22
  205.8 7.5 %collective-permute-done.22 = f32[256,256]{1,0:T(8,128)S(1)} collective-permute-done((f32[256,256]{1,0:T(8,128)S(1)}, f32[256,256]{1,0:T(8,128)S(1)}, u32[]{:S(2)}, u32[]{:S(2)}) %collective-permute-start.22) | collective-permute-done | bytes 262176 | tf_op jit(solution)/shard_map/ppermute | solution.py:17
  213.4 1.9 collective-permute-start.23
  215.3 7.6 %collective-permute-done.23 = f32[256,256]{1,0:T(8,128)S(1)} collective-permute-done((f32[256,256]{1,0:T(8,128)S(1)}, f32[256,256]{1,0:T(8,128)S(1)}, u32[]{:S(2)}, u32[]{:S(2)}) %collective-permute-start.23) | collective-permute-done | bytes 262176 | tf_op jit(solution)/shard_map/ppermute | solution.py:17
  223.0 1.9 collective-permute-start.24
  224.9 2.3 collective-permute-start.27
  227.2 3.0 %collective-permute-start.26 = (f32[256,256]{1,0:T(8,128)S(1)}, f32[256,256]{1,0:T(8,128)S(1)}, u32[]{:S(2)}, u32[]{:S(2)}) collective-permute-start(f32[256,256]{1,0:T(8,128)S(1)} %get-tuple-element.6), channel_id=1, source_target_pairs={{192,0},{384,192},{576,384},{193,1},{385,193},{577,385},{194,2},{3... | collective-permute-start | bytes 786440 | tf_op jit(solution)/shard_map/ppermute | solution.py:17
  230.2 3.6 %collective-permute-done.24 = f32[256,256]{1,0:T(8,128)S(1)} collective-permute-done((f32[256,256]{1,0:T(8,128)S(1)}, f32[256,256]{1,0:T(8,128)S(1)}, u32[]{:S(2)}, u32[]{:S(2)}) %collective-permute-start.24) | collective-permute-done | bytes 262176 | tf_op jit(solution)/shard_map/ppermute | solution.py:17
  233.9 1.9 collective-permute-start.25
  235.9 2.1 convolution_convert_fusion
  238.1 1.9 collective-permute-start.16
  240.0 5.7 %collective-permute-done.16 = bf16[256,256]{1,0:T(8,128)(2,1)S(1)} collective-permute-done((bf16[256,256]{1,0:T(8,128)(2,1)S(1)}, bf16[256,256]{1,0:T(8,128)(2,1)S(1)}, u32[]{:S(2)}, u32[]{:S(2)}) %collective-permute-start.16) | collective-permute-done | bytes 131104 | tf_op jit(solution)/shard_map/ppermute | solution.py:17
  (94 shorter events, 8.5 us)
Async XLA Ops:
  7.2 121.2 %all-gather.3.cloned.1.call-start = ((), (), s32[]{:S(2)}) async-start(), calls=%async_computation | async-start | bytes 2457600 | tf_op jit(solution)/shard_map/all_gather | solution.py:96
  7.2 60.1 %collective-permute-start.9 = (bf16[256,576]{0,1:T(8,128)(2,1)}, bf16[256,576]{0,1:T(8,128)(2,1)S(1)}, u32[]{:S(2)}, u32[]{:S(2)}) collective-permute-start(bf16[256,576]{0,1:T(8,128)(2,1)} %bitcast.194), channel_id=1, source_target_pairs={{0,7},{1,0},{2,1},{3,2},{4,3},{5,4},{6,5},{7,6},{8,15},{9,8},{10,9... | collective-permute-start | bytes 884744 | tf_op jit(solution)/shard_map/ppermute | solution.py:22
  12.6 59.6 %collective-permute-start.12 = (bf16[256,576]{0,1:T(8,128)(2,1)}, bf16[256,576]{0,1:T(8,128)(2,1)S(1)}, u32[]{:S(2)}, u32[]{:S(2)}) collective-permute-start(bf16[256,576]{0,1:T(8,128)(2,1)} %bitcast.195), channel_id=1, source_target_pairs={{0,1},{1,2},{2,3},{3,4},{4,5},{5,6},{6,7},{7,0},{8,9},{9,10},{10,1... | collective-permute-start | bytes 884744 | tf_op jit(solution)/shard_map/ppermute | solution.py:22
  15.4 37.8 %collective-permute-start = (bf16[256,256]{1,0:T(8,128)(2,1)S(1)}, bf16[256,256]{1,0:T(8,128)(2,1)S(1)}, u32[]{:S(2)}, u32[]{:S(2)}) collective-permute-start(bf16[256,256]{1,0:T(8,128)(2,1)S(1)} %pad_maximum_fusion.1), channel_id=1, source_target_pairs={{0,16},{8,24},{16,32},{24,40},{32,48},{40,56},{48,64},{56,72},{64,... | collective-permute-start | bytes 393224 | tf_op jit(solution)/shard_map/ppermute | solution.py:17
  22.7 24.1 %copy-start.8 = (s32[1,8]{1,0:T(1,128)S(1)}, s32[1,8]{1,0:T(1,128)}, u32[]{:S(2)}) copy-start(s32[1,8]{1,0:T(1,128)} %param.13) | copy-start | bytes 100
  22.7 28.9 %copy-start.5 = (bf16[1,256,128]{2,1,0:T(8,128)(2,1)S(1)}, bf16[1,256,128]{2,1,0:T(8,128)(2,1)}, u32[]{:S(2)}) copy-start(bf16[1,256,128]{2,1,0:T(8,128)(2,1)} %param.11) | copy-start | bytes 196612
  22.7 28.9 %copy-start.6 = (bf16[1,256,128]{2,1,0:T(8,128)(2,1)S(1)}, bf16[1,256,128]{2,1,0:T(8,128)(2,1)}, u32[]{:S(2)}) copy-start(bf16[1,256,128]{2,1,0:T(8,128)(2,1)} %param.10) | copy-start | bytes 196612
  22.7 29.7 %copy-start.7 = (bf16[1,256,256]{2,1,0:T(8,128)(2,1)S(1)}, bf16[1,256,256]{2,1,0:T(8,128)(2,1)}, u32[]{:S(2)}) copy-start(bf16[1,256,256]{2,1,0:T(8,128)(2,1)} %param.9) | copy-start | bytes 393220
  22.7 30.4 %copy-start.1 = (bf16[1,256,576]{1,2,0:T(8,128)(2,1)S(1)}, bf16[1,256,576]{1,2,0:T(8,128)(2,1)}, u32[]{:S(2)}) copy-start(bf16[1,256,576]{1,2,0:T(8,128)(2,1)} %param.7) | copy-start | bytes 884740
  53.2 7.8 %collective-permute-start.1 = (bf16[256,256]{1,0:T(8,128)(2,1)S(1)}, bf16[256,256]{1,0:T(8,128)(2,1)S(1)}, u32[]{:S(2)}, u32[]{:S(2)}) collective-permute-start(bf16[256,256]{1,0:T(8,128)(2,1)S(1)} %collective-permute-done), channel_id=1, source_target_pairs={{0,16},{8,24},{16,32},{24,40},{32,48},{40,56},{48,64},{56,72},{64,... | collective-permute-start | bytes 393224 | tf_op jit(solution)/shard_map/ppermute | solution.py:17
  61.0 13.1 %collective-permute-start.2 = (bf16[256,256]{1,0:T(8,128)(2,1)S(1)}, bf16[256,256]{1,0:T(8,128)(2,1)S(1)}, u32[]{:S(2)}, u32[]{:S(2)}) collective-permute-start(bf16[256,256]{1,0:T(8,128)(2,1)S(1)} %collective-permute-done.1), channel_id=1, source_target_pairs={{0,16},{8,24},{16,32},{24,40},{32,48},{40,56},{48,64},{56,72},{64,... | collective-permute-start | bytes 393224 | tf_op jit(solution)/shard_map/ppermute | solution.py:17
  67.4 18.7 %collective-permute-start.10 = (bf16[256,576]{0,1:T(8,128)(2,1)S(1)}, bf16[256,576]{0,1:T(8,128)(2,1)S(1)}, u32[]{:S(2)}, u32[]{:S(2)}) collective-permute-start(bf16[256,576]{0,1:T(8,128)(2,1)S(1)} %collective-permute-done.9), channel_id=1, source_target_pairs={{0,7},{1,0},{2,1},{3,2},{4,3},{5,4},{6,5},{7,6},{8,15},{9,8},{10,9... | collective-permute-start | bytes 884744 | tf_op jit(solution)/shard_map/ppermute | solution.py:22
  72.2 19.0 %collective-permute-start.13 = (bf16[256,576]{0,1:T(8,128)(2,1)S(1)}, bf16[256,576]{0,1:T(8,128)(2,1)S(1)}, u32[]{:S(2)}, u32[]{:S(2)}) collective-permute-start(bf16[256,576]{0,1:T(8,128)(2,1)S(1)} %collective-permute-done.12), channel_id=1, source_target_pairs={{0,1},{1,2},{2,3},{3,4},{4,5},{5,6},{6,7},{7,0},{8,9},{9,10},{10,1... | collective-permute-start | bytes 884744 | tf_op jit(solution)/shard_map/ppermute | solution.py:22
  74.1 6.9 %collective-permute-start.3 = (bf16[256,256]{1,0:T(8,128)(2,1)S(1)}, bf16[256,256]{1,0:T(8,128)(2,1)S(1)}, u32[]{:S(2)}, u32[]{:S(2)}) collective-permute-start(bf16[256,256]{1,0:T(8,128)(2,1)S(1)} %collective-permute-done.2), channel_id=1, source_target_pairs={{0,16},{8,24},{16,32},{24,40},{32,48},{40,56},{48,64},{56,72},{64,... | collective-permute-start | bytes 393224 | tf_op jit(solution)/shard_map/ppermute | solution.py:17
  81.0 12.2 %collective-permute-start.4 = (bf16[256,256]{1,0:T(8,128)(2,1)S(1)}, bf16[256,256]{1,0:T(8,128)(2,1)S(1)}, u32[]{:S(2)}, u32[]{:S(2)}) collective-permute-start(bf16[256,256]{1,0:T(8,128)(2,1)S(1)} %collective-permute-done.3), channel_id=1, source_target_pairs={{0,16},{8,24},{16,32},{24,40},{32,48},{40,56},{48,64},{56,72},{64,... | collective-permute-start | bytes 393224 | tf_op jit(solution)/shard_map/ppermute | solution.py:17
  86.1 20.2 %collective-permute-start.11 = (bf16[256,576]{0,1:T(8,128)(2,1)S(1)}, bf16[256,576]{0,1:T(8,128)(2,1)S(1)}, u32[]{:S(2)}, u32[]{:S(2)}) collective-permute-start(bf16[256,576]{0,1:T(8,128)(2,1)S(1)} %collective-permute-done.10), channel_id=1, source_target_pairs={{0,7},{1,0},{2,1},{3,2},{4,3},{5,4},{6,5},{7,6},{8,15},{9,8},{10,9... | collective-permute-start | bytes 884744 | tf_op jit(solution)/shard_map/ppermute | solution.py:22
  91.2 13.1 %collective-permute-start.14 = (bf16[256,576]{0,1:T(8,128)(2,1)S(1)}, bf16[256,576]{0,1:T(8,128)(2,1)S(1)}, u32[]{:S(2)}, u32[]{:S(2)}) collective-permute-start(bf16[256,576]{0,1:T(8,128)(2,1)S(1)} %collective-permute-done.13), channel_id=1, source_target_pairs={{0,1},{1,2},{2,3},{3,4},{4,5},{5,6},{6,7},{7,0},{8,9},{9,10},{10,1... | collective-permute-start | bytes 884744 | tf_op jit(solution)/shard_map/ppermute | solution.py:22
  93.2 6.9 %collective-permute-start.5 = (bf16[256,256]{1,0:T(8,128)(2,1)S(1)}, bf16[256,256]{1,0:T(8,128)(2,1)S(1)}, u32[]{:S(2)}, u32[]{:S(2)}) collective-permute-start(bf16[256,256]{1,0:T(8,128)(2,1)S(1)} %collective-permute-done.4), channel_id=1, source_target_pairs={{0,16},{8,24},{16,32},{24,40},{32,48},{40,56},{48,64},{56,72},{64,... | collective-permute-start | bytes 393224 | tf_op jit(solution)/shard_map/ppermute | solution.py:17
  100.1 8.0 %collective-permute-start.6 = (bf16[256,256]{1,0:T(8,128)(2,1)S(1)}, bf16[256,256]{1,0:T(8,128)(2,1)S(1)}, u32[]{:S(2)}, u32[]{:S(2)}) collective-permute-start(bf16[256,256]{1,0:T(8,128)(2,1)S(1)} %collective-permute-done.5), channel_id=1, source_target_pairs={{0,16},{8,24},{16,32},{24,40},{32,48},{40,56},{48,64},{56,72},{64,... | collective-permute-start | bytes 393224 | tf_op jit(solution)/shard_map/ppermute | solution.py:17
  104.3 13.5 %collective-permute-start.15 = (bf16[256,576]{0,1:T(8,128)(2,1)S(1)}, bf16[256,576]{0,1:T(8,128)(2,1)S(1)}, u32[]{:S(2)}, u32[]{:S(2)}) collective-permute-start(bf16[256,576]{0,1:T(8,128)(2,1)S(1)} %collective-permute-done.14), channel_id=1, source_target_pairs={{0,1},{1,2},{2,3},{3,4},{4,5},{5,6},{6,7},{7,0},{8,9},{9,10},{10,1... | collective-permute-start | bytes 884744 | tf_op jit(solution)/shard_map/ppermute | solution.py:22
  108.1 6.8 %collective-permute-start.7 = (bf16[256,256]{1,0:T(8,128)(2,1)S(1)}, bf16[256,256]{1,0:T(8,128)(2,1)S(1)}, u32[]{:S(2)}, u32[]{:S(2)}) collective-permute-start(bf16[256,256]{1,0:T(8,128)(2,1)S(1)} %collective-permute-done.6), channel_id=1, source_target_pairs={{0,16},{8,24},{16,32},{24,40},{32,48},{40,56},{48,64},{56,72},{64,... | collective-permute-start | bytes 393224 | tf_op jit(solution)/shard_map/ppermute | solution.py:17
  115.7 4.9 %collective-permute-start.8 = (bf16[9,256,256]{2,1,0:T(8,128)(2,1)}, bf16[9,256,256]{2,1,0:T(8,128)(2,1)S(1)}, u32[]{:S(2)}, u32[]{:S(2)}) collective-permute-start(bf16[9,256,256]{2,1,0:T(8,128)(2,1)} %get-tuple-element.10), channel_id=1, source_target_pairs={{0,8},{8,0},{16,24},{24,16},{32,40},{40,32},{48,56},{56,48},{64,72... | collective-permute-start | bytes 3538952 | tf_op jit(solution)/shard_map/ppermute | solution.py:122
  118.3 3.4 %copy-start.3 = (bf16[1,256,256]{1,2,0:T(8,128)(2,1)S(1)}, bf16[1,256,256]{1,2,0:T(8,128)(2,1)}, u32[]{:S(2)}) copy-start(bf16[1,256,256]{1,2,0:T(8,128)(2,1)} %copy.47) | copy-start | bytes 393220
  128.3 9.2 %slice-start.2 = ((s8[9437184]{0:T(1024)(128)(4,1)}), s8[4194304]{0:T(1024)(128)(4,1)S(1)}, s32[]{:S(2)}) async-start(s8[9437184]{0:T(1024)(128)(4,1)} %bitcast.188), calls=%async_computation.3 | async-start | bytes 8388608
  131.2 6.3 %slice-start.3 = ((s8[9437184]{0:T(1024)(128)(4,1)}), s8[4194304]{0:T(1024)(128)(4,1)S(1)}, s32[]{:S(2)}) async-start(s8[9437184]{0:T(1024)(128)(4,1)} %bitcast.188), calls=%async_computation.4 | async-start | bytes 8388608
  131.2 6.3 %slice-start.4 = ((s8[9437184]{0:T(1024)(128)(4,1)}), s8[1048576]{0:T(1024)(128)(4,1)S(1)}, s32[]{:S(2)}) async-start(s8[9437184]{0:T(1024)(128)(4,1)} %bitcast.188), calls=%async_computation.5 | async-start | bytes 2097152
  141.0 6.8 %copy-start.4 = (bf16[1,256,256]{1,2,0:T(8,128)(2,1)S(1)}, bf16[1,256,256]{1,2,0:T(8,128)(2,1)}, u32[]{:S(2)}) copy-start(bf16[1,256,256]{1,2,0:T(8,128)(2,1)} %copy.47) | copy-start | bytes 393220
  145.6 2.2 copy-start
  153.2 6.8 %collective-permute-start.17 = (f32[9,256,256]{2,1,0:T(8,128)}, f32[9,256,256]{2,1,0:T(8,128)}, u32[]{:S(2)}, u32[]{:S(2)}) collective-permute-start(f32[9,256,256]{2,1,0:T(8,128)} %bitcast.192), channel_id=1, source_target_pairs={{0,8},{8,0},{16,24},{24,16},{32,40},{40,32},{48,56},{56,48},{64,72... | collective-permute-start | bytes 7077896 | tf_op jit(solution)/shard_map/ppermute | solution.py:146
  159.9 75.9 %slice-start = ((s8[4718592]{0:T(1024)(128)(4,1)}), s8[4194304]{0:T(1024)(128)(4,1)S(1)}, s32[]{:S(2)}) async-start(s8[4718592]{0:T(1024)(128)(4,1)} %bitcast.186), calls=%async_computation.1 | async-start | bytes 8388608
  159.9 75.9 %slice-start.1 = ((s8[4718592]{0:T(1024)(128)(4,1)}), s8[524288]{0:T(1024)(128)(4,1)S(1)}, s32[]{:S(2)}) async-start(s8[4718592]{0:T(1024)(128)(4,1)} %bitcast.186), calls=%async_computation.2 | async-start | bytes 1048576
  162.1 62.8 %copy-start.2 = (bf16[1,256,576]{1,2,0:T(8,128)(2,1)S(1)}, bf16[1,256,576]{1,2,0:T(8,128)(2,1)}, u32[]{:S(2)}) copy-start(bf16[1,256,576]{1,2,0:T(8,128)(2,1)} %param.7) | copy-start | bytes 884740
  162.1 11.7 %collective-permute-start.18 = (f32[256,256]{1,0:T(8,128)S(1)}, f32[256,256]{1,0:T(8,128)S(1)}, u32[]{:S(2)}, u32[]{:S(2)}) collective-permute-start(f32[256,256]{1,0:T(8,128)S(1)} %get-tuple-element.7), channel_id=1, source_target_pairs={{16,0},{24,8},{32,16},{40,24},{48,32},{56,40},{64,48},{72,56},{80,... | collective-permute-start | bytes 786440 | tf_op jit(solution)/shard_map/ppermute | solution.py:17
  173.8 10.7 %collective-permute-start.19 = (f32[256,256]{1,0:T(8,128)S(1)}, f32[256,256]{1,0:T(8,128)S(1)}, u32[]{:S(2)}, u32[]{:S(2)}) collective-permute-start(f32[256,256]{1,0:T(8,128)S(1)} %fusion.26), channel_id=1, source_target_pairs={{16,0},{24,8},{32,16},{40,24},{48,32},{56,40},{64,48},{72,56},{80,... | collective-permute-start | bytes 786440 | tf_op jit(solution)/shard_map/ppermute | solution.py:17
  184.5 9.8 %collective-permute-start.20 = (f32[256,256]{1,0:T(8,128)S(1)}, f32[256,256]{1,0:T(8,128)S(1)}, u32[]{:S(2)}, u32[]{:S(2)}) collective-permute-start(f32[256,256]{1,0:T(8,128)S(1)} %fusion.25), channel_id=1, source_target_pairs={{16,0},{24,8},{32,16},{40,24},{48,32},{56,40},{64,48},{72,56},{80,... | collective-permute-start | bytes 786440 | tf_op jit(solution)/shard_map/ppermute | solution.py:17
  194.4 9.5 %collective-permute-start.21 = (f32[256,256]{1,0:T(8,128)S(1)}, f32[256,256]{1,0:T(8,128)S(1)}, u32[]{:S(2)}, u32[]{:S(2)}) collective-permute-start(f32[256,256]{1,0:T(8,128)S(1)} %fusion.24), channel_id=1, source_target_pairs={{16,0},{24,8},{32,16},{40,24},{48,32},{56,40},{64,48},{72,56},{80,... | collective-permute-start | bytes 786440 | tf_op jit(solution)/shard_map/ppermute | solution.py:17
  203.9 9.5 %collective-permute-start.22 = (f32[256,256]{1,0:T(8,128)S(1)}, f32[256,256]{1,0:T(8,128)S(1)}, u32[]{:S(2)}, u32[]{:S(2)}) collective-permute-start(f32[256,256]{1,0:T(8,128)S(1)} %fusion.23), channel_id=1, source_target_pairs={{16,0},{24,8},{32,16},{40,24},{48,32},{56,40},{64,48},{72,56},{80,... | collective-permute-start | bytes 786440 | tf_op jit(solution)/shard_map/ppermute | solution.py:17
  213.4 9.6 %collective-permute-start.23 = (f32[256,256]{1,0:T(8,128)S(1)}, f32[256,256]{1,0:T(8,128)S(1)}, u32[]{:S(2)}, u32[]{:S(2)}) collective-permute-start(f32[256,256]{1,0:T(8,128)S(1)} %fusion.22), channel_id=1, source_target_pairs={{16,0},{24,8},{32,16},{40,24},{48,32},{56,40},{64,48},{72,56},{80,... | collective-permute-start | bytes 786440 | tf_op jit(solution)/shard_map/ppermute | solution.py:17
  223.0 10.9 %collective-permute-start.24 = (f32[256,256]{1,0:T(8,128)S(1)}, f32[256,256]{1,0:T(8,128)S(1)}, u32[]{:S(2)}, u32[]{:S(2)}) collective-permute-start(f32[256,256]{1,0:T(8,128)S(1)} %fusion.21), channel_id=1, source_target_pairs={{16,0},{24,8},{32,16},{40,24},{48,32},{56,40},{64,48},{72,56},{80,... | collective-permute-start | bytes 786440 | tf_op jit(solution)/shard_map/ppermute | solution.py:17
  224.9 15.1 %collective-permute-start.27 = (bf16[256,576]{0,1:T(8,128)(2,1)S(1)}, bf16[256,576]{0,1:T(8,128)(2,1)S(1)}, u32[]{:S(2)}, u32[]{:S(2)}) collective-permute-start(bf16[256,576]{0,1:T(8,128)(2,1)S(1)} %bitcast.196), channel_id=1, source_target_pairs={{192,0},{384,192},{576,384},{193,1},{385,193},{577,385},{194,2},{3... | collective-permute-start | bytes 884744 | tf_op jit(solution)/shard_map/ppermute | solution.py:17
  227.2 18.4 %collective-permute-start.26 = (f32[256,256]{1,0:T(8,128)S(1)}, f32[256,256]{1,0:T(8,128)S(1)}, u32[]{:S(2)}, u32[]{:S(2)}) collective-permute-start(f32[256,256]{1,0:T(8,128)S(1)} %get-tuple-element.6), channel_id=1, source_target_pairs={{192,0},{384,192},{576,384},{193,1},{385,193},{577,385},{194,2},{3... | collective-permute-start | bytes 786440 | tf_op jit(solution)/shard_map/ppermute | solution.py:17
  233.9 11.8 %collective-permute-start.25 = (f32[256,256]{1,0:T(8,128)S(1)}, f32[256,256]{1,0:T(8,128)S(1)}, u32[]{:S(2)}, u32[]{:S(2)}) collective-permute-start(f32[256,256]{1,0:T(8,128)S(1)} %fusion.20), channel_id=1, source_target_pairs={{208,0},{216,8},{224,16},{232,24},{240,32},{248,40},{256,48},{264,... | collective-permute-start | bytes 786440 | tf_op jit(solution)/shard_map/ppermute | solution.py:156
  238.1 7.6 %collective-permute-start.16 = (bf16[256,256]{1,0:T(8,128)(2,1)S(1)}, bf16[256,256]{1,0:T(8,128)(2,1)S(1)}, u32[]{:S(2)}, u32[]{:S(2)}) collective-permute-start(bf16[256,256]{1,0:T(8,128)(2,1)S(1)} %copy.35), channel_id=1, source_target_pairs={{192,0},{384,192},{576,384},{193,1},{385,193},{577,385},{194,2},{3... | collective-permute-start | bytes 393224 | tf_op jit(solution)/shard_map/ppermute | solution.py:17
Sparse Core Ops, SparseCore 0:
  21.1 58.8 all-gather.2

commit v7 on v6

--- a/solution.py
+++ b/solution.py
@@ -128,7 +128,15 @@
     query_doc = lax.dynamic_slice_in_dim(doc_list, query_start, tok_rows)
     lead = reach_rows * tok_rows
     padded_docs = jnp.concatenate([jnp.full((lead,), -1, jnp.int32), doc_list])
-    key_doc = jnp.take(padded_docs, jnp.clip(key_pos + lead, 0, padded_docs.shape[0] - 1))
+    run_rows = (2 * hops + 1) * tok_rows
+    key_doc = jnp.concatenate(
+        [
+            lax.dynamic_slice_in_dim(padded_docs, start * tok_rows, run_rows)
+            .reshape(2 * hops + 1, tok_rows)[::-2]
+            .reshape(-1)
+            for start in (row_index, partner_index)
+        ]
+    )
     key_shared = shared_lookup(key_doc, shared_flags)
     allowed = (
         (key_pos[None, :] >= 0)

time: 256 us -> 235 us (0.918)
  the two profiles are of different devices: /device:TPU:196 before, /device:TPU:250 now
where the time goes in v7:
time: 235 us; the launch traced here: 234 us
  starting transfers between devices  82.2 us (35%)
  waiting for transfers between devices  78.3 us (33%)
  matrix products  22.9 us (10%)
  local copies, waits for them, and re-layouts  18.4 us (8%)
  other arithmetic  16.8 us (7%)
  between operations  14.8 us (6%)
    ppermute x18, waiting for transfers between devices, from_behind(): return lax.ppermute(block, axis, route)  73.3 us
    ppermute x18, starting transfers between devices, from_behind(): return lax.ppermute(block, axis, route)  53 us
    ppermute x7, starting transfers between devices, cyclic_shift(): lax.ppermute(block, axis, [(i, (i + distance) % size) for i in range(size)])  23.2 us
    unnamed x47, local copies, waits for them, and re-layouts  9.02 us
    dot_general x1, matrix products, attend(): jnp.einsum('qgrd,kgd->grqk', query_g, key_g, preferred_element_type=jnp.f...  6.56 us
    dot_general x1, matrix products, attend(): jnp.einsum('qgrd,kgd->grqk', attn_g, value_g, preferred_element_type=jnp....  6.28 us
  transfers between devices with their start and end apart: 29, of which 15 were waited for; matrix products, arithmetic and copies ran while one was open for 12% of the time, Pallas kernels for 0%

profile of v7, /device:TPU:250, one launch (start us, length us, event | category | flops | bytes accessed | tf_op | source)
XLA Modules:
  0.0 233.5 jit_solution(12217591228214740209)
XLA Ops:
  7.2 3.4 %collective-permute-start.9 = (bf16[256,576]{0,1:T(8,128)(2,1)}, bf16[256,576]{0,1:T(8,128)(2,1)S(1)}, u32[]{:S(2)}, u32[]{:S(2)}) collective-permute-start(bf16[256,576]{0,1:T(8,128)(2,1)} %bitcast.189), channel_id=1, source_target_pairs={{0,7},{1,0},{2,1},{3,2},{4,3},{5,4},{6,5},{7,6},{8,15},{9,8},{10,9... | collective-permute-start | bytes 884744 | tf_op jit(solution)/shard_map/ppermute | solution.py:22
  10.6 3.8 %collective-permute-start.12 = (bf16[256,576]{0,1:T(8,128)(2,1)}, bf16[256,576]{0,1:T(8,128)(2,1)S(1)}, u32[]{:S(2)}, u32[]{:S(2)}) collective-permute-start(bf16[256,576]{0,1:T(8,128)(2,1)} %bitcast.190), channel_id=1, source_target_pairs={{0,1},{1,2},{2,3},{3,4},{4,5},{5,6},{6,7},{7,0},{8,9},{9,10},{10,1... | collective-permute-start | bytes 884744 | tf_op jit(solution)/shard_map/ppermute | solution.py:22
  14.4 0.9 pad_maximum_fusion.1
  15.3 5.5 %collective-permute-start = (bf16[256,256]{1,0:T(8,128)(2,1)S(1)}, bf16[256,256]{1,0:T(8,128)(2,1)S(1)}, u32[]{:S(2)}, u32[]{:S(2)}) collective-permute-start(bf16[256,256]{1,0:T(8,128)(2,1)S(1)} %pad_maximum_fusion.1), channel_id=1, source_target_pairs={{0,16},{8,24},{16,32},{24,40},{32,48},{40,56},{48,64},{56,72},{64,... | collective-permute-start | bytes 393224 | tf_op jit(solution)/shard_map/ppermute | solution.py:17
  21.6 0.9 pad_dynamic-slice_fusion
  22.9 0.8 select_reduce_fusion
  23.7 4.6 %fusion.10 = pred[256,4608]{0,1:T(8,128)(4,1)S(1)} fusion(s32[256]{0:T(256)S(1)} %bitcast.201, s32[256]{0:T(256)S(1)} %iota_add_fusion.1, s32[4608]{0:T(1024)S(1)} %constant_dynamic-update-slice_fusion.4, s32[4608]{0:T(1024)S(1)} %add.94, pred[4608]{0:T(1024)(128)(4,1)S(1)} %broadcast_compare_fusion, pred[4608]{0:T(1024)(128)(4,1)S(1)} %broadcast_compare_fusion.1), kind=kLoop, calls=%fused_computation.20 | loop fusion | flops 9437184 | bytes 1227776 | tf_op jit(solution)/shard_map/and | solution.py:146
  28.4 1.6 bitcast_dynamic-update-slice_fusion.31
  30.0 0.8 copy.47
  30.8 4.3 %collective-permute-start.1 = (bf16[256,256]{1,0:T(8,128)(2,1)S(1)}, bf16[256,256]{1,0:T(8,128)(2,1)S(1)}, u32[]{:S(2)}, u32[]{:S(2)}) collective-permute-start(bf16[256,256]{1,0:T(8,128)(2,1)S(1)} %collective-permute-done), channel_id=1, source_target_pairs={{0,16},{8,24},{16,32},{24,40},{32,48},{40,56},{48,64},{56,72},{64,... | collective-permute-start | bytes 393224 | tf_op jit(solution)/shard_map/ppermute | solution.py:17
  35.1 0.7 bitcast_dynamic-update-slice_fusion.29
  35.8 1.8 collective-permute-done.1
  37.6 5.5 %collective-permute-start.2 = (bf16[256,256]{1,0:T(8,128)(2,1)S(1)}, bf16[256,256]{1,0:T(8,128)(2,1)S(1)}, u32[]{:S(2)}, u32[]{:S(2)}) collective-permute-start(bf16[256,256]{1,0:T(8,128)(2,1)S(1)} %collective-permute-done.1), channel_id=1, source_target_pairs={{0,16},{8,24},{16,32},{24,40},{32,48},{40,56},{48,64},{56,72},{64,... | collective-permute-start | bytes 393224 | tf_op jit(solution)/shard_map/ppermute | solution.py:17
  43.9 2.0 collective-permute-start.10
  45.9 5.0 %collective-permute-start.13 = (bf16[256,576]{0,1:T(8,128)(2,1)S(1)}, bf16[256,576]{0,1:T(8,128)(2,1)S(1)}, u32[]{:S(2)}, u32[]{:S(2)}) collective-permute-start(bf16[256,576]{0,1:T(8,128)(2,1)S(1)} %collective-permute-done.12), channel_id=1, source_target_pairs={{0,1},{1,2},{2,3},{3,4},{4,5},{5,6},{6,7},{7,0},{8,9},{9,10},{10,1... | collective-permute-start | bytes 884744 | tf_op jit(solution)/shard_map/ppermute | solution.py:22
  51.0 3.1 %collective-permute-start.3 = (bf16[256,256]{1,0:T(8,128)(2,1)S(1)}, bf16[256,256]{1,0:T(8,128)(2,1)S(1)}, u32[]{:S(2)}, u32[]{:S(2)}) collective-permute-start(bf16[256,256]{1,0:T(8,128)(2,1)S(1)} %collective-permute-done.2), channel_id=1, source_target_pairs={{0,16},{8,24},{16,32},{24,40},{32,48},{40,56},{48,64},{56,72},{64,... | collective-permute-start | bytes 393224 | tf_op jit(solution)/shard_map/ppermute | solution.py:17
  54.1 0.7 bitcast_dynamic-update-slice_fusion.25
  54.8 3.7 %collective-permute-done.3 = bf16[256,256]{1,0:T(8,128)(2,1)S(1)} collective-permute-done((bf16[256,256]{1,0:T(8,128)(2,1)S(1)}, bf16[256,256]{1,0:T(8,128)(2,1)S(1)}, u32[]{:S(2)}, u32[]{:S(2)}) %collective-permute-start.3) | collective-permute-done | bytes 131104 | tf_op jit(solution)/shard_map/ppermute | solution.py:17
  58.5 4.0 %collective-permute-start.4 = (bf16[256,256]{1,0:T(8,128)(2,1)S(1)}, bf16[256,256]{1,0:T(8,128)(2,1)S(1)}, u32[]{:S(2)}, u32[]{:S(2)}) collective-permute-start(bf16[256,256]{1,0:T(8,128)(2,1)S(1)} %collective-permute-done.3), channel_id=1, source_target_pairs={{0,16},{8,24},{16,32},{24,40},{32,48},{40,56},{48,64},{56,72},{64,... | collective-permute-start | bytes 393224 | tf_op jit(solution)/shard_map/ppermute | solution.py:17
  63.2 1.9 collective-permute-start.11
  65.2 5.1 %collective-permute-start.14 = (bf16[256,576]{0,1:T(8,128)(2,1)S(1)}, bf16[256,576]{0,1:T(8,128)(2,1)S(1)}, u32[]{:S(2)}, u32[]{:S(2)}) collective-permute-start(bf16[256,576]{0,1:T(8,128)(2,1)S(1)} %collective-permute-done.13), channel_id=1, source_target_pairs={{0,1},{1,2},{2,3},{3,4},{4,5},{5,6},{6,7},{7,0},{8,9},{9,10},{10,1... | collective-permute-start | bytes 884744 | tf_op jit(solution)/shard_map/ppermute | solution.py:22
  70.3 2.9 %collective-permute-start.5 = (bf16[256,256]{1,0:T(8,128)(2,1)S(1)}, bf16[256,256]{1,0:T(8,128)(2,1)S(1)}, u32[]{:S(2)}, u32[]{:S(2)}) collective-permute-start(bf16[256,256]{1,0:T(8,128)(2,1)S(1)} %collective-permute-done.4), channel_id=1, source_target_pairs={{0,16},{8,24},{16,32},{24,40},{32,48},{40,56},{48,64},{56,72},{64,... | collective-permute-start | bytes 393224 | tf_op jit(solution)/shard_map/ppermute | solution.py:17
  74.0 4.3 %collective-permute-done.5 = bf16[256,256]{1,0:T(8,128)(2,1)S(1)} collective-permute-done((bf16[256,256]{1,0:T(8,128)(2,1)S(1)}, bf16[256,256]{1,0:T(8,128)(2,1)S(1)}, u32[]{:S(2)}, u32[]{:S(2)}) %collective-permute-start.5) | collective-permute-done | bytes 131104 | tf_op jit(solution)/shard_map/ppermute | solution.py:17
  78.3 3.3 %collective-permute-start.6 = (bf16[256,256]{1,0:T(8,128)(2,1)S(1)}, bf16[256,256]{1,0:T(8,128)(2,1)S(1)}, u32[]{:S(2)}, u32[]{:S(2)}) collective-permute-start(bf16[256,256]{1,0:T(8,128)(2,1)S(1)} %collective-permute-done.5), channel_id=1, source_target_pairs={{0,16},{8,24},{16,32},{24,40},{32,48},{40,56},{48,64},{56,72},{64,... | collective-permute-start | bytes 393224 | tf_op jit(solution)/shard_map/ppermute | solution.py:17
  82.3 1.9 collective-permute-start.15
  84.3 1.7 collective-permute-done.6
  86.0 4.7 %collective-permute-start.7 = (bf16[256,256]{1,0:T(8,128)(2,1)S(1)}, bf16[256,256]{1,0:T(8,128)(2,1)S(1)}, u32[]{:S(2)}, u32[]{:S(2)}) collective-permute-start(bf16[256,256]{1,0:T(8,128)(2,1)S(1)} %collective-permute-done.6), channel_id=1, source_target_pairs={{0,16},{8,24},{16,32},{24,40},{32,48},{40,56},{48,64},{56,72},{64,... | collective-permute-start | bytes 393224 | tf_op jit(solution)/shard_map/ppermute | solution.py:17
  91.4 1.8 collective-permute-done.7
  93.9 2.1 collective-permute-start.8
  96.5 2.3 collective-permute-done.8
  98.8 1.1 constant_dynamic-update-slice_fusion
  99.9 6.6 %fusion.5 = (f32[2,256]{1,0:T(2,128)S(1)}, f32[4608,256,2]{1,0,2:T(8,128)}) fusion(pred[256,4608]{0,1:T(8,128)(4,1)S(1)} %fusion.10, bf16[256,2,128]{0,2,1:T(8,128)(2,1)S(1)} %bitcast.192, bf16[4608,256]{1,0:T(8,128)(2,1)} %bitcast.11), kind=kOutput, calls=%fused_computation.10 | convolution fusion | flops 613416448 | bytes 11929600 | tf_op jit(solution)/shard_map/qgrd,kgd->grqk/dot_general | solution.py:52
  106.5 2.8 %fusion.16 = bf16[256,256]{0,1:T(8,128)(2,1)S(1)} fusion(bf16[256,4608]{0,1:T(8,128)(2,1)S(1)} %bitcast.186, bf16[1,256,4608]{1,2,0:T(8,128)(2,1)} %all-gather.3.cloned.1.call-done), kind=kOutput, calls=%fused_computation.28 | convolution fusion | flops 604045312 | bytes 4849664 | tf_op jit(solution)/shard_map/dot_general | solution.py:94
  109.4 6.3 %fusion.2 = (f32[2,256]{1,0:T(2,128)S(1)}, f32[4608,256,2]{1,0,2:T(8,128)S(1)}) fusion(f32[2,256]{1,0:T(2,128)S(1)} %get-tuple-element.30, f32[4608,256,2]{1,0,2:T(8,128)} %get-tuple-element.31, pred[256,4608]{0,1:T(8,128)(4,1)S(1)} %fusion.10, bf16[256,2,128]{0,2,1:T(8,128)(2,1)S(1)} %bitcast.203, bf16[4608,256]{1,0:T(8,128)(2,1)} %bitcast.11), kind=kOutput, calls=%fused_computation.6 | convolution fusion | flops 618135040 | bytes 21368832 | tf_op jit(solution)/shard_map/qgrd,kgd->grqk/dot_general | solution.py:62
  115.7 3.5 %convolution_bitcast_fusion = f32[4608,128]{0,1:T(8,128)S(1)} fusion(bf16[256,2,128]{0,2,1:T(8,128)(2,1)S(1)} %bitcast.204, f32[4608,256,2]{1,0,2:T(8,128)S(1)} %bitcast.184, f32[2,256]{1,0:T(2,128)S(1)} %get-tuple-element.30, pred[256,4608]{0,1:T(8,128)(4,1)S(1)} %fusion.10), kind=kOutput, calls=%fused_computation.11 | convolution fusion | flops 615776256 | bytes 13109248 | tf_op jit(solution)/shard_map/grqk,qgrd->kgd/dot_general | solution.py:59
  119.2 4.6 %fusion.6 = bf16[2,256,4608]{1,2,0:T(8,128)(2,1)S(1)} fusion(f32[4608,256,2]{1,0,2:T(8,128)S(1)} %bitcast.184, f32[4608,256,2]{1,0,2:T(8,128)S(1)} %get-tuple-element.33, f32[2,256]{1,0:T(2,128)S(1)} %get-tuple-element.32, f32[2,256]{1,0:T(2,128)S(1)} %get-tuple-element.30, pred[256,4608]{0,1:T(8,128)(4,1)S(1)} %fusion.10), kind=kLoop, calls=%fused_computation.13 | loop fusion | flops 25952256 | bytes 24776704 | tf_op jit(solution)/shard_map/reshape.12
  123.8 2.2 copy-done
  126.0 1.6 convolution_bitcast_fusion.1
  127.7 1.7 pad_maximum_fusion
  129.4 2.0 copy.40
  131.4 2.0 collective-permute-start.17
  133.4 2.0 copy.39
  135.5 2.7 %collective-permute-done.17 = f32[9,256,256]{2,1,0:T(8,128)} collective-permute-done((f32[9,256,256]{2,1,0:T(8,128)}, f32[9,256,256]{2,1,0:T(8,128)}, u32[]{:S(2)}, u32[]{:S(2)}) %collective-permute-start.17) | collective-permute-done | bytes 2359328 | tf_op jit(solution)/shard_map/ppermute | solution.py:154
  138.1 2.1 add.102
  140.3 2.1 collective-permute-start.18
  142.4 10.2 %collective-permute-done.18 = f32[256,256]{1,0:T(8,128)S(1)} collective-permute-done((f32[256,256]{1,0:T(8,128)S(1)}, f32[256,256]{1,0:T(8,128)S(1)}, u32[]{:S(2)}, u32[]{:S(2)}) %collective-permute-start.18) | collective-permute-done | bytes 262176 | tf_op jit(solution)/shard_map/ppermute | solution.py:17
  152.7 1.9 collective-permute-start.19
  154.6 8.9 %collective-permute-done.19 = f32[256,256]{1,0:T(8,128)S(1)} collective-permute-done((f32[256,256]{1,0:T(8,128)S(1)}, f32[256,256]{1,0:T(8,128)S(1)}, u32[]{:S(2)}, u32[]{:S(2)}) %collective-permute-start.19) | collective-permute-done | bytes 262176 | tf_op jit(solution)/shard_map/ppermute | solution.py:17
  163.6 1.9 collective-permute-start.20
  165.5 8.1 %collective-permute-done.20 = f32[256,256]{1,0:T(8,128)S(1)} collective-permute-done((f32[256,256]{1,0:T(8,128)S(1)}, f32[256,256]{1,0:T(8,128)S(1)}, u32[]{:S(2)}, u32[]{:S(2)}) %collective-permute-start.20) | collective-permute-done | bytes 262176 | tf_op jit(solution)/shard_map/ppermute | solution.py:17
  173.6 1.9 collective-permute-start.21
  175.6 7.5 %collective-permute-done.21 = f32[256,256]{1,0:T(8,128)S(1)} collective-permute-done((f32[256,256]{1,0:T(8,128)S(1)}, f32[256,256]{1,0:T(8,128)S(1)}, u32[]{:S(2)}, u32[]{:S(2)}) %collective-permute-start.21) | collective-permute-done | bytes 262176 | tf_op jit(solution)/shard_map/ppermute | solution.py:17
  183.2 1.9 collective-permute-start.22
  185.1 7.5 %collective-permute-done.22 = f32[256,256]{1,0:T(8,128)S(1)} collective-permute-done((f32[256,256]{1,0:T(8,128)S(1)}, f32[256,256]{1,0:T(8,128)S(1)}, u32[]{:S(2)}, u32[]{:S(2)}) %collective-permute-start.22) | collective-permute-done | bytes 262176 | tf_op jit(solution)/shard_map/ppermute | solution.py:17
  192.7 1.9 collective-permute-start.23
  194.6 7.5 %collective-permute-done.23 = f32[256,256]{1,0:T(8,128)S(1)} collective-permute-done((f32[256,256]{1,0:T(8,128)S(1)}, f32[256,256]{1,0:T(8,128)S(1)}, u32[]{:S(2)}, u32[]{:S(2)}) %collective-permute-start.23) | collective-permute-done | bytes 262176 | tf_op jit(solution)/shard_map/ppermute | solution.py:17
  202.2 1.9 collective-permute-start.24
  204.1 2.3 collective-permute-start.27
  206.5 1.9 collective-permute-start.26
  208.4 4.4 %collective-permute-done.24 = f32[256,256]{1,0:T(8,128)S(1)} collective-permute-done((f32[256,256]{1,0:T(8,128)S(1)}, f32[256,256]{1,0:T(8,128)S(1)}, u32[]{:S(2)}, u32[]{:S(2)}) %collective-permute-start.24) | collective-permute-done | bytes 262176 | tf_op jit(solution)/shard_map/ppermute | solution.py:17
  212.8 1.9 collective-permute-start.25
  214.8 2.1 convolution_convert_fusion
  217.0 1.9 collective-permute-start.16
  218.9 5.7 %collective-permute-done.16 = bf16[256,256]{1,0:T(8,128)(2,1)S(1)} collective-permute-done((bf16[256,256]{1,0:T(8,128)(2,1)S(1)}, bf16[256,256]{1,0:T(8,128)(2,1)S(1)}, u32[]{:S(2)}, u32[]{:S(2)}) %collective-permute-start.16) | collective-permute-done | bytes 131104 | tf_op jit(solution)/shard_map/ppermute | solution.py:17
  (94 shorter events, 8.5 us)
Async XLA Ops:
  7.2 23.6 %copy-start.1 = (bf16[1,256,576]{1,2,0:T(8,128)(2,1)S(1)}, bf16[1,256,576]{1,2,0:T(8,128)(2,1)}, u32[]{:S(2)}) copy-start(bf16[1,256,576]{1,2,0:T(8,128)(2,1)} %param.7) | copy-start | bytes 884740
  7.2 22.8 %copy-start.5 = (bf16[1,256,256]{2,1,0:T(8,128)(2,1)S(1)}, bf16[1,256,256]{2,1,0:T(8,128)(2,1)}, u32[]{:S(2)}) copy-start(bf16[1,256,256]{2,1,0:T(8,128)(2,1)} %param.9) | copy-start | bytes 393220
  7.2 99.3 %all-gather.3.cloned.1.call-start = ((), (), s32[]{:S(2)}) async-start(), calls=%async_computation | async-start | bytes 2457600 | tf_op jit(solution)/shard_map/all_gather | solution.py:96
  7.2 36.6 %collective-permute-start.9 = (bf16[256,576]{0,1:T(8,128)(2,1)}, bf16[256,576]{0,1:T(8,128)(2,1)S(1)}, u32[]{:S(2)}, u32[]{:S(2)}) collective-permute-start(bf16[256,576]{0,1:T(8,128)(2,1)} %bitcast.189), channel_id=1, source_target_pairs={{0,7},{1,0},{2,1},{3,2},{4,3},{5,4},{6,5},{7,6},{8,15},{9,8},{10,9... | collective-permute-start | bytes 884744 | tf_op jit(solution)/shard_map/ppermute | solution.py:22
  10.6 35.3 %collective-permute-start.12 = (bf16[256,576]{0,1:T(8,128)(2,1)}, bf16[256,576]{0,1:T(8,128)(2,1)S(1)}, u32[]{:S(2)}, u32[]{:S(2)}) collective-permute-start(bf16[256,576]{0,1:T(8,128)(2,1)} %bitcast.190), channel_id=1, source_target_pairs={{0,1},{1,2},{2,3},{3,4},{4,5},{5,6},{6,7},{7,0},{8,9},{9,10},{10,1... | collective-permute-start | bytes 884744 | tf_op jit(solution)/shard_map/ppermute | solution.py:22
  15.3 15.4 %collective-permute-start = (bf16[256,256]{1,0:T(8,128)(2,1)S(1)}, bf16[256,256]{1,0:T(8,128)(2,1)S(1)}, u32[]{:S(2)}, u32[]{:S(2)}) collective-permute-start(bf16[256,256]{1,0:T(8,128)(2,1)S(1)} %pad_maximum_fusion.1), channel_id=1, source_target_pairs={{0,16},{8,24},{16,32},{24,40},{32,48},{40,56},{48,64},{56,72},{64,... | collective-permute-start | bytes 393224 | tf_op jit(solution)/shard_map/ppermute | solution.py:17
  30.8 6.9 %collective-permute-start.1 = (bf16[256,256]{1,0:T(8,128)(2,1)S(1)}, bf16[256,256]{1,0:T(8,128)(2,1)S(1)}, u32[]{:S(2)}, u32[]{:S(2)}) collective-permute-start(bf16[256,256]{1,0:T(8,128)(2,1)S(1)} %collective-permute-done), channel_id=1, source_target_pairs={{0,16},{8,24},{16,32},{24,40},{32,48},{40,56},{48,64},{56,72},{64,... | collective-permute-start | bytes 393224 | tf_op jit(solution)/shard_map/ppermute | solution.py:17
  37.6 13.3 %collective-permute-start.2 = (bf16[256,256]{1,0:T(8,128)(2,1)S(1)}, bf16[256,256]{1,0:T(8,128)(2,1)S(1)}, u32[]{:S(2)}, u32[]{:S(2)}) collective-permute-start(bf16[256,256]{1,0:T(8,128)(2,1)S(1)} %collective-permute-done.1), channel_id=1, source_target_pairs={{0,16},{8,24},{16,32},{24,40},{32,48},{40,56},{48,64},{56,72},{64,... | collective-permute-start | bytes 393224 | tf_op jit(solution)/shard_map/ppermute | solution.py:17
  43.9 19.4 %collective-permute-start.10 = (bf16[256,576]{0,1:T(8,128)(2,1)S(1)}, bf16[256,576]{0,1:T(8,128)(2,1)S(1)}, u32[]{:S(2)}, u32[]{:S(2)}) collective-permute-start(bf16[256,576]{0,1:T(8,128)(2,1)S(1)} %collective-permute-done.9), channel_id=1, source_target_pairs={{0,7},{1,0},{2,1},{3,2},{4,3},{5,4},{6,5},{7,6},{8,15},{9,8},{10,9... | collective-permute-start | bytes 884744 | tf_op jit(solution)/shard_map/ppermute | solution.py:22
  45.9 19.2 %collective-permute-start.13 = (bf16[256,576]{0,1:T(8,128)(2,1)S(1)}, bf16[256,576]{0,1:T(8,128)(2,1)S(1)}, u32[]{:S(2)}, u32[]{:S(2)}) collective-permute-start(bf16[256,576]{0,1:T(8,128)(2,1)S(1)} %collective-permute-done.12), channel_id=1, source_target_pairs={{0,1},{1,2},{2,3},{3,4},{4,5},{5,6},{6,7},{7,0},{8,9},{9,10},{10,1... | collective-permute-start | bytes 884744 | tf_op jit(solution)/shard_map/ppermute | solution.py:22
  51.0 7.5 %collective-permute-start.3 = (bf16[256,256]{1,0:T(8,128)(2,1)S(1)}, bf16[256,256]{1,0:T(8,128)(2,1)S(1)}, u32[]{:S(2)}, u32[]{:S(2)}) collective-permute-start(bf16[256,256]{1,0:T(8,128)(2,1)S(1)} %collective-permute-done.2), channel_id=1, source_target_pairs={{0,16},{8,24},{16,32},{24,40},{32,48},{40,56},{48,64},{56,72},{64,... | collective-permute-start | bytes 393224 | tf_op jit(solution)/shard_map/ppermute | solution.py:17
  58.5 11.8 %collective-permute-start.4 = (bf16[256,256]{1,0:T(8,128)(2,1)S(1)}, bf16[256,256]{1,0:T(8,128)(2,1)S(1)}, u32[]{:S(2)}, u32[]{:S(2)}) collective-permute-start(bf16[256,256]{1,0:T(8,128)(2,1)S(1)} %collective-permute-done.3), channel_id=1, source_target_pairs={{0,16},{8,24},{16,32},{24,40},{32,48},{40,56},{48,64},{56,72},{64,... | collective-permute-start | bytes 393224 | tf_op jit(solution)/shard_map/ppermute | solution.py:17
  63.2 21.0 %collective-permute-start.11 = (bf16[256,576]{0,1:T(8,128)(2,1)S(1)}, bf16[256,576]{0,1:T(8,128)(2,1)S(1)}, u32[]{:S(2)}, u32[]{:S(2)}) collective-permute-start(bf16[256,576]{0,1:T(8,128)(2,1)S(1)} %collective-permute-done.10), channel_id=1, source_target_pairs={{0,7},{1,0},{2,1},{3,2},{4,3},{5,4},{6,5},{7,6},{8,15},{9,8},{10,9... | collective-permute-start | bytes 884744 | tf_op jit(solution)/shard_map/ppermute | solution.py:22
  65.2 17.2 %collective-permute-start.14 = (bf16[256,576]{0,1:T(8,128)(2,1)S(1)}, bf16[256,576]{0,1:T(8,128)(2,1)S(1)}, u32[]{:S(2)}, u32[]{:S(2)}) collective-permute-start(bf16[256,576]{0,1:T(8,128)(2,1)S(1)} %collective-permute-done.13), channel_id=1, source_target_pairs={{0,1},{1,2},{2,3},{3,4},{4,5},{5,6},{6,7},{7,0},{8,9},{9,10},{10,1... | collective-permute-start | bytes 884744 | tf_op jit(solution)/shard_map/ppermute | solution.py:22
  70.3 8.0 %collective-permute-start.5 = (bf16[256,256]{1,0:T(8,128)(2,1)S(1)}, bf16[256,256]{1,0:T(8,128)(2,1)S(1)}, u32[]{:S(2)}, u32[]{:S(2)}) collective-permute-start(bf16[256,256]{1,0:T(8,128)(2,1)S(1)} %collective-permute-done.4), channel_id=1, source_target_pairs={{0,16},{8,24},{16,32},{24,40},{32,48},{40,56},{48,64},{56,72},{64,... | collective-permute-start | bytes 393224 | tf_op jit(solution)/shard_map/ppermute | solution.py:17
  78.3 7.7 %collective-permute-start.6 = (bf16[256,256]{1,0:T(8,128)(2,1)S(1)}, bf16[256,256]{1,0:T(8,128)(2,1)S(1)}, u32[]{:S(2)}, u32[]{:S(2)}) collective-permute-start(bf16[256,256]{1,0:T(8,128)(2,1)S(1)} %collective-permute-done.5), channel_id=1, source_target_pairs={{0,16},{8,24},{16,32},{24,40},{32,48},{40,56},{48,64},{56,72},{64,... | collective-permute-start | bytes 393224 | tf_op jit(solution)/shard_map/ppermute | solution.py:17
  82.3 13.7 %collective-permute-start.15 = (bf16[256,576]{0,1:T(8,128)(2,1)S(1)}, bf16[256,576]{0,1:T(8,128)(2,1)S(1)}, u32[]{:S(2)}, u32[]{:S(2)}) collective-permute-start(bf16[256,576]{0,1:T(8,128)(2,1)S(1)} %collective-permute-done.14), channel_id=1, source_target_pairs={{0,1},{1,2},{2,3},{3,4},{4,5},{5,6},{6,7},{7,0},{8,9},{9,10},{10,1... | collective-permute-start | bytes 884744 | tf_op jit(solution)/shard_map/ppermute | solution.py:22
  86.0 7.2 %collective-permute-start.7 = (bf16[256,256]{1,0:T(8,128)(2,1)S(1)}, bf16[256,256]{1,0:T(8,128)(2,1)S(1)}, u32[]{:S(2)}, u32[]{:S(2)}) collective-permute-start(bf16[256,256]{1,0:T(8,128)(2,1)S(1)} %collective-permute-done.6), channel_id=1, source_target_pairs={{0,16},{8,24},{16,32},{24,40},{32,48},{40,56},{48,64},{56,72},{64,... | collective-permute-start | bytes 393224 | tf_op jit(solution)/shard_map/ppermute | solution.py:17
  93.9 4.9 %collective-permute-start.8 = (bf16[9,256,256]{2,1,0:T(8,128)(2,1)}, bf16[9,256,256]{2,1,0:T(8,128)(2,1)S(1)}, u32[]{:S(2)}, u32[]{:S(2)}) collective-permute-start(bf16[9,256,256]{2,1,0:T(8,128)(2,1)} %get-tuple-element.10), channel_id=1, source_target_pairs={{0,8},{8,0},{16,24},{24,16},{32,40},{40,32},{48,56},{56,48},{64,72... | collective-permute-start | bytes 3538952 | tf_op jit(solution)/shard_map/ppermute | solution.py:122
  96.5 3.4 %copy-start.3 = (bf16[1,256,256]{1,2,0:T(8,128)(2,1)S(1)}, bf16[1,256,256]{1,2,0:T(8,128)(2,1)}, u32[]{:S(2)}) copy-start(bf16[1,256,256]{1,2,0:T(8,128)(2,1)} %copy.47) | copy-start | bytes 393220
  106.5 9.2 %slice-start.2 = ((s8[9437184]{0:T(1024)(128)(4,1)}), s8[4194304]{0:T(1024)(128)(4,1)S(1)}, s32[]{:S(2)}) async-start(s8[9437184]{0:T(1024)(128)(4,1)} %bitcast.183), calls=%async_computation.3 | async-start | bytes 8388608
  109.4 6.3 %slice-start.3 = ((s8[9437184]{0:T(1024)(128)(4,1)}), s8[4194304]{0:T(1024)(128)(4,1)S(1)}, s32[]{:S(2)}) async-start(s8[9437184]{0:T(1024)(128)(4,1)} %bitcast.183), calls=%async_computation.4 | async-start | bytes 8388608
  109.4 6.3 %slice-start.4 = ((s8[9437184]{0:T(1024)(128)(4,1)}), s8[1048576]{0:T(1024)(128)(4,1)S(1)}, s32[]{:S(2)}) async-start(s8[9437184]{0:T(1024)(128)(4,1)} %bitcast.183), calls=%async_computation.5 | async-start | bytes 2097152
  119.2 6.8 %copy-start.4 = (bf16[1,256,256]{1,2,0:T(8,128)(2,1)S(1)}, bf16[1,256,256]{1,2,0:T(8,128)(2,1)}, u32[]{:S(2)}) copy-start(bf16[1,256,256]{1,2,0:T(8,128)(2,1)} %copy.47) | copy-start | bytes 393220
  123.8 2.2 copy-start
  131.4 6.8 %collective-permute-start.17 = (f32[9,256,256]{2,1,0:T(8,128)}, f32[9,256,256]{2,1,0:T(8,128)}, u32[]{:S(2)}, u32[]{:S(2)}) collective-permute-start(f32[9,256,256]{2,1,0:T(8,128)} %bitcast.187), channel_id=1, source_target_pairs={{0,8},{8,0},{16,24},{24,16},{32,40},{40,32},{48,56},{56,48},{64,72... | collective-permute-start | bytes 7077896 | tf_op jit(solution)/shard_map/ppermute | solution.py:154
  138.1 76.6 %slice-start = ((s8[4718592]{0:T(1024)(128)(4,1)}), s8[4194304]{0:T(1024)(128)(4,1)S(1)}, s32[]{:S(2)}) async-start(s8[4718592]{0:T(1024)(128)(4,1)} %bitcast.181), calls=%async_computation.1 | async-start | bytes 8388608
  138.1 76.7 %slice-start.1 = ((s8[4718592]{0:T(1024)(128)(4,1)}), s8[524288]{0:T(1024)(128)(4,1)S(1)}, s32[]{:S(2)}) async-start(s8[4718592]{0:T(1024)(128)(4,1)} %bitcast.181), calls=%async_computation.2 | async-start | bytes 1048576
  140.3 63.8 %copy-start.2 = (bf16[1,256,576]{1,2,0:T(8,128)(2,1)S(1)}, bf16[1,256,576]{1,2,0:T(8,128)(2,1)}, u32[]{:S(2)}) copy-start(bf16[1,256,576]{1,2,0:T(8,128)(2,1)} %param.7) | copy-start | bytes 884740
  140.3 12.3 %collective-permute-start.18 = (f32[256,256]{1,0:T(8,128)S(1)}, f32[256,256]{1,0:T(8,128)S(1)}, u32[]{:S(2)}, u32[]{:S(2)}) collective-permute-start(f32[256,256]{1,0:T(8,128)S(1)} %get-tuple-element.7), channel_id=1, source_target_pairs={{16,0},{24,8},{32,16},{40,24},{48,32},{56,40},{64,48},{72,56},{80,... | collective-permute-start | bytes 786440 | tf_op jit(solution)/shard_map/ppermute | solution.py:17
  152.7 10.9 %collective-permute-start.19 = (f32[256,256]{1,0:T(8,128)S(1)}, f32[256,256]{1,0:T(8,128)S(1)}, u32[]{:S(2)}, u32[]{:S(2)}) collective-permute-start(f32[256,256]{1,0:T(8,128)S(1)} %fusion.26), channel_id=1, source_target_pairs={{16,0},{24,8},{32,16},{40,24},{48,32},{56,40},{64,48},{72,56},{80,... | collective-permute-start | bytes 786440 | tf_op jit(solution)/shard_map/ppermute | solution.py:17
  163.6 10.0 %collective-permute-start.20 = (f32[256,256]{1,0:T(8,128)S(1)}, f32[256,256]{1,0:T(8,128)S(1)}, u32[]{:S(2)}, u32[]{:S(2)}) collective-permute-start(f32[256,256]{1,0:T(8,128)S(1)} %fusion.25), channel_id=1, source_target_pairs={{16,0},{24,8},{32,16},{40,24},{48,32},{56,40},{64,48},{72,56},{80,... | collective-permute-start | bytes 786440 | tf_op jit(solution)/shard_map/ppermute | solution.py:17
  173.6 9.5 %collective-permute-start.21 = (f32[256,256]{1,0:T(8,128)S(1)}, f32[256,256]{1,0:T(8,128)S(1)}, u32[]{:S(2)}, u32[]{:S(2)}) collective-permute-start(f32[256,256]{1,0:T(8,128)S(1)} %fusion.24), channel_id=1, source_target_pairs={{16,0},{24,8},{32,16},{40,24},{48,32},{56,40},{64,48},{72,56},{80,... | collective-permute-start | bytes 786440 | tf_op jit(solution)/shard_map/ppermute | solution.py:17
  183.2 9.5 %collective-permute-start.22 = (f32[256,256]{1,0:T(8,128)S(1)}, f32[256,256]{1,0:T(8,128)S(1)}, u32[]{:S(2)}, u32[]{:S(2)}) collective-permute-start(f32[256,256]{1,0:T(8,128)S(1)} %fusion.23), channel_id=1, source_target_pairs={{16,0},{24,8},{32,16},{40,24},{48,32},{56,40},{64,48},{72,56},{80,... | collective-permute-start | bytes 786440 | tf_op jit(solution)/shard_map/ppermute | solution.py:17
  192.7 9.5 %collective-permute-start.23 = (f32[256,256]{1,0:T(8,128)S(1)}, f32[256,256]{1,0:T(8,128)S(1)}, u32[]{:S(2)}, u32[]{:S(2)}) collective-permute-start(f32[256,256]{1,0:T(8,128)S(1)} %fusion.22), channel_id=1, source_target_pairs={{16,0},{24,8},{32,16},{40,24},{48,32},{56,40},{64,48},{72,56},{80,... | collective-permute-start | bytes 786440 | tf_op jit(solution)/shard_map/ppermute | solution.py:17
  202.2 10.6 %collective-permute-start.24 = (f32[256,256]{1,0:T(8,128)S(1)}, f32[256,256]{1,0:T(8,128)S(1)}, u32[]{:S(2)}, u32[]{:S(2)}) collective-permute-start(f32[256,256]{1,0:T(8,128)S(1)} %fusion.21), channel_id=1, source_target_pairs={{16,0},{24,8},{32,16},{40,24},{48,32},{56,40},{64,48},{72,56},{80,... | collective-permute-start | bytes 786440 | tf_op jit(solution)/shard_map/ppermute | solution.py:17
  204.1 14.8 %collective-permute-start.27 = (bf16[256,576]{0,1:T(8,128)(2,1)S(1)}, bf16[256,576]{0,1:T(8,128)(2,1)S(1)}, u32[]{:S(2)}, u32[]{:S(2)}) collective-permute-start(bf16[256,576]{0,1:T(8,128)(2,1)S(1)} %bitcast.191), channel_id=1, source_target_pairs={{192,0},{384,192},{576,384},{193,1},{385,193},{577,385},{194,2},{3... | collective-permute-start | bytes 884744 | tf_op jit(solution)/shard_map/ppermute | solution.py:17
  206.5 18.2 %collective-permute-start.26 = (f32[256,256]{1,0:T(8,128)S(1)}, f32[256,256]{1,0:T(8,128)S(1)}, u32[]{:S(2)}, u32[]{:S(2)}) collective-permute-start(f32[256,256]{1,0:T(8,128)S(1)} %get-tuple-element.6), channel_id=1, source_target_pairs={{192,0},{384,192},{576,384},{193,1},{385,193},{577,385},{194,2},{3... | collective-permute-start | bytes 786440 | tf_op jit(solution)/shard_map/ppermute | solution.py:17
  212.8 11.8 %collective-permute-start.25 = (f32[256,256]{1,0:T(8,128)S(1)}, f32[256,256]{1,0:T(8,128)S(1)}, u32[]{:S(2)}, u32[]{:S(2)}) collective-permute-start(f32[256,256]{1,0:T(8,128)S(1)} %fusion.20), channel_id=1, source_target_pairs={{208,0},{216,8},{224,16},{232,24},{240,32},{248,40},{256,48},{264,... | collective-permute-start | bytes 786440 | tf_op jit(solution)/shard_map/ppermute | solution.py:164
  217.0 7.6 %collective-permute-start.16 = (bf16[256,256]{1,0:T(8,128)(2,1)S(1)}, bf16[256,256]{1,0:T(8,128)(2,1)S(1)}, u32[]{:S(2)}, u32[]{:S(2)}) collective-permute-start(bf16[256,256]{1,0:T(8,128)(2,1)S(1)} %copy.35), channel_id=1, source_target_pairs={{192,0},{384,192},{576,384},{193,1},{385,193},{577,385},{194,2},{3... | collective-permute-start | bytes 393224 | tf_op jit(solution)/shard_map/ppermute | solution.py:17
Sparse Core Ops, SparseCore 0:
  21.0 58.5 all-gather.2

commit v8 on v7

--- a/solution.py
+++ b/solution.py
@@ -147,6 +147,7 @@
     query_grad, key_sum, value_sum = attend(
         query_local, pair_near[:, :key_width], pair_near[:, key_width:], d_attn, allowed
     )
+    query_grad, key_sum, value_sum = lax.optimization_barrier((query_grad, key_sum, value_sum))
     query_handed = from_behind(query_grad, "pipe", -1)
     pair_sum = jnp.concatenate([key_sum, value_sum], axis=1).reshape(
         2, hops + 1, tok_rows, 2 * key_width
@@ -156,6 +157,8 @@
     running = chip_sum[hops]
     for step in range(1, hops):
         running = from_behind(running, "row", -2) + chip_sum[hops - step]
+        if step == hops // 2:
+            running, query_handed = lax.optimization_barrier((running, query_handed))
     last_pairs = [
         (p * row_count + r, (p - 1) * row_count + r - 2)
         for p in range(1, pipe_count)

time: 235 us -> 232 us (0.987)
  the two profiles are of different devices: /device:TPU:250 before, /device:TPU:196 now
where the time goes in v8:
time: 232 us; the launch traced here: 231 us
  starting transfers between devices  85.5 us (37%)
  waiting for transfers between devices  79.4 us (34%)
  matrix products  21.9 us (9%)
  local copies, waits for them, and re-layouts  15.9 us (7%)
  between operations  14.8 us (6%)
  other arithmetic  13.3 us (6%)
    ppermute x18, waiting for transfers between devices, from_behind(): return lax.ppermute(block, axis, route)  67.9 us
    ppermute x18, starting transfers between devices, from_behind(): return lax.ppermute(block, axis, route)  56.2 us
    ppermute x7, starting transfers between devices, cyclic_shift(): lax.ppermute(block, axis, [(i, (i + distance) % size) for i in range(size)])  23.2 us
    unnamed x40, local copies, waits for them, and re-layouts  8.47 us
    dot_general x1, matrix products, attend(): jnp.einsum('qgrd,kgd->grqk', query_g, key_g, preferred_element_type=jnp.f...  6.59 us
    dot_general x1, matrix products, attend(): jnp.einsum('qgrd,kgd->grqk', attn_g, value_g, preferred_element_type=jnp....  6.28 us
    ppermute x1, waiting for transfers between devices, per_device(): total = lax.ppermute(running, ('pipe', 'row'), last_pairs) + own_handed  4.78 us
    and x1, other arithmetic, per_device(): allowed & ((key_doc[None, :] == query_doc[:, None]) | (key_shared[None, :...  4.64 us
  transfers between devices with their start and end apart: 29, of which 17 were waited for; matrix products, arithmetic and copies ran while one was open for 12% of the time, Pallas kernels for 0%

profile of v8, /device:TPU:196, one launch (start us, length us, event | category | flops | bytes accessed | tf_op | source)
XLA Modules:
  0.0 230.7 jit_solution(9920239128139094313)
XLA Ops:
  7.2 5.4 %collective-permute-start.9 = (bf16[256,576]{0,1:T(8,128)(2,1)}, bf16[256,576]{0,1:T(8,128)(2,1)S(1)}, u32[]{:S(2)}, u32[]{:S(2)}) collective-permute-start(bf16[256,576]{0,1:T(8,128)(2,1)} %bitcast.184), channel_id=1, source_target_pairs={{0,7},{1,0},{2,1},{3,2},{4,3},{5,4},{6,5},{7,6},{8,15},{9,8},{10,9... | collective-permute-start | bytes 884744 | tf_op jit(solution)/shard_map/ppermute | solution.py:22
  12.6 1.9 collective-permute-start.12
  14.5 0.9 pad_maximum_fusion
  15.4 5.5 %collective-permute-start = (bf16[256,256]{1,0:T(8,128)(2,1)S(1)}, bf16[256,256]{1,0:T(8,128)(2,1)S(1)}, u32[]{:S(2)}, u32[]{:S(2)}) collective-permute-start(bf16[256,256]{1,0:T(8,128)(2,1)S(1)} %pad_maximum_fusion), channel_id=1, source_target_pairs={{0,16},{8,24},{16,32},{24,40},{32,48},{40,56},{48,64},{56,72},{64,... | collective-permute-start | bytes 393224 | tf_op jit(solution)/shard_map/ppermute | solution.py:17
  21.7 0.9 pad_dynamic-slice_fusion
  23.0 0.8 select_reduce_fusion
  23.8 4.6 %fusion.10 = pred[256,4608]{0,1:T(8,128)(4,1)S(1)} fusion(s32[256]{0:T(256)S(1)} %bitcast.194, s32[256]{0:T(256)S(1)} %iota_add_fusion.1, s32[4608]{0:T(1024)S(1)} %constant_dynamic-update-slice_fusion.6, s32[4608]{0:T(1024)S(1)} %add.94, pred[4608]{0:T(1024)(128)(4,1)S(1)} %broadcast_compare_fusion, pred[4608]{0:T(1024)(128)(4,1)S(1)} %broadcast_compare_fusion.1), kind=kLoop, calls=%fused_computation.18 | loop fusion | flops 9437184 | bytes 1227776 | tf_op jit(solution)/shard_map/and | solution.py:146
  28.5 1.6 bitcast_dynamic-update-slice_fusion.31
  30.1 1.6 reshape.261
  31.7 1.0 constant_dynamic-update-slice_fusion.3
  32.7 4.3 %collective-permute-start.1 = (bf16[256,256]{1,0:T(8,128)(2,1)S(1)}, bf16[256,256]{1,0:T(8,128)(2,1)S(1)}, u32[]{:S(2)}, u32[]{:S(2)}) collective-permute-start(bf16[256,256]{1,0:T(8,128)(2,1)S(1)} %collective-permute-done), channel_id=1, source_target_pairs={{0,16},{8,24},{16,32},{24,40},{32,48},{40,56},{48,64},{56,72},{64,... | collective-permute-start | bytes 393224 | tf_op jit(solution)/shard_map/ppermute | solution.py:17
  37.7 2.9 %collective-permute-done.1 = bf16[256,256]{1,0:T(8,128)(2,1)S(1)} collective-permute-done((bf16[256,256]{1,0:T(8,128)(2,1)S(1)}, bf16[256,256]{1,0:T(8,128)(2,1)S(1)}, u32[]{:S(2)}, u32[]{:S(2)}) %collective-permute-start.1) | collective-permute-done | bytes 131104 | tf_op jit(solution)/shard_map/ppermute | solution.py:17
  40.7 5.6 %collective-permute-start.2 = (bf16[256,256]{1,0:T(8,128)(2,1)S(1)}, bf16[256,256]{1,0:T(8,128)(2,1)S(1)}, u32[]{:S(2)}, u32[]{:S(2)}) collective-permute-start(bf16[256,256]{1,0:T(8,128)(2,1)S(1)} %collective-permute-done.1), channel_id=1, source_target_pairs={{0,16},{8,24},{16,32},{24,40},{32,48},{40,56},{48,64},{56,72},{64,... | collective-permute-start | bytes 393224 | tf_op jit(solution)/shard_map/ppermute | solution.py:17
  47.0 5.1 %collective-permute-start.10 = (bf16[256,576]{0,1:T(8,128)(2,1)S(1)}, bf16[256,576]{0,1:T(8,128)(2,1)S(1)}, u32[]{:S(2)}, u32[]{:S(2)}) collective-permute-start(bf16[256,576]{0,1:T(8,128)(2,1)S(1)} %collective-permute-done.9), channel_id=1, source_target_pairs={{0,7},{1,0},{2,1},{3,2},{4,3},{5,4},{6,5},{7,6},{8,15},{9,8},{10,9... | collective-permute-start | bytes 884744 | tf_op jit(solution)/shard_map/ppermute | solution.py:22
  52.1 1.9 collective-permute-start.13
  54.1 2.9 %collective-permute-start.3 = (bf16[256,256]{1,0:T(8,128)(2,1)S(1)}, bf16[256,256]{1,0:T(8,128)(2,1)S(1)}, u32[]{:S(2)}, u32[]{:S(2)}) collective-permute-start(bf16[256,256]{1,0:T(8,128)(2,1)S(1)} %collective-permute-done.2), channel_id=1, source_target_pairs={{0,16},{8,24},{16,32},{24,40},{32,48},{40,56},{48,64},{56,72},{64,... | collective-permute-start | bytes 393224 | tf_op jit(solution)/shard_map/ppermute | solution.py:17
  57.7 3.4 %collective-permute-done.3 = bf16[256,256]{1,0:T(8,128)(2,1)S(1)} collective-permute-done((bf16[256,256]{1,0:T(8,128)(2,1)S(1)}, bf16[256,256]{1,0:T(8,128)(2,1)S(1)}, u32[]{:S(2)}, u32[]{:S(2)}) %collective-permute-start.3) | collective-permute-done | bytes 131104 | tf_op jit(solution)/shard_map/ppermute | solution.py:17
  61.2 4.8 %collective-permute-start.4 = (bf16[256,256]{1,0:T(8,128)(2,1)S(1)}, bf16[256,256]{1,0:T(8,128)(2,1)S(1)}, u32[]{:S(2)}, u32[]{:S(2)}) collective-permute-start(bf16[256,256]{1,0:T(8,128)(2,1)S(1)} %collective-permute-done.3), channel_id=1, source_target_pairs={{0,16},{8,24},{16,32},{24,40},{32,48},{40,56},{48,64},{56,72},{64,... | collective-permute-start | bytes 393224 | tf_op jit(solution)/shard_map/ppermute | solution.py:17
  66.7 5.0 %collective-permute-start.11 = (bf16[256,576]{0,1:T(8,128)(2,1)S(1)}, bf16[256,576]{0,1:T(8,128)(2,1)S(1)}, u32[]{:S(2)}, u32[]{:S(2)}) collective-permute-start(bf16[256,576]{0,1:T(8,128)(2,1)S(1)} %collective-permute-done.10), channel_id=1, source_target_pairs={{0,7},{1,0},{2,1},{3,2},{4,3},{5,4},{6,5},{7,6},{8,15},{9,8},{10,9... | collective-permute-start | bytes 884744 | tf_op jit(solution)/shard_map/ppermute | solution.py:22
  71.7 1.9 collective-permute-start.14
  73.7 3.1 %collective-permute-start.5 = (bf16[256,256]{1,0:T(8,128)(2,1)S(1)}, bf16[256,256]{1,0:T(8,128)(2,1)S(1)}, u32[]{:S(2)}, u32[]{:S(2)}) collective-permute-start(bf16[256,256]{1,0:T(8,128)(2,1)S(1)} %collective-permute-done.4), channel_id=1, source_target_pairs={{0,16},{8,24},{16,32},{24,40},{32,48},{40,56},{48,64},{56,72},{64,... | collective-permute-start | bytes 393224 | tf_op jit(solution)/shard_map/ppermute | solution.py:17
  77.5 4.0 %collective-permute-done.5 = bf16[256,256]{1,0:T(8,128)(2,1)S(1)} collective-permute-done((bf16[256,256]{1,0:T(8,128)(2,1)S(1)}, bf16[256,256]{1,0:T(8,128)(2,1)S(1)}, u32[]{:S(2)}, u32[]{:S(2)}) %collective-permute-start.5) | collective-permute-done | bytes 131104 | tf_op jit(solution)/shard_map/ppermute | solution.py:17
  81.5 3.9 %collective-permute-start.6 = (bf16[256,256]{1,0:T(8,128)(2,1)S(1)}, bf16[256,256]{1,0:T(8,128)(2,1)S(1)}, u32[]{:S(2)}, u32[]{:S(2)}) collective-permute-start(bf16[256,256]{1,0:T(8,128)(2,1)S(1)} %collective-permute-done.5), channel_id=1, source_target_pairs={{0,16},{8,24},{16,32},{24,40},{32,48},{40,56},{48,64},{56,72},{64,... | collective-permute-start | bytes 393224 | tf_op jit(solution)/shard_map/ppermute | solution.py:17
  85.4 0.7 bitcast_dynamic-update-slice_fusion.19
  86.1 1.9 collective-permute-start.15
  88.1 0.9 collective-permute-done.6
  89.0 5.6 %collective-permute-start.7 = (bf16[256,256]{1,0:T(8,128)(2,1)S(1)}, bf16[256,256]{1,0:T(8,128)(2,1)S(1)}, u32[]{:S(2)}, u32[]{:S(2)}) collective-permute-start(bf16[256,256]{1,0:T(8,128)(2,1)S(1)} %collective-permute-done.6), channel_id=1, source_target_pairs={{0,16},{8,24},{16,32},{24,40},{32,48},{40,56},{48,64},{56,72},{64,... | collective-permute-start | bytes 393224 | tf_op jit(solution)/shard_map/ppermute | solution.py:17
  94.6 0.7 bitcast_dynamic-update-slice_fusion.17
  95.3 1.8 collective-permute-done.7
  97.1 0.7 bitcast_dynamic-update-slice_fusion.15
  97.8 2.1 collective-permute-start.8
  100.5 2.3 collective-permute-done.8
  102.7 1.1 constant_dynamic-update-slice_fusion
  103.8 6.6 %fusion.5 = (f32[2,256]{1,0:T(2,128)S(1)}, f32[4608,256,2]{1,0,2:T(8,128)}) fusion(pred[256,4608]{0,1:T(8,128)(4,1)S(1)} %fusion.10, bf16[256,2,128]{2,1,0:T(2,128)(2,1)S(1)} %copy-done.2, bf16[4608,256]{1,0:T(8,128)(2,1)} %bitcast.11), kind=kOutput, calls=%fused_computation.10 | convolution fusion | flops 613416448 | bytes 11929600 | tf_op jit(solution)/shard_map/qgrd,kgd->grqk/dot_general | solution.py:52
  110.4 2.7 %fusion.15 = bf16[256,256]{0,1:T(8,128)(2,1)S(1)} fusion(bf16[256,4608]{0,1:T(8,128)(2,1)S(1)} %bitcast.181, bf16[1,256,4608]{1,2,0:T(8,128)(2,1)} %all-gather.3.cloned.1.call-done), kind=kOutput, calls=%fused_computation.24 | convolution fusion | flops 604045312 | bytes 4849664 | tf_op jit(solution)/shard_map/dot_general | solution.py:94
  113.2 6.3 %fusion.2 = (f32[2,256]{1,0:T(2,128)S(1)}, f32[4608,256,2]{1,0,2:T(8,128)S(1)}) fusion(f32[2,256]{1,0:T(2,128)S(1)} %get-tuple-element.40, f32[4608,256,2]{1,0,2:T(8,128)} %get-tuple-element.41, pred[256,4608]{0,1:T(8,128)(4,1)S(1)} %fusion.10, bf16[256,2,128]{0,2,1:T(8,128)(2,1)S(1)} %bitcast.196, bf16[4608,256]{1,0:T(8,128)(2,1)} %bitcast.11), kind=kOutput, calls=%fused_computation.6 | convolution fusion | flops 618135040 | bytes 21368832 | tf_op jit(solution)/shard_map/qgrd,kgd->grqk/dot_general | solution.py:62
  119.9 4.6 %fusion.6 = bf16[2,256,4608]{1,2,0:T(8,128)(2,1)S(1)} fusion(f32[4608,256,2]{1,0,2:T(8,128)S(1)} %bitcast.179, f32[4608,256,2]{1,0,2:T(8,128)S(1)} %get-tuple-element.43, f32[2,256]{1,0:T(2,128)S(1)} %get-tuple-element.42, f32[2,256]{1,0:T(2,128)S(1)} %get-tuple-element.40, pred[256,4608]{0,1:T(8,128)(4,1)S(1)} %fusion.10), kind=kLoop, calls=%fused_computation.13 | loop fusion | flops 25952256 | bytes 24776704 | tf_op jit(solution)/shard_map/reshape.12
  124.5 2.2 convolution_convert_fusion
  126.7 1.4 convolution_bitcast_fusion.1
  128.1 2.8 %convolution_bitcast_fusion = f32[4608,128]{1,0:T(8,128)S(1)} fusion(bf16[256,2,128]{0,2,1:T(8,128)(2,1)S(1)} %bitcast.197, f32[4608,256,2]{1,0,2:T(8,128)S(1)} %bitcast.179, f32[2,256]{1,0:T(2,128)S(1)} %get-tuple-element.40, pred[256,4608]{0,1:T(8,128)(4,1)S(1)} %fusion.10), kind=kOutput, calls=%fused_computation.11 | convolution fusion | flops 615776256 | bytes 13109248 | tf_op jit(solution)/shard_map/grqk,qgrd->kgd/dot_general | solution.py:59
  131.6 2.0 collective-permute-start.16
  133.6 4.4 %collective-permute-done.16 = f32[9,256,256]{2,1,0:T(8,128)S(1)} collective-permute-done((f32[9,256,256]{2,1,0:T(8,128)S(1)}, f32[9,256,256]{2,1,0:T(8,128)S(1)}, u32[]{:S(2)}, u32[]{:S(2)}) %collective-permute-start.16) | collective-permute-done | bytes 2359328 | tf_op jit(solution)/shard_map/ppermute | solution.py:155
  138.4 0.7 slice_bitcast_fusion.5
  139.1 1.9 collective-permute-start.17
  141.0 10.2 %collective-permute-done.17 = f32[256,256]{1,0:T(8,128)S(1)} collective-permute-done((f32[256,256]{1,0:T(8,128)S(1)}, f32[256,256]{1,0:T(8,128)S(1)}, u32[]{:S(2)}, u32[]{:S(2)}) %collective-permute-start.17) | collective-permute-done | bytes 262176 | tf_op jit(solution)/shard_map/ppermute | solution.py:17
  151.3 1.9 collective-permute-start.18
  153.2 8.9 %collective-permute-done.18 = f32[256,256]{1,0:T(8,128)S(1)} collective-permute-done((f32[256,256]{1,0:T(8,128)S(1)}, f32[256,256]{1,0:T(8,128)S(1)}, u32[]{:S(2)}, u32[]{:S(2)}) %collective-permute-start.18) | collective-permute-done | bytes 262176 | tf_op jit(solution)/shard_map/ppermute | solution.py:17
  162.2 1.9 collective-permute-start.19
  164.1 8.1 %collective-permute-done.19 = f32[256,256]{1,0:T(8,128)S(1)} collective-permute-done((f32[256,256]{1,0:T(8,128)S(1)}, f32[256,256]{1,0:T(8,128)S(1)}, u32[]{:S(2)}, u32[]{:S(2)}) %collective-permute-start.19) | collective-permute-done | bytes 262176 | tf_op jit(solution)/shard_map/ppermute | solution.py:17
  172.3 1.9 collective-permute-start.20
  174.3 2.4 %collective-permute-start.21 = (bf16[256,256]{1,0:T(8,128)(2,1)S(1)}, bf16[256,256]{1,0:T(8,128)(2,1)S(1)}, u32[]{:S(2)}, u32[]{:S(2)}) collective-permute-start(bf16[256,256]{1,0:T(8,128)(2,1)S(1)} %copy.26), channel_id=1, source_target_pairs={{192,0},{384,192},{576,384},{193,1},{385,193},{577,385},{194,2},{3... | collective-permute-start | bytes 393224 | tf_op jit(solution)/shard_map/ppermute | solution.py:17
  176.7 5.0 %collective-permute-done.20 = f32[256,256]{1,0:T(8,128)S(1)} collective-permute-done((f32[256,256]{1,0:T(8,128)S(1)}, f32[256,256]{1,0:T(8,128)S(1)}, u32[]{:S(2)}, u32[]{:S(2)}) %collective-permute-start.20) | collective-permute-done | bytes 262176 | tf_op jit(solution)/shard_map/ppermute | solution.py:17
  181.8 1.9 collective-permute-start.22
  183.7 7.5 %collective-permute-done.22 = f32[256,256]{1,0:T(8,128)S(1)} collective-permute-done((f32[256,256]{1,0:T(8,128)S(1)}, f32[256,256]{1,0:T(8,128)S(1)}, u32[]{:S(2)}, u32[]{:S(2)}) %collective-permute-start.22) | collective-permute-done | bytes 262176 | tf_op jit(solution)/shard_map/ppermute | solution.py:17
  191.3 1.9 collective-permute-start.23
  193.2 7.5 %collective-permute-done.23 = f32[256,256]{1,0:T(8,128)S(1)} collective-permute-done((f32[256,256]{1,0:T(8,128)S(1)}, f32[256,256]{1,0:T(8,128)S(1)}, u32[]{:S(2)}, u32[]{:S(2)}) %collective-permute-start.23) | collective-permute-done | bytes 262176 | tf_op jit(solution)/shard_map/ppermute | solution.py:17
  200.8 1.9 collective-permute-start.24
  202.8 2.4 %collective-permute-start.27 = (bf16[256,576]{0,1:T(8,128)(2,1)S(1)}, bf16[256,576]{0,1:T(8,128)(2,1)S(1)}, u32[]{:S(2)}, u32[]{:S(2)}) collective-permute-start(bf16[256,576]{0,1:T(8,128)(2,1)S(1)} %bitcast.186), channel_id=1, source_target_pairs={{192,0},{384,192},{576,384},{193,1},{385,193},{577,385},{194,2},{3... | collective-permute-start | bytes 884744 | tf_op jit(solution)/shard_map/ppermute | solution.py:17
  205.2 2.4 %collective-permute-start.26 = (f32[256,256]{1,0:T(8,128)}, f32[256,256]{1,0:T(8,128)S(1)}, u32[]{:S(2)}, u32[]{:S(2)}) collective-permute-start(f32[256,256]{1,0:T(8,128)} %get-tuple-element.16), channel_id=1, source_target_pairs={{192,0},{384,192},{576,384},{193,1},{385,193},{577,385},{194,2},{3... | collective-permute-start | bytes 786440 | tf_op jit(solution)/shard_map/ppermute | solution.py:17
  207.6 3.8 %collective-permute-done.24 = f32[256,256]{1,0:T(8,128)S(1)} collective-permute-done((f32[256,256]{1,0:T(8,128)S(1)}, f32[256,256]{1,0:T(8,128)S(1)}, u32[]{:S(2)}, u32[]{:S(2)}) %collective-permute-start.24) | collective-permute-done | bytes 262176 | tf_op jit(solution)/shard_map/ppermute | solution.py:17
  211.4 1.9 collective-permute-start.25
  213.3 0.9 collective-permute-done.27
  214.2 2.8 %collective-permute-done.26 = f32[256,256]{1,0:T(8,128)S(1)} collective-permute-done((f32[256,256]{1,0:T(8,128)}, f32[256,256]{1,0:T(8,128)S(1)}, u32[]{:S(2)}, u32[]{:S(2)}) %collective-permute-start.26) | collective-permute-done | bytes 262176 | tf_op jit(solution)/shard_map/ppermute | solution.py:17
  217.0 4.8 %collective-permute-done.25 = f32[256,256]{1,0:T(8,128)S(1)} collective-permute-done((f32[256,256]{1,0:T(8,128)S(1)}, f32[256,256]{1,0:T(8,128)S(1)}, u32[]{:S(2)}, u32[]{:S(2)}) %collective-permute-start.25) | collective-permute-done | bytes 262176 | tf_op jit(solution)/shard_map/ppermute | solution.py:167
  (85 shorter events, 9.2 us)
Async XLA Ops:
  7.2 103.3 %all-gather.3.cloned.1.call-start = ((), (), s32[]{:S(2)}) async-start(), calls=%async_computation | async-start | bytes 2457600 | tf_op jit(solution)/shard_map/all_gather | solution.py:96
  7.2 39.7 %collective-permute-start.9 = (bf16[256,576]{0,1:T(8,128)(2,1)}, bf16[256,576]{0,1:T(8,128)(2,1)S(1)}, u32[]{:S(2)}, u32[]{:S(2)}) collective-permute-start(bf16[256,576]{0,1:T(8,128)(2,1)} %bitcast.184), channel_id=1, source_target_pairs={{0,7},{1,0},{2,1},{3,2},{4,3},{5,4},{6,5},{7,6},{8,15},{9,8},{10,9... | collective-permute-start | bytes 884744 | tf_op jit(solution)/shard_map/ppermute | solution.py:22
  12.6 39.5 %collective-permute-start.12 = (bf16[256,576]{0,1:T(8,128)(2,1)}, bf16[256,576]{0,1:T(8,128)(2,1)S(1)}, u32[]{:S(2)}, u32[]{:S(2)}) collective-permute-start(bf16[256,576]{0,1:T(8,128)(2,1)} %bitcast.185), channel_id=1, source_target_pairs={{0,1},{1,2},{2,3},{3,4},{4,5},{5,6},{6,7},{7,0},{8,9},{9,10},{10,1... | collective-permute-start | bytes 884744 | tf_op jit(solution)/shard_map/ppermute | solution.py:22
  15.4 17.3 %collective-permute-start = (bf16[256,256]{1,0:T(8,128)(2,1)S(1)}, bf16[256,256]{1,0:T(8,128)(2,1)S(1)}, u32[]{:S(2)}, u32[]{:S(2)}) collective-permute-start(bf16[256,256]{1,0:T(8,128)(2,1)S(1)} %pad_maximum_fusion), channel_id=1, source_target_pairs={{0,16},{8,24},{16,32},{24,40},{32,48},{40,56},{48,64},{56,72},{64,... | collective-permute-start | bytes 393224 | tf_op jit(solution)/shard_map/ppermute | solution.py:17
  23.8 76.2 %copy-start = (bf16[1,256,576]{1,2,0:T(8,128)(2,1)S(1)}, bf16[1,256,576]{1,2,0:T(8,128)(2,1)}, u32[]{:S(2)}) copy-start(bf16[1,256,576]{1,2,0:T(8,128)(2,1)} %param.7) | copy-start | bytes 884740
  32.7 8.0 %collective-permute-start.1 = (bf16[256,256]{1,0:T(8,128)(2,1)S(1)}, bf16[256,256]{1,0:T(8,128)(2,1)S(1)}, u32[]{:S(2)}, u32[]{:S(2)}) collective-permute-start(bf16[256,256]{1,0:T(8,128)(2,1)S(1)} %collective-permute-done), channel_id=1, source_target_pairs={{0,16},{8,24},{16,32},{24,40},{32,48},{40,56},{48,64},{56,72},{64,... | collective-permute-start | bytes 393224 | tf_op jit(solution)/shard_map/ppermute | solution.py:17
  40.7 13.4 %collective-permute-start.2 = (bf16[256,256]{1,0:T(8,128)(2,1)S(1)}, bf16[256,256]{1,0:T(8,128)(2,1)S(1)}, u32[]{:S(2)}, u32[]{:S(2)}) collective-permute-start(bf16[256,256]{1,0:T(8,128)(2,1)S(1)} %collective-permute-done.1), channel_id=1, source_target_pairs={{0,16},{8,24},{16,32},{24,40},{32,48},{40,56},{48,64},{56,72},{64,... | collective-permute-start | bytes 393224 | tf_op jit(solution)/shard_map/ppermute | solution.py:17
  47.0 19.8 %collective-permute-start.10 = (bf16[256,576]{0,1:T(8,128)(2,1)S(1)}, bf16[256,576]{0,1:T(8,128)(2,1)S(1)}, u32[]{:S(2)}, u32[]{:S(2)}) collective-permute-start(bf16[256,576]{0,1:T(8,128)(2,1)S(1)} %collective-permute-done.9), channel_id=1, source_target_pairs={{0,7},{1,0},{2,1},{3,2},{4,3},{5,4},{6,5},{7,6},{8,15},{9,8},{10,9... | collective-permute-start | bytes 884744 | tf_op jit(solution)/shard_map/ppermute | solution.py:22
  52.1 19.6 %collective-permute-start.13 = (bf16[256,576]{0,1:T(8,128)(2,1)S(1)}, bf16[256,576]{0,1:T(8,128)(2,1)S(1)}, u32[]{:S(2)}, u32[]{:S(2)}) collective-permute-start(bf16[256,576]{0,1:T(8,128)(2,1)S(1)} %collective-permute-done.12), channel_id=1, source_target_pairs={{0,1},{1,2},{2,3},{3,4},{4,5},{5,6},{6,7},{7,0},{8,9},{9,10},{10,1... | collective-permute-start | bytes 884744 | tf_op jit(solution)/shard_map/ppermute | solution.py:22
  54.1 7.1 %collective-permute-start.3 = (bf16[256,256]{1,0:T(8,128)(2,1)S(1)}, bf16[256,256]{1,0:T(8,128)(2,1)S(1)}, u32[]{:S(2)}, u32[]{:S(2)}) collective-permute-start(bf16[256,256]{1,0:T(8,128)(2,1)S(1)} %collective-permute-done.2), channel_id=1, source_target_pairs={{0,16},{8,24},{16,32},{24,40},{32,48},{40,56},{48,64},{56,72},{64,... | collective-permute-start | bytes 393224 | tf_op jit(solution)/shard_map/ppermute | solution.py:17
  61.2 12.5 %collective-permute-start.4 = (bf16[256,256]{1,0:T(8,128)(2,1)S(1)}, bf16[256,256]{1,0:T(8,128)(2,1)S(1)}, u32[]{:S(2)}, u32[]{:S(2)}) collective-permute-start(bf16[256,256]{1,0:T(8,128)(2,1)S(1)} %collective-permute-done.3), channel_id=1, source_target_pairs={{0,16},{8,24},{16,32},{24,40},{32,48},{40,56},{48,64},{56,72},{64,... | collective-permute-start | bytes 393224 | tf_op jit(solution)/shard_map/ppermute | solution.py:17
  66.7 21.3 %collective-permute-start.11 = (bf16[256,576]{0,1:T(8,128)(2,1)S(1)}, bf16[256,576]{0,1:T(8,128)(2,1)S(1)}, u32[]{:S(2)}, u32[]{:S(2)}) collective-permute-start(bf16[256,576]{0,1:T(8,128)(2,1)S(1)} %collective-permute-done.10), channel_id=1, source_target_pairs={{0,7},{1,0},{2,1},{3,2},{4,3},{5,4},{6,5},{7,6},{8,15},{9,8},{10,9... | collective-permute-start | bytes 884744 | tf_op jit(solution)/shard_map/ppermute | solution.py:22
  71.7 14.4 %collective-permute-start.14 = (bf16[256,576]{0,1:T(8,128)(2,1)S(1)}, bf16[256,576]{0,1:T(8,128)(2,1)S(1)}, u32[]{:S(2)}, u32[]{:S(2)}) collective-permute-start(bf16[256,576]{0,1:T(8,128)(2,1)S(1)} %collective-permute-done.13), channel_id=1, source_target_pairs={{0,1},{1,2},{2,3},{3,4},{4,5},{5,6},{6,7},{7,0},{8,9},{9,10},{10,1... | collective-permute-start | bytes 884744 | tf_op jit(solution)/shard_map/ppermute | solution.py:22
  73.7 7.8 %collective-permute-start.5 = (bf16[256,256]{1,0:T(8,128)(2,1)S(1)}, bf16[256,256]{1,0:T(8,128)(2,1)S(1)}, u32[]{:S(2)}, u32[]{:S(2)}) collective-permute-start(bf16[256,256]{1,0:T(8,128)(2,1)S(1)} %collective-permute-done.4), channel_id=1, source_target_pairs={{0,16},{8,24},{16,32},{24,40},{32,48},{40,56},{48,64},{56,72},{64,... | collective-permute-start | bytes 393224 | tf_op jit(solution)/shard_map/ppermute | solution.py:17
  81.5 7.5 %collective-permute-start.6 = (bf16[256,256]{1,0:T(8,128)(2,1)S(1)}, bf16[256,256]{1,0:T(8,128)(2,1)S(1)}, u32[]{:S(2)}, u32[]{:S(2)}) collective-permute-start(bf16[256,256]{1,0:T(8,128)(2,1)S(1)} %collective-permute-done.5), channel_id=1, source_target_pairs={{0,16},{8,24},{16,32},{24,40},{32,48},{40,56},{48,64},{56,72},{64,... | collective-permute-start | bytes 393224 | tf_op jit(solution)/shard_map/ppermute | solution.py:17
  86.1 13.8 %collective-permute-start.15 = (bf16[256,576]{0,1:T(8,128)(2,1)S(1)}, bf16[256,576]{0,1:T(8,128)(2,1)S(1)}, u32[]{:S(2)}, u32[]{:S(2)}) collective-permute-start(bf16[256,576]{0,1:T(8,128)(2,1)S(1)} %collective-permute-done.14), channel_id=1, source_target_pairs={{0,1},{1,2},{2,3},{3,4},{4,5},{5,6},{6,7},{7,0},{8,9},{9,10},{10,1... | collective-permute-start | bytes 884744 | tf_op jit(solution)/shard_map/ppermute | solution.py:22
  89.0 8.1 %collective-permute-start.7 = (bf16[256,256]{1,0:T(8,128)(2,1)S(1)}, bf16[256,256]{1,0:T(8,128)(2,1)S(1)}, u32[]{:S(2)}, u32[]{:S(2)}) collective-permute-start(bf16[256,256]{1,0:T(8,128)(2,1)S(1)} %collective-permute-done.6), channel_id=1, source_target_pairs={{0,16},{8,24},{16,32},{24,40},{32,48},{40,56},{48,64},{56,72},{64,... | collective-permute-start | bytes 393224 | tf_op jit(solution)/shard_map/ppermute | solution.py:17
  97.8 4.9 %collective-permute-start.8 = (bf16[9,256,256]{2,1,0:T(8,128)(2,1)}, bf16[9,256,256]{2,1,0:T(8,128)(2,1)S(1)}, u32[]{:S(2)}, u32[]{:S(2)}) collective-permute-start(bf16[9,256,256]{2,1,0:T(8,128)(2,1)} %get-tuple-element.20), channel_id=1, source_target_pairs={{0,8},{8,0},{16,24},{24,16},{32,40},{40,32},{48,56},{56,48},{64,72... | collective-permute-start | bytes 3538952 | tf_op jit(solution)/shard_map/ppermute | solution.py:122
  100.2 3.7 %copy-start.2 = (bf16[256,2,128]{2,1,0:T(2,128)(2,1)S(1)}, bf16[256,2,128]{2,1,0:T(2,128)(2,1)}, u32[]{:S(2)}) copy-start(bf16[256,2,128]{2,1,0:T(2,128)(2,1)} %reshape.261) | copy-start | bytes 393220
  113.1 6.3 %slice-start = ((s8[9437184]{0:T(1024)(128)(4,1)}), s8[4194304]{0:T(1024)(128)(4,1)S(1)}, s32[]{:S(2)}) async-start(s8[9437184]{0:T(1024)(128)(4,1)} %bitcast.178), calls=%async_computation.1 | async-start | bytes 8388608
  113.1 6.6 %slice-start.1 = ((s8[9437184]{0:T(1024)(128)(4,1)}), s8[4194304]{0:T(1024)(128)(4,1)S(1)}, s32[]{:S(2)}) async-start(s8[9437184]{0:T(1024)(128)(4,1)} %bitcast.178), calls=%async_computation.2 | async-start | bytes 8388608
  113.2 6.8 %slice-start.2 = ((s8[9437184]{0:T(1024)(128)(4,1)}), s8[1048576]{0:T(1024)(128)(4,1)S(1)}, s32[]{:S(2)}) async-start(s8[9437184]{0:T(1024)(128)(4,1)} %bitcast.178), calls=%async_computation.3 | async-start | bytes 2097152
  124.5 2.2 copy-start.3
  131.6 6.4 %collective-permute-start.16 = (f32[9,256,256]{2,1,0:T(8,128)S(1)}, f32[9,256,256]{2,1,0:T(8,128)S(1)}, u32[]{:S(2)}, u32[]{:S(2)}) collective-permute-start(f32[9,256,256]{2,1,0:T(8,128)S(1)} %bitcast.182), channel_id=1, source_target_pairs={{0,8},{8,0},{16,24},{24,16},{32,40},{40,32},{48,56},{56,48},{64,72... | collective-permute-start | bytes 7077896 | tf_op jit(solution)/shard_map/ppermute | solution.py:155
  138.3 64.4 %copy-start.1 = (bf16[1,256,576]{1,2,0:T(8,128)(2,1)S(1)}, bf16[1,256,576]{1,2,0:T(8,128)(2,1)}, u32[]{:S(2)}) copy-start(bf16[1,256,576]{1,2,0:T(8,128)(2,1)} %param.7) | copy-start | bytes 884740
  139.1 12.1 %collective-permute-start.17 = (f32[256,256]{1,0:T(8,128)S(1)}, f32[256,256]{1,0:T(8,128)S(1)}, u32[]{:S(2)}, u32[]{:S(2)}) collective-permute-start(f32[256,256]{1,0:T(8,128)S(1)} %get-tuple-element.17), channel_id=1, source_target_pairs={{16,0},{24,8},{32,16},{40,24},{48,32},{56,40},{64,48},{72,56},{80,... | collective-permute-start | bytes 786440 | tf_op jit(solution)/shard_map/ppermute | solution.py:17
  151.3 10.9 %collective-permute-start.18 = (f32[256,256]{1,0:T(8,128)S(1)}, f32[256,256]{1,0:T(8,128)S(1)}, u32[]{:S(2)}, u32[]{:S(2)}) collective-permute-start(f32[256,256]{1,0:T(8,128)S(1)} %fusion.25), channel_id=1, source_target_pairs={{16,0},{24,8},{32,16},{40,24},{48,32},{56,40},{64,48},{72,56},{80,... | collective-permute-start | bytes 786440 | tf_op jit(solution)/shard_map/ppermute | solution.py:17
  162.2 10.0 %collective-permute-start.19 = (f32[256,256]{1,0:T(8,128)S(1)}, f32[256,256]{1,0:T(8,128)S(1)}, u32[]{:S(2)}, u32[]{:S(2)}) collective-permute-start(f32[256,256]{1,0:T(8,128)S(1)} %fusion.24), channel_id=1, source_target_pairs={{16,0},{24,8},{32,16},{40,24},{48,32},{56,40},{64,48},{72,56},{80,... | collective-permute-start | bytes 786440 | tf_op jit(solution)/shard_map/ppermute | solution.py:17
  172.3 9.5 %collective-permute-start.20 = (f32[256,256]{1,0:T(8,128)S(1)}, f32[256,256]{1,0:T(8,128)S(1)}, u32[]{:S(2)}, u32[]{:S(2)}) collective-permute-start(f32[256,256]{1,0:T(8,128)S(1)} %fusion.23), channel_id=1, source_target_pairs={{16,0},{24,8},{32,16},{40,24},{48,32},{56,40},{64,48},{72,56},{80,... | collective-permute-start | bytes 786440 | tf_op jit(solution)/shard_map/ppermute | solution.py:17
  174.3 7.5 %collective-permute-start.21 = (bf16[256,256]{1,0:T(8,128)(2,1)S(1)}, bf16[256,256]{1,0:T(8,128)(2,1)S(1)}, u32[]{:S(2)}, u32[]{:S(2)}) collective-permute-start(bf16[256,256]{1,0:T(8,128)(2,1)S(1)} %copy.26), channel_id=1, source_target_pairs={{192,0},{384,192},{576,384},{193,1},{385,193},{577,385},{194,2},{3... | collective-permute-start | bytes 393224 | tf_op jit(solution)/shard_map/ppermute | solution.py:17
  181.8 9.5 %collective-permute-start.22 = (f32[256,256]{1,0:T(8,128)S(1)}, f32[256,256]{1,0:T(8,128)S(1)}, u32[]{:S(2)}, u32[]{:S(2)}) collective-permute-start(f32[256,256]{1,0:T(8,128)S(1)} %fusion.22), channel_id=1, source_target_pairs={{16,0},{24,8},{32,16},{40,24},{48,32},{56,40},{64,48},{72,56},{80,... | collective-permute-start | bytes 786440 | tf_op jit(solution)/shard_map/ppermute | solution.py:17
  191.3 9.5 %collective-permute-start.23 = (f32[256,256]{1,0:T(8,128)S(1)}, f32[256,256]{1,0:T(8,128)S(1)}, u32[]{:S(2)}, u32[]{:S(2)}) collective-permute-start(f32[256,256]{1,0:T(8,128)S(1)} %fusion.21), channel_id=1, source_target_pairs={{16,0},{24,8},{32,16},{40,24},{48,32},{56,40},{64,48},{72,56},{80,... | collective-permute-start | bytes 786440 | tf_op jit(solution)/shard_map/ppermute | solution.py:17
  200.8 10.5 %collective-permute-start.24 = (f32[256,256]{1,0:T(8,128)S(1)}, f32[256,256]{1,0:T(8,128)S(1)}, u32[]{:S(2)}, u32[]{:S(2)}) collective-permute-start(f32[256,256]{1,0:T(8,128)S(1)} %fusion.20), channel_id=1, source_target_pairs={{16,0},{24,8},{32,16},{40,24},{48,32},{56,40},{64,48},{72,56},{80,... | collective-permute-start | bytes 786440 | tf_op jit(solution)/shard_map/ppermute | solution.py:17
  202.8 11.4 %collective-permute-start.27 = (bf16[256,576]{0,1:T(8,128)(2,1)S(1)}, bf16[256,576]{0,1:T(8,128)(2,1)S(1)}, u32[]{:S(2)}, u32[]{:S(2)}) collective-permute-start(bf16[256,576]{0,1:T(8,128)(2,1)S(1)} %bitcast.186), channel_id=1, source_target_pairs={{192,0},{384,192},{576,384},{193,1},{385,193},{577,385},{194,2},{3... | collective-permute-start | bytes 884744 | tf_op jit(solution)/shard_map/ppermute | solution.py:17
  205.2 11.8 %collective-permute-start.26 = (f32[256,256]{1,0:T(8,128)}, f32[256,256]{1,0:T(8,128)S(1)}, u32[]{:S(2)}, u32[]{:S(2)}) collective-permute-start(f32[256,256]{1,0:T(8,128)} %get-tuple-element.16), channel_id=1, source_target_pairs={{192,0},{384,192},{576,384},{193,1},{385,193},{577,385},{194,2},{3... | collective-permute-start | bytes 786440 | tf_op jit(solution)/shard_map/ppermute | solution.py:17
  211.4 10.4 %collective-permute-start.25 = (f32[256,256]{1,0:T(8,128)S(1)}, f32[256,256]{1,0:T(8,128)S(1)}, u32[]{:S(2)}, u32[]{:S(2)}) collective-permute-start(f32[256,256]{1,0:T(8,128)S(1)} %fusion.19), channel_id=1, source_target_pairs={{208,0},{216,8},{224,16},{232,24},{240,32},{248,40},{256,48},{264,... | collective-permute-start | bytes 786440 | tf_op jit(solution)/shard_map/ppermute | solution.py:167
Sparse Core Ops, SparseCore 0:
  21.1 58.8 all-gather.2

commit v9 on v8

--- a/solution.py
+++ b/solution.py
@@ -158,7 +158,9 @@
     for step in range(1, hops):
         running = from_behind(running, "row", -2) + chip_sum[hops - step]
         if step == hops // 2:
-            running, query_handed = lax.optimization_barrier((running, query_handed))
+            running, query_handed, own_handed = lax.optimization_barrier(
+                (running, query_handed, own_handed)
+            )
     last_pairs = [
         (p * row_count + r, (p - 1) * row_count + r - 2)
         for p in range(1, pipe_count)

time: 232 us -> 236 us (1.017)
  the two profiles are of different devices: /device:TPU:196 before, /device:TPU:194 now
where the time goes in v9:
time: 236 us; the launch traced here: 235 us
  starting transfers between devices  84.8 us (36%)
  waiting for transfers between devices  83 us (35%)
  matrix products  21.9 us (9%)
  local copies, waits for them, and re-layouts  15.9 us (7%)
  between operations  14.8 us (6%)
  other arithmetic  14.2 us (6%)
    ppermute x18, waiting for transfers between devices, from_behind(): return lax.ppermute(block, axis, route)  69.1 us
    ppermute x18, starting transfers between devices, from_behind(): return lax.ppermute(block, axis, route)  55.6 us
    ppermute x7, starting transfers between devices, cyclic_shift(): lax.ppermute(block, axis, [(i, (i + distance) % size) for i in range(size)])  23.2 us
    unnamed x40, local copies, waits for them, and re-layouts  8.47 us
    ppermute x1, waiting for transfers between devices, per_device(): total = lax.ppermute(running, ('pipe', 'row'), last_pairs) + own_handed  7.22 us
    dot_general x1, matrix products, attend(): jnp.einsum('qgrd,kgd->grqk', query_g, key_g, preferred_element_type=jnp.f...  6.6 us
    dot_general x1, matrix products, attend(): jnp.einsum('qgrd,kgd->grqk', attn_g, value_g, preferred_element_type=jnp....  6.28 us
    another operation x2, other arithmetic  5.56 us
  transfers between devices with their start and end apart: 29, of which 17 were waited for; matrix products, arithmetic and copies ran while one was open for 11% of the time, Pallas kernels for 0%

profile of v9, /device:TPU:194, one launch (start us, length us, event | category | flops | bytes accessed | tf_op | source)
XLA Modules:
  0.0 234.6 jit_solution(16874428295550108006)
XLA Ops:
  7.2 5.4 %collective-permute-start.9 = (bf16[256,576]{0,1:T(8,128)(2,1)}, bf16[256,576]{0,1:T(8,128)(2,1)S(1)}, u32[]{:S(2)}, u32[]{:S(2)}) collective-permute-start(bf16[256,576]{0,1:T(8,128)(2,1)} %bitcast.184), channel_id=1, source_target_pairs={{0,7},{1,0},{2,1},{3,2},{4,3},{5,4},{6,5},{7,6},{8,15},{9,8},{10,9... | collective-permute-start | bytes 884744 | tf_op jit(solution)/shard_map/ppermute | solution.py:22
  12.6 1.9 collective-permute-start.12
  14.5 0.9 pad_maximum_fusion
  15.4 5.5 %collective-permute-start = (bf16[256,256]{1,0:T(8,128)(2,1)S(1)}, bf16[256,256]{1,0:T(8,128)(2,1)S(1)}, u32[]{:S(2)}, u32[]{:S(2)}) collective-permute-start(bf16[256,256]{1,0:T(8,128)(2,1)S(1)} %pad_maximum_fusion), channel_id=1, source_target_pairs={{0,16},{8,24},{16,32},{24,40},{32,48},{40,56},{48,64},{56,72},{64,... | collective-permute-start | bytes 393224 | tf_op jit(solution)/shard_map/ppermute | solution.py:17
  21.7 0.9 pad_dynamic-slice_fusion
  23.0 0.8 select_reduce_fusion
  23.8 4.6 %fusion.10 = pred[256,4608]{0,1:T(8,128)(4,1)S(1)} fusion(s32[256]{0:T(256)S(1)} %bitcast.194, s32[256]{0:T(256)S(1)} %iota_add_fusion.1, s32[4608]{0:T(1024)S(1)} %constant_dynamic-update-slice_fusion.6, s32[4608]{0:T(1024)S(1)} %add.94, pred[4608]{0:T(1024)(128)(4,1)S(1)} %broadcast_compare_fusion, pred[4608]{0:T(1024)(128)(4,1)S(1)} %broadcast_compare_fusion.1), kind=kLoop, calls=%fused_computation.18 | loop fusion | flops 9437184 | bytes 1227776 | tf_op jit(solution)/shard_map/and | solution.py:146
  28.5 1.6 bitcast_dynamic-update-slice_fusion.31
  30.1 1.6 reshape.261
  31.7 1.0 constant_dynamic-update-slice_fusion.3
  32.7 4.3 %collective-permute-start.1 = (bf16[256,256]{1,0:T(8,128)(2,1)S(1)}, bf16[256,256]{1,0:T(8,128)(2,1)S(1)}, u32[]{:S(2)}, u32[]{:S(2)}) collective-permute-start(bf16[256,256]{1,0:T(8,128)(2,1)S(1)} %collective-permute-done), channel_id=1, source_target_pairs={{0,16},{8,24},{16,32},{24,40},{32,48},{40,56},{48,64},{56,72},{64,... | collective-permute-start | bytes 393224 | tf_op jit(solution)/shard_map/ppermute | solution.py:17
  37.7 2.9 %collective-permute-done.1 = bf16[256,256]{1,0:T(8,128)(2,1)S(1)} collective-permute-done((bf16[256,256]{1,0:T(8,128)(2,1)S(1)}, bf16[256,256]{1,0:T(8,128)(2,1)S(1)}, u32[]{:S(2)}, u32[]{:S(2)}) %collective-permute-start.1) | collective-permute-done | bytes 131104 | tf_op jit(solution)/shard_map/ppermute | solution.py:17
  40.7 5.6 %collective-permute-start.2 = (bf16[256,256]{1,0:T(8,128)(2,1)S(1)}, bf16[256,256]{1,0:T(8,128)(2,1)S(1)}, u32[]{:S(2)}, u32[]{:S(2)}) collective-permute-start(bf16[256,256]{1,0:T(8,128)(2,1)S(1)} %collective-permute-done.1), channel_id=1, source_target_pairs={{0,16},{8,24},{16,32},{24,40},{32,48},{40,56},{48,64},{56,72},{64,... | collective-permute-start | bytes 393224 | tf_op jit(solution)/shard_map/ppermute | solution.py:17
  47.0 5.1 %collective-permute-start.10 = (bf16[256,576]{0,1:T(8,128)(2,1)S(1)}, bf16[256,576]{0,1:T(8,128)(2,1)S(1)}, u32[]{:S(2)}, u32[]{:S(2)}) collective-permute-start(bf16[256,576]{0,1:T(8,128)(2,1)S(1)} %collective-permute-done.9), channel_id=1, source_target_pairs={{0,7},{1,0},{2,1},{3,2},{4,3},{5,4},{6,5},{7,6},{8,15},{9,8},{10,9... | collective-permute-start | bytes 884744 | tf_op jit(solution)/shard_map/ppermute | solution.py:22
  52.1 1.9 collective-permute-start.13
  54.1 2.9 %collective-permute-start.3 = (bf16[256,256]{1,0:T(8,128)(2,1)S(1)}, bf16[256,256]{1,0:T(8,128)(2,1)S(1)}, u32[]{:S(2)}, u32[]{:S(2)}) collective-permute-start(bf16[256,256]{1,0:T(8,128)(2,1)S(1)} %collective-permute-done.2), channel_id=1, source_target_pairs={{0,16},{8,24},{16,32},{24,40},{32,48},{40,56},{48,64},{56,72},{64,... | collective-permute-start | bytes 393224 | tf_op jit(solution)/shard_map/ppermute | solution.py:17
  57.7 3.4 %collective-permute-done.3 = bf16[256,256]{1,0:T(8,128)(2,1)S(1)} collective-permute-done((bf16[256,256]{1,0:T(8,128)(2,1)S(1)}, bf16[256,256]{1,0:T(8,128)(2,1)S(1)}, u32[]{:S(2)}, u32[]{:S(2)}) %collective-permute-start.3) | collective-permute-done | bytes 131104 | tf_op jit(solution)/shard_map/ppermute | solution.py:17
  61.2 4.8 %collective-permute-start.4 = (bf16[256,256]{1,0:T(8,128)(2,1)S(1)}, bf16[256,256]{1,0:T(8,128)(2,1)S(1)}, u32[]{:S(2)}, u32[]{:S(2)}) collective-permute-start(bf16[256,256]{1,0:T(8,128)(2,1)S(1)} %collective-permute-done.3), channel_id=1, source_target_pairs={{0,16},{8,24},{16,32},{24,40},{32,48},{40,56},{48,64},{56,72},{64,... | collective-permute-start | bytes 393224 | tf_op jit(solution)/shard_map/ppermute | solution.py:17
  66.7 5.0 %collective-permute-start.11 = (bf16[256,576]{0,1:T(8,128)(2,1)S(1)}, bf16[256,576]{0,1:T(8,128)(2,1)S(1)}, u32[]{:S(2)}, u32[]{:S(2)}) collective-permute-start(bf16[256,576]{0,1:T(8,128)(2,1)S(1)} %collective-permute-done.10), channel_id=1, source_target_pairs={{0,7},{1,0},{2,1},{3,2},{4,3},{5,4},{6,5},{7,6},{8,15},{9,8},{10,9... | collective-permute-start | bytes 884744 | tf_op jit(solution)/shard_map/ppermute | solution.py:22
  71.7 1.9 collective-permute-start.14
  73.7 3.0 %collective-permute-start.5 = (bf16[256,256]{1,0:T(8,128)(2,1)S(1)}, bf16[256,256]{1,0:T(8,128)(2,1)S(1)}, u32[]{:S(2)}, u32[]{:S(2)}) collective-permute-start(bf16[256,256]{1,0:T(8,128)(2,1)S(1)} %collective-permute-done.4), channel_id=1, source_target_pairs={{0,16},{8,24},{16,32},{24,40},{32,48},{40,56},{48,64},{56,72},{64,... | collective-permute-start | bytes 393224 | tf_op jit(solution)/shard_map/ppermute | solution.py:17
  77.4 4.0 %collective-permute-done.5 = bf16[256,256]{1,0:T(8,128)(2,1)S(1)} collective-permute-done((bf16[256,256]{1,0:T(8,128)(2,1)S(1)}, bf16[256,256]{1,0:T(8,128)(2,1)S(1)}, u32[]{:S(2)}, u32[]{:S(2)}) %collective-permute-start.5) | collective-permute-done | bytes 131104 | tf_op jit(solution)/shard_map/ppermute | solution.py:17
  81.4 3.8 %collective-permute-start.6 = (bf16[256,256]{1,0:T(8,128)(2,1)S(1)}, bf16[256,256]{1,0:T(8,128)(2,1)S(1)}, u32[]{:S(2)}, u32[]{:S(2)}) collective-permute-start(bf16[256,256]{1,0:T(8,128)(2,1)S(1)} %collective-permute-done.5), channel_id=1, source_target_pairs={{0,16},{8,24},{16,32},{24,40},{32,48},{40,56},{48,64},{56,72},{64,... | collective-permute-start | bytes 393224 | tf_op jit(solution)/shard_map/ppermute | solution.py:17
  85.2 0.7 bitcast_dynamic-update-slice_fusion.19
  86.0 1.9 collective-permute-start.15
  87.9 1.0 collective-permute-done.6
  88.9 5.6 %collective-permute-start.7 = (bf16[256,256]{1,0:T(8,128)(2,1)S(1)}, bf16[256,256]{1,0:T(8,128)(2,1)S(1)}, u32[]{:S(2)}, u32[]{:S(2)}) collective-permute-start(bf16[256,256]{1,0:T(8,128)(2,1)S(1)} %collective-permute-done.6), channel_id=1, source_target_pairs={{0,16},{8,24},{16,32},{24,40},{32,48},{40,56},{48,64},{56,72},{64,... | collective-permute-start | bytes 393224 | tf_op jit(solution)/shard_map/ppermute | solution.py:17
  94.5 0.7 bitcast_dynamic-update-slice_fusion.17
  95.2 1.8 collective-permute-done.7
  97.0 0.7 bitcast_dynamic-update-slice_fusion.15
  97.7 2.1 collective-permute-start.8
  100.4 2.3 collective-permute-done.8
  102.7 1.1 constant_dynamic-update-slice_fusion
  103.8 6.6 %fusion.5 = (f32[2,256]{1,0:T(2,128)S(1)}, f32[4608,256,2]{1,0,2:T(8,128)}) fusion(pred[256,4608]{0,1:T(8,128)(4,1)S(1)} %fusion.10, bf16[256,2,128]{2,1,0:T(2,128)(2,1)S(1)} %copy-done.2, bf16[4608,256]{1,0:T(8,128)(2,1)} %bitcast.11), kind=kOutput, calls=%fused_computation.10 | convolution fusion | flops 613416448 | bytes 11929600 | tf_op jit(solution)/shard_map/qgrd,kgd->grqk/dot_general | solution.py:52
  110.4 2.7 %fusion.15 = bf16[256,256]{0,1:T(8,128)(2,1)S(1)} fusion(bf16[256,4608]{0,1:T(8,128)(2,1)S(1)} %bitcast.181, bf16[1,256,4608]{1,2,0:T(8,128)(2,1)} %all-gather.3.cloned.1.call-done), kind=kOutput, calls=%fused_computation.24 | convolution fusion | flops 604045312 | bytes 4849664 | tf_op jit(solution)/shard_map/dot_general | solution.py:94
  113.1 6.3 %fusion.2 = (f32[2,256]{1,0:T(2,128)S(1)}, f32[4608,256,2]{1,0,2:T(8,128)S(1)}) fusion(f32[2,256]{1,0:T(2,128)S(1)} %get-tuple-element.42, f32[4608,256,2]{1,0,2:T(8,128)} %get-tuple-element.43, pred[256,4608]{0,1:T(8,128)(4,1)S(1)} %fusion.10, bf16[256,2,128]{0,2,1:T(8,128)(2,1)S(1)} %bitcast.196, bf16[4608,256]{1,0:T(8,128)(2,1)} %bitcast.11), kind=kOutput, calls=%fused_computation.6 | convolution fusion | flops 618135040 | bytes 21368832 | tf_op jit(solution)/shard_map/qgrd,kgd->grqk/dot_general | solution.py:62
  119.9 4.6 %fusion.6 = bf16[2,256,4608]{1,2,0:T(8,128)(2,1)S(1)} fusion(f32[4608,256,2]{1,0,2:T(8,128)S(1)} %bitcast.179, f32[4608,256,2]{1,0,2:T(8,128)S(1)} %get-tuple-element.45, f32[2,256]{1,0:T(2,128)S(1)} %get-tuple-element.44, f32[2,256]{1,0:T(2,128)S(1)} %get-tuple-element.42, pred[256,4608]{0,1:T(8,128)(4,1)S(1)} %fusion.10), kind=kLoop, calls=%fused_computation.13 | loop fusion | flops 25952256 | bytes 24776704 | tf_op jit(solution)/shard_map/reshape.12
  124.5 2.1 convolution_convert_fusion
  126.6 1.4 convolution_bitcast_fusion.1
  128.0 2.8 %convolution_bitcast_fusion = f32[4608,128]{1,0:T(8,128)S(1)} fusion(bf16[256,2,128]{0,2,1:T(8,128)(2,1)S(1)} %bitcast.197, f32[4608,256,2]{1,0,2:T(8,128)S(1)} %bitcast.179, f32[2,256]{1,0:T(2,128)S(1)} %get-tuple-element.42, pred[256,4608]{0,1:T(8,128)(4,1)S(1)} %fusion.10), kind=kOutput, calls=%fused_computation.11 | convolution fusion | flops 615776256 | bytes 13109248 | tf_op jit(solution)/shard_map/grqk,qgrd->kgd/dot_general | solution.py:59
  131.5 2.1 collective-permute-start.16
  133.6 4.4 %collective-permute-done.16 = f32[9,256,256]{2,1,0:T(8,128)S(1)} collective-permute-done((f32[9,256,256]{2,1,0:T(8,128)S(1)}, f32[9,256,256]{2,1,0:T(8,128)S(1)}, u32[]{:S(2)}, u32[]{:S(2)}) %collective-permute-start.16) | collective-permute-done | bytes 2359328 | tf_op jit(solution)/shard_map/ppermute | solution.py:155
  139.0 1.9 collective-permute-start.17
  140.9 10.2 %collective-permute-done.17 = f32[256,256]{1,0:T(8,128)S(1)} collective-permute-done((f32[256,256]{1,0:T(8,128)S(1)}, f32[256,256]{1,0:T(8,128)S(1)}, u32[]{:S(2)}, u32[]{:S(2)}) %collective-permute-start.17) | collective-permute-done | bytes 262176 | tf_op jit(solution)/shard_map/ppermute | solution.py:17
  151.2 1.9 collective-permute-start.18
  153.2 9.0 %collective-permute-done.18 = f32[256,256]{1,0:T(8,128)S(1)} collective-permute-done((f32[256,256]{1,0:T(8,128)S(1)}, f32[256,256]{1,0:T(8,128)S(1)}, u32[]{:S(2)}, u32[]{:S(2)}) %collective-permute-start.18) | collective-permute-done | bytes 262176 | tf_op jit(solution)/shard_map/ppermute | solution.py:17
  162.2 1.9 collective-permute-start.19
  164.1 8.1 %collective-permute-done.19 = f32[256,256]{1,0:T(8,128)S(1)} collective-permute-done((f32[256,256]{1,0:T(8,128)S(1)}, f32[256,256]{1,0:T(8,128)S(1)}, u32[]{:S(2)}, u32[]{:S(2)}) %collective-permute-start.19) | collective-permute-done | bytes 262176 | tf_op jit(solution)/shard_map/ppermute | solution.py:17
  172.2 1.9 collective-permute-start.20
  174.1 2.4 %collective-permute-start.22 = (f32[256,256]{1,0:T(8,128)}, f32[256,256]{1,0:T(8,128)}, u32[]{:S(2)}, u32[]{:S(2)}) collective-permute-start(f32[256,256]{1,0:T(8,128)} %get-tuple-element.18), channel_id=1, source_target_pairs={{192,0},{384,192},{576,384},{193,1},{385,193},{577,385},{194,2},{3... | collective-permute-start | bytes 786440 | tf_op jit(solution)/shard_map/ppermute | solution.py:17
  176.6 1.9 collective-permute-start.21
  178.6 3.1 %collective-permute-done.20 = f32[256,256]{1,0:T(8,128)S(1)} collective-permute-done((f32[256,256]{1,0:T(8,128)S(1)}, f32[256,256]{1,0:T(8,128)S(1)}, u32[]{:S(2)}, u32[]{:S(2)}) %collective-permute-start.20) | collective-permute-done | bytes 262176 | tf_op jit(solution)/shard_map/ppermute | solution.py:17
  181.7 3.4 %collective-permute-done.21 = bf16[256,256]{1,0:T(8,128)(2,1)S(1)} collective-permute-done((bf16[256,256]{1,0:T(8,128)(2,1)S(1)}, bf16[256,256]{1,0:T(8,128)(2,1)S(1)}, u32[]{:S(2)}, u32[]{:S(2)}) %collective-permute-start.21) | collective-permute-done | bytes 131104 | tf_op jit(solution)/shard_map/ppermute | solution.py:17
  185.1 1.9 collective-permute-start.23
  187.1 7.5 %collective-permute-done.23 = f32[256,256]{1,0:T(8,128)S(1)} collective-permute-done((f32[256,256]{1,0:T(8,128)S(1)}, f32[256,256]{1,0:T(8,128)S(1)}, u32[]{:S(2)}, u32[]{:S(2)}) %collective-permute-start.23) | collective-permute-done | bytes 262176 | tf_op jit(solution)/shard_map/ppermute | solution.py:17
  194.6 1.9 collective-permute-start.24
  196.6 7.5 %collective-permute-done.24 = f32[256,256]{1,0:T(8,128)S(1)} collective-permute-done((f32[256,256]{1,0:T(8,128)S(1)}, f32[256,256]{1,0:T(8,128)S(1)}, u32[]{:S(2)}, u32[]{:S(2)}) %collective-permute-start.24) | collective-permute-done | bytes 262176 | tf_op jit(solution)/shard_map/ppermute | solution.py:17
  204.2 1.9 collective-permute-start.25
  206.1 2.4 %collective-permute-start.27 = (bf16[256,576]{0,1:T(8,128)(2,1)S(1)}, bf16[256,576]{0,1:T(8,128)(2,1)S(1)}, u32[]{:S(2)}, u32[]{:S(2)}) collective-permute-start(bf16[256,576]{0,1:T(8,128)(2,1)S(1)} %bitcast.186), channel_id=1, source_target_pairs={{192,0},{384,192},{576,384},{193,1},{385,193},{577,385},{194,2},{3... | collective-permute-start | bytes 884744 | tf_op jit(solution)/shard_map/ppermute | solution.py:17
  208.5 5.8 %collective-permute-done.25 = f32[256,256]{1,0:T(8,128)S(1)} collective-permute-done((f32[256,256]{1,0:T(8,128)S(1)}, f32[256,256]{1,0:T(8,128)S(1)}, u32[]{:S(2)}, u32[]{:S(2)}) %collective-permute-start.25) | collective-permute-done | bytes 262176 | tf_op jit(solution)/shard_map/ppermute | solution.py:17
  214.4 1.9 collective-permute-start.26
  216.3 1.2 collective-permute-done.27
  217.5 7.2 %collective-permute-done.26 = f32[256,256]{1,0:T(8,128)S(1)} collective-permute-done((f32[256,256]{1,0:T(8,128)S(1)}, f32[256,256]{1,0:T(8,128)S(1)}, u32[]{:S(2)}, u32[]{:S(2)}) %collective-permute-start.26) | collective-permute-done | bytes 262176 | tf_op jit(solution)/shard_map/ppermute | solution.py:169
  224.7 1.0 add_convert_fusion
  (85 shorter events, 9.9 us)
Async XLA Ops:
  7.2 103.2 %all-gather.3.cloned.1.call-start = ((), (), s32[]{:S(2)}) async-start(), calls=%async_computation | async-start | bytes 2457600 | tf_op jit(solution)/shard_map/all_gather | solution.py:96
  7.2 39.7 %collective-permute-start.9 = (bf16[256,576]{0,1:T(8,128)(2,1)}, bf16[256,576]{0,1:T(8,128)(2,1)S(1)}, u32[]{:S(2)}, u32[]{:S(2)}) collective-permute-start(bf16[256,576]{0,1:T(8,128)(2,1)} %bitcast.184), channel_id=1, source_target_pairs={{0,7},{1,0},{2,1},{3,2},{4,3},{5,4},{6,5},{7,6},{8,15},{9,8},{10,9... | collective-permute-start | bytes 884744 | tf_op jit(solution)/shard_map/ppermute | solution.py:22
  12.6 39.5 %collective-permute-start.12 = (bf16[256,576]{0,1:T(8,128)(2,1)}, bf16[256,576]{0,1:T(8,128)(2,1)S(1)}, u32[]{:S(2)}, u32[]{:S(2)}) collective-permute-start(bf16[256,576]{0,1:T(8,128)(2,1)} %bitcast.185), channel_id=1, source_target_pairs={{0,1},{1,2},{2,3},{3,4},{4,5},{5,6},{6,7},{7,0},{8,9},{9,10},{10,1... | collective-permute-start | bytes 884744 | tf_op jit(solution)/shard_map/ppermute | solution.py:22
  15.4 17.3 %collective-permute-start = (bf16[256,256]{1,0:T(8,128)(2,1)S(1)}, bf16[256,256]{1,0:T(8,128)(2,1)S(1)}, u32[]{:S(2)}, u32[]{:S(2)}) collective-permute-start(bf16[256,256]{1,0:T(8,128)(2,1)S(1)} %pad_maximum_fusion), channel_id=1, source_target_pairs={{0,16},{8,24},{16,32},{24,40},{32,48},{40,56},{48,64},{56,72},{64,... | collective-permute-start | bytes 393224 | tf_op jit(solution)/shard_map/ppermute | solution.py:17
  23.8 76.2 %copy-start = (bf16[1,256,576]{1,2,0:T(8,128)(2,1)S(1)}, bf16[1,256,576]{1,2,0:T(8,128)(2,1)}, u32[]{:S(2)}) copy-start(bf16[1,256,576]{1,2,0:T(8,128)(2,1)} %param.7) | copy-start | bytes 884740
  32.7 8.0 %collective-permute-start.1 = (bf16[256,256]{1,0:T(8,128)(2,1)S(1)}, bf16[256,256]{1,0:T(8,128)(2,1)S(1)}, u32[]{:S(2)}, u32[]{:S(2)}) collective-permute-start(bf16[256,256]{1,0:T(8,128)(2,1)S(1)} %collective-permute-done), channel_id=1, source_target_pairs={{0,16},{8,24},{16,32},{24,40},{32,48},{40,56},{48,64},{56,72},{64,... | collective-permute-start | bytes 393224 | tf_op jit(solution)/shard_map/ppermute | solution.py:17
  40.7 13.4 %collective-permute-start.2 = (bf16[256,256]{1,0:T(8,128)(2,1)S(1)}, bf16[256,256]{1,0:T(8,128)(2,1)S(1)}, u32[]{:S(2)}, u32[]{:S(2)}) collective-permute-start(bf16[256,256]{1,0:T(8,128)(2,1)S(1)} %collective-permute-done.1), channel_id=1, source_target_pairs={{0,16},{8,24},{16,32},{24,40},{32,48},{40,56},{48,64},{56,72},{64,... | collective-permute-start | bytes 393224 | tf_op jit(solution)/shard_map/ppermute | solution.py:17
  47.0 19.8 %collective-permute-start.10 = (bf16[256,576]{0,1:T(8,128)(2,1)S(1)}, bf16[256,576]{0,1:T(8,128)(2,1)S(1)}, u32[]{:S(2)}, u32[]{:S(2)}) collective-permute-start(bf16[256,576]{0,1:T(8,128)(2,1)S(1)} %collective-permute-done.9), channel_id=1, source_target_pairs={{0,7},{1,0},{2,1},{3,2},{4,3},{5,4},{6,5},{7,6},{8,15},{9,8},{10,9... | collective-permute-start | bytes 884744 | tf_op jit(solution)/shard_map/ppermute | solution.py:22
  52.1 19.6 %collective-permute-start.13 = (bf16[256,576]{0,1:T(8,128)(2,1)S(1)}, bf16[256,576]{0,1:T(8,128)(2,1)S(1)}, u32[]{:S(2)}, u32[]{:S(2)}) collective-permute-start(bf16[256,576]{0,1:T(8,128)(2,1)S(1)} %collective-permute-done.12), channel_id=1, source_target_pairs={{0,1},{1,2},{2,3},{3,4},{4,5},{5,6},{6,7},{7,0},{8,9},{9,10},{10,1... | collective-permute-start | bytes 884744 | tf_op jit(solution)/shard_map/ppermute | solution.py:22
  54.1 7.1 %collective-permute-start.3 = (bf16[256,256]{1,0:T(8,128)(2,1)S(1)}, bf16[256,256]{1,0:T(8,128)(2,1)S(1)}, u32[]{:S(2)}, u32[]{:S(2)}) collective-permute-start(bf16[256,256]{1,0:T(8,128)(2,1)S(1)} %collective-permute-done.2), channel_id=1, source_target_pairs={{0,16},{8,24},{16,32},{24,40},{32,48},{40,56},{48,64},{56,72},{64,... | collective-permute-start | bytes 393224 | tf_op jit(solution)/shard_map/ppermute | solution.py:17
  61.2 12.5 %collective-permute-start.4 = (bf16[256,256]{1,0:T(8,128)(2,1)S(1)}, bf16[256,256]{1,0:T(8,128)(2,1)S(1)}, u32[]{:S(2)}, u32[]{:S(2)}) collective-permute-start(bf16[256,256]{1,0:T(8,128)(2,1)S(1)} %collective-permute-done.3), channel_id=1, source_target_pairs={{0,16},{8,24},{16,32},{24,40},{32,48},{40,56},{48,64},{56,72},{64,... | collective-permute-start | bytes 393224 | tf_op jit(solution)/shard_map/ppermute | solution.py:17
  66.7 21.2 %collective-permute-start.11 = (bf16[256,576]{0,1:T(8,128)(2,1)S(1)}, bf16[256,576]{0,1:T(8,128)(2,1)S(1)}, u32[]{:S(2)}, u32[]{:S(2)}) collective-permute-start(bf16[256,576]{0,1:T(8,128)(2,1)S(1)} %collective-permute-done.10), channel_id=1, source_target_pairs={{0,7},{1,0},{2,1},{3,2},{4,3},{5,4},{6,5},{7,6},{8,15},{9,8},{10,9... | collective-permute-start | bytes 884744 | tf_op jit(solution)/shard_map/ppermute | solution.py:22
  71.7 14.2 %collective-permute-start.14 = (bf16[256,576]{0,1:T(8,128)(2,1)S(1)}, bf16[256,576]{0,1:T(8,128)(2,1)S(1)}, u32[]{:S(2)}, u32[]{:S(2)}) collective-permute-start(bf16[256,576]{0,1:T(8,128)(2,1)S(1)} %collective-permute-done.13), channel_id=1, source_target_pairs={{0,1},{1,2},{2,3},{3,4},{4,5},{5,6},{6,7},{7,0},{8,9},{9,10},{10,1... | collective-permute-start | bytes 884744 | tf_op jit(solution)/shard_map/ppermute | solution.py:22
  73.7 7.7 %collective-permute-start.5 = (bf16[256,256]{1,0:T(8,128)(2,1)S(1)}, bf16[256,256]{1,0:T(8,128)(2,1)S(1)}, u32[]{:S(2)}, u32[]{:S(2)}) collective-permute-start(bf16[256,256]{1,0:T(8,128)(2,1)S(1)} %collective-permute-done.4), channel_id=1, source_target_pairs={{0,16},{8,24},{16,32},{24,40},{32,48},{40,56},{48,64},{56,72},{64,... | collective-permute-start | bytes 393224 | tf_op jit(solution)/shard_map/ppermute | solution.py:17
  81.4 7.5 %collective-permute-start.6 = (bf16[256,256]{1,0:T(8,128)(2,1)S(1)}, bf16[256,256]{1,0:T(8,128)(2,1)S(1)}, u32[]{:S(2)}, u32[]{:S(2)}) collective-permute-start(bf16[256,256]{1,0:T(8,128)(2,1)S(1)} %collective-permute-done.5), channel_id=1, source_target_pairs={{0,16},{8,24},{16,32},{24,40},{32,48},{40,56},{48,64},{56,72},{64,... | collective-permute-start | bytes 393224 | tf_op jit(solution)/shard_map/ppermute | solution.py:17
  86.0 13.9 %collective-permute-start.15 = (bf16[256,576]{0,1:T(8,128)(2,1)S(1)}, bf16[256,576]{0,1:T(8,128)(2,1)S(1)}, u32[]{:S(2)}, u32[]{:S(2)}) collective-permute-start(bf16[256,576]{0,1:T(8,128)(2,1)S(1)} %collective-permute-done.14), channel_id=1, source_target_pairs={{0,1},{1,2},{2,3},{3,4},{4,5},{5,6},{6,7},{7,0},{8,9},{9,10},{10,1... | collective-permute-start | bytes 884744 | tf_op jit(solution)/shard_map/ppermute | solution.py:22
  88.9 8.1 %collective-permute-start.7 = (bf16[256,256]{1,0:T(8,128)(2,1)S(1)}, bf16[256,256]{1,0:T(8,128)(2,1)S(1)}, u32[]{:S(2)}, u32[]{:S(2)}) collective-permute-start(bf16[256,256]{1,0:T(8,128)(2,1)S(1)} %collective-permute-done.6), channel_id=1, source_target_pairs={{0,16},{8,24},{16,32},{24,40},{32,48},{40,56},{48,64},{56,72},{64,... | collective-permute-start | bytes 393224 | tf_op jit(solution)/shard_map/ppermute | solution.py:17
  97.7 4.9 %collective-permute-start.8 = (bf16[9,256,256]{2,1,0:T(8,128)(2,1)}, bf16[9,256,256]{2,1,0:T(8,128)(2,1)S(1)}, u32[]{:S(2)}, u32[]{:S(2)}) collective-permute-start(bf16[9,256,256]{2,1,0:T(8,128)(2,1)} %get-tuple-element.22), channel_id=1, source_target_pairs={{0,8},{8,0},{16,24},{24,16},{32,40},{40,32},{48,56},{56,48},{64,72... | collective-permute-start | bytes 3538952 | tf_op jit(solution)/shard_map/ppermute | solution.py:122
  100.1 3.7 %copy-start.2 = (bf16[256,2,128]{2,1,0:T(2,128)(2,1)S(1)}, bf16[256,2,128]{2,1,0:T(2,128)(2,1)}, u32[]{:S(2)}) copy-start(bf16[256,2,128]{2,1,0:T(2,128)(2,1)} %reshape.261) | copy-start | bytes 393220
  113.1 6.3 %slice-start = ((s8[9437184]{0:T(1024)(128)(4,1)}), s8[4194304]{0:T(1024)(128)(4,1)S(1)}, s32[]{:S(2)}) async-start(s8[9437184]{0:T(1024)(128)(4,1)} %bitcast.178), calls=%async_computation.1 | async-start | bytes 8388608
  113.1 6.6 %slice-start.1 = ((s8[9437184]{0:T(1024)(128)(4,1)}), s8[4194304]{0:T(1024)(128)(4,1)S(1)}, s32[]{:S(2)}) async-start(s8[9437184]{0:T(1024)(128)(4,1)} %bitcast.178), calls=%async_computation.2 | async-start | bytes 8388608
  113.1 6.8 %slice-start.2 = ((s8[9437184]{0:T(1024)(128)(4,1)}), s8[1048576]{0:T(1024)(128)(4,1)S(1)}, s32[]{:S(2)}) async-start(s8[9437184]{0:T(1024)(128)(4,1)} %bitcast.178), calls=%async_computation.3 | async-start | bytes 2097152
  124.5 2.2 copy-start.3
  131.5 6.4 %collective-permute-start.16 = (f32[9,256,256]{2,1,0:T(8,128)S(1)}, f32[9,256,256]{2,1,0:T(8,128)S(1)}, u32[]{:S(2)}, u32[]{:S(2)}) collective-permute-start(f32[9,256,256]{2,1,0:T(8,128)S(1)} %bitcast.182), channel_id=1, source_target_pairs={{0,8},{8,0},{16,24},{24,16},{32,40},{40,32},{48,56},{56,48},{64,72... | collective-permute-start | bytes 7077896 | tf_op jit(solution)/shard_map/ppermute | solution.py:155
  138.3 67.8 %copy-start.1 = (bf16[1,256,576]{1,2,0:T(8,128)(2,1)S(1)}, bf16[1,256,576]{1,2,0:T(8,128)(2,1)}, u32[]{:S(2)}) copy-start(bf16[1,256,576]{1,2,0:T(8,128)(2,1)} %param.7) | copy-start | bytes 884740
  139.0 12.2 %collective-permute-start.17 = (f32[256,256]{1,0:T(8,128)S(1)}, f32[256,256]{1,0:T(8,128)S(1)}, u32[]{:S(2)}, u32[]{:S(2)}) collective-permute-start(f32[256,256]{1,0:T(8,128)S(1)} %get-tuple-element.19), channel_id=1, source_target_pairs={{16,0},{24,8},{32,16},{40,24},{48,32},{56,40},{64,48},{72,56},{80,... | collective-permute-start | bytes 786440 | tf_op jit(solution)/shard_map/ppermute | solution.py:17
  151.2 10.9 %collective-permute-start.18 = (f32[256,256]{1,0:T(8,128)S(1)}, f32[256,256]{1,0:T(8,128)S(1)}, u32[]{:S(2)}, u32[]{:S(2)}) collective-permute-start(f32[256,256]{1,0:T(8,128)S(1)} %fusion.25), channel_id=1, source_target_pairs={{16,0},{24,8},{32,16},{40,24},{48,32},{56,40},{64,48},{72,56},{80,... | collective-permute-start | bytes 786440 | tf_op jit(solution)/shard_map/ppermute | solution.py:17
  162.2 10.0 %collective-permute-start.19 = (f32[256,256]{1,0:T(8,128)S(1)}, f32[256,256]{1,0:T(8,128)S(1)}, u32[]{:S(2)}, u32[]{:S(2)}) collective-permute-start(f32[256,256]{1,0:T(8,128)S(1)} %fusion.24), channel_id=1, source_target_pairs={{16,0},{24,8},{32,16},{40,24},{48,32},{56,40},{64,48},{72,56},{80,... | collective-permute-start | bytes 786440 | tf_op jit(solution)/shard_map/ppermute | solution.py:17
  172.2 9.5 %collective-permute-start.20 = (f32[256,256]{1,0:T(8,128)S(1)}, f32[256,256]{1,0:T(8,128)S(1)}, u32[]{:S(2)}, u32[]{:S(2)}) collective-permute-start(f32[256,256]{1,0:T(8,128)S(1)} %fusion.23), channel_id=1, source_target_pairs={{16,0},{24,8},{32,16},{40,24},{48,32},{56,40},{64,48},{72,56},{80,... | collective-permute-start | bytes 786440 | tf_op jit(solution)/shard_map/ppermute | solution.py:17
  174.1 11.0 %collective-permute-start.22 = (f32[256,256]{1,0:T(8,128)}, f32[256,256]{1,0:T(8,128)}, u32[]{:S(2)}, u32[]{:S(2)}) collective-permute-start(f32[256,256]{1,0:T(8,128)} %get-tuple-element.18), channel_id=1, source_target_pairs={{192,0},{384,192},{576,384},{193,1},{385,193},{577,385},{194,2},{3... | collective-permute-start | bytes 786440 | tf_op jit(solution)/shard_map/ppermute | solution.py:17
  176.6 8.5 %collective-permute-start.21 = (bf16[256,256]{1,0:T(8,128)(2,1)S(1)}, bf16[256,256]{1,0:T(8,128)(2,1)S(1)}, u32[]{:S(2)}, u32[]{:S(2)}) collective-permute-start(bf16[256,256]{1,0:T(8,128)(2,1)S(1)} %copy.26), channel_id=1, source_target_pairs={{192,0},{384,192},{576,384},{193,1},{385,193},{577,385},{194,2},{3... | collective-permute-start | bytes 393224 | tf_op jit(solution)/shard_map/ppermute | solution.py:17
  185.1 9.5 %collective-permute-start.23 = (f32[256,256]{1,0:T(8,128)S(1)}, f32[256,256]{1,0:T(8,128)S(1)}, u32[]{:S(2)}, u32[]{:S(2)}) collective-permute-start(f32[256,256]{1,0:T(8,128)S(1)} %fusion.22), channel_id=1, source_target_pairs={{16,0},{24,8},{32,16},{40,24},{48,32},{56,40},{64,48},{72,56},{80,... | collective-permute-start | bytes 786440 | tf_op jit(solution)/shard_map/ppermute | solution.py:17
  194.6 9.5 %collective-permute-start.24 = (f32[256,256]{1,0:T(8,128)S(1)}, f32[256,256]{1,0:T(8,128)S(1)}, u32[]{:S(2)}, u32[]{:S(2)}) collective-permute-start(f32[256,256]{1,0:T(8,128)S(1)} %fusion.21), channel_id=1, source_target_pairs={{16,0},{24,8},{32,16},{40,24},{48,32},{56,40},{64,48},{72,56},{80,... | collective-permute-start | bytes 786440 | tf_op jit(solution)/shard_map/ppermute | solution.py:17
  204.2 10.2 %collective-permute-start.25 = (f32[256,256]{1,0:T(8,128)S(1)}, f32[256,256]{1,0:T(8,128)S(1)}, u32[]{:S(2)}, u32[]{:S(2)}) collective-permute-start(f32[256,256]{1,0:T(8,128)S(1)} %fusion.20), channel_id=1, source_target_pairs={{16,0},{24,8},{32,16},{40,24},{48,32},{56,40},{64,48},{72,56},{80,... | collective-permute-start | bytes 786440 | tf_op jit(solution)/shard_map/ppermute | solution.py:17
  206.1 11.4 %collective-permute-start.27 = (bf16[256,576]{0,1:T(8,128)(2,1)S(1)}, bf16[256,576]{0,1:T(8,128)(2,1)S(1)}, u32[]{:S(2)}, u32[]{:S(2)}) collective-permute-start(bf16[256,576]{0,1:T(8,128)(2,1)S(1)} %bitcast.186), channel_id=1, source_target_pairs={{192,0},{384,192},{576,384},{193,1},{385,193},{577,385},{194,2},{3... | collective-permute-start | bytes 884744 | tf_op jit(solution)/shard_map/ppermute | solution.py:17
  214.4 10.4 %collective-permute-start.26 = (f32[256,256]{1,0:T(8,128)S(1)}, f32[256,256]{1,0:T(8,128)S(1)}, u32[]{:S(2)}, u32[]{:S(2)}) collective-permute-start(f32[256,256]{1,0:T(8,128)S(1)} %fusion.19), channel_id=1, source_target_pairs={{208,0},{216,8},{224,16},{232,24},{240,32},{248,40},{256,48},{264,... | collective-permute-start | bytes 786440 | tf_op jit(solution)/shard_map/ppermute | solution.py:169
Sparse Core Ops, SparseCore 0:
  21.1 58.9 all-gather.2

commit v10 on v8

--- a/solution.py
+++ b/solution.py
@@ -152,9 +152,10 @@
     pair_sum = jnp.concatenate([key_sum, value_sum], axis=1).reshape(
         2, hops + 1, tok_rows, 2 * key_width
     )
-    chip_sum = pair_sum[0] + lax.ppermute(pair_sum[1], "row", swap_pairs)
+    far_sum = pair_sum[0][hops] + lax.ppermute(pair_sum[1][hops], "row", swap_pairs)
+    chip_sum = pair_sum[0][:hops] + lax.ppermute(pair_sum[1][:hops], "row", swap_pairs)
     own_handed = from_behind(chip_sum[0], "pipe", -1)
-    running = chip_sum[hops]
+    running = far_sum
     for step in range(1, hops):
         running = from_behind(running, "row", -2) + chip_sum[hops - step]
         if step == hops // 2:

time: 232 us -> 231 us (level)
  waiting for transfers between devices: 79.4 us -> 76.6 us
    ppermute x1 -> x2, waiting for transfers between devices: 4.39 us -> 2.06 us  [the longest x1 2.06 us: per_device(): lax.ppermute(pair_sum[1][hops], 'row', swap_pairs)]
  transfers between devices with their start and end apart: 29 -> 30, of which waited for: 17 -> 17; matrix products, arithmetic and copies ran while one was open for 12% -> 12% of each run, Pallas kernels for 0% -> 0%
where the time goes in v10:
time: 231 us; the launch traced here: 230 us
  starting transfers between devices  87.8 us (38%)
  waiting for transfers between devices  76.6 us (33%)
  matrix products  21.9 us (9%)
  local copies, waits for them, and re-layouts  15.1 us (7%)
  between operations  14.8 us (6%)
  other arithmetic  13.4 us (6%)
    ppermute x18, waiting for transfers between devices, from_behind(): return lax.ppermute(block, axis, route)  67.5 us
    ppermute x18, starting transfers between devices, from_behind(): return lax.ppermute(block, axis, route)  56.2 us
    ppermute x7, starting transfers between devices, cyclic_shift(): lax.ppermute(block, axis, [(i, (i + distance) % size) for i in range(size)])  23.2 us
    unnamed x40, local copies, waits for them, and re-layouts  8.47 us
    dot_general x1, matrix products, attend(): jnp.einsum('qgrd,kgd->grqk', query_g, key_g, preferred_element_type=jnp.f...  6.59 us
    dot_general x1, matrix products, attend(): jnp.einsum('qgrd,kgd->grqk', attn_g, value_g, preferred_element_type=jnp....  6.28 us
    ppermute x1, waiting for transfers between devices, per_device(): total = lax.ppermute(running, ('pipe', 'row'), last_pairs) + own_handed  4.78 us
    and x1, other arithmetic, per_device(): allowed & ((key_doc[None, :] == query_doc[:, None]) | (key_shared[None, :...  4.64 us
  transfers between devices with their start and end apart: 30, of which 17 were waited for; matrix products, arithmetic and copies ran while one was open for 12% of the time, Pallas kernels for 0%

profile of v10, /device:TPU:196, one launch (start us, length us, event | category | flops | bytes accessed | tf_op | source)
XLA Modules:
  0.0 229.6 jit_solution(10395266701063050064)
XLA Ops:
  7.2 5.4 %collective-permute-start.9 = (bf16[256,576]{0,1:T(8,128)(2,1)}, bf16[256,576]{0,1:T(8,128)(2,1)S(1)}, u32[]{:S(2)}, u32[]{:S(2)}) collective-permute-start(bf16[256,576]{0,1:T(8,128)(2,1)} %bitcast.182), channel_id=1, source_target_pairs={{0,7},{1,0},{2,1},{3,2},{4,3},{5,4},{6,5},{7,6},{8,15},{9,8},{10,9... | collective-permute-start | bytes 884744 | tf_op jit(solution)/shard_map/ppermute | solution.py:22
  12.6 1.9 collective-permute-start.12
  14.5 0.9 pad_maximum_fusion
  15.4 5.5 %collective-permute-start = (bf16[256,256]{1,0:T(8,128)(2,1)S(1)}, bf16[256,256]{1,0:T(8,128)(2,1)S(1)}, u32[]{:S(2)}, u32[]{:S(2)}) collective-permute-start(bf16[256,256]{1,0:T(8,128)(2,1)S(1)} %pad_maximum_fusion), channel_id=1, source_target_pairs={{0,16},{8,24},{16,32},{24,40},{32,48},{40,56},{48,64},{56,72},{64,... | collective-permute-start | bytes 393224 | tf_op jit(solution)/shard_map/ppermute | solution.py:17
  21.7 0.9 pad_dynamic-slice_fusion
  23.0 0.8 select_reduce_fusion
  23.8 4.6 %fusion.10 = pred[256,4608]{0,1:T(8,128)(4,1)S(1)} fusion(s32[256]{0:T(256)S(1)} %bitcast.192, s32[256]{0:T(256)S(1)} %iota_add_fusion.1, s32[4608]{0:T(1024)S(1)} %constant_dynamic-update-slice_fusion.6, s32[4608]{0:T(1024)S(1)} %add.97, pred[4608]{0:T(1024)(128)(4,1)S(1)} %broadcast_compare_fusion, pred[4608]{0:T(1024)(128)(4,1)S(1)} %broadcast_compare_fusion.1), kind=kLoop, calls=%fused_computation.18 | loop fusion | flops 9437184 | bytes 1227776 | tf_op jit(solution)/shard_map/and | solution.py:146
  28.5 1.6 bitcast_dynamic-update-slice_fusion.31
  30.1 1.6 reshape.267
  31.7 1.0 constant_dynamic-update-slice_fusion.3
  32.7 4.3 %collective-permute-start.1 = (bf16[256,256]{1,0:T(8,128)(2,1)S(1)}, bf16[256,256]{1,0:T(8,128)(2,1)S(1)}, u32[]{:S(2)}, u32[]{:S(2)}) collective-permute-start(bf16[256,256]{1,0:T(8,128)(2,1)S(1)} %collective-permute-done), channel_id=1, source_target_pairs={{0,16},{8,24},{16,32},{24,40},{32,48},{40,56},{48,64},{56,72},{64,... | collective-permute-start | bytes 393224 | tf_op jit(solution)/shard_map/ppermute | solution.py:17
  37.7 2.9 %collective-permute-done.1 = bf16[256,256]{1,0:T(8,128)(2,1)S(1)} collective-permute-done((bf16[256,256]{1,0:T(8,128)(2,1)S(1)}, bf16[256,256]{1,0:T(8,128)(2,1)S(1)}, u32[]{:S(2)}, u32[]{:S(2)}) %collective-permute-start.1) | collective-permute-done | bytes 131104 | tf_op jit(solution)/shard_map/ppermute | solution.py:17
  40.7 5.6 %collective-permute-start.2 = (bf16[256,256]{1,0:T(8,128)(2,1)S(1)}, bf16[256,256]{1,0:T(8,128)(2,1)S(1)}, u32[]{:S(2)}, u32[]{:S(2)}) collective-permute-start(bf16[256,256]{1,0:T(8,128)(2,1)S(1)} %collective-permute-done.1), channel_id=1, source_target_pairs={{0,16},{8,24},{16,32},{24,40},{32,48},{40,56},{48,64},{56,72},{64,... | collective-permute-start | bytes 393224 | tf_op jit(solution)/shard_map/ppermute | solution.py:17
  47.0 5.1 %collective-permute-start.10 = (bf16[256,576]{0,1:T(8,128)(2,1)S(1)}, bf16[256,576]{0,1:T(8,128)(2,1)S(1)}, u32[]{:S(2)}, u32[]{:S(2)}) collective-permute-start(bf16[256,576]{0,1:T(8,128)(2,1)S(1)} %collective-permute-done.9), channel_id=1, source_target_pairs={{0,7},{1,0},{2,1},{3,2},{4,3},{5,4},{6,5},{7,6},{8,15},{9,8},{10,9... | collective-permute-start | bytes 884744 | tf_op jit(solution)/shard_map/ppermute | solution.py:22
  52.1 1.9 collective-permute-start.13
  54.1 2.9 %collective-permute-start.3 = (bf16[256,256]{1,0:T(8,128)(2,1)S(1)}, bf16[256,256]{1,0:T(8,128)(2,1)S(1)}, u32[]{:S(2)}, u32[]{:S(2)}) collective-permute-start(bf16[256,256]{1,0:T(8,128)(2,1)S(1)} %collective-permute-done.2), channel_id=1, source_target_pairs={{0,16},{8,24},{16,32},{24,40},{32,48},{40,56},{48,64},{56,72},{64,... | collective-permute-start | bytes 393224 | tf_op jit(solution)/shard_map/ppermute | solution.py:17
  57.7 3.4 %collective-permute-done.3 = bf16[256,256]{1,0:T(8,128)(2,1)S(1)} collective-permute-done((bf16[256,256]{1,0:T(8,128)(2,1)S(1)}, bf16[256,256]{1,0:T(8,128)(2,1)S(1)}, u32[]{:S(2)}, u32[]{:S(2)}) %collective-permute-start.3) | collective-permute-done | bytes 131104 | tf_op jit(solution)/shard_map/ppermute | solution.py:17
  61.2 4.8 %collective-permute-start.4 = (bf16[256,256]{1,0:T(8,128)(2,1)S(1)}, bf16[256,256]{1,0:T(8,128)(2,1)S(1)}, u32[]{:S(2)}, u32[]{:S(2)}) collective-permute-start(bf16[256,256]{1,0:T(8,128)(2,1)S(1)} %collective-permute-done.3), channel_id=1, source_target_pairs={{0,16},{8,24},{16,32},{24,40},{32,48},{40,56},{48,64},{56,72},{64,... | collective-permute-start | bytes 393224 | tf_op jit(solution)/shard_map/ppermute | solution.py:17
  66.7 5.0 %collective-permute-start.11 = (bf16[256,576]{0,1:T(8,128)(2,1)S(1)}, bf16[256,576]{0,1:T(8,128)(2,1)S(1)}, u32[]{:S(2)}, u32[]{:S(2)}) collective-permute-start(bf16[256,576]{0,1:T(8,128)(2,1)S(1)} %collective-permute-done.10), channel_id=1, source_target_pairs={{0,7},{1,0},{2,1},{3,2},{4,3},{5,4},{6,5},{7,6},{8,15},{9,8},{10,9... | collective-permute-start | bytes 884744 | tf_op jit(solution)/shard_map/ppermute | solution.py:22
  71.7 1.9 collective-permute-start.14
  73.7 3.1 %collective-permute-start.5 = (bf16[256,256]{1,0:T(8,128)(2,1)S(1)}, bf16[256,256]{1,0:T(8,128)(2,1)S(1)}, u32[]{:S(2)}, u32[]{:S(2)}) collective-permute-start(bf16[256,256]{1,0:T(8,128)(2,1)S(1)} %collective-permute-done.4), channel_id=1, source_target_pairs={{0,16},{8,24},{16,32},{24,40},{32,48},{40,56},{48,64},{56,72},{64,... | collective-permute-start | bytes 393224 | tf_op jit(solution)/shard_map/ppermute | solution.py:17
  77.5 4.0 %collective-permute-done.5 = bf16[256,256]{1,0:T(8,128)(2,1)S(1)} collective-permute-done((bf16[256,256]{1,0:T(8,128)(2,1)S(1)}, bf16[256,256]{1,0:T(8,128)(2,1)S(1)}, u32[]{:S(2)}, u32[]{:S(2)}) %collective-permute-start.5) | collective-permute-done | bytes 131104 | tf_op jit(solution)/shard_map/ppermute | solution.py:17
  81.5 3.9 %collective-permute-start.6 = (bf16[256,256]{1,0:T(8,128)(2,1)S(1)}, bf16[256,256]{1,0:T(8,128)(2,1)S(1)}, u32[]{:S(2)}, u32[]{:S(2)}) collective-permute-start(bf16[256,256]{1,0:T(8,128)(2,1)S(1)} %collective-permute-done.5), channel_id=1, source_target_pairs={{0,16},{8,24},{16,32},{24,40},{32,48},{40,56},{48,64},{56,72},{64,... | collective-permute-start | bytes 393224 | tf_op jit(solution)/shard_map/ppermute | solution.py:17
  85.4 0.7 bitcast_dynamic-update-slice_fusion.19
  86.1 1.9 collective-permute-start.15
  88.1 0.9 collective-permute-done.6
  89.0 5.6 %collective-permute-start.7 = (bf16[256,256]{1,0:T(8,128)(2,1)S(1)}, bf16[256,256]{1,0:T(8,128)(2,1)S(1)}, u32[]{:S(2)}, u32[]{:S(2)}) collective-permute-start(bf16[256,256]{1,0:T(8,128)(2,1)S(1)} %collective-permute-done.6), channel_id=1, source_target_pairs={{0,16},{8,24},{16,32},{24,40},{32,48},{40,56},{48,64},{56,72},{64,... | collective-permute-start | bytes 393224 | tf_op jit(solution)/shard_map/ppermute | solution.py:17
  94.6 0.7 bitcast_dynamic-update-slice_fusion.17
  95.3 1.8 collective-permute-done.7
  97.1 0.7 bitcast_dynamic-update-slice_fusion.15
  97.8 2.1 collective-permute-start.8
  100.5 2.3 collective-permute-done.8
  102.7 1.1 constant_dynamic-update-slice_fusion
  103.8 6.6 %fusion.5 = (f32[2,256]{1,0:T(2,128)S(1)}, f32[4608,256,2]{1,0,2:T(8,128)}) fusion(pred[256,4608]{0,1:T(8,128)(4,1)S(1)} %fusion.10, bf16[256,2,128]{2,1,0:T(2,128)(2,1)S(1)} %copy-done.2, bf16[4608,256]{1,0:T(8,128)(2,1)} %bitcast.11), kind=kOutput, calls=%fused_computation.10 | convolution fusion | flops 613416448 | bytes 11929600 | tf_op jit(solution)/shard_map/qgrd,kgd->grqk/dot_general | solution.py:52
  110.4 2.7 %fusion.15 = bf16[256,256]{0,1:T(8,128)(2,1)S(1)} fusion(bf16[256,4608]{0,1:T(8,128)(2,1)S(1)} %bitcast.179, bf16[1,256,4608]{1,2,0:T(8,128)(2,1)} %all-gather.3.cloned.1.call-done), kind=kOutput, calls=%fused_computation.24 | convolution fusion | flops 604045312 | bytes 4849664 | tf_op jit(solution)/shard_map/dot_general | solution.py:94
  113.2 6.3 %fusion.2 = (f32[2,256]{1,0:T(2,128)S(1)}, f32[4608,256,2]{1,0,2:T(8,128)S(1)}) fusion(f32[2,256]{1,0:T(2,128)S(1)} %get-tuple-element.38, f32[4608,256,2]{1,0,2:T(8,128)} %get-tuple-element.39, pred[256,4608]{0,1:T(8,128)(4,1)S(1)} %fusion.10, bf16[256,2,128]{0,2,1:T(8,128)(2,1)S(1)} %bitcast.194, bf16[4608,256]{1,0:T(8,128)(2,1)} %bitcast.11), kind=kOutput, calls=%fused_computation.6 | convolution fusion | flops 618135040 | bytes 21368832 | tf_op jit(solution)/shard_map/qgrd,kgd->grqk/dot_general | solution.py:62
  119.9 4.6 %fusion.6 = bf16[2,256,4608]{1,2,0:T(8,128)(2,1)S(1)} fusion(f32[4608,256,2]{1,0,2:T(8,128)S(1)} %bitcast.177, f32[4608,256,2]{1,0,2:T(8,128)S(1)} %get-tuple-element.41, f32[2,256]{1,0:T(2,128)S(1)} %get-tuple-element.40, f32[2,256]{1,0:T(2,128)S(1)} %get-tuple-element.38, pred[256,4608]{0,1:T(8,128)(4,1)S(1)} %fusion.10), kind=kLoop, calls=%fused_computation.13 | loop fusion | flops 25952256 | bytes 24776704 | tf_op jit(solution)/shard_map/reshape.12
  124.5 2.2 convolution_convert_fusion
  126.7 1.4 convolution_bitcast_fusion.1
  128.1 2.8 %convolution_bitcast_fusion = f32[4608,128]{1,0:T(8,128)S(1)} fusion(bf16[256,2,128]{0,2,1:T(8,128)(2,1)S(1)} %bitcast.195, f32[4608,256,2]{1,0,2:T(8,128)S(1)} %bitcast.177, f32[2,256]{1,0:T(2,128)S(1)} %get-tuple-element.38, pred[256,4608]{0,1:T(8,128)(4,1)S(1)} %fusion.10), kind=kOutput, calls=%fused_computation.11 | convolution fusion | flops 615776256 | bytes 13109248 | tf_op jit(solution)/shard_map/grqk,qgrd->kgd/dot_general | solution.py:59
  131.6 2.0 collective-permute-start.18
  133.6 2.3 collective-permute-start.16
  135.9 2.1 collective-permute-done.16
  138.0 1.9 collective-permute-start.17
  140.4 9.8 %collective-permute-done.17 = f32[256,256]{1,0:T(8,128)S(1)} collective-permute-done((f32[256,256]{1,0:T(8,128)S(1)}, f32[256,256]{1,0:T(8,128)S(1)}, u32[]{:S(2)}, u32[]{:S(2)}) %collective-permute-start.17) | collective-permute-done | bytes 262176 | tf_op jit(solution)/shard_map/ppermute | solution.py:17
  150.2 1.9 collective-permute-start.19
  152.2 8.9 %collective-permute-done.19 = f32[256,256]{1,0:T(8,128)S(1)} collective-permute-done((f32[256,256]{1,0:T(8,128)S(1)}, f32[256,256]{1,0:T(8,128)S(1)}, u32[]{:S(2)}, u32[]{:S(2)}) %collective-permute-start.19) | collective-permute-done | bytes 262176 | tf_op jit(solution)/shard_map/ppermute | solution.py:17
  161.1 1.9 collective-permute-start.20
  163.1 8.1 %collective-permute-done.20 = f32[256,256]{1,0:T(8,128)S(1)} collective-permute-done((f32[256,256]{1,0:T(8,128)S(1)}, f32[256,256]{1,0:T(8,128)S(1)}, u32[]{:S(2)}, u32[]{:S(2)}) %collective-permute-start.20) | collective-permute-done | bytes 262176 | tf_op jit(solution)/shard_map/ppermute | solution.py:17
  171.2 1.9 collective-permute-start.21
  173.2 2.4 %collective-permute-start.22 = (bf16[256,256]{1,0:T(8,128)(2,1)S(1)}, bf16[256,256]{1,0:T(8,128)(2,1)S(1)}, u32[]{:S(2)}, u32[]{:S(2)}) collective-permute-start(bf16[256,256]{1,0:T(8,128)(2,1)S(1)} %copy.26), channel_id=1, source_target_pairs={{192,0},{384,192},{576,384},{193,1},{385,193},{577,385},{194,2},{3... | collective-permute-start | bytes 393224 | tf_op jit(solution)/shard_map/ppermute | solution.py:17
  175.7 5.0 %collective-permute-done.21 = f32[256,256]{1,0:T(8,128)S(1)} collective-permute-done((f32[256,256]{1,0:T(8,128)S(1)}, f32[256,256]{1,0:T(8,128)S(1)}, u32[]{:S(2)}, u32[]{:S(2)}) %collective-permute-start.21) | collective-permute-done | bytes 262176 | tf_op jit(solution)/shard_map/ppermute | solution.py:17
  180.7 1.9 collective-permute-start.23
  182.7 7.5 %collective-permute-done.23 = f32[256,256]{1,0:T(8,128)S(1)} collective-permute-done((f32[256,256]{1,0:T(8,128)S(1)}, f32[256,256]{1,0:T(8,128)S(1)}, u32[]{:S(2)}, u32[]{:S(2)}) %collective-permute-start.23) | collective-permute-done | bytes 262176 | tf_op jit(solution)/shard_map/ppermute | solution.py:17
  190.2 1.9 collective-permute-start.24
  192.2 7.5 %collective-permute-done.24 = f32[256,256]{1,0:T(8,128)S(1)} collective-permute-done((f32[256,256]{1,0:T(8,128)S(1)}, f32[256,256]{1,0:T(8,128)S(1)}, u32[]{:S(2)}, u32[]{:S(2)}) %collective-permute-start.24) | collective-permute-done | bytes 262176 | tf_op jit(solution)/shard_map/ppermute | solution.py:17
  199.8 1.9 collective-permute-start.25
  201.7 2.4 %collective-permute-start.28 = (bf16[256,576]{0,1:T(8,128)(2,1)S(1)}, bf16[256,576]{0,1:T(8,128)(2,1)S(1)}, u32[]{:S(2)}, u32[]{:S(2)}) collective-permute-start(bf16[256,576]{0,1:T(8,128)(2,1)S(1)} %bitcast.184), channel_id=1, source_target_pairs={{192,0},{384,192},{576,384},{193,1},{385,193},{577,385},{194,2},{3... | collective-permute-start | bytes 884744 | tf_op jit(solution)/shard_map/ppermute | solution.py:17
  204.1 2.4 %collective-permute-start.27 = (f32[256,256]{1,0:T(8,128)S(1)}, f32[256,256]{1,0:T(8,128)S(1)}, u32[]{:S(2)}, u32[]{:S(2)}) collective-permute-start(f32[256,256]{1,0:T(8,128)S(1)} %slice_bitcast_fusion.5), channel_id=1, source_target_pairs={{192,0},{384,192},{576,384},{193,1},{385,193},{577,385},{194,2},{3... | collective-permute-start | bytes 786440 | tf_op jit(solution)/shard_map/ppermute | solution.py:17
  206.5 3.8 %collective-permute-done.25 = f32[256,256]{1,0:T(8,128)S(1)} collective-permute-done((f32[256,256]{1,0:T(8,128)S(1)}, f32[256,256]{1,0:T(8,128)S(1)}, u32[]{:S(2)}, u32[]{:S(2)}) %collective-permute-start.25) | collective-permute-done | bytes 262176 | tf_op jit(solution)/shard_map/ppermute | solution.py:17
  210.3 1.9 collective-permute-start.26
  212.3 0.9 collective-permute-done.28
  213.1 2.8 %collective-permute-done.27 = f32[256,256]{1,0:T(8,128)S(1)} collective-permute-done((f32[256,256]{1,0:T(8,128)S(1)}, f32[256,256]{1,0:T(8,128)S(1)}, u32[]{:S(2)}, u32[]{:S(2)}) %collective-permute-start.27) | collective-permute-done | bytes 262176 | tf_op jit(solution)/shard_map/ppermute | solution.py:17
  215.9 4.8 %collective-permute-done.26 = f32[256,256]{1,0:T(8,128)S(1)} collective-permute-done((f32[256,256]{1,0:T(8,128)S(1)}, f32[256,256]{1,0:T(8,128)S(1)}, u32[]{:S(2)}, u32[]{:S(2)}) %collective-permute-start.26) | collective-permute-done | bytes 262176 | tf_op jit(solution)/shard_map/ppermute | solution.py:168
  (89 shorter events, 9.3 us)
Async XLA Ops:
  7.2 103.3 %all-gather.3.cloned.1.call-start = ((), (), s32[]{:S(2)}) async-start(), calls=%async_computation | async-start | bytes 2457600 | tf_op jit(solution)/shard_map/all_gather | solution.py:96
  7.2 39.7 %collective-permute-start.9 = (bf16[256,576]{0,1:T(8,128)(2,1)}, bf16[256,576]{0,1:T(8,128)(2,1)S(1)}, u32[]{:S(2)}, u32[]{:S(2)}) collective-permute-start(bf16[256,576]{0,1:T(8,128)(2,1)} %bitcast.182), channel_id=1, source_target_pairs={{0,7},{1,0},{2,1},{3,2},{4,3},{5,4},{6,5},{7,6},{8,15},{9,8},{10,9... | collective-permute-start | bytes 884744 | tf_op jit(solution)/shard_map/ppermute | solution.py:22
  12.6 39.5 %collective-permute-start.12 = (bf16[256,576]{0,1:T(8,128)(2,1)}, bf16[256,576]{0,1:T(8,128)(2,1)S(1)}, u32[]{:S(2)}, u32[]{:S(2)}) collective-permute-start(bf16[256,576]{0,1:T(8,128)(2,1)} %bitcast.183), channel_id=1, source_target_pairs={{0,1},{1,2},{2,3},{3,4},{4,5},{5,6},{6,7},{7,0},{8,9},{9,10},{10,1... | collective-permute-start | bytes 884744 | tf_op jit(solution)/shard_map/ppermute | solution.py:22
  15.4 17.3 %collective-permute-start = (bf16[256,256]{1,0:T(8,128)(2,1)S(1)}, bf16[256,256]{1,0:T(8,128)(2,1)S(1)}, u32[]{:S(2)}, u32[]{:S(2)}) collective-permute-start(bf16[256,256]{1,0:T(8,128)(2,1)S(1)} %pad_maximum_fusion), channel_id=1, source_target_pairs={{0,16},{8,24},{16,32},{24,40},{32,48},{40,56},{48,64},{56,72},{64,... | collective-permute-start | bytes 393224 | tf_op jit(solution)/shard_map/ppermute | solution.py:17
  23.8 76.2 %copy-start = (bf16[1,256,576]{1,2,0:T(8,128)(2,1)S(1)}, bf16[1,256,576]{1,2,0:T(8,128)(2,1)}, u32[]{:S(2)}) copy-start(bf16[1,256,576]{1,2,0:T(8,128)(2,1)} %param.7) | copy-start | bytes 884740
  32.7 8.0 %collective-permute-start.1 = (bf16[256,256]{1,0:T(8,128)(2,1)S(1)}, bf16[256,256]{1,0:T(8,128)(2,1)S(1)}, u32[]{:S(2)}, u32[]{:S(2)}) collective-permute-start(bf16[256,256]{1,0:T(8,128)(2,1)S(1)} %collective-permute-done), channel_id=1, source_target_pairs={{0,16},{8,24},{16,32},{24,40},{32,48},{40,56},{48,64},{56,72},{64,... | collective-permute-start | bytes 393224 | tf_op jit(solution)/shard_map/ppermute | solution.py:17
  40.7 13.4 %collective-permute-start.2 = (bf16[256,256]{1,0:T(8,128)(2,1)S(1)}, bf16[256,256]{1,0:T(8,128)(2,1)S(1)}, u32[]{:S(2)}, u32[]{:S(2)}) collective-permute-start(bf16[256,256]{1,0:T(8,128)(2,1)S(1)} %collective-permute-done.1), channel_id=1, source_target_pairs={{0,16},{8,24},{16,32},{24,40},{32,48},{40,56},{48,64},{56,72},{64,... | collective-permute-start | bytes 393224 | tf_op jit(solution)/shard_map/ppermute | solution.py:17
  47.0 19.8 %collective-permute-start.10 = (bf16[256,576]{0,1:T(8,128)(2,1)S(1)}, bf16[256,576]{0,1:T(8,128)(2,1)S(1)}, u32[]{:S(2)}, u32[]{:S(2)}) collective-permute-start(bf16[256,576]{0,1:T(8,128)(2,1)S(1)} %collective-permute-done.9), channel_id=1, source_target_pairs={{0,7},{1,0},{2,1},{3,2},{4,3},{5,4},{6,5},{7,6},{8,15},{9,8},{10,9... | collective-permute-start | bytes 884744 | tf_op jit(solution)/shard_map/ppermute | solution.py:22
  52.1 19.6 %collective-permute-start.13 = (bf16[256,576]{0,1:T(8,128)(2,1)S(1)}, bf16[256,576]{0,1:T(8,128)(2,1)S(1)}, u32[]{:S(2)}, u32[]{:S(2)}) collective-permute-start(bf16[256,576]{0,1:T(8,128)(2,1)S(1)} %collective-permute-done.12), channel_id=1, source_target_pairs={{0,1},{1,2},{2,3},{3,4},{4,5},{5,6},{6,7},{7,0},{8,9},{9,10},{10,1... | collective-permute-start | bytes 884744 | tf_op jit(solution)/shard_map/ppermute | solution.py:22
  54.1 7.1 %collective-permute-start.3 = (bf16[256,256]{1,0:T(8,128)(2,1)S(1)}, bf16[256,256]{1,0:T(8,128)(2,1)S(1)}, u32[]{:S(2)}, u32[]{:S(2)}) collective-permute-start(bf16[256,256]{1,0:T(8,128)(2,1)S(1)} %collective-permute-done.2), channel_id=1, source_target_pairs={{0,16},{8,24},{16,32},{24,40},{32,48},{40,56},{48,64},{56,72},{64,... | collective-permute-start | bytes 393224 | tf_op jit(solution)/shard_map/ppermute | solution.py:17
  61.2 12.5 %collective-permute-start.4 = (bf16[256,256]{1,0:T(8,128)(2,1)S(1)}, bf16[256,256]{1,0:T(8,128)(2,1)S(1)}, u32[]{:S(2)}, u32[]{:S(2)}) collective-permute-start(bf16[256,256]{1,0:T(8,128)(2,1)S(1)} %collective-permute-done.3), channel_id=1, source_target_pairs={{0,16},{8,24},{16,32},{24,40},{32,48},{40,56},{48,64},{56,72},{64,... | collective-permute-start | bytes 393224 | tf_op jit(solution)/shard_map/ppermute | solution.py:17
  66.7 21.3 %collective-permute-start.11 = (bf16[256,576]{0,1:T(8,128)(2,1)S(1)}, bf16[256,576]{0,1:T(8,128)(2,1)S(1)}, u32[]{:S(2)}, u32[]{:S(2)}) collective-permute-start(bf16[256,576]{0,1:T(8,128)(2,1)S(1)} %collective-permute-done.10), channel_id=1, source_target_pairs={{0,7},{1,0},{2,1},{3,2},{4,3},{5,4},{6,5},{7,6},{8,15},{9,8},{10,9... | collective-permute-start | bytes 884744 | tf_op jit(solution)/shard_map/ppermute | solution.py:22
  71.7 14.4 %collective-permute-start.14 = (bf16[256,576]{0,1:T(8,128)(2,1)S(1)}, bf16[256,576]{0,1:T(8,128)(2,1)S(1)}, u32[]{:S(2)}, u32[]{:S(2)}) collective-permute-start(bf16[256,576]{0,1:T(8,128)(2,1)S(1)} %collective-permute-done.13), channel_id=1, source_target_pairs={{0,1},{1,2},{2,3},{3,4},{4,5},{5,6},{6,7},{7,0},{8,9},{9,10},{10,1... | collective-permute-start | bytes 884744 | tf_op jit(solution)/shard_map/ppermute | solution.py:22
  73.7 7.8 %collective-permute-start.5 = (bf16[256,256]{1,0:T(8,128)(2,1)S(1)}, bf16[256,256]{1,0:T(8,128)(2,1)S(1)}, u32[]{:S(2)}, u32[]{:S(2)}) collective-permute-start(bf16[256,256]{1,0:T(8,128)(2,1)S(1)} %collective-permute-done.4), channel_id=1, source_target_pairs={{0,16},{8,24},{16,32},{24,40},{32,48},{40,56},{48,64},{56,72},{64,... | collective-permute-start | bytes 393224 | tf_op jit(solution)/shard_map/ppermute | solution.py:17
  81.5 7.5 %collective-permute-start.6 = (bf16[256,256]{1,0:T(8,128)(2,1)S(1)}, bf16[256,256]{1,0:T(8,128)(2,1)S(1)}, u32[]{:S(2)}, u32[]{:S(2)}) collective-permute-start(bf16[256,256]{1,0:T(8,128)(2,1)S(1)} %collective-permute-done.5), channel_id=1, source_target_pairs={{0,16},{8,24},{16,32},{24,40},{32,48},{40,56},{48,64},{56,72},{64,... | collective-permute-start | bytes 393224 | tf_op jit(solution)/shard_map/ppermute | solution.py:17
  86.1 13.8 %collective-permute-start.15 = (bf16[256,576]{0,1:T(8,128)(2,1)S(1)}, bf16[256,576]{0,1:T(8,128)(2,1)S(1)}, u32[]{:S(2)}, u32[]{:S(2)}) collective-permute-start(bf16[256,576]{0,1:T(8,128)(2,1)S(1)} %collective-permute-done.14), channel_id=1, source_target_pairs={{0,1},{1,2},{2,3},{3,4},{4,5},{5,6},{6,7},{7,0},{8,9},{9,10},{10,1... | collective-permute-start | bytes 884744 | tf_op jit(solution)/shard_map/ppermute | solution.py:22
  89.0 8.1 %collective-permute-start.7 = (bf16[256,256]{1,0:T(8,128)(2,1)S(1)}, bf16[256,256]{1,0:T(8,128)(2,1)S(1)}, u32[]{:S(2)}, u32[]{:S(2)}) collective-permute-start(bf16[256,256]{1,0:T(8,128)(2,1)S(1)} %collective-permute-done.6), channel_id=1, source_target_pairs={{0,16},{8,24},{16,32},{24,40},{32,48},{40,56},{48,64},{56,72},{64,... | collective-permute-start | bytes 393224 | tf_op jit(solution)/shard_map/ppermute | solution.py:17
  97.8 4.9 %collective-permute-start.8 = (bf16[9,256,256]{2,1,0:T(8,128)(2,1)}, bf16[9,256,256]{2,1,0:T(8,128)(2,1)S(1)}, u32[]{:S(2)}, u32[]{:S(2)}) collective-permute-start(bf16[9,256,256]{2,1,0:T(8,128)(2,1)} %get-tuple-element.18), channel_id=1, source_target_pairs={{0,8},{8,0},{16,24},{24,16},{32,40},{40,32},{48,56},{56,48},{64,72... | collective-permute-start | bytes 3538952 | tf_op jit(solution)/shard_map/ppermute | solution.py:122
  100.2 3.7 %copy-start.2 = (bf16[256,2,128]{2,1,0:T(2,128)(2,1)S(1)}, bf16[256,2,128]{2,1,0:T(2,128)(2,1)}, u32[]{:S(2)}) copy-start(bf16[256,2,128]{2,1,0:T(2,128)(2,1)} %reshape.267) | copy-start | bytes 393220
  113.1 6.3 %slice-start = ((s8[9437184]{0:T(1024)(128)(4,1)}), s8[4194304]{0:T(1024)(128)(4,1)S(1)}, s32[]{:S(2)}) async-start(s8[9437184]{0:T(1024)(128)(4,1)} %bitcast.176), calls=%async_computation.1 | async-start | bytes 8388608
  113.1 6.6 %slice-start.1 = ((s8[9437184]{0:T(1024)(128)(4,1)}), s8[4194304]{0:T(1024)(128)(4,1)S(1)}, s32[]{:S(2)}) async-start(s8[9437184]{0:T(1024)(128)(4,1)} %bitcast.176), calls=%async_computation.2 | async-start | bytes 8388608
  113.2 6.8 %slice-start.2 = ((s8[9437184]{0:T(1024)(128)(4,1)}), s8[1048576]{0:T(1024)(128)(4,1)S(1)}, s32[]{:S(2)}) async-start(s8[9437184]{0:T(1024)(128)(4,1)} %bitcast.176), calls=%async_computation.3 | async-start | bytes 2097152
  124.5 2.2 copy-start.3
  131.6 8.4 %collective-permute-start.18 = (f32[8,256,256]{2,1,0:T(8,128)S(1)}, f32[8,256,256]{2,1,0:T(8,128)S(1)}, u32[]{:S(2)}, u32[]{:S(2)}) collective-permute-start(f32[8,256,256]{2,1,0:T(8,128)S(1)} %bitcast.180), channel_id=1, source_target_pairs={{0,8},{8,0},{16,24},{24,16},{32,40},{40,32},{48,56},{56,48},{64,72... | collective-permute-start | bytes 6291464 | tf_op jit(solution)/shard_map/ppermute | solution.py:156
  133.6 4.4 %collective-permute-start.16 = (f32[256,256]{1,0:T(8,128)S(1)}, f32[256,256]{1,0:T(8,128)S(1)}, u32[]{:S(2)}, u32[]{:S(2)}) collective-permute-start(f32[256,256]{1,0:T(8,128)S(1)} %slice.97), channel_id=1, source_target_pairs={{0,8},{8,0},{16,24},{24,16},{32,40},{40,32},{48,56},{56,48},{64,72... | collective-permute-start | bytes 786440 | tf_op jit(solution)/shard_map/ppermute | solution.py:155
  138.0 12.2 %collective-permute-start.17 = (f32[256,256]{1,0:T(8,128)S(1)}, f32[256,256]{1,0:T(8,128)S(1)}, u32[]{:S(2)}, u32[]{:S(2)}) collective-permute-start(f32[256,256]{1,0:T(8,128)S(1)} %slice_add_fusion), channel_id=1, source_target_pairs={{16,0},{24,8},{32,16},{40,24},{48,32},{56,40},{64,48},{72,56},{80,... | collective-permute-start | bytes 786440 | tf_op jit(solution)/shard_map/ppermute | solution.py:17
  140.0 61.7 %copy-start.1 = (bf16[1,256,576]{1,2,0:T(8,128)(2,1)S(1)}, bf16[1,256,576]{1,2,0:T(8,128)(2,1)}, u32[]{:S(2)}) copy-start(bf16[1,256,576]{1,2,0:T(8,128)(2,1)} %param.7) | copy-start | bytes 884740
  150.2 10.9 %collective-permute-start.19 = (f32[256,256]{1,0:T(8,128)S(1)}, f32[256,256]{1,0:T(8,128)S(1)}, u32[]{:S(2)}, u32[]{:S(2)}) collective-permute-start(f32[256,256]{1,0:T(8,128)S(1)} %fusion.25), channel_id=1, source_target_pairs={{16,0},{24,8},{32,16},{40,24},{48,32},{56,40},{64,48},{72,56},{80,... | collective-permute-start | bytes 786440 | tf_op jit(solution)/shard_map/ppermute | solution.py:17
  161.1 10.0 %collective-permute-start.20 = (f32[256,256]{1,0:T(8,128)S(1)}, f32[256,256]{1,0:T(8,128)S(1)}, u32[]{:S(2)}, u32[]{:S(2)}) collective-permute-start(f32[256,256]{1,0:T(8,128)S(1)} %fusion.24), channel_id=1, source_target_pairs={{16,0},{24,8},{32,16},{40,24},{48,32},{56,40},{64,48},{72,56},{80,... | collective-permute-start | bytes 786440 | tf_op jit(solution)/shard_map/ppermute | solution.py:17
  171.2 9.5 %collective-permute-start.21 = (f32[256,256]{1,0:T(8,128)S(1)}, f32[256,256]{1,0:T(8,128)S(1)}, u32[]{:S(2)}, u32[]{:S(2)}) collective-permute-start(f32[256,256]{1,0:T(8,128)S(1)} %fusion.23), channel_id=1, source_target_pairs={{16,0},{24,8},{32,16},{40,24},{48,32},{56,40},{64,48},{72,56},{80,... | collective-permute-start | bytes 786440 | tf_op jit(solution)/shard_map/ppermute | solution.py:17
  173.2 7.5 %collective-permute-start.22 = (bf16[256,256]{1,0:T(8,128)(2,1)S(1)}, bf16[256,256]{1,0:T(8,128)(2,1)S(1)}, u32[]{:S(2)}, u32[]{:S(2)}) collective-permute-start(bf16[256,256]{1,0:T(8,128)(2,1)S(1)} %copy.26), channel_id=1, source_target_pairs={{192,0},{384,192},{576,384},{193,1},{385,193},{577,385},{194,2},{3... | collective-permute-start | bytes 393224 | tf_op jit(solution)/shard_map/ppermute | solution.py:17
  180.7 9.5 %collective-permute-start.23 = (f32[256,256]{1,0:T(8,128)S(1)}, f32[256,256]{1,0:T(8,128)S(1)}, u32[]{:S(2)}, u32[]{:S(2)}) collective-permute-start(f32[256,256]{1,0:T(8,128)S(1)} %fusion.22), channel_id=1, source_target_pairs={{16,0},{24,8},{32,16},{40,24},{48,32},{56,40},{64,48},{72,56},{80,... | collective-permute-start | bytes 786440 | tf_op jit(solution)/shard_map/ppermute | solution.py:17
  190.2 9.5 %collective-permute-start.24 = (f32[256,256]{1,0:T(8,128)S(1)}, f32[256,256]{1,0:T(8,128)S(1)}, u32[]{:S(2)}, u32[]{:S(2)}) collective-permute-start(f32[256,256]{1,0:T(8,128)S(1)} %fusion.21), channel_id=1, source_target_pairs={{16,0},{24,8},{32,16},{40,24},{48,32},{56,40},{64,48},{72,56},{80,... | collective-permute-start | bytes 786440 | tf_op jit(solution)/shard_map/ppermute | solution.py:17
  199.8 10.5 %collective-permute-start.25 = (f32[256,256]{1,0:T(8,128)S(1)}, f32[256,256]{1,0:T(8,128)S(1)}, u32[]{:S(2)}, u32[]{:S(2)}) collective-permute-start(f32[256,256]{1,0:T(8,128)S(1)} %fusion.20), channel_id=1, source_target_pairs={{16,0},{24,8},{32,16},{40,24},{48,32},{56,40},{64,48},{72,56},{80,... | collective-permute-start | bytes 786440 | tf_op jit(solution)/shard_map/ppermute | solution.py:17
  201.7 11.4 %collective-permute-start.28 = (bf16[256,576]{0,1:T(8,128)(2,1)S(1)}, bf16[256,576]{0,1:T(8,128)(2,1)S(1)}, u32[]{:S(2)}, u32[]{:S(2)}) collective-permute-start(bf16[256,576]{0,1:T(8,128)(2,1)S(1)} %bitcast.184), channel_id=1, source_target_pairs={{192,0},{384,192},{576,384},{193,1},{385,193},{577,385},{194,2},{3... | collective-permute-start | bytes 884744 | tf_op jit(solution)/shard_map/ppermute | solution.py:17
  204.1 11.8 %collective-permute-start.27 = (f32[256,256]{1,0:T(8,128)S(1)}, f32[256,256]{1,0:T(8,128)S(1)}, u32[]{:S(2)}, u32[]{:S(2)}) collective-permute-start(f32[256,256]{1,0:T(8,128)S(1)} %slice_bitcast_fusion.5), channel_id=1, source_target_pairs={{192,0},{384,192},{576,384},{193,1},{385,193},{577,385},{194,2},{3... | collective-permute-start | bytes 786440 | tf_op jit(solution)/shard_map/ppermute | solution.py:17
  210.3 10.4 %collective-permute-start.26 = (f32[256,256]{1,0:T(8,128)S(1)}, f32[256,256]{1,0:T(8,128)S(1)}, u32[]{:S(2)}, u32[]{:S(2)}) collective-permute-start(f32[256,256]{1,0:T(8,128)S(1)} %fusion.19), channel_id=1, source_target_pairs={{208,0},{216,8},{224,16},{232,24},{240,32},{248,40},{256,48},{264,... | collective-permute-start | bytes 786440 | tf_op jit(solution)/shard_map/ppermute | solution.py:168
Sparse Core Ops, SparseCore 0:
  21.1 58.8 all-gather.2

commit v11 on v10

--- a/solution.py
+++ b/solution.py
@@ -160,6 +160,8 @@
         running = from_behind(running, "row", -2) + chip_sum[hops - step]
         if step == hops // 2:
             running, query_handed = lax.optimization_barrier((running, query_handed))
+        if step == hops - 2:
+            running, own_handed = lax.optimization_barrier((running, own_handed))
     last_pairs = [
         (p * row_count + r, (p - 1) * row_count + r - 2)
         for p in range(1, pipe_count)

time: 231 us -> 232 us (level)
  the two profiles are of different devices: /device:TPU:196 before, /device:TPU:194 now
where the time goes in v11:
time: 232 us; the launch traced here: 230 us
  starting transfers between devices  87.6 us (38%)
  waiting for transfers between devices  77.5 us (33%)
  matrix products  21.9 us (9%)
  local copies, waits for them, and re-layouts  15.1 us (7%)
  between operations  14.8 us (6%)
  other arithmetic  13.4 us (6%)
    ppermute x18, waiting for transfers between devices, from_behind(): return lax.ppermute(block, axis, route)  65.5 us
    ppermute x18, starting transfers between devices, from_behind(): return lax.ppermute(block, axis, route)  56 us
    ppermute x7, starting transfers between devices, cyclic_shift(): lax.ppermute(block, axis, [(i, (i + distance) % size) for i in range(size)])  23.2 us
    unnamed x40, local copies, waits for them, and re-layouts  8.47 us
    ppermute x1, waiting for transfers between devices, per_device(): total = lax.ppermute(running, ('pipe', 'row'), last_pairs) + own_handed  7.64 us
    dot_general x1, matrix products, attend(): jnp.einsum('qgrd,kgd->grqk', query_g, key_g, preferred_element_type=jnp.f...  6.6 us
    dot_general x1, matrix products, attend(): jnp.einsum('qgrd,kgd->grqk', attn_g, value_g, preferred_element_type=jnp....  6.28 us
    and x1, other arithmetic, per_device(): allowed & ((key_doc[None, :] == query_doc[:, None]) | (key_shared[None, :...  4.64 us
  transfers between devices with their start and end apart: 30, of which 17 were waited for; matrix products, arithmetic and copies ran while one was open for 12% of the time, Pallas kernels for 0%

profile of v11, /device:TPU:194, one launch (start us, length us, event | category | flops | bytes accessed | tf_op | source)
XLA Modules:
  0.0 230.3 jit_solution(4695938645272482194)
XLA Ops:
  7.2 5.4 %collective-permute-start.9 = (bf16[256,576]{0,1:T(8,128)(2,1)}, bf16[256,576]{0,1:T(8,128)(2,1)S(1)}, u32[]{:S(2)}, u32[]{:S(2)}) collective-permute-start(bf16[256,576]{0,1:T(8,128)(2,1)} %bitcast.182), channel_id=1, source_target_pairs={{0,7},{1,0},{2,1},{3,2},{4,3},{5,4},{6,5},{7,6},{8,15},{9,8},{10,9... | collective-permute-start | bytes 884744 | tf_op jit(solution)/shard_map/ppermute | solution.py:22
  12.6 1.9 collective-permute-start.12
  14.5 0.9 pad_maximum_fusion
  15.4 5.5 %collective-permute-start = (bf16[256,256]{1,0:T(8,128)(2,1)S(1)}, bf16[256,256]{1,0:T(8,128)(2,1)S(1)}, u32[]{:S(2)}, u32[]{:S(2)}) collective-permute-start(bf16[256,256]{1,0:T(8,128)(2,1)S(1)} %pad_maximum_fusion), channel_id=1, source_target_pairs={{0,16},{8,24},{16,32},{24,40},{32,48},{40,56},{48,64},{56,72},{64,... | collective-permute-start | bytes 393224 | tf_op jit(solution)/shard_map/ppermute | solution.py:17
  21.7 0.9 pad_dynamic-slice_fusion
  23.0 0.8 select_reduce_fusion
  23.8 4.6 %fusion.10 = pred[256,4608]{0,1:T(8,128)(4,1)S(1)} fusion(s32[256]{0:T(256)S(1)} %bitcast.192, s32[256]{0:T(256)S(1)} %iota_add_fusion.1, s32[4608]{0:T(1024)S(1)} %constant_dynamic-update-slice_fusion.6, s32[4608]{0:T(1024)S(1)} %add.97, pred[4608]{0:T(1024)(128)(4,1)S(1)} %broadcast_compare_fusion, pred[4608]{0:T(1024)(128)(4,1)S(1)} %broadcast_compare_fusion.1), kind=kLoop, calls=%fused_computation.18 | loop fusion | flops 9437184 | bytes 1227776 | tf_op jit(solution)/shard_map/and | solution.py:146
  28.5 1.6 bitcast_dynamic-update-slice_fusion.31
  30.1 1.6 reshape.267
  31.7 1.0 constant_dynamic-update-slice_fusion.3
  32.7 4.3 %collective-permute-start.1 = (bf16[256,256]{1,0:T(8,128)(2,1)S(1)}, bf16[256,256]{1,0:T(8,128)(2,1)S(1)}, u32[]{:S(2)}, u32[]{:S(2)}) collective-permute-start(bf16[256,256]{1,0:T(8,128)(2,1)S(1)} %collective-permute-done), channel_id=1, source_target_pairs={{0,16},{8,24},{16,32},{24,40},{32,48},{40,56},{48,64},{56,72},{64,... | collective-permute-start | bytes 393224 | tf_op jit(solution)/shard_map/ppermute | solution.py:17
  37.7 2.9 %collective-permute-done.1 = bf16[256,256]{1,0:T(8,128)(2,1)S(1)} collective-permute-done((bf16[256,256]{1,0:T(8,128)(2,1)S(1)}, bf16[256,256]{1,0:T(8,128)(2,1)S(1)}, u32[]{:S(2)}, u32[]{:S(2)}) %collective-permute-start.1) | collective-permute-done | bytes 131104 | tf_op jit(solution)/shard_map/ppermute | solution.py:17
  40.7 5.6 %collective-permute-start.2 = (bf16[256,256]{1,0:T(8,128)(2,1)S(1)}, bf16[256,256]{1,0:T(8,128)(2,1)S(1)}, u32[]{:S(2)}, u32[]{:S(2)}) collective-permute-start(bf16[256,256]{1,0:T(8,128)(2,1)S(1)} %collective-permute-done.1), channel_id=1, source_target_pairs={{0,16},{8,24},{16,32},{24,40},{32,48},{40,56},{48,64},{56,72},{64,... | collective-permute-start | bytes 393224 | tf_op jit(solution)/shard_map/ppermute | solution.py:17
  47.0 5.1 %collective-permute-start.10 = (bf16[256,576]{0,1:T(8,128)(2,1)S(1)}, bf16[256,576]{0,1:T(8,128)(2,1)S(1)}, u32[]{:S(2)}, u32[]{:S(2)}) collective-permute-start(bf16[256,576]{0,1:T(8,128)(2,1)S(1)} %collective-permute-done.9), channel_id=1, source_target_pairs={{0,7},{1,0},{2,1},{3,2},{4,3},{5,4},{6,5},{7,6},{8,15},{9,8},{10,9... | collective-permute-start | bytes 884744 | tf_op jit(solution)/shard_map/ppermute | solution.py:22
  52.1 1.9 collective-permute-start.13
  54.1 2.9 %collective-permute-start.3 = (bf16[256,256]{1,0:T(8,128)(2,1)S(1)}, bf16[256,256]{1,0:T(8,128)(2,1)S(1)}, u32[]{:S(2)}, u32[]{:S(2)}) collective-permute-start(bf16[256,256]{1,0:T(8,128)(2,1)S(1)} %collective-permute-done.2), channel_id=1, source_target_pairs={{0,16},{8,24},{16,32},{24,40},{32,48},{40,56},{48,64},{56,72},{64,... | collective-permute-start | bytes 393224 | tf_op jit(solution)/shard_map/ppermute | solution.py:17
  57.7 3.4 %collective-permute-done.3 = bf16[256,256]{1,0:T(8,128)(2,1)S(1)} collective-permute-done((bf16[256,256]{1,0:T(8,128)(2,1)S(1)}, bf16[256,256]{1,0:T(8,128)(2,1)S(1)}, u32[]{:S(2)}, u32[]{:S(2)}) %collective-permute-start.3) | collective-permute-done | bytes 131104 | tf_op jit(solution)/shard_map/ppermute | solution.py:17
  61.2 4.8 %collective-permute-start.4 = (bf16[256,256]{1,0:T(8,128)(2,1)S(1)}, bf16[256,256]{1,0:T(8,128)(2,1)S(1)}, u32[]{:S(2)}, u32[]{:S(2)}) collective-permute-start(bf16[256,256]{1,0:T(8,128)(2,1)S(1)} %collective-permute-done.3), channel_id=1, source_target_pairs={{0,16},{8,24},{16,32},{24,40},{32,48},{40,56},{48,64},{56,72},{64,... | collective-permute-start | bytes 393224 | tf_op jit(solution)/shard_map/ppermute | solution.py:17
  66.0 0.7 bitcast_dynamic-update-slice_fusion.23
  66.7 5.0 %collective-permute-start.11 = (bf16[256,576]{0,1:T(8,128)(2,1)S(1)}, bf16[256,576]{0,1:T(8,128)(2,1)S(1)}, u32[]{:S(2)}, u32[]{:S(2)}) collective-permute-start(bf16[256,576]{0,1:T(8,128)(2,1)S(1)} %collective-permute-done.10), channel_id=1, source_target_pairs={{0,7},{1,0},{2,1},{3,2},{4,3},{5,4},{6,5},{7,6},{8,15},{9,8},{10,9... | collective-permute-start | bytes 884744 | tf_op jit(solution)/shard_map/ppermute | solution.py:22
  71.7 1.9 collective-permute-start.14
  73.7 3.0 %collective-permute-start.5 = (bf16[256,256]{1,0:T(8,128)(2,1)S(1)}, bf16[256,256]{1,0:T(8,128)(2,1)S(1)}, u32[]{:S(2)}, u32[]{:S(2)}) collective-permute-start(bf16[256,256]{1,0:T(8,128)(2,1)S(1)} %collective-permute-done.4), channel_id=1, source_target_pairs={{0,16},{8,24},{16,32},{24,40},{32,48},{40,56},{48,64},{56,72},{64,... | collective-permute-start | bytes 393224 | tf_op jit(solution)/shard_map/ppermute | solution.py:17
  77.4 4.0 %collective-permute-done.5 = bf16[256,256]{1,0:T(8,128)(2,1)S(1)} collective-permute-done((bf16[256,256]{1,0:T(8,128)(2,1)S(1)}, bf16[256,256]{1,0:T(8,128)(2,1)S(1)}, u32[]{:S(2)}, u32[]{:S(2)}) %collective-permute-start.5) | collective-permute-done | bytes 131104 | tf_op jit(solution)/shard_map/ppermute | solution.py:17
  81.4 3.8 %collective-permute-start.6 = (bf16[256,256]{1,0:T(8,128)(2,1)S(1)}, bf16[256,256]{1,0:T(8,128)(2,1)S(1)}, u32[]{:S(2)}, u32[]{:S(2)}) collective-permute-start(bf16[256,256]{1,0:T(8,128)(2,1)S(1)} %collective-permute-done.5), channel_id=1, source_target_pairs={{0,16},{8,24},{16,32},{24,40},{32,48},{40,56},{48,64},{56,72},{64,... | collective-permute-start | bytes 393224 | tf_op jit(solution)/shard_map/ppermute | solution.py:17
  85.2 0.7 bitcast_dynamic-update-slice_fusion.19
  86.0 1.9 collective-permute-start.15
  87.9 1.0 collective-permute-done.6
  88.9 5.6 %collective-permute-start.7 = (bf16[256,256]{1,0:T(8,128)(2,1)S(1)}, bf16[256,256]{1,0:T(8,128)(2,1)S(1)}, u32[]{:S(2)}, u32[]{:S(2)}) collective-permute-start(bf16[256,256]{1,0:T(8,128)(2,1)S(1)} %collective-permute-done.6), channel_id=1, source_target_pairs={{0,16},{8,24},{16,32},{24,40},{32,48},{40,56},{48,64},{56,72},{64,... | collective-permute-start | bytes 393224 | tf_op jit(solution)/shard_map/ppermute | solution.py:17
  94.5 0.7 bitcast_dynamic-update-slice_fusion.17
  95.2 1.8 collective-permute-done.7
  97.0 0.7 bitcast_dynamic-update-slice_fusion.15
  97.7 2.1 collective-permute-start.8
  100.4 2.3 collective-permute-done.8
  102.7 1.1 constant_dynamic-update-slice_fusion
  103.8 6.6 %fusion.5 = (f32[2,256]{1,0:T(2,128)S(1)}, f32[4608,256,2]{1,0,2:T(8,128)}) fusion(pred[256,4608]{0,1:T(8,128)(4,1)S(1)} %fusion.10, bf16[256,2,128]{2,1,0:T(2,128)(2,1)S(1)} %copy-done.2, bf16[4608,256]{1,0:T(8,128)(2,1)} %bitcast.11), kind=kOutput, calls=%fused_computation.10 | convolution fusion | flops 613416448 | bytes 11929600 | tf_op jit(solution)/shard_map/qgrd,kgd->grqk/dot_general | solution.py:52
  110.4 2.7 %fusion.15 = bf16[256,256]{0,1:T(8,128)(2,1)S(1)} fusion(bf16[256,4608]{0,1:T(8,128)(2,1)S(1)} %bitcast.179, bf16[1,256,4608]{1,2,0:T(8,128)(2,1)} %all-gather.3.cloned.1.call-done), kind=kOutput, calls=%fused_computation.24 | convolution fusion | flops 604045312 | bytes 4849664 | tf_op jit(solution)/shard_map/dot_general | solution.py:94
  113.1 6.3 %fusion.2 = (f32[2,256]{1,0:T(2,128)S(1)}, f32[4608,256,2]{1,0,2:T(8,128)S(1)}) fusion(f32[2,256]{1,0:T(2,128)S(1)} %get-tuple-element.42, f32[4608,256,2]{1,0,2:T(8,128)} %get-tuple-element.43, pred[256,4608]{0,1:T(8,128)(4,1)S(1)} %fusion.10, bf16[256,2,128]{0,2,1:T(8,128)(2,1)S(1)} %bitcast.194, bf16[4608,256]{1,0:T(8,128)(2,1)} %bitcast.11), kind=kOutput, calls=%fused_computation.6 | convolution fusion | flops 618135040 | bytes 21368832 | tf_op jit(solution)/shard_map/qgrd,kgd->grqk/dot_general | solution.py:62
  119.9 4.6 %fusion.6 = bf16[2,256,4608]{1,2,0:T(8,128)(2,1)S(1)} fusion(f32[4608,256,2]{1,0,2:T(8,128)S(1)} %bitcast.177, f32[4608,256,2]{1,0,2:T(8,128)S(1)} %get-tuple-element.45, f32[2,256]{1,0:T(2,128)S(1)} %get-tuple-element.44, f32[2,256]{1,0:T(2,128)S(1)} %get-tuple-element.42, pred[256,4608]{0,1:T(8,128)(4,1)S(1)} %fusion.10), kind=kLoop, calls=%fused_computation.13 | loop fusion | flops 25952256 | bytes 24776704 | tf_op jit(solution)/shard_map/reshape.12
  124.5 2.1 convolution_convert_fusion
  126.6 1.4 convolution_bitcast_fusion.1
  128.0 2.8 %convolution_bitcast_fusion = f32[4608,128]{1,0:T(8,128)S(1)} fusion(bf16[256,2,128]{0,2,1:T(8,128)(2,1)S(1)} %bitcast.195, f32[4608,256,2]{1,0,2:T(8,128)S(1)} %bitcast.177, f32[2,256]{1,0:T(2,128)S(1)} %get-tuple-element.42, pred[256,4608]{0,1:T(8,128)(4,1)S(1)} %fusion.10), kind=kOutput, calls=%fused_computation.11 | convolution fusion | flops 615776256 | bytes 13109248 | tf_op jit(solution)/shard_map/grqk,qgrd->kgd/dot_general | solution.py:59
  131.5 2.1 collective-permute-start.18
  133.6 2.3 collective-permute-start.16
  135.9 2.1 collective-permute-done.16
  138.0 1.9 collective-permute-start.17
  140.3 9.8 %collective-permute-done.17 = f32[256,256]{1,0:T(8,128)S(1)} collective-permute-done((f32[256,256]{1,0:T(8,128)S(1)}, f32[256,256]{1,0:T(8,128)S(1)}, u32[]{:S(2)}, u32[]{:S(2)}) %collective-permute-start.17) | collective-permute-done | bytes 262176 | tf_op jit(solution)/shard_map/ppermute | solution.py:17
  150.2 1.9 collective-permute-start.19
  152.1 9.0 %collective-permute-done.19 = f32[256,256]{1,0:T(8,128)S(1)} collective-permute-done((f32[256,256]{1,0:T(8,128)S(1)}, f32[256,256]{1,0:T(8,128)S(1)}, u32[]{:S(2)}, u32[]{:S(2)}) %collective-permute-start.19) | collective-permute-done | bytes 262176 | tf_op jit(solution)/shard_map/ppermute | solution.py:17
  161.1 1.9 collective-permute-start.20
  163.0 8.1 %collective-permute-done.20 = f32[256,256]{1,0:T(8,128)S(1)} collective-permute-done((f32[256,256]{1,0:T(8,128)S(1)}, f32[256,256]{1,0:T(8,128)S(1)}, u32[]{:S(2)}, u32[]{:S(2)}) %collective-permute-start.20) | collective-permute-done | bytes 262176 | tf_op jit(solution)/shard_map/ppermute | solution.py:17
  171.2 1.9 collective-permute-start.21
  173.2 2.4 %collective-permute-start.22 = (bf16[256,256]{1,0:T(8,128)(2,1)S(1)}, bf16[256,256]{1,0:T(8,128)(2,1)S(1)}, u32[]{:S(2)}, u32[]{:S(2)}) collective-permute-start(bf16[256,256]{1,0:T(8,128)(2,1)S(1)} %copy.26), channel_id=1, source_target_pairs={{192,0},{384,192},{576,384},{193,1},{385,193},{577,385},{194,2},{3... | collective-permute-start | bytes 393224 | tf_op jit(solution)/shard_map/ppermute | solution.py:17
  175.6 5.1 %collective-permute-done.21 = f32[256,256]{1,0:T(8,128)S(1)} collective-permute-done((f32[256,256]{1,0:T(8,128)S(1)}, f32[256,256]{1,0:T(8,128)S(1)}, u32[]{:S(2)}, u32[]{:S(2)}) %collective-permute-start.21) | collective-permute-done | bytes 262176 | tf_op jit(solution)/shard_map/ppermute | solution.py:17
  180.7 1.9 collective-permute-start.23
  182.6 7.5 %collective-permute-done.23 = f32[256,256]{1,0:T(8,128)S(1)} collective-permute-done((f32[256,256]{1,0:T(8,128)S(1)}, f32[256,256]{1,0:T(8,128)S(1)}, u32[]{:S(2)}, u32[]{:S(2)}) %collective-permute-start.23) | collective-permute-done | bytes 262176 | tf_op jit(solution)/shard_map/ppermute | solution.py:17
  190.2 1.9 collective-permute-start.24
  192.2 2.4 %collective-permute-start.25 = (f32[256,256]{1,0:T(8,128)S(1)}, f32[256,256]{1,0:T(8,128)S(1)}, u32[]{:S(2)}, u32[]{:S(2)}) collective-permute-start(f32[256,256]{1,0:T(8,128)S(1)} %slice_bitcast_fusion.6), channel_id=1, source_target_pairs={{192,0},{384,192},{576,384},{193,1},{385,193},{577,385},{194,2},{3... | collective-permute-start | bytes 786440 | tf_op jit(solution)/shard_map/ppermute | solution.py:17
  194.6 5.1 %collective-permute-done.24 = f32[256,256]{1,0:T(8,128)S(1)} collective-permute-done((f32[256,256]{1,0:T(8,128)S(1)}, f32[256,256]{1,0:T(8,128)S(1)}, u32[]{:S(2)}, u32[]{:S(2)}) %collective-permute-start.24) | collective-permute-done | bytes 262176 | tf_op jit(solution)/shard_map/ppermute | solution.py:17
  200.4 1.9 collective-permute-start.26
  202.4 2.4 %collective-permute-start.28 = (bf16[256,576]{0,1:T(8,128)(2,1)S(1)}, bf16[256,576]{0,1:T(8,128)(2,1)S(1)}, u32[]{:S(2)}, u32[]{:S(2)}) collective-permute-start(bf16[256,576]{0,1:T(8,128)(2,1)S(1)} %bitcast.184), channel_id=1, source_target_pairs={{192,0},{384,192},{576,384},{193,1},{385,193},{577,385},{194,2},{3... | collective-permute-start | bytes 884744 | tf_op jit(solution)/shard_map/ppermute | solution.py:17
  204.7 6.0 %collective-permute-done.26 = f32[256,256]{1,0:T(8,128)S(1)} collective-permute-done((f32[256,256]{1,0:T(8,128)S(1)}, f32[256,256]{1,0:T(8,128)S(1)}, u32[]{:S(2)}, u32[]{:S(2)}) %collective-permute-start.26) | collective-permute-done | bytes 262176 | tf_op jit(solution)/shard_map/ppermute | solution.py:17
  210.7 1.9 collective-permute-start.27
  212.7 1.1 collective-permute-done.28
  213.8 7.6 %collective-permute-done.27 = f32[256,256]{1,0:T(8,128)S(1)} collective-permute-done((f32[256,256]{1,0:T(8,128)S(1)}, f32[256,256]{1,0:T(8,128)S(1)}, u32[]{:S(2)}, u32[]{:S(2)}) %collective-permute-start.27) | collective-permute-done | bytes 262176 | tf_op jit(solution)/shard_map/ppermute | solution.py:170
  (89 shorter events, 9.3 us)
Async XLA Ops:
  7.2 103.2 %all-gather.3.cloned.1.call-start = ((), (), s32[]{:S(2)}) async-start(), calls=%async_computation | async-start | bytes 2457600 | tf_op jit(solution)/shard_map/all_gather | solution.py:96
  7.2 39.7 %collective-permute-start.9 = (bf16[256,576]{0,1:T(8,128)(2,1)}, bf16[256,576]{0,1:T(8,128)(2,1)S(1)}, u32[]{:S(2)}, u32[]{:S(2)}) collective-permute-start(bf16[256,576]{0,1:T(8,128)(2,1)} %bitcast.182), channel_id=1, source_target_pairs={{0,7},{1,0},{2,1},{3,2},{4,3},{5,4},{6,5},{7,6},{8,15},{9,8},{10,9... | collective-permute-start | bytes 884744 | tf_op jit(solution)/shard_map/ppermute | solution.py:22
  12.6 39.5 %collective-permute-start.12 = (bf16[256,576]{0,1:T(8,128)(2,1)}, bf16[256,576]{0,1:T(8,128)(2,1)S(1)}, u32[]{:S(2)}, u32[]{:S(2)}) collective-permute-start(bf16[256,576]{0,1:T(8,128)(2,1)} %bitcast.183), channel_id=1, source_target_pairs={{0,1},{1,2},{2,3},{3,4},{4,5},{5,6},{6,7},{7,0},{8,9},{9,10},{10,1... | collective-permute-start | bytes 884744 | tf_op jit(solution)/shard_map/ppermute | solution.py:22
  15.4 17.3 %collective-permute-start = (bf16[256,256]{1,0:T(8,128)(2,1)S(1)}, bf16[256,256]{1,0:T(8,128)(2,1)S(1)}, u32[]{:S(2)}, u32[]{:S(2)}) collective-permute-start(bf16[256,256]{1,0:T(8,128)(2,1)S(1)} %pad_maximum_fusion), channel_id=1, source_target_pairs={{0,16},{8,24},{16,32},{24,40},{32,48},{40,56},{48,64},{56,72},{64,... | collective-permute-start | bytes 393224 | tf_op jit(solution)/shard_map/ppermute | solution.py:17
  23.8 76.2 %copy-start = (bf16[1,256,576]{1,2,0:T(8,128)(2,1)S(1)}, bf16[1,256,576]{1,2,0:T(8,128)(2,1)}, u32[]{:S(2)}) copy-start(bf16[1,256,576]{1,2,0:T(8,128)(2,1)} %param.7) | copy-start | bytes 884740
  32.7 8.0 %collective-permute-start.1 = (bf16[256,256]{1,0:T(8,128)(2,1)S(1)}, bf16[256,256]{1,0:T(8,128)(2,1)S(1)}, u32[]{:S(2)}, u32[]{:S(2)}) collective-permute-start(bf16[256,256]{1,0:T(8,128)(2,1)S(1)} %collective-permute-done), channel_id=1, source_target_pairs={{0,16},{8,24},{16,32},{24,40},{32,48},{40,56},{48,64},{56,72},{64,... | collective-permute-start | bytes 393224 | tf_op jit(solution)/shard_map/ppermute | solution.py:17
  40.7 13.4 %collective-permute-start.2 = (bf16[256,256]{1,0:T(8,128)(2,1)S(1)}, bf16[256,256]{1,0:T(8,128)(2,1)S(1)}, u32[]{:S(2)}, u32[]{:S(2)}) collective-permute-start(bf16[256,256]{1,0:T(8,128)(2,1)S(1)} %collective-permute-done.1), channel_id=1, source_target_pairs={{0,16},{8,24},{16,32},{24,40},{32,48},{40,56},{48,64},{56,72},{64,... | collective-permute-start | bytes 393224 | tf_op jit(solution)/shard_map/ppermute | solution.py:17
  47.0 19.8 %collective-permute-start.10 = (bf16[256,576]{0,1:T(8,128)(2,1)S(1)}, bf16[256,576]{0,1:T(8,128)(2,1)S(1)}, u32[]{:S(2)}, u32[]{:S(2)}) collective-permute-start(bf16[256,576]{0,1:T(8,128)(2,1)S(1)} %collective-permute-done.9), channel_id=1, source_target_pairs={{0,7},{1,0},{2,1},{3,2},{4,3},{5,4},{6,5},{7,6},{8,15},{9,8},{10,9... | collective-permute-start | bytes 884744 | tf_op jit(solution)/shard_map/ppermute | solution.py:22
  52.1 19.6 %collective-permute-start.13 = (bf16[256,576]{0,1:T(8,128)(2,1)S(1)}, bf16[256,576]{0,1:T(8,128)(2,1)S(1)}, u32[]{:S(2)}, u32[]{:S(2)}) collective-permute-start(bf16[256,576]{0,1:T(8,128)(2,1)S(1)} %collective-permute-done.12), channel_id=1, source_target_pairs={{0,1},{1,2},{2,3},{3,4},{4,5},{5,6},{6,7},{7,0},{8,9},{9,10},{10,1... | collective-permute-start | bytes 884744 | tf_op jit(solution)/shard_map/ppermute | solution.py:22
  54.1 7.1 %collective-permute-start.3 = (bf16[256,256]{1,0:T(8,128)(2,1)S(1)}, bf16[256,256]{1,0:T(8,128)(2,1)S(1)}, u32[]{:S(2)}, u32[]{:S(2)}) collective-permute-start(bf16[256,256]{1,0:T(8,128)(2,1)S(1)} %collective-permute-done.2), channel_id=1, source_target_pairs={{0,16},{8,24},{16,32},{24,40},{32,48},{40,56},{48,64},{56,72},{64,... | collective-permute-start | bytes 393224 | tf_op jit(solution)/shard_map/ppermute | solution.py:17
  61.2 12.5 %collective-permute-start.4 = (bf16[256,256]{1,0:T(8,128)(2,1)S(1)}, bf16[256,256]{1,0:T(8,128)(2,1)S(1)}, u32[]{:S(2)}, u32[]{:S(2)}) collective-permute-start(bf16[256,256]{1,0:T(8,128)(2,1)S(1)} %collective-permute-done.3), channel_id=1, source_target_pairs={{0,16},{8,24},{16,32},{24,40},{32,48},{40,56},{48,64},{56,72},{64,... | collective-permute-start | bytes 393224 | tf_op jit(solution)/shard_map/ppermute | solution.py:17
  66.7 21.2 %collective-permute-start.11 = (bf16[256,576]{0,1:T(8,128)(2,1)S(1)}, bf16[256,576]{0,1:T(8,128)(2,1)S(1)}, u32[]{:S(2)}, u32[]{:S(2)}) collective-permute-start(bf16[256,576]{0,1:T(8,128)(2,1)S(1)} %collective-permute-done.10), channel_id=1, source_target_pairs={{0,7},{1,0},{2,1},{3,2},{4,3},{5,4},{6,5},{7,6},{8,15},{9,8},{10,9... | collective-permute-start | bytes 884744 | tf_op jit(solution)/shard_map/ppermute | solution.py:22
  71.7 14.2 %collective-permute-start.14 = (bf16[256,576]{0,1:T(8,128)(2,1)S(1)}, bf16[256,576]{0,1:T(8,128)(2,1)S(1)}, u32[]{:S(2)}, u32[]{:S(2)}) collective-permute-start(bf16[256,576]{0,1:T(8,128)(2,1)S(1)} %collective-permute-done.13), channel_id=1, source_target_pairs={{0,1},{1,2},{2,3},{3,4},{4,5},{5,6},{6,7},{7,0},{8,9},{9,10},{10,1... | collective-permute-start | bytes 884744 | tf_op jit(solution)/shard_map/ppermute | solution.py:22
  73.7 7.7 %collective-permute-start.5 = (bf16[256,256]{1,0:T(8,128)(2,1)S(1)}, bf16[256,256]{1,0:T(8,128)(2,1)S(1)}, u32[]{:S(2)}, u32[]{:S(2)}) collective-permute-start(bf16[256,256]{1,0:T(8,128)(2,1)S(1)} %collective-permute-done.4), channel_id=1, source_target_pairs={{0,16},{8,24},{16,32},{24,40},{32,48},{40,56},{48,64},{56,72},{64,... | collective-permute-start | bytes 393224 | tf_op jit(solution)/shard_map/ppermute | solution.py:17
  81.4 7.5 %collective-permute-start.6 = (bf16[256,256]{1,0:T(8,128)(2,1)S(1)}, bf16[256,256]{1,0:T(8,128)(2,1)S(1)}, u32[]{:S(2)}, u32[]{:S(2)}) collective-permute-start(bf16[256,256]{1,0:T(8,128)(2,1)S(1)} %collective-permute-done.5), channel_id=1, source_target_pairs={{0,16},{8,24},{16,32},{24,40},{32,48},{40,56},{48,64},{56,72},{64,... | collective-permute-start | bytes 393224 | tf_op jit(solution)/shard_map/ppermute | solution.py:17
  86.0 13.9 %collective-permute-start.15 = (bf16[256,576]{0,1:T(8,128)(2,1)S(1)}, bf16[256,576]{0,1:T(8,128)(2,1)S(1)}, u32[]{:S(2)}, u32[]{:S(2)}) collective-permute-start(bf16[256,576]{0,1:T(8,128)(2,1)S(1)} %collective-permute-done.14), channel_id=1, source_target_pairs={{0,1},{1,2},{2,3},{3,4},{4,5},{5,6},{6,7},{7,0},{8,9},{9,10},{10,1... | collective-permute-start | bytes 884744 | tf_op jit(solution)/shard_map/ppermute | solution.py:22
  88.9 8.1 %collective-permute-start.7 = (bf16[256,256]{1,0:T(8,128)(2,1)S(1)}, bf16[256,256]{1,0:T(8,128)(2,1)S(1)}, u32[]{:S(2)}, u32[]{:S(2)}) collective-permute-start(bf16[256,256]{1,0:T(8,128)(2,1)S(1)} %collective-permute-done.6), channel_id=1, source_target_pairs={{0,16},{8,24},{16,32},{24,40},{32,48},{40,56},{48,64},{56,72},{64,... | collective-permute-start | bytes 393224 | tf_op jit(solution)/shard_map/ppermute | solution.py:17
  97.7 4.9 %collective-permute-start.8 = (bf16[9,256,256]{2,1,0:T(8,128)(2,1)}, bf16[9,256,256]{2,1,0:T(8,128)(2,1)S(1)}, u32[]{:S(2)}, u32[]{:S(2)}) collective-permute-start(bf16[9,256,256]{2,1,0:T(8,128)(2,1)} %get-tuple-element.22), channel_id=1, source_target_pairs={{0,8},{8,0},{16,24},{24,16},{32,40},{40,32},{48,56},{56,48},{64,72... | collective-permute-start | bytes 3538952 | tf_op jit(solution)/shard_map/ppermute | solution.py:122
  100.1 3.7 %copy-start.2 = (bf16[256,2,128]{2,1,0:T(2,128)(2,1)S(1)}, bf16[256,2,128]{2,1,0:T(2,128)(2,1)}, u32[]{:S(2)}) copy-start(bf16[256,2,128]{2,1,0:T(2,128)(2,1)} %reshape.267) | copy-start | bytes 393220
  113.1 6.3 %slice-start = ((s8[9437184]{0:T(1024)(128)(4,1)}), s8[4194304]{0:T(1024)(128)(4,1)S(1)}, s32[]{:S(2)}) async-start(s8[9437184]{0:T(1024)(128)(4,1)} %bitcast.176), calls=%async_computation.1 | async-start | bytes 8388608
  113.1 6.6 %slice-start.1 = ((s8[9437184]{0:T(1024)(128)(4,1)}), s8[4194304]{0:T(1024)(128)(4,1)S(1)}, s32[]{:S(2)}) async-start(s8[9437184]{0:T(1024)(128)(4,1)} %bitcast.176), calls=%async_computation.2 | async-start | bytes 8388608
  113.1 6.8 %slice-start.2 = ((s8[9437184]{0:T(1024)(128)(4,1)}), s8[1048576]{0:T(1024)(128)(4,1)S(1)}, s32[]{:S(2)}) async-start(s8[9437184]{0:T(1024)(128)(4,1)} %bitcast.176), calls=%async_computation.3 | async-start | bytes 2097152
  124.5 2.2 copy-start.3
  131.5 8.4 %collective-permute-start.18 = (f32[8,256,256]{2,1,0:T(8,128)S(1)}, f32[8,256,256]{2,1,0:T(8,128)S(1)}, u32[]{:S(2)}, u32[]{:S(2)}) collective-permute-start(f32[8,256,256]{2,1,0:T(8,128)S(1)} %bitcast.180), channel_id=1, source_target_pairs={{0,8},{8,0},{16,24},{24,16},{32,40},{40,32},{48,56},{56,48},{64,72... | collective-permute-start | bytes 6291464 | tf_op jit(solution)/shard_map/ppermute | solution.py:156
  133.6 4.3 %collective-permute-start.16 = (f32[256,256]{1,0:T(8,128)S(1)}, f32[256,256]{1,0:T(8,128)S(1)}, u32[]{:S(2)}, u32[]{:S(2)}) collective-permute-start(f32[256,256]{1,0:T(8,128)S(1)} %slice.97), channel_id=1, source_target_pairs={{0,8},{8,0},{16,24},{24,16},{32,40},{40,32},{48,56},{56,48},{64,72... | collective-permute-start | bytes 786440 | tf_op jit(solution)/shard_map/ppermute | solution.py:155
  138.0 12.2 %collective-permute-start.17 = (f32[256,256]{1,0:T(8,128)S(1)}, f32[256,256]{1,0:T(8,128)S(1)}, u32[]{:S(2)}, u32[]{:S(2)}) collective-permute-start(f32[256,256]{1,0:T(8,128)S(1)} %slice_add_fusion), channel_id=1, source_target_pairs={{16,0},{24,8},{32,16},{40,24},{48,32},{56,40},{64,48},{72,56},{80,... | collective-permute-start | bytes 786440 | tf_op jit(solution)/shard_map/ppermute | solution.py:17
  139.9 62.4 %copy-start.1 = (bf16[1,256,576]{1,2,0:T(8,128)(2,1)S(1)}, bf16[1,256,576]{1,2,0:T(8,128)(2,1)}, u32[]{:S(2)}) copy-start(bf16[1,256,576]{1,2,0:T(8,128)(2,1)} %param.7) | copy-start | bytes 884740
  150.2 10.9 %collective-permute-start.19 = (f32[256,256]{1,0:T(8,128)S(1)}, f32[256,256]{1,0:T(8,128)S(1)}, u32[]{:S(2)}, u32[]{:S(2)}) collective-permute-start(f32[256,256]{1,0:T(8,128)S(1)} %fusion.25), channel_id=1, source_target_pairs={{16,0},{24,8},{32,16},{40,24},{48,32},{56,40},{64,48},{72,56},{80,... | collective-permute-start | bytes 786440 | tf_op jit(solution)/shard_map/ppermute | solution.py:17
  161.1 10.0 %collective-permute-start.20 = (f32[256,256]{1,0:T(8,128)S(1)}, f32[256,256]{1,0:T(8,128)S(1)}, u32[]{:S(2)}, u32[]{:S(2)}) collective-permute-start(f32[256,256]{1,0:T(8,128)S(1)} %fusion.24), channel_id=1, source_target_pairs={{16,0},{24,8},{32,16},{40,24},{48,32},{56,40},{64,48},{72,56},{80,... | collective-permute-start | bytes 786440 | tf_op jit(solution)/shard_map/ppermute | solution.py:17
  171.2 9.5 %collective-permute-start.21 = (f32[256,256]{1,0:T(8,128)S(1)}, f32[256,256]{1,0:T(8,128)S(1)}, u32[]{:S(2)}, u32[]{:S(2)}) collective-permute-start(f32[256,256]{1,0:T(8,128)S(1)} %fusion.23), channel_id=1, source_target_pairs={{16,0},{24,8},{32,16},{40,24},{48,32},{56,40},{64,48},{72,56},{80,... | collective-permute-start | bytes 786440 | tf_op jit(solution)/shard_map/ppermute | solution.py:17
  173.2 7.5 %collective-permute-start.22 = (bf16[256,256]{1,0:T(8,128)(2,1)S(1)}, bf16[256,256]{1,0:T(8,128)(2,1)S(1)}, u32[]{:S(2)}, u32[]{:S(2)}) collective-permute-start(bf16[256,256]{1,0:T(8,128)(2,1)S(1)} %copy.26), channel_id=1, source_target_pairs={{192,0},{384,192},{576,384},{193,1},{385,193},{577,385},{194,2},{3... | collective-permute-start | bytes 393224 | tf_op jit(solution)/shard_map/ppermute | solution.py:17
  180.7 9.5 %collective-permute-start.23 = (f32[256,256]{1,0:T(8,128)S(1)}, f32[256,256]{1,0:T(8,128)S(1)}, u32[]{:S(2)}, u32[]{:S(2)}) collective-permute-start(f32[256,256]{1,0:T(8,128)S(1)} %fusion.22), channel_id=1, source_target_pairs={{16,0},{24,8},{32,16},{40,24},{48,32},{56,40},{64,48},{72,56},{80,... | collective-permute-start | bytes 786440 | tf_op jit(solution)/shard_map/ppermute | solution.py:17
  190.2 9.5 %collective-permute-start.24 = (f32[256,256]{1,0:T(8,128)S(1)}, f32[256,256]{1,0:T(8,128)S(1)}, u32[]{:S(2)}, u32[]{:S(2)}) collective-permute-start(f32[256,256]{1,0:T(8,128)S(1)} %fusion.21), channel_id=1, source_target_pairs={{16,0},{24,8},{32,16},{40,24},{48,32},{56,40},{64,48},{72,56},{80,... | collective-permute-start | bytes 786440 | tf_op jit(solution)/shard_map/ppermute | solution.py:17
  192.2 8.3 %collective-permute-start.25 = (f32[256,256]{1,0:T(8,128)S(1)}, f32[256,256]{1,0:T(8,128)S(1)}, u32[]{:S(2)}, u32[]{:S(2)}) collective-permute-start(f32[256,256]{1,0:T(8,128)S(1)} %slice_bitcast_fusion.6), channel_id=1, source_target_pairs={{192,0},{384,192},{576,384},{193,1},{385,193},{577,385},{194,2},{3... | collective-permute-start | bytes 786440 | tf_op jit(solution)/shard_map/ppermute | solution.py:17
  200.4 10.3 %collective-permute-start.26 = (f32[256,256]{1,0:T(8,128)S(1)}, f32[256,256]{1,0:T(8,128)S(1)}, u32[]{:S(2)}, u32[]{:S(2)}) collective-permute-start(f32[256,256]{1,0:T(8,128)S(1)} %fusion.20), channel_id=1, source_target_pairs={{16,0},{24,8},{32,16},{40,24},{48,32},{56,40},{64,48},{72,56},{80,... | collective-permute-start | bytes 786440 | tf_op jit(solution)/shard_map/ppermute | solution.py:17
  202.4 11.4 %collective-permute-start.28 = (bf16[256,576]{0,1:T(8,128)(2,1)S(1)}, bf16[256,576]{0,1:T(8,128)(2,1)S(1)}, u32[]{:S(2)}, u32[]{:S(2)}) collective-permute-start(bf16[256,576]{0,1:T(8,128)(2,1)S(1)} %bitcast.184), channel_id=1, source_target_pairs={{192,0},{384,192},{576,384},{193,1},{385,193},{577,385},{194,2},{3... | collective-permute-start | bytes 884744 | tf_op jit(solution)/shard_map/ppermute | solution.py:17
  210.7 10.7 %collective-permute-start.27 = (f32[256,256]{1,0:T(8,128)S(1)}, f32[256,256]{1,0:T(8,128)S(1)}, u32[]{:S(2)}, u32[]{:S(2)}) collective-permute-start(f32[256,256]{1,0:T(8,128)S(1)} %fusion.19), channel_id=1, source_target_pairs={{208,0},{216,8},{224,16},{232,24},{240,32},{248,40},{256,48},{264,... | collective-permute-start | bytes 786440 | tf_op jit(solution)/shard_map/ppermute | solution.py:170
Sparse Core Ops, SparseCore 0:
  21.1 58.9 all-gather.2
